TPU v7x, 32 devices: a whole 2x2x4 slice. The times are simulated.
32 devices in a mesh: gx: 8 (over z, x), gy: 4 (over y, core).
Axes of the slice: x: 2, y: 2, z: 4, core: 2. Of those that a mesh axis runs over, the one named last changes fastest.
Arguments:
- fields: bfloat16 [4, 64, 128, 256], P(None, 'gx', 'gy'), may hold values from -6 to 6
- rows_live: int32 [8], replicated, may hold values from 4 to 8, as said below
- cols_live: int32 [4], replicated, may hold values from 16 to 32, as said below
- weight: bfloat16 [32, 108], replicated, may hold values from -0.625 to 0.625
- bias: float32 [32], replicated, may hold values from -3 to 3
- grad_out: bfloat16 [32, 32, 64, 128], P('gy', 'gx'), may hold values from -0.0625 to 0.0625
Outputs:
- stem: bfloat16 [32, 32, 64, 128], P('gy', 'gx')
- weight_grad: float32 [32, 108], P('gy')
- bias_grad: float32 [32], P('gy')
Inputs may be any that keep to these rules, and one draw needn't show every extreme that they name: `rows_live`: every entry is even, and some entry equals 8. `cols_live`: every entry is even, and some entry equals 32.
All inputs are finite; a program needn't handle non-finite values.
Results may differ from a plain program's by a relative error of at most 0.0054.
Values may be sent and summed in bfloat16 or wider, within the bound.
No kernel may reach another device: no remote copies, remote signals or barrier semaphores. Data moves between devices by JAX's collectives and lax.ppermute only.
A program may use at most 64 MiB of HBM per device.

v0:
```python
import jax
import jax.numpy as jnp
from jax import lax
from jax.sharding import PartitionSpec as P


def from_behind(block, axis, distance):
    devices = range(lax.axis_size(axis))
    route = [(i - distance, i) for i in devices if i - distance in devices]
    return lax.ppermute(block, axis, route)


def extend(data, border, count, dim):
    length = data.shape[dim]
    border_wide = jnp.expand_dims(border, dim)
    joined = jnp.concatenate([jnp.zeros_like(border_wide), data], axis=dim)
    shape = [1] * joined.ndim
    shape[dim] = length + 1
    places = jnp.arange(length + 1, dtype=jnp.int32).reshape(shape)
    edge_at = length - count
    kept = jnp.where(places > edge_at, joined, jnp.zeros_like(joined))
    return jnp.where(places == edge_at, border_wide, kept)


def taps(padded, axes, halves):
    pieces = []
    for off_x in range(3):
        for off_y in range(3):
            for off_z in range(3):
                piece = padded
                for axis_no, offset, half in zip(axes, (off_x, off_y, off_z), halves):
                    piece = lax.slice_in_dim(piece, offset, offset + 2 * half - 1, 2, axis_no)
                pieces.append(piece)
    return pieces


def local(fields, rows_live, cols_live, weight, bias, grad_out):
    in_chans, cap_x, cap_y, depth = fields.shape
    half_x = cap_x // 2
    half_y = cap_y // 2
    half_z = depth // 2
    out_chans = weight.shape[0]
    tiles_y = lax.axis_size("gy")
    row_count = rows_live[lax.axis_index("gx")]
    above = from_behind(fields[:, cap_x - 1], "gx", 1)
    ext_rows = extend(fields, above, row_count, 1)
    row_ok = jnp.arange(half_x, dtype=jnp.int32) >= half_x - row_count // 2
    col_count = cols_live[lax.axis_index("gy")]
    beside = from_behind(ext_rows[:, :, cap_y - 1], "gy", 1)
    ext_full = extend(ext_rows, beside, col_count, 2)
    padded = jnp.pad(ext_full, ((0, 0), (0, 0), (0, 0), (1, 0)))
    patches = jnp.stack(taps(padded, (1, 2, 3), (half_x, half_y, half_z)), axis=1).reshape(
        in_chans * 27, -1
    )
    conv = jnp.dot(weight, patches, preferred_element_type=jnp.float32) + bias[:, None]
    col_ok = jnp.arange(half_y, dtype=jnp.int32) >= half_y - col_count // 2
    live = (row_ok[:, None] & col_ok[None, :]).reshape(1, half_x, half_y, 1)
    conv = conv.reshape(out_chans, half_x, half_y, half_z)
    pre_local = jnp.where(live, conv, 0.0).astype(jnp.bfloat16)
    regrouped = lax.all_to_all(pre_local, "gy", split_axis=0, concat_axis=2, tiled=True)
    pre_wide = regrouped.astype(jnp.float32)
    sigma = jax.nn.sigmoid(pre_wide)
    stem = (pre_wide * sigma).astype(jnp.bfloat16)
    wide_cols = jnp.arange(half_y, dtype=jnp.int32)[None, :] >= half_y - (cols_live // 2)[:, None]
    wide_live = row_ok.reshape(1, half_x, 1, 1) & wide_cols.reshape(1, 1, tiles_y * half_y, 1)
    slope = sigma * (1.0 + pre_wide * (1.0 - sigma))
    grad_pre = jnp.where(wide_live, grad_out.astype(jnp.float32) * slope, 0.0).astype(jnp.bfloat16)
    returned = lax.all_to_all(grad_pre, "gy", split_axis=2, concat_axis=0, tiled=True)
    flat = returned.reshape(out_chans, -1)
    weight_full = lax.dot_general(
        flat, patches, (((1,), (1,)), ((), ())), preferred_element_type=jnp.float32
    )
    bias_full = jnp.sum(flat.astype(jnp.float32), axis=1)
    weight_part, bias_part = (
        lax.psum_scatter(weight_full, "gy", scatter_dimension=0, tiled=True),
        lax.psum_scatter(bias_full, "gy", scatter_dimension=0, tiled=True),
    )
    weight_grad, bias_grad = lax.psum((weight_part, bias_part), "gx")
    return (stem, weight_grad, bias_grad)


def solution(mesh):
    in_specs = (P(None, "gx", "gy", None), P(), P(), P(), P(), P("gy", "gx", None, None))
    out_specs = (P("gy", "gx", None, None), P("gy", None), P("gy"))
    return jax.shard_map(local, mesh=mesh, in_specs=in_specs, out_specs=out_specs, check_vma=False)
```

profile of v0, /device:TPU:0, one launch (start us, length us, event | category | flops | bytes accessed | tf_op | source)
XLA Modules:
  0.0 160.4 jit_solution(18269219123622887395)
XLA Ops:
  0.6 0.9 slice_bitcast_fusion
  1.5 4.9 %collective-permute-start = (bf16[4,32,256]{2,1,0:T(8,128)(2,1)S(1)}, bf16[4,32,256]{2,1,0:T(8,128)(2,1)S(1)}, u32[]{:S(2)}, u32[]{:S(2)}) collective-permute-start(bf16[4,32,256]{2,1,0:T(8,128)(2,1)S(1)} %slice_bitcast_fusion), channel_id=1, source_target_pairs={{0,4},{4,8},{8,12},{12,16},{16,20},{20,24},{24,28},{1,5},{5,9},{9,... | collective-permute-start | bytes 196616 | tf_op jit(solution)/shard_map/ppermute | solution.py:10
  6.4 1.2 dynamic_slice.7
  10.2 1.2 dynamic_slice.6
  14.7 0.7 fusion.10
  16.2 1.2 select_select_fusion.1
  17.4 1.5 collective-permute-start.1
  18.9 0.8 collective-permute-done.1
  19.7 0.5 select_select_fusion
  20.2 0.6 pad_slice_fusion
  20.8 0.4 slice.202
  21.1 2.5 %slice.205 = bf16[4,4,16,128]{3,2,1,0:T(8,128)(2,1)S(1)} slice(bf16[4,4,16,257]{3,2,1,0:T(8,128)(2,1)S(1)} %slice.202), slice={[0:4:1], [0:4:1], [0:16:1], [2:257:2]} | slice | bytes 131072 | tf_op jit(solution)/shard_map/slice | solution.py:32
  23.7 2.5 %slice.204 = bf16[4,4,16,128]{3,2,1,0:T(8,128)(2,1)S(1)} slice(bf16[4,4,16,257]{3,2,1,0:T(8,128)(2,1)S(1)} %slice.202), slice={[0:4:1], [0:4:1], [0:16:1], [1:256:2]} | slice | bytes 131072 | tf_op jit(solution)/shard_map/slice | solution.py:32
  26.2 2.5 %slice.203 = bf16[4,4,16,128]{3,2,1,0:T(8,128)(2,1)S(1)} slice(bf16[4,4,16,257]{3,2,1,0:T(8,128)(2,1)S(1)} %slice.202), slice={[0:4:1], [0:4:1], [0:16:1], [0:255:2]} | slice | bytes 131072 | tf_op jit(solution)/shard_map/slice | solution.py:32
  28.8 0.3 slice.198
  29.1 0.3 slice.194
  29.4 2.5 %slice.197 = bf16[4,4,16,128]{3,2,1,0:T(8,128)(2,1)S(1)} slice(bf16[4,4,16,257]{3,2,1,0:T(8,128)(2,1)S(1)} %slice.194), slice={[0:4:1], [0:4:1], [0:16:1], [2:257:2]} | slice | bytes 131072 | tf_op jit(solution)/shard_map/slice | solution.py:32
  31.9 2.5 %slice.196 = bf16[4,4,16,128]{3,2,1,0:T(8,128)(2,1)S(1)} slice(bf16[4,4,16,257]{3,2,1,0:T(8,128)(2,1)S(1)} %slice.194), slice={[0:4:1], [0:4:1], [0:16:1], [1:256:2]} | slice | bytes 131072 | tf_op jit(solution)/shard_map/slice | solution.py:32
  34.5 2.5 %slice.195 = bf16[4,4,16,128]{3,2,1,0:T(8,128)(2,1)S(1)} slice(bf16[4,4,16,257]{3,2,1,0:T(8,128)(2,1)S(1)} %slice.194), slice={[0:4:1], [0:4:1], [0:16:1], [0:255:2]} | slice | bytes 131072 | tf_op jit(solution)/shard_map/slice | solution.py:32
  37.0 2.5 %slice.201 = bf16[4,4,16,128]{3,2,1,0:T(8,128)(2,1)S(1)} slice(bf16[4,4,16,257]{3,2,1,0:T(8,128)(2,1)S(1)} %slice.198), slice={[0:4:1], [0:4:1], [0:16:1], [2:257:2]} | slice | bytes 131072 | tf_op jit(solution)/shard_map/slice | solution.py:32
  39.6 2.5 %slice.200 = bf16[4,4,16,128]{3,2,1,0:T(8,128)(2,1)S(1)} slice(bf16[4,4,16,257]{3,2,1,0:T(8,128)(2,1)S(1)} %slice.198), slice={[0:4:1], [0:4:1], [0:16:1], [1:256:2]} | slice | bytes 131072 | tf_op jit(solution)/shard_map/slice | solution.py:32
  42.1 2.5 %slice.199 = bf16[4,4,16,128]{3,2,1,0:T(8,128)(2,1)S(1)} slice(bf16[4,4,16,257]{3,2,1,0:T(8,128)(2,1)S(1)} %slice.198), slice={[0:4:1], [0:4:1], [0:16:1], [0:255:2]} | slice | bytes 131072 | tf_op jit(solution)/shard_map/slice | solution.py:32
  44.6 0.4 slice.189
  45.0 2.5 %slice.192 = bf16[4,4,16,128]{3,2,1,0:T(8,128)(2,1)S(1)} slice(bf16[4,4,16,257]{3,2,1,0:T(8,128)(2,1)S(1)} %slice.189), slice={[0:4:1], [0:4:1], [0:16:1], [2:257:2]} | slice | bytes 131072 | tf_op jit(solution)/shard_map/slice | solution.py:32
  47.5 2.5 %slice.191 = bf16[4,4,16,128]{3,2,1,0:T(8,128)(2,1)S(1)} slice(bf16[4,4,16,257]{3,2,1,0:T(8,128)(2,1)S(1)} %slice.189), slice={[0:4:1], [0:4:1], [0:16:1], [1:256:2]} | slice | bytes 131072 | tf_op jit(solution)/shard_map/slice | solution.py:32
  50.1 2.5 %slice.190 = bf16[4,4,16,128]{3,2,1,0:T(8,128)(2,1)S(1)} slice(bf16[4,4,16,257]{3,2,1,0:T(8,128)(2,1)S(1)} %slice.189), slice={[0:4:1], [0:4:1], [0:16:1], [0:255:2]} | slice | bytes 131072 | tf_op jit(solution)/shard_map/slice | solution.py:32
  52.6 0.3 slice.185
  52.9 0.3 slice.181
  53.2 2.5 %slice.184 = bf16[4,4,16,128]{3,2,1,0:T(8,128)(2,1)S(1)} slice(bf16[4,4,16,257]{3,2,1,0:T(8,128)(2,1)S(1)} %slice.181), slice={[0:4:1], [0:4:1], [0:16:1], [2:257:2]} | slice | bytes 131072 | tf_op jit(solution)/shard_map/slice | solution.py:32
  55.8 2.5 %slice.183 = bf16[4,4,16,128]{3,2,1,0:T(8,128)(2,1)S(1)} slice(bf16[4,4,16,257]{3,2,1,0:T(8,128)(2,1)S(1)} %slice.181), slice={[0:4:1], [0:4:1], [0:16:1], [1:256:2]} | slice | bytes 131072 | tf_op jit(solution)/shard_map/slice | solution.py:32
  58.3 2.5 %slice.182 = bf16[4,4,16,128]{3,2,1,0:T(8,128)(2,1)S(1)} slice(bf16[4,4,16,257]{3,2,1,0:T(8,128)(2,1)S(1)} %slice.181), slice={[0:4:1], [0:4:1], [0:16:1], [0:255:2]} | slice | bytes 131072 | tf_op jit(solution)/shard_map/slice | solution.py:32
  60.9 2.5 %slice.188 = bf16[4,4,16,128]{3,2,1,0:T(8,128)(2,1)S(1)} slice(bf16[4,4,16,257]{3,2,1,0:T(8,128)(2,1)S(1)} %slice.185), slice={[0:4:1], [0:4:1], [0:16:1], [2:257:2]} | slice | bytes 131072 | tf_op jit(solution)/shard_map/slice | solution.py:32
  63.4 2.5 %slice.187 = bf16[4,4,16,128]{3,2,1,0:T(8,128)(2,1)S(1)} slice(bf16[4,4,16,257]{3,2,1,0:T(8,128)(2,1)S(1)} %slice.185), slice={[0:4:1], [0:4:1], [0:16:1], [1:256:2]} | slice | bytes 131072 | tf_op jit(solution)/shard_map/slice | solution.py:32
  66.0 2.5 %slice.186 = bf16[4,4,16,128]{3,2,1,0:T(8,128)(2,1)S(1)} slice(bf16[4,4,16,257]{3,2,1,0:T(8,128)(2,1)S(1)} %slice.185), slice={[0:4:1], [0:4:1], [0:16:1], [0:255:2]} | slice | bytes 131072 | tf_op jit(solution)/shard_map/slice | solution.py:32
  68.5 0.4 slice.176
  68.9 2.5 %slice.179 = bf16[4,4,16,128]{3,2,1,0:T(8,128)(2,1)S(1)} slice(bf16[4,4,16,257]{3,2,1,0:T(8,128)(2,1)S(1)} %slice.176), slice={[0:4:1], [0:4:1], [0:16:1], [2:257:2]} | slice | bytes 131072 | tf_op jit(solution)/shard_map/slice | solution.py:32
  71.4 2.5 %slice.178 = bf16[4,4,16,128]{3,2,1,0:T(8,128)(2,1)S(1)} slice(bf16[4,4,16,257]{3,2,1,0:T(8,128)(2,1)S(1)} %slice.176), slice={[0:4:1], [0:4:1], [0:16:1], [1:256:2]} | slice | bytes 131072 | tf_op jit(solution)/shard_map/slice | solution.py:32
  73.9 2.5 %slice.177 = bf16[4,4,16,128]{3,2,1,0:T(8,128)(2,1)S(1)} slice(bf16[4,4,16,257]{3,2,1,0:T(8,128)(2,1)S(1)} %slice.176), slice={[0:4:1], [0:4:1], [0:16:1], [0:255:2]} | slice | bytes 131072 | tf_op jit(solution)/shard_map/slice | solution.py:32
  76.5 0.3 slice.172
  76.8 0.3 slice.168
  77.1 2.7 %slice.171 = bf16[4,4,16,128]{3,2,1,0:T(8,128)(2,1)S(1)} slice(bf16[4,4,16,257]{3,2,1,0:T(8,128)(2,1)S(1)} %slice.168), slice={[0:4:1], [0:4:1], [0:16:1], [2:257:2]} | slice | bytes 131072 | tf_op jit(solution)/shard_map/slice | solution.py:32
  79.8 2.5 %slice.170 = bf16[4,4,16,128]{3,2,1,0:T(8,128)(2,1)S(1)} slice(bf16[4,4,16,257]{3,2,1,0:T(8,128)(2,1)S(1)} %slice.168), slice={[0:4:1], [0:4:1], [0:16:1], [1:256:2]} | slice | bytes 131072 | tf_op jit(solution)/shard_map/slice | solution.py:32
  82.4 2.5 %slice.169 = bf16[4,4,16,128]{3,2,1,0:T(8,128)(2,1)S(1)} slice(bf16[4,4,16,257]{3,2,1,0:T(8,128)(2,1)S(1)} %slice.168), slice={[0:4:1], [0:4:1], [0:16:1], [0:255:2]} | slice | bytes 131072 | tf_op jit(solution)/shard_map/slice | solution.py:32
  84.9 2.5 %slice.175 = bf16[4,4,16,128]{3,2,1,0:T(8,128)(2,1)S(1)} slice(bf16[4,4,16,257]{3,2,1,0:T(8,128)(2,1)S(1)} %slice.172), slice={[0:4:1], [0:4:1], [0:16:1], [2:257:2]} | slice | bytes 131072 | tf_op jit(solution)/shard_map/slice | solution.py:32
  87.5 2.5 %slice.174 = bf16[4,4,16,128]{3,2,1,0:T(8,128)(2,1)S(1)} slice(bf16[4,4,16,257]{3,2,1,0:T(8,128)(2,1)S(1)} %slice.172), slice={[0:4:1], [0:4:1], [0:16:1], [1:256:2]} | slice | bytes 131072 | tf_op jit(solution)/shard_map/slice | solution.py:32
  90.0 2.5 %slice.173 = bf16[4,4,16,128]{3,2,1,0:T(8,128)(2,1)S(1)} slice(bf16[4,4,16,257]{3,2,1,0:T(8,128)(2,1)S(1)} %slice.172), slice={[0:4:1], [0:4:1], [0:16:1], [0:255:2]} | slice | bytes 131072 | tf_op jit(solution)/shard_map/slice | solution.py:32
  93.1 1.6 copy.24
  94.6 2.7 %reshape.144 = bf16[108,8192]{1,0:T(8,128)(2,1)S(1)} reshape(bf16[4,27,4,16,128]{4,3,2,1,0:T(8,128)(2,1)} %copy.24) | data formatting | bytes 3538944 | tf_op jit(solution)/shard_map/reshape | solution.py:52
  97.4 0.4 fusion
  97.9 1.0 select_convert_fusion
  98.9 5.6 %all-to-all-start = ((bf16[32,4,16,128]{3,2,1,0:T(8,128)(2,1)}), bf16[32,4,16,128]{3,2,1,0:T(8,128)(2,1)S(1)}, u32[]{:S(2)}, u32[]{:S(2)}) async-start(bf16[32,4,16,128]{3,2,1,0:T(8,128)(2,1)} %select_convert_fusion), calls=%async_computation | async-start | bytes 1048576 | tf_op jit(solution)/shard_map/all_to_all | solution.py:60
  104.7 8.6 %all-to-all-done = bf16[32,4,16,128]{3,2,1,0:T(8,128)(2,1)S(1)} async-done(((bf16[32,4,16,128]{3,2,1,0:T(8,128)(2,1)}), bf16[32,4,16,128]{3,2,1,0:T(8,128)(2,1)S(1)}, u32[]{:S(2)}, u32[]{:S(2)}) %all-to-all-start) | async-done | bytes 524320 | tf_op jit(solution)/shard_map/all_to_all | solution.py:60
  113.3 0.3 copy.25
  113.6 2.4 %fusion.9 = (bf16[8,4,64,128]{3,0,1,2:T(8,128)(2,1)}, bf16[8,4,64,128]{3,0,1,2:T(8,128)(2,1)S(1)}) fusion(f32[4,8,4,16,128]{4,1,2,3,0:T(8,128)S(1)} %copy.25, bf16[8,4,64,128]{3,2,1,0:T(8,128)(2,1)S(1)} %copy-done.1, pred[4,64]{0,1:T(8,128)(4,1)S(1)} %broadcast_and_fusion), kind=kLoop, calls=%fused_computation.16 | loop fusion | flops 3407872 | bytes 2621696 | tf_op jit(solution)/shard_map/convert_element_type | solution.py:67
  116.0 3.5 %all-to-all-start.1 = ((bf16[8,4,64,128]{3,0,1,2:T(8,128)(2,1)}), bf16[8,4,64,128]{3,0,1,2:T(8,128)(2,1)S(1)}, u32[]{:S(2)}, u32[]{:S(2)}) async-start(bf16[8,4,64,128]{3,0,1,2:T(8,128)(2,1)} %get-tuple-element.13), calls=%async_computation.1 | async-start | bytes 1048576 | tf_op jit(solution)/shard_map/all_to_all | solution.py:68
  119.5 0.6 dynamic-slice
  120.7 1.0 copy.28
  121.7 6.5 %all-to-all-done.1 = bf16[8,4,64,128]{3,0,1,2:T(8,128)(2,1)S(1)} async-done(((bf16[8,4,64,128]{3,0,1,2:T(8,128)(2,1)}), bf16[8,4,64,128]{3,0,1,2:T(8,128)(2,1)S(1)}, u32[]{:S(2)}, u32[]{:S(2)}) %all-to-all-start.1) | async-done | bytes 524320 | tf_op jit(solution)/shard_map/all_to_all | solution.py:68
  128.2 0.3 convert_reduce_fusion
  128.5 0.2 copy.35
  128.8 0.2 reshape.146
  129.0 0.7 fusion.11
  129.8 10.3 %all-reduce.6 = (f32[32,108]{1,0:T(8,128)S(1)}, f32[32]{0:T(128)S(1)}) all-reduce(f32[32,108]{1,0:T(8,128)S(1)} %fusion.11, f32[32]{0:T(128)S(1)} %reduce_sum.12), channel_id=2, replica_groups=mesh['gx'=8,'gy'=4] {'gy'}, use_global_device_ids=true, to_apply=%region_0.1.clone | all-reduce | flops 3488 | bytes 27904
  140.1 20.3 %all-reduce.5 = (f32[8,108]{1,0:T(8,128)}, f32[8]{0:T(128)}) all-reduce(f32[8,108]{1,0:T(8,128)S(1)} %constant_dynamic-slice_fusion, f32[8]{0:T(128)S(1)} %dynamic-slice.3), channel_id=1, replica_groups=mesh['gx'=8,'gy'=4] {'gx'}, use_global_device_ids=true, to_apply=%region_1.2 | all-reduce | flops 872 | bytes 6976 | tf_op jit(solution)/shard_map/psum | solution.py:78
  (51 shorter events, 1.1 us)
Async XLA Ops:
  0.6 96.7 %copy-start = (bf16[32,108]{1,0:T(8,128)(2,1)S(1)}, bf16[32,108]{1,0:T(8,128)(2,1)}, u32[]{:S(2)}) copy-start(bf16[32,108]{1,0:T(8,128)(2,1)} %param.9) | copy-start | bytes 20740
  1.5 14.7 %collective-permute-start = (bf16[4,32,256]{2,1,0:T(8,128)(2,1)S(1)}, bf16[4,32,256]{2,1,0:T(8,128)(2,1)S(1)}, u32[]{:S(2)}, u32[]{:S(2)}) collective-permute-start(bf16[4,32,256]{2,1,0:T(8,128)(2,1)S(1)} %slice_bitcast_fusion), channel_id=1, source_target_pairs={{0,4},{4,8},{8,12},{12,16},{16,20},{20,24},{24,28},{1,5},{5,9},{9,... | collective-permute-start | bytes 196616 | tf_op jit(solution)/shard_map/ppermute | solution.py:10
  17.4 2.3 %collective-permute-start.1 = (bf16[4,9,256]{2,0,1:T(4,128)(2,1)S(1)}, bf16[4,9,256]{2,0,1:T(4,128)(2,1)S(1)}, u32[]{:S(2)}, u32[]{:S(2)}) collective-permute-start(bf16[4,9,256]{2,0,1:T(4,128)(2,1)S(1)} %bitcast.116), channel_id=1, source_target_pairs={{0,1},{1,2},{2,3},{4,5},{5,6},{6,7},{8,9},{9,10},{10,11},{12,13},{... | collective-permute-start | bytes 55304 | tf_op jit(solution)/shard_map/ppermute | solution.py:10
  94.6 2.7 %copy-start.2 = (f32[32]{0:T(128)S(1)}, f32[32]{0:T(128)}, u32[]{:S(2)}) copy-start(f32[32]{0:T(128)} %param.10) | copy-start | bytes 388
  97.9 15.7 %copy-start.1 = (bf16[8,4,64,128]{3,2,1,0:T(8,128)(2,1)S(1)}, bf16[8,4,64,128]{3,2,1,0:T(8,128)(2,1)}, u32[]{:S(2)}) copy-start(bf16[8,4,64,128]{3,2,1,0:T(8,128)(2,1)} %param.11) | copy-start | bytes 1572868
  98.9 14.4 %all-to-all-start = ((bf16[32,4,16,128]{3,2,1,0:T(8,128)(2,1)}), bf16[32,4,16,128]{3,2,1,0:T(8,128)(2,1)S(1)}, u32[]{:S(2)}, u32[]{:S(2)}) async-start(bf16[32,4,16,128]{3,2,1,0:T(8,128)(2,1)} %select_convert_fusion), calls=%async_computation | async-start | bytes 1048576 | tf_op jit(solution)/shard_map/all_to_all | solution.py:60
  113.6 5.9 %copy-start.3 = (u32[32]{0:T(128)S(1)}, u32[32]{0:T(128)}, u32[]{:S(2)}) copy-start(u32[32]{0:T(128)} %constant.68) | copy-start | bytes 388
  116.0 12.3 %all-to-all-start.1 = ((bf16[8,4,64,128]{3,0,1,2:T(8,128)(2,1)}), bf16[8,4,64,128]{3,0,1,2:T(8,128)(2,1)S(1)}, u32[]{:S(2)}, u32[]{:S(2)}) async-start(bf16[8,4,64,128]{3,0,1,2:T(8,128)(2,1)} %get-tuple-element.13), calls=%async_computation.1 | async-start | bytes 1048576 | tf_op jit(solution)/shard_map/all_to_all | solution.py:68
where the time goes:
time: 161 us; the launch traced here: 160 us
  local copies, waits for them, and re-layouts  82.8 us (51%)
  blocking collectives  30.6 us (19%)
  waiting for transfers between devices  15.9 us (10%)
  starting transfers between devices  15.4 us (10%)
  between operations  8.42 us (5%)
  other arithmetic  6.2 us (4%)
    slice x37, local copies, waits for them, and re-layouts, taps(): piece = lax.slice_in_dim(piece, offset, offset + 2 * half - 1, 2, axis_no)  72.1 us
    psum x1, blocking collectives, local(): weight_grad, bias_grad = lax.psum((weight_part, bias_part), 'gx')  20.3 us
    unnamed x1, blocking collectives  10.3 us
    all_to_all x1, waiting for transfers between devices, local(): lax.all_to_all(pre_local, 'gy', split_axis=0, concat_axis=2, tiled=True)  8.57 us
    all_to_all x1, waiting for transfers between devices, local(): lax.all_to_all(grad_pre, 'gy', split_axis=2, concat_axis=0, tiled=True)  6.53 us
    ppermute x2, starting transfers between devices, from_behind(): return lax.ppermute(block, axis, route)  6.32 us
    all_to_all x1, starting transfers between devices, local(): lax.all_to_all(pre_local, 'gy', split_axis=0, concat_axis=2, tiled=True)  5.58 us
    all_to_all x1, starting transfers between devices, local(): lax.all_to_all(grad_pre, 'gy', split_axis=2, concat_axis=0, tiled=True)  3.47 us
  transfers between devices with their start and end apart: 4, of which 3 were waited for; matrix products, arithmetic and copies ran while one was open for 3% of the time, Pallas kernels for 0%

commit v1 on v0

--- a/solution.py
+++ b/solution.py
@@ -48,14 +48,15 @@
     col_count = cols_live[lax.axis_index("gy")]
     beside = from_behind(ext_rows[:, :, cap_y - 1], "gy", 1)
     ext_full = extend(ext_rows, beside, col_count, 2)
-    padded = jnp.pad(ext_full, ((0, 0), (0, 0), (0, 0), (1, 0)))
-    patches = jnp.stack(taps(padded, (1, 2, 3), (half_x, half_y, half_z)), axis=1).reshape(
-        in_chans * 27, -1
-    )
-    conv = jnp.dot(weight, patches, preferred_element_type=jnp.float32) + bias[:, None]
+    lhs = ext_full[None]
+    kernel = weight.reshape(out_chans, in_chans, 3, 3, 3)
+    dims = ("NCDHW", "OIDHW", "NCDHW")
+    conv = lax.conv_general_dilated(
+        lhs, kernel, (2, 2, 2), ((0, 0), (0, 0), (1, 0)),
+        dimension_numbers=dims, preferred_element_type=jnp.float32,
+    )[0] + bias[:, None, None, None]
     col_ok = jnp.arange(half_y, dtype=jnp.int32) >= half_y - col_count // 2
     live = (row_ok[:, None] & col_ok[None, :]).reshape(1, half_x, half_y, 1)
-    conv = conv.reshape(out_chans, half_x, half_y, half_z)
     pre_local = jnp.where(live, conv, 0.0).astype(jnp.bfloat16)
     regrouped = lax.all_to_all(pre_local, "gy", split_axis=0, concat_axis=2, tiled=True)
     pre_wide = regrouped.astype(jnp.float32)
@@ -66,16 +67,18 @@
     slope = sigma * (1.0 + pre_wide * (1.0 - sigma))
     grad_pre = jnp.where(wide_live, grad_out.astype(jnp.float32) * slope, 0.0).astype(jnp.bfloat16)
     returned = lax.all_to_all(grad_pre, "gy", split_axis=2, concat_axis=0, tiled=True)
-    flat = returned.reshape(out_chans, -1)
-    weight_full = lax.dot_general(
-        flat, patches, (((1,), (1,)), ((), ())), preferred_element_type=jnp.float32
+    filt = lax.conv_general_dilated(
+        ext_full[:, None], returned[:, None], (1, 1, 1), ((0, 0), (0, 0), (1, 0)),
+        rhs_dilation=(2, 2, 2), dimension_numbers=dims,
+        preferred_element_type=jnp.float32,
     )
-    bias_full = jnp.sum(flat.astype(jnp.float32), axis=1)
-    weight_part, bias_part = (
-        lax.psum_scatter(weight_full, "gy", scatter_dimension=0, tiled=True),
-        lax.psum_scatter(bias_full, "gy", scatter_dimension=0, tiled=True),
-    )
-    weight_grad, bias_grad = lax.psum((weight_part, bias_part), "gx")
+    weight_full = jnp.swapaxes(filt, 0, 1).reshape(out_chans, -1)
+    bias_full = jnp.sum(returned.astype(jnp.float32), axis=(1, 2, 3))
+    packed = jnp.concatenate([weight_full, bias_full[:, None]], axis=1)
+    total = lax.psum(packed, ("gx", "gy"))
+    rows = out_chans // tiles_y
+    mine = lax.dynamic_slice_in_dim(total, lax.axis_index("gy") * rows, rows, 0)
+    weight_grad, bias_grad = mine[:, :-1], mine[:, -1]
     return (stem, weight_grad, bias_grad)
 
 

time: 161 us -> 265 us (1.65)
  matrix products: 1.1 us -> 102 us
  blocking collectives: 30.6 us -> 40.8 us
  waiting for transfers between devices: 15.9 us -> 8.58 us
    transpose x0 -> x1, matrix products: none -> 87.7 us  [local(): weight_full = jnp.swapaxes(filt, 0, 1).reshape(out_chans, -1)]
    slice x37 -> x1, local copies, waits for them, and re-layouts: 72.1 us -> 0.69 us  [local(): weight_grad, bias_grad = (mine[:, :-1], mine[:, -1])]
    broadcast_in_dim x0 -> x4, local copies, waits for them, and re-layouts: none -> 54.6 us  [the longest x1 48.7 us: local(): ext_full[:, None]]
    psum x1, blocking collectives: 20.3 us -> 40.8 us  [local(): total = lax.psum(packed, ('gx', 'gy'))]
    conv_general_dilated x0 -> x5, local copies, waits for them, and re-layouts: none -> 19.2 us  [local(): lax.conv_general_dilated(lhs, kernel, (2, 2, 2), ((0, 0), (0, 0), (1, 0))...]
    conv_general_dilated x0 -> x1, matrix products: none -> 14.1 us  [local(): lax.conv_general_dilated(lhs, kernel, (2, 2, 2), ((0, 0), (0, 0), (1, 0))...]
    unnamed x1 -> x0, blocking collectives: 10.3 us -> none
    all_to_all x1, waiting for transfers between devices: 6.53 us -> 0.01 us  [local(): lax.all_to_all(grad_pre, 'gy', split_axis=2, concat_axis=0, tiled=True)]
  transfers between devices with their start and end apart: 4 -> 4, of which waited for: 3 -> 1; matrix products, arithmetic and copies ran while one was open for 3% -> 20% of each run, Pallas kernels for 0% -> 0%
where the time goes in v1:
time: 265 us
  matrix products  102 us (38%)
  local copies, waits for them, and re-layouts  84.9 us (32%)
  blocking collectives  40.8 us (15%)
  starting transfers between devices  14.9 us (6%)
  waiting for transfers between devices  8.58 us (3%)
  between operations  7.43 us (3%)
  other arithmetic  6.22 us (2%)
    transpose x1, matrix products, local(): weight_full = jnp.swapaxes(filt, 0, 1).reshape(out_chans, -1)  87.7 us
    broadcast_in_dim x1, local copies, waits for them, and re-layouts, local(): ext_full[:, None]  48.7 us
    psum x1, blocking collectives, local(): total = lax.psum(packed, ('gx', 'gy'))  40.8 us
    conv_general_dilated x5, local copies, waits for them, and re-layouts, local(): lax.conv_general_dilated(lhs, kernel, (2, 2, 2), ((0, 0), (0, 0), (1, 0))...  19.2 us
    conv_general_dilated x1, matrix products, local(): lax.conv_general_dilated(lhs, kernel, (2, 2, 2), ((0, 0), (0, 0), (1, 0))...  14.1 us
    all_to_all x1, waiting for transfers between devices, local(): lax.all_to_all(pre_local, 'gy', split_axis=0, concat_axis=2, tiled=True)  8.57 us
    ppermute x2, starting transfers between devices, from_behind(): return lax.ppermute(block, axis, route)  6.32 us
  transfers between devices with their start and end apart: 4, of which 1 were waited for; matrix products, arithmetic and copies ran while one was open for 20% of the time, Pallas kernels for 0%

profile of v1, /device:TPU:0, one launch (start us, length us, event | category | flops | bytes accessed | tf_op | source)
XLA Modules:
  0.0 264.5 jit_solution(15220797202595424917)
XLA Ops:
  0.6 0.9 slice_bitcast_fusion
  1.5 4.9 %collective-permute-start = (bf16[4,32,256]{2,1,0:T(8,128)(2,1)S(1)}, bf16[4,32,256]{2,1,0:T(8,128)(2,1)S(1)}, u32[]{:S(2)}, u32[]{:S(2)}) collective-permute-start(bf16[4,32,256]{2,1,0:T(8,128)(2,1)S(1)} %slice_bitcast_fusion), channel_id=1, source_target_pairs={{0,4},{4,8},{8,12},{12,16},{16,20},{20,24},{24,28},{1,5},{5,9},{9,... | collective-permute-start | bytes 196616 | tf_op jit(solution)/shard_map/ppermute | solution.py:10
  6.4 1.2 dynamic_slice.10
  10.2 1.2 dynamic_slice.9
  14.7 0.7 fusion.20
  16.1 0.1 broadcast_and_fusion.1
  16.1 0.0 collective-permute-done
  16.1 1.2 select_select_fusion.1
  17.4 1.5 collective-permute-start.1
  18.9 0.8 copy.105
  19.7 0.7 reshape.142
  20.4 0.0 collective-permute-done.1
  20.4 0.0 copy-start.6
  20.4 1.3 fusion.24
  21.7 0.5 pad.2
  22.2 2.2 reshape.158
  24.4 0.0 copy-start.3
  24.4 12.6 %copy.104 = bf16[4,9,33,1,8,34]{4,0,5,2,1,3:T(4,128)(2,1)} copy(bf16[4,9,33,1,8,34]{5,4,2,1,0,3:T(8,128)(2,1)S(1)} %reshape.158) | data formatting | bytes 1292544 | tf_op jit(solution)/shard_map/conv_general_dilated | solution.py:54
  37.0 1.5 slice.19
  38.5 0.0 copy-done.6
  38.5 0.0 copy-done.3
  38.5 14.1 %broadcast_select_fusion = f32[4,16,8,17,32]{4,2,3,1,0:T(8,128)S(1)} fusion(pred[8,17]{0,1:T(8,128)(4,1)S(1)} %copy-done.6, bf16[4,9,33,1,7,2]{4,0,5,2,1,3:T(4,128)(2,1)S(1)} %slice.19, bf16[4,9,33,1,8,34]{4,0,5,2,1,3:T(4,128)(2,1)} %copy.104, bf16[32,4,3,3,3]{0,4,3,2,1:T(4,128)(2,1)S(1)} %copy-done.3), kind=kOutput, calls=%fused_computation.6 | convolution fusion | flops 62493440 | bytes 1800696 | tf_op jit(solution)/shard_map/conv_general_dilated | solution.py:54
  52.6 0.0 copy-start.5
  52.6 0.8 copy.107
  53.4 0.0 copy-start.1
  53.4 0.0 copy-start
  53.4 2.2 slice.20
  55.6 3.5 %copy.121 = f32[4,16,1,128,32]{3,1,0,4,2:T(8,128)S(1)} copy(f32[4,16,1,128,32]{4,1,3,0,2:T(8,128)} %slice.20) | data formatting | bytes 2097152
  59.2 0.0 copy-done.5
  59.2 1.1 fusion.9
  60.2 4.9 %all-to-all-start = ((bf16[32,4,16,128]{3,2,1,0:T(8,128)(2,1)}), bf16[32,4,16,128]{3,2,1,0:T(8,128)(2,1)S(1)}, u32[]{:S(2)}, u32[]{:S(2)}) async-start(bf16[32,4,16,128]{3,2,1,0:T(8,128)(2,1)} %fusion.9), calls=%async_computation | async-start | bytes 1048576 | tf_op jit(solution)/shard_map/all_to_all | solution.py:61
  65.1 0.1 iota_compare_fusion.1
  65.2 0.1 ge.51
  65.3 0.1 broadcast_and_fusion
  65.4 8.6 %all-to-all-done = bf16[32,4,16,128]{3,2,1,0:T(8,128)(2,1)S(1)} async-done(((bf16[32,4,16,128]{3,2,1,0:T(8,128)(2,1)}), bf16[32,4,16,128]{3,2,1,0:T(8,128)(2,1)S(1)}, u32[]{:S(2)}, u32[]{:S(2)}) %all-to-all-start) | async-done | bytes 524320 | tf_op jit(solution)/shard_map/all_to_all | solution.py:61
  74.0 0.1 convert_bitcast_fusion
  74.1 0.1 copy.109
  74.2 0.0 copy-done.1
  74.2 1.3 fusion.18
  75.5 1.2 copy.110
  76.7 3.6 %all-to-all-start.1 = ((bf16[8,4,64,128]{3,1,0,2:T(4,128)(2,1)}), bf16[8,4,64,128]{3,1,0,2:T(4,128)(2,1)S(1)}, u32[]{:S(2)}, u32[]{:S(2)}) async-start(bf16[8,4,64,128]{3,1,0,2:T(4,128)(2,1)} %copy.110), calls=%async_computation.1 | async-start | bytes 1048576 | tf_op jit(solution)/shard_map/all_to_all | solution.py:69
  80.4 0.0 copy-done
  80.4 48.7 %copy.113 = bf16[4,1,9,33,256]{0,1,4,3,2:T(2,128)(2,1)} copy(bf16[4,1,9,33,256]{4,3,2,0,1:T(8,128)(2,1)S(1)} %copy-done) | data formatting | bytes 1216512 | tf_op jit(solution)/shard_map/broadcast_in_dim | solution.py:71
  129.1 0.0 all-to-all-done.1
  129.1 0.2 copy.111
  129.3 0.2 convert_reduce_fusion
  129.5 0.1 copy.112
  129.6 0.1 copy.116
  129.7 0.7 broadcast_in_dim.115
  130.4 4.8 %copy.114 = bf16[32,1,4,16,128]{0,1,4,3,2:T(2,128)(2,1)} copy(bf16[32,1,4,16,128]{4,3,2,0,1:T(8,128)(2,1)S(1)} %bitcast.72) | data formatting | bytes 1048576 | tf_op jit(solution)/shard_map/broadcast_in_dim | solution.py:71
  135.1 0.0 copy-start.2
  135.1 87.7 %fusion.26 = f32[32,4,3,3,3]{0,1,4,3,2:T(4,128)S(1)} fusion(bf16[4,1,9,33,256]{0,1,4,3,2:T(2,128)(2,1)} %copy.113, bf16[32,1,4,16,128]{0,1,4,3,2:T(2,128)(2,1)} %copy.114), kind=kOutput, calls=%fused_computation.51 | convolution fusion | flops 56475648 | bytes 1146368 | tf_op jit(solution)/shard_map/transpose | solution.py:75
  222.9 0.1 copy.117
  222.9 0.0 copy-done.2
  222.9 0.1 pad_maximum_fusion
  223.0 40.8 %psum.7 = f32[32,109]{1,0:T(8,128)S(1)} all-reduce(f32[32,109]{1,0:T(8,128)S(1)} %pad_maximum_fusion), channel_id=1, replica_groups=mesh['gx'=8,'gy'=4] {'gx','gy'}, use_global_device_ids=true, to_apply=%region_1.2 | all-reduce | flops 3488 | bytes 27904 | tf_op jit(solution)/shard_map/psum | solution.py:78
  263.8 0.0 copy-start.4
  263.8 0.7 slice_reduce_fusion
  264.5 0.0 copy-done.4
  (10 shorter events, 0.1 us)
Async XLA Ops:
  1.5 14.7 %collective-permute-start = (bf16[4,32,256]{2,1,0:T(8,128)(2,1)S(1)}, bf16[4,32,256]{2,1,0:T(8,128)(2,1)S(1)}, u32[]{:S(2)}, u32[]{:S(2)}) collective-permute-start(bf16[4,32,256]{2,1,0:T(8,128)(2,1)S(1)} %slice_bitcast_fusion), channel_id=1, source_target_pairs={{0,4},{4,8},{8,12},{12,16},{16,20},{20,24},{24,28},{1,5},{5,9},{9,... | collective-permute-start | bytes 196616 | tf_op jit(solution)/shard_map/ppermute | solution.py:10
  17.4 3.0 %collective-permute-start.1 = (bf16[4,9,256]{2,0,1:T(4,128)(2,1)S(1)}, bf16[4,9,256]{2,0,1:T(4,128)(2,1)S(1)}, u32[]{:S(2)}, u32[]{:S(2)}) collective-permute-start(bf16[4,9,256]{2,0,1:T(4,128)(2,1)S(1)} %bitcast.73), channel_id=1, source_target_pairs={{0,1},{1,2},{2,3},{4,5},{5,6},{6,7},{8,9},{9,10},{10,11},{12,13},{... | collective-permute-start | bytes 55304 | tf_op jit(solution)/shard_map/ppermute | solution.py:10
  20.4 18.1 %copy-start.6 = (pred[8,17]{0,1:T(8,128)(4,1)S(1)}, pred[8,17]{0,1:T(8,128)(4,1)}, u32[]{:S(2)}) copy-start(pred[8,17]{0,1:T(8,128)(4,1)} %constant.67) | copy-start | bytes 412
  24.4 14.1 %copy-start.3 = (bf16[32,4,3,3,3]{0,4,3,2,1:T(4,128)(2,1)S(1)}, bf16[32,4,3,3,3]{0,4,3,2,1:T(4,128)(2,1)}, u32[]{:S(2)}) copy-start(bf16[32,4,3,3,3]{0,4,3,2,1:T(4,128)(2,1)} %reshape.142) | copy-start | bytes 20740
  52.6 6.6 %copy-start.5 = (f32[32]{0:T(128)S(1)}, f32[32]{0:T(128)}, u32[]{:S(2)}) copy-start(f32[32]{0:T(128)} %param.10) | copy-start | bytes 388
  53.4 20.8 %copy-start.1 = (bf16[8,4,64,128]{3,2,1,0:T(8,128)(2,1)S(1)}, bf16[8,4,64,128]{3,2,1,0:T(8,128)(2,1)}, u32[]{:S(2)}) copy-start(bf16[8,4,64,128]{3,2,1,0:T(8,128)(2,1)} %param.11) | copy-start | bytes 1572868
  53.4 27.0 %copy-start = (bf16[4,1,9,33,256]{4,3,2,0,1:T(8,128)(2,1)S(1)}, bf16[4,1,9,33,256]{4,3,2,0,1:T(8,128)(2,1)}, u32[]{:S(2)}) copy-start(bf16[4,1,9,33,256]{4,3,2,0,1:T(8,128)(2,1)} %get-tuple-element.11) | copy-start | bytes 1824772
  60.2 13.7 %all-to-all-start = ((bf16[32,4,16,128]{3,2,1,0:T(8,128)(2,1)}), bf16[32,4,16,128]{3,2,1,0:T(8,128)(2,1)S(1)}, u32[]{:S(2)}, u32[]{:S(2)}) async-start(bf16[32,4,16,128]{3,2,1,0:T(8,128)(2,1)} %fusion.9), calls=%async_computation | async-start | bytes 1048576 | tf_op jit(solution)/shard_map/all_to_all | solution.py:61
  76.7 52.4 %all-to-all-start.1 = ((bf16[8,4,64,128]{3,1,0,2:T(4,128)(2,1)}), bf16[8,4,64,128]{3,1,0,2:T(4,128)(2,1)S(1)}, u32[]{:S(2)}, u32[]{:S(2)}) async-start(bf16[8,4,64,128]{3,1,0,2:T(4,128)(2,1)} %copy.110), calls=%async_computation.1 | async-start | bytes 1048576 | tf_op jit(solution)/shard_map/all_to_all | solution.py:69
  135.1 87.8 %copy-start.2 = (f32[32,1]{1,0:T(8,128)S(1)}, f32[32,1]{1,0:T(8,128)}, u32[]{:S(2)}) copy-start(f32[32,1]{1,0:T(8,128)} %broadcast_in_dim.115) | copy-start | bytes 388
  263.8 0.7 copy-start.4

commit v2 on v0

--- a/solution.py
+++ b/solution.py
@@ -48,14 +48,23 @@
     col_count = cols_live[lax.axis_index("gy")]
     beside = from_behind(ext_rows[:, :, cap_y - 1], "gy", 1)
     ext_full = extend(ext_rows, beside, col_count, 2)
-    padded = jnp.pad(ext_full, ((0, 0), (0, 0), (0, 0), (1, 0)))
-    patches = jnp.stack(taps(padded, (1, 2, 3), (half_x, half_y, half_z)), axis=1).reshape(
-        in_chans * 27, -1
-    )
-    conv = jnp.dot(weight, patches, preferred_element_type=jnp.float32) + bias[:, None]
+    lanes = jnp.arange(3 * half_z, dtype=jnp.int32)
+    source = 2 * (lanes % half_z) + lanes // half_z - 1
+    pick = (jnp.arange(depth, dtype=jnp.int32)[:, None] == source[None, :]).astype(fields.dtype)
+    ztaps = jnp.einsum("cxyz,zk->cxyk", ext_full, pick, preferred_element_type=jnp.float32)
+    ztaps = ztaps.astype(fields.dtype)
+    blocks = []
+    for off_x in range(3):
+        for off_y in range(3):
+            blocks.append(ztaps[:, off_x : off_x + 2 * half_x - 1 : 2, off_y : off_y + 2 * half_y - 1 : 2])
+    stacked = jnp.stack(blocks, axis=1).reshape(in_chans * 9, half_x, half_y, 3 * half_z)
+    kernel = weight.reshape(out_chans, in_chans * 9, 3)
+    conv = bias[:, None, None, None]
+    for off_z in range(3):
+        part = stacked[..., off_z * half_z : (off_z + 1) * half_z]
+        conv = conv + jnp.einsum("ok,kpqr->opqr", kernel[:, :, off_z], part, preferred_element_type=jnp.float32)
     col_ok = jnp.arange(half_y, dtype=jnp.int32) >= half_y - col_count // 2
     live = (row_ok[:, None] & col_ok[None, :]).reshape(1, half_x, half_y, 1)
-    conv = conv.reshape(out_chans, half_x, half_y, half_z)
     pre_local = jnp.where(live, conv, 0.0).astype(jnp.bfloat16)
     regrouped = lax.all_to_all(pre_local, "gy", split_axis=0, concat_axis=2, tiled=True)
     pre_wide = regrouped.astype(jnp.float32)
@@ -66,11 +75,12 @@
     slope = sigma * (1.0 + pre_wide * (1.0 - sigma))
     grad_pre = jnp.where(wide_live, grad_out.astype(jnp.float32) * slope, 0.0).astype(jnp.bfloat16)
     returned = lax.all_to_all(grad_pre, "gy", split_axis=2, concat_axis=0, tiled=True)
-    flat = returned.reshape(out_chans, -1)
-    weight_full = lax.dot_general(
-        flat, patches, (((1,), (1,)), ((), ())), preferred_element_type=jnp.float32
-    )
-    bias_full = jnp.sum(flat.astype(jnp.float32), axis=1)
+    grads = []
+    for off_z in range(3):
+        part = stacked[..., off_z * half_z : (off_z + 1) * half_z]
+        grads.append(jnp.einsum("opqr,kpqr->ok", returned, part, preferred_element_type=jnp.float32))
+    weight_full = jnp.stack(grads, axis=-1).reshape(out_chans, -1)
+    bias_full = jnp.sum(returned.astype(jnp.float32), axis=(1, 2, 3))
     weight_part, bias_part = (
         lax.psum_scatter(weight_full, "gy", scatter_dimension=0, tiled=True),
         lax.psum_scatter(bias_full, "gy", scatter_dimension=0, tiled=True),

time: 161 us -> 112 us (0.70)
  local copies, waits for them, and re-layouts: 82.8 us -> 17.6 us
  blocking collectives: 30.6 us -> 46.5 us
  matrix products: 1.1 us -> 3.43 us
    slice x37 -> x11, local copies, waits for them, and re-layouts: 72.1 us -> 7.84 us  [the longest x9 7.27 us: local(): ztaps[:, off_x:off_x + 2 * half_x - 1:2, off_y:off_y + 2 * half_y - 1:2]]
    psum x1, blocking collectives: 20.3 us -> 35.8 us  [local(): weight_grad, bias_grad = lax.psum((weight_part, bias_part), 'gx')]
    reshape x2, local copies, waits for them, and re-layouts: 2.93 us -> 0.06 us  [the longest x1 0.03 us: local(): weight_full = jnp.stack(grads, axis=-1).reshape(out_chans, -1)]
    dot_general x2 -> x7, matrix products: 1.1 us -> 3.43 us  [the longest x3 1.47 us: local(): jnp.einsum('opqr,kpqr->ok', returned, part, preferred_element_type=jnp.fl...]
    unnamed x39 -> x23, local copies, waits for them, and re-layouts: 2.18 us -> 4.18 us
  transfers between devices with their start and end apart: 4 -> 4, of which waited for: 3 -> 3; matrix products, arithmetic and copies ran while one was open for 3% -> 6% of each run, Pallas kernels for 0% -> 0%
where the time goes in v2:
time: 112 us; the launch traced here: 111 us
  blocking collectives  46.5 us (42%)
  local copies, waits for them, and re-layouts  17.6 us (16%)
  waiting for transfers between devices  15.6 us (14%)
  starting transfers between devices  15.4 us (14%)
  between operations  8.17 us (7%)
  other arithmetic  4.76 us (4%)
  matrix products  3.43 us (3%)
    psum x1, blocking collectives, local(): weight_grad, bias_grad = lax.psum((weight_part, bias_part), 'gx')  35.8 us
    unnamed x1, blocking collectives  10.7 us
    all_to_all x1, waiting for transfers between devices, local(): lax.all_to_all(pre_local, 'gy', split_axis=0, concat_axis=2, tiled=True)  8.57 us
    slice x9, local copies, waits for them, and re-layouts, local(): ztaps[:, off_x:off_x + 2 * half_x - 1:2, off_y:off_y + 2 * half_y - 1:2]  7.27 us
    all_to_all x1, waiting for transfers between devices, local(): lax.all_to_all(grad_pre, 'gy', split_axis=2, concat_axis=0, tiled=True)  6.53 us
    ppermute x2, starting transfers between devices, from_behind(): return lax.ppermute(block, axis, route)  6.32 us
    all_to_all x1, starting transfers between devices, local(): lax.all_to_all(pre_local, 'gy', split_axis=0, concat_axis=2, tiled=True)  5.58 us
    unnamed x23, local copies, waits for them, and re-layouts  4.18 us
  transfers between devices with their start and end apart: 4, of which 3 were waited for; matrix products, arithmetic and copies ran while one was open for 6% of the time, Pallas kernels for 0%

profile of v2, /device:TPU:0, one launch (start us, length us, event | category | flops | bytes accessed | tf_op | source)
XLA Modules:
  0.0 111.4 jit_solution(357769320026733566)
XLA Ops:
  0.6 0.9 slice_bitcast_fusion
  1.5 4.9 %collective-permute-start = (bf16[4,32,256]{2,1,0:T(8,128)(2,1)S(1)}, bf16[4,32,256]{2,1,0:T(8,128)(2,1)S(1)}, u32[]{:S(2)}, u32[]{:S(2)}) collective-permute-start(bf16[4,32,256]{2,1,0:T(8,128)(2,1)S(1)} %slice_bitcast_fusion), channel_id=1, source_target_pairs={{0,4},{4,8},{8,12},{12,16},{16,20},{20,24},{24,28},{1,5},{5,9},{9,... | collective-permute-start | bytes 196616 | tf_op jit(solution)/shard_map/ppermute | solution.py:10
  6.4 1.2 %dynamic_slice.7 = s32[1]{0:T(128)} dynamic-slice(s32[4]{0:T(128)} %param.8, s32[]{:T(128)S(6)} %select_n.67), dynamic_slice_sizes={1} | dynamic-slice | bytes 12 | tf_op jit(solution)/shard_map/dynamic_slice | solution.py:48
  10.2 1.2 %dynamic_slice.6 = s32[1]{0:T(128)} dynamic-slice(s32[8]{0:T(128)} %param.7, s32[]{:T(128)S(6)} %select_n.65), dynamic_slice_sizes={1} | dynamic-slice | bytes 12 | tf_op jit(solution)/shard_map/dynamic_slice | solution.py:44
  14.7 0.7 fusion.47
  16.0 0.8 copy.46
  17.0 0.1 broadcast_and_fusion.1
  17.1 0.0 collective-permute-done
  17.1 1.2 %select_select_fusion = bf16[4,9,32,256]{3,2,1,0:T(8,128)(2,1)S(1)} fusion(bf16[4,8,32,256]{3,2,1,0:T(8,128)(2,1)} %param.6, pred[9]{0:T(512)(128)(4,1)S(1)} %get-tuple-element.24, pred[9]{0:T(512)(128)(4,1)S(1)} %get-tuple-element.25, bf16[4,32,256]{2,1,0:T(8,128)(2,1)S(1)} %collective-permute-done), kind=kLoop, calls=%fused_computation.35 | loop fusion | flops 589824 | bytes 1179666 | tf_op jit(solution)/shard_map/jit(_where)/select_n | solution.py:22
  18.3 1.5 %collective-permute-start.1 = (bf16[4,9,256]{2,0,1:T(4,128)(2,1)S(1)}, bf16[4,9,256]{2,0,1:T(4,128)(2,1)S(1)}, u32[]{:S(2)}, u32[]{:S(2)}) collective-permute-start(bf16[4,9,256]{2,0,1:T(4,128)(2,1)S(1)} %bitcast.126), channel_id=1, source_target_pairs={{0,1},{1,2},{2,3},{4,5},{5,6},{6,7},{8,9},{9,10},{10,11},{12,13},{... | collective-permute-start | bytes 55304 | tf_op jit(solution)/shard_map/ppermute | solution.py:10
  19.8 0.1 copy.69
  19.9 0.1 copy.71
  20.0 0.1 copy.73
  20.1 0.5 collective-permute-done.1
  20.6 0.6 convolution_convert_fusion
  21.2 0.6 slice.56
  21.8 0.6 slice.57
  22.5 0.7 slice.58
  23.2 0.6 slice.59
  23.8 0.6 slice.60
  24.4 0.7 slice.61
  25.2 1.0 slice.62
  26.2 1.0 slice.63
  27.2 1.4 %slice.64 = bf16[4,4,16,384]{3,2,1,0:T(8,128)(2,1)S(1)} slice(bf16[4,9,33,384]{3,2,1,0:T(8,128)(2,1)S(1)} %convolution_convert_fusion), slice={[0:4:1], [2:9:2], [2:33:2], [0:384:1]} | slice | bytes 393216 | tf_op jit(solution)/shard_map/slice | solution.py:59
  28.9 0.2 copy.44
  29.1 0.0 copy-start.1
  29.1 0.5 fusion.49
  29.7 0.1 copy-done.1
  29.8 0.4 convolution_add_fusion.2
  30.2 0.5 convolution_add_fusion.1
  30.7 0.5 fusion.2
  31.2 1.0 copy.52
  32.2 5.6 %all-to-all-start = ((bf16[32,4,16,128]{3,2,1,0:T(8,128)(2,1)}), bf16[32,4,16,128]{3,2,1,0:T(8,128)(2,1)S(1)}, u32[]{:S(2)}, u32[]{:S(2)}) async-start(bf16[32,4,16,128]{3,2,1,0:T(8,128)(2,1)} %copy.52), calls=%async_computation | async-start | bytes 1048576 | tf_op jit(solution)/shard_map/all_to_all | solution.py:69
  37.8 0.1 iota_compare_fusion.1
  37.8 0.1 ge.51
  37.9 0.1 broadcast_and_fusion
  38.0 8.6 %all-to-all-done = bf16[32,4,16,128]{3,2,1,0:T(8,128)(2,1)S(1)} async-done(((bf16[32,4,16,128]{3,2,1,0:T(8,128)(2,1)}), bf16[32,4,16,128]{3,2,1,0:T(8,128)(2,1)S(1)}, u32[]{:S(2)}, u32[]{:S(2)}) %all-to-all-start) | async-done | bytes 524320 | tf_op jit(solution)/shard_map/all_to_all | solution.py:69
  46.6 0.0 copy-start
  46.6 0.1 convert_bitcast_fusion
  46.7 0.6 copy.53
  47.3 0.3 copy-done
  47.6 0.0 copy-start.2
  47.6 2.3 %fusion.11 = (bf16[8,4,64,128]{3,0,1,2:T(8,128)(2,1)}, bf16[8,4,64,128]{3,0,1,2:T(8,128)(2,1)S(1)}) fusion(f32[8,4,4,16,128]{4,0,1,3,2:T(8,128)S(1)} %copy.53, bf16[8,4,64,128]{3,2,1,0:T(8,128)(2,1)S(1)} %copy-done, pred[4,64]{0,1:T(8,128)(4,1)S(1)} %broadcast_and_fusion), kind=kLoop, calls=%fused_computation.22 | loop fusion | flops 3407872 | bytes 2621696 | tf_op jit(solution)/shard_map/convert_element_type | solution.py:76
  50.0 3.5 %all-to-all-start.1 = ((bf16[8,4,64,128]{3,0,1,2:T(8,128)(2,1)}), bf16[8,4,64,128]{3,0,1,2:T(8,128)(2,1)S(1)}, u32[]{:S(2)}, u32[]{:S(2)}) async-start(bf16[8,4,64,128]{3,0,1,2:T(8,128)(2,1)} %get-tuple-element.19), calls=%async_computation.1 | async-start | bytes 1048576 | tf_op jit(solution)/shard_map/all_to_all | solution.py:77
  53.4 0.0 copy-done.2
  53.4 0.6 dynamic-slice
  54.7 1.0 copy.57
  55.7 6.5 %all-to-all-done.1 = bf16[8,4,64,128]{3,0,1,2:T(8,128)(2,1)S(1)} async-done(((bf16[8,4,64,128]{3,0,1,2:T(8,128)(2,1)}), bf16[8,4,64,128]{3,0,1,2:T(8,128)(2,1)S(1)}, u32[]{:S(2)}, u32[]{:S(2)}) %all-to-all-start.1) | async-done | bytes 524320 | tf_op jit(solution)/shard_map/all_to_all | solution.py:77
  62.2 0.5 convolution_bitcast_fusion.2
  62.7 0.5 convolution_bitcast_fusion.1
  63.2 0.5 convolution_bitcast_fusion
  63.7 0.2 convert_reduce_fusion
  63.9 0.1 copy.56
  64.0 0.1 reduce_sum.12
  64.1 10.7 %all-reduce.5 = (f32[32,108]{0,1:T(8,128)S(1)}, f32[32]{0:T(128)S(1)}) all-reduce(f32[32,108]{0,1:T(8,128)S(1)} %reshape.168, f32[32]{0:T(128)S(1)} %reduce_sum.12), channel_id=2, replica_groups=mesh['gx'=8,'gy'=4] {'gy'}, use_global_device_ids=true, to_apply=%region_0.1.clone | all-reduce | flops 3488 | bytes 27904
  74.8 0.1 constant_dynamic-slice_fusion
  74.9 0.1 dynamic-slice.3
  75.0 35.8 %all-reduce.4 = (f32[8,108]{0,1:T(8,128)S(1)}, f32[8]{0:T(128)}) all-reduce(f32[8,108]{0,1:T(8,128)S(1)} %constant_dynamic-slice_fusion, f32[8]{0:T(128)S(1)} %dynamic-slice.3), channel_id=1, replica_groups=mesh['gx'=8,'gy'=4] {'gx'}, use_global_device_ids=true, to_apply=%region_1.2 | all-reduce | flops 872 | bytes 6976 | tf_op jit(solution)/shard_map/psum | solution.py:88
  110.7 0.7 copy.58
  (21 shorter events, 0.5 us)
Async XLA Ops:
  1.5 15.6 %collective-permute-start = (bf16[4,32,256]{2,1,0:T(8,128)(2,1)S(1)}, bf16[4,32,256]{2,1,0:T(8,128)(2,1)S(1)}, u32[]{:S(2)}, u32[]{:S(2)}) collective-permute-start(bf16[4,32,256]{2,1,0:T(8,128)(2,1)S(1)} %slice_bitcast_fusion), channel_id=1, source_target_pairs={{0,4},{4,8},{8,12},{12,16},{16,20},{20,24},{24,28},{1,5},{5,9},{9,... | collective-permute-start | bytes 196616 | tf_op jit(solution)/shard_map/ppermute | solution.py:10
  18.3 2.3 %collective-permute-start.1 = (bf16[4,9,256]{2,0,1:T(4,128)(2,1)S(1)}, bf16[4,9,256]{2,0,1:T(4,128)(2,1)S(1)}, u32[]{:S(2)}, u32[]{:S(2)}) collective-permute-start(bf16[4,9,256]{2,0,1:T(4,128)(2,1)S(1)} %bitcast.126), channel_id=1, source_target_pairs={{0,1},{1,2},{2,3},{4,5},{5,6},{6,7},{8,9},{9,10},{10,11},{12,13},{... | collective-permute-start | bytes 55304 | tf_op jit(solution)/shard_map/ppermute | solution.py:10
  29.1 0.7 copy-start.1
  32.2 14.4 %all-to-all-start = ((bf16[32,4,16,128]{3,2,1,0:T(8,128)(2,1)}), bf16[32,4,16,128]{3,2,1,0:T(8,128)(2,1)S(1)}, u32[]{:S(2)}, u32[]{:S(2)}) async-start(bf16[32,4,16,128]{3,2,1,0:T(8,128)(2,1)} %copy.52), calls=%async_computation | async-start | bytes 1048576 | tf_op jit(solution)/shard_map/all_to_all | solution.py:69
  46.6 1.0 copy-start
  47.6 5.8 %copy-start.2 = (u32[32]{0:T(128)S(1)}, u32[32]{0:T(128)}, u32[]{:S(2)}) copy-start(u32[32]{0:T(128)} %constant.97) | copy-start | bytes 388
  50.0 12.3 %all-to-all-start.1 = ((bf16[8,4,64,128]{3,0,1,2:T(8,128)(2,1)}), bf16[8,4,64,128]{3,0,1,2:T(8,128)(2,1)S(1)}, u32[]{:S(2)}, u32[]{:S(2)}) async-start(bf16[8,4,64,128]{3,0,1,2:T(8,128)(2,1)} %get-tuple-element.19), calls=%async_computation.1 | async-start | bytes 1048576 | tf_op jit(solution)/shard_map/all_to_all | solution.py:77

commit v3 on v2

--- a/solution.py
+++ b/solution.py
@@ -8,6 +8,18 @@
     devices = range(lax.axis_size(axis))
     route = [(i - distance, i) for i in devices if i - distance in devices]
     return lax.ppermute(block, axis, route)
+
+
+def butterfly_sum(value, axis):
+    size = lax.axis_size(axis)
+    if size & (size - 1):
+        return lax.psum(value, axis)
+    step = 1
+    while step < size:
+        swap = [(i, i ^ step) for i in range(size)]
+        value = value + lax.ppermute(value, axis, swap)
+        step *= 2
+    return value
 
 
 def extend(data, border, count, dim):
@@ -81,11 +93,11 @@
         grads.append(jnp.einsum("opqr,kpqr->ok", returned, part, preferred_element_type=jnp.float32))
     weight_full = jnp.stack(grads, axis=-1).reshape(out_chans, -1)
     bias_full = jnp.sum(returned.astype(jnp.float32), axis=(1, 2, 3))
-    weight_part, bias_part = (
-        lax.psum_scatter(weight_full, "gy", scatter_dimension=0, tiled=True),
-        lax.psum_scatter(bias_full, "gy", scatter_dimension=0, tiled=True),
-    )
-    weight_grad, bias_grad = lax.psum((weight_part, bias_part), "gx")
+    packed = jnp.concatenate([weight_full, bias_full[:, None]], axis=1)
+    total = butterfly_sum(butterfly_sum(packed, "gx"), "gy")
+    rows = out_chans // tiles_y
+    mine = lax.dynamic_slice_in_dim(total, lax.axis_index("gy") * rows, rows, 0)
+    weight_grad, bias_grad = mine[:, :-1], mine[:, -1]
     return (stem, weight_grad, bias_grad)
 
 

time: 112 us -> 81 us (0.72)
  blocking collectives: 46.5 us -> 11.2 us
  waiting for transfers between devices: 15.6 us -> 19 us
  starting transfers between devices: 15.4 us -> 18 us
    psum x1 -> x0, blocking collectives: 35.8 us -> none  [local(): weight_grad, bias_grad = lax.psum((weight_part, bias_part), 'gx')]
    all_to_all x0 -> x1, blocking collectives: none -> 11.2 us  [local(): lax.all_to_all(grad_pre, 'gy', split_axis=2, concat_axis=0, tiled=True)]
    unnamed x1 -> x0, blocking collectives: 10.7 us -> none
    ppermute x0 -> x5, waiting for transfers between devices: none -> 9.92 us  [butterfly_sum(): value = value + lax.ppermute(value, axis, swap)]
    all_to_all x1 -> x0, waiting for transfers between devices: 6.53 us -> none  [local(): lax.all_to_all(grad_pre, 'gy', split_axis=2, concat_axis=0, tiled=True)]
    ppermute x0 -> x5, starting transfers between devices: none -> 6.12 us  [butterfly_sum(): value = value + lax.ppermute(value, axis, swap)]
    all_to_all x1 -> x0, starting transfers between devices: 3.47 us -> none  [local(): lax.all_to_all(grad_pre, 'gy', split_axis=2, concat_axis=0, tiled=True)]
    unnamed x23 -> x19, local copies, waits for them, and re-layouts: 4.18 us -> 2.78 us
  transfers between devices with their start and end apart: 4 -> 8, of which waited for: 3 -> 7; matrix products, arithmetic and copies ran while one was open for 6% -> 7% of each run, Pallas kernels for 0% -> 0%
where the time goes in v3:
time: 81 us; the launch traced here: 80.4 us
  waiting for transfers between devices  19 us (23%)
  starting transfers between devices  18 us (22%)
  local copies, waits for them, and re-layouts  16.9 us (21%)
  blocking collectives  11.2 us (14%)
  between operations  7.5 us (9%)
  other arithmetic  4.26 us (5%)
  matrix products  3.46 us (4%)
    all_to_all x1, blocking collectives, local(): lax.all_to_all(grad_pre, 'gy', split_axis=2, concat_axis=0, tiled=True)  11.2 us
    ppermute x5, waiting for transfers between devices, butterfly_sum(): value = value + lax.ppermute(value, axis, swap)  9.92 us
    all_to_all x1, waiting for transfers between devices, local(): lax.all_to_all(pre_local, 'gy', split_axis=0, concat_axis=2, tiled=True)  8.57 us
    slice x9, local copies, waits for them, and re-layouts, local(): ztaps[:, off_x:off_x + 2 * half_x - 1:2, off_y:off_y + 2 * half_y - 1:2]  7.27 us
    ppermute x2, starting transfers between devices, from_behind(): return lax.ppermute(block, axis, route)  6.32 us
    ppermute x5, starting transfers between devices, butterfly_sum(): value = value + lax.ppermute(value, axis, swap)  6.12 us
    all_to_all x1, starting transfers between devices, local(): lax.all_to_all(pre_local, 'gy', split_axis=0, concat_axis=2, tiled=True)  5.58 us
    unnamed x19, local copies, waits for them, and re-layouts  2.78 us
  transfers between devices with their start and end apart: 8, of which 7 were waited for; matrix products, arithmetic and copies ran while one was open for 7% of the time, Pallas kernels for 0%

profile of v3, /device:TPU:0, one launch (start us, length us, event | category | flops | bytes accessed | tf_op | source)
XLA Modules:
  0.0 80.4 jit_solution(3823554458893099262)
XLA Ops:
  0.6 0.9 %slice_bitcast_fusion = bf16[4,32,256]{2,1,0:T(8,128)(2,1)S(1)} fusion(bf16[4,8,32,256]{3,2,1,0:T(8,128)(2,1)} %param.6), kind=kLoop, calls=%fused_computation.56 | loop fusion | bytes 131072 | tf_op jit(solution)/shard_map/squeeze | solution.py:57
  1.5 4.9 %collective-permute-start = (bf16[4,32,256]{2,1,0:T(8,128)(2,1)S(1)}, bf16[4,32,256]{2,1,0:T(8,128)(2,1)S(1)}, u32[]{:S(2)}, u32[]{:S(2)}) collective-permute-start(bf16[4,32,256]{2,1,0:T(8,128)(2,1)S(1)} %slice_bitcast_fusion), channel_id=1, source_target_pairs={{0,4},{4,8},{8,12},{12,16},{16,20},{20,24},{24,28},{1,5},{5,9},{9,... | collective-permute-start | bytes 196616 | tf_op jit(solution)/shard_map/ppermute | solution.py:10
  6.4 1.2 %dynamic_slice.10 = s32[1]{0:T(128)} dynamic-slice(s32[4]{0:T(128)} %param.8, s32[]{:T(128)S(6)} %select_n.70), dynamic_slice_sizes={1} | dynamic-slice | bytes 12 | tf_op jit(solution)/shard_map/dynamic_slice | solution.py:60
  10.2 1.2 %dynamic_slice.9 = s32[1]{0:T(128)} dynamic-slice(s32[8]{0:T(128)} %param.7, s32[]{:T(128)S(6)} %select_n.68), dynamic_slice_sizes={1} | dynamic-slice | bytes 12 | tf_op jit(solution)/shard_map/dynamic_slice | solution.py:56
  14.7 0.7 fusion.47
  16.0 0.8 %copy.66 = bf16[32,108]{0,1:T(8,128)(2,1)S(1)} copy(bf16[32,108]{1,0:T(8,128)(2,1)} %param.9) | data formatting | bytes 13824 | tf_op args[3]
  17.0 0.1 broadcast_and_fusion.1
  17.1 0.0 collective-permute-done
  17.1 1.2 %select_select_fusion = bf16[4,9,32,256]{3,2,1,0:T(8,128)(2,1)S(1)} fusion(bf16[4,8,32,256]{3,2,1,0:T(8,128)(2,1)} %param.6, pred[9]{0:T(512)(128)(4,1)S(1)} %get-tuple-element.23, pred[9]{0:T(512)(128)(4,1)S(1)} %get-tuple-element.24, bf16[4,32,256]{2,1,0:T(8,128)(2,1)S(1)} %collective-permute-done), kind=kLoop, calls=%fused_computation.35 | loop fusion | flops 589824 | bytes 1179666 | tf_op jit(solution)/shard_map/jit(_where)/select_n | solution.py:34
  18.3 1.5 %collective-permute-start.1 = (bf16[4,9,256]{2,0,1:T(4,128)(2,1)S(1)}, bf16[4,9,256]{2,0,1:T(4,128)(2,1)S(1)}, u32[]{:S(2)}, u32[]{:S(2)}) collective-permute-start(bf16[4,9,256]{2,0,1:T(4,128)(2,1)S(1)} %bitcast.124), channel_id=1, source_target_pairs={{0,1},{1,2},{2,3},{4,5},{5,6},{6,7},{8,9},{9,10},{10,11},{12,13},{... | collective-permute-start | bytes 55304 | tf_op jit(solution)/shard_map/ppermute | solution.py:10
  19.8 0.1 copy.88
  19.9 0.1 copy.90
  20.0 0.1 copy.92
  20.1 0.5 collective-permute-done.1
  20.6 0.6 convolution_convert_fusion
  21.2 0.6 slice.62
  21.8 0.6 slice.63
  22.5 0.7 slice.64
  23.2 0.6 slice.65
  23.8 0.6 slice.66
  24.4 0.7 slice.67
  25.2 1.0 %slice.68 = bf16[4,4,16,384]{3,2,1,0:T(8,128)(2,1)S(1)} slice(bf16[4,9,33,384]{3,2,1,0:T(8,128)(2,1)S(1)} %convolution_convert_fusion), slice={[0:4:1], [2:9:2], [0:31:2], [0:384:1]} | slice | bytes 393216 | tf_op jit(solution)/shard_map/slice | solution.py:71
  26.2 1.0 %slice.69 = bf16[4,4,16,384]{3,2,1,0:T(8,128)(2,1)S(1)} slice(bf16[4,9,33,384]{3,2,1,0:T(8,128)(2,1)S(1)} %convolution_convert_fusion), slice={[0:4:1], [2:9:2], [1:32:2], [0:384:1]} | slice | bytes 393216 | tf_op jit(solution)/shard_map/slice | solution.py:71
  27.2 1.4 %slice.70 = bf16[4,4,16,384]{3,2,1,0:T(8,128)(2,1)S(1)} slice(bf16[4,9,33,384]{3,2,1,0:T(8,128)(2,1)S(1)} %convolution_convert_fusion), slice={[0:4:1], [2:9:2], [2:33:2], [0:384:1]} | slice | bytes 393216 | tf_op jit(solution)/shard_map/slice | solution.py:71
  28.9 0.2 copy.64
  29.1 0.0 copy-start.2
  29.1 0.5 fusion.49
  29.7 0.1 copy-done.2
  29.8 0.4 convolution_add_fusion.2
  30.2 0.5 convolution_add_fusion.1
  30.7 0.5 fusion.2
  31.2 1.0 %copy.72 = bf16[32,4,16,128]{3,2,1,0:T(8,128)(2,1)} copy(bf16[32,4,16,128]{3,0,2,1:T(8,128)(2,1)S(1)} %fusion.2) | data formatting | bytes 1048576 | tf_op jit(solution)/shard_map/jit(_where)/select_n | solution.py:80
  32.2 5.6 %all-to-all-start = ((bf16[32,4,16,128]{3,2,1,0:T(8,128)(2,1)}), bf16[32,4,16,128]{3,2,1,0:T(8,128)(2,1)S(1)}, u32[]{:S(2)}, u32[]{:S(2)}) async-start(bf16[32,4,16,128]{3,2,1,0:T(8,128)(2,1)} %copy.72), calls=%async_computation | async-start | bytes 1048576 | tf_op jit(solution)/shard_map/all_to_all | solution.py:81
  37.7 0.1 iota_compare_fusion.1
  37.8 0.1 ge.51
  37.9 0.1 broadcast_and_fusion
  38.0 8.6 %all-to-all-done = bf16[32,4,16,128]{3,2,1,0:T(8,128)(2,1)S(1)} async-done(((bf16[32,4,16,128]{3,2,1,0:T(8,128)(2,1)}), bf16[32,4,16,128]{3,2,1,0:T(8,128)(2,1)S(1)}, u32[]{:S(2)}, u32[]{:S(2)}) %all-to-all-start) | async-done | bytes 524320 | tf_op jit(solution)/shard_map/all_to_all | solution.py:81
  46.6 0.1 convert_bitcast_fusion
  46.7 0.6 copy.73
  47.3 0.3 copy-done
  47.6 1.7 %fusion.11 = (bf16[8,4,64,128]{3,0,1,2:T(8,128)(2,1)S(1)}, bf16[8,4,64,128]{3,0,1,2:T(8,128)(2,1)S(1)}) fusion(f32[8,4,4,16,128]{4,0,1,3,2:T(8,128)S(1)} %copy.73, bf16[8,4,64,128]{3,2,1,0:T(8,128)(2,1)S(1)} %copy-done, pred[4,64]{0,1:T(8,128)(4,1)S(1)} %broadcast_and_fusion), kind=kLoop, calls=%fused_computation.22 | loop fusion | flops 3407872 | bytes 2621696 | tf_op jit(solution)/shard_map/convert_element_type | solution.py:88
  49.3 11.2 %all_to_all.27 = bf16[8,4,64,128]{3,0,1,2:T(8,128)(2,1)S(1)} all-to-all(bf16[8,4,64,128]{3,0,1,2:T(8,128)(2,1)S(1)} %get-tuple-element.18), channel_id=1, replica_groups=mesh['gx'=8,'gy'=4] {'gy'}, dimensions={2} | all-to-all | bytes 1048576 | tf_op jit(solution)/shard_map/all_to_all | solution.py:89
  60.5 0.5 convolution_bitcast_fusion.2
  61.0 0.5 convolution_bitcast_fusion.1
  61.5 0.5 convolution_bitcast_fusion
  62.0 0.2 convert_reduce_fusion
  62.2 0.1 copy.76
  62.3 0.1 copy.77
  62.4 0.1 broadcast_in_dim.105
  62.5 0.1 pad_maximum_fusion.1
  62.6 1.6 %collective-permute-start.2 = (f32[32,109]{1,0:T(8,128)S(1)}, f32[32,109]{1,0:T(8,128)S(1)}, u32[]{:S(2)}, u32[]{:S(2)}) collective-permute-start(f32[32,109]{1,0:T(8,128)S(1)} %pad_maximum_fusion.1), channel_id=1, source_target_pairs={{0,4},{4,0},{8,12},{12,8},{16,20},{20,16},{24,28},{28,24},{1,5},{5... | collective-permute-start | bytes 41864 | tf_op jit(solution)/shard_map/ppermute | solution.py:20
  64.1 2.2 %collective-permute-done.2 = f32[32,109]{1,0:T(8,128)S(1)} collective-permute-done((f32[32,109]{1,0:T(8,128)S(1)}, f32[32,109]{1,0:T(8,128)S(1)}, u32[]{:S(2)}, u32[]{:S(2)}) %collective-permute-start.2) | collective-permute-done | bytes 13984 | tf_op jit(solution)/shard_map/ppermute | solution.py:20
  66.3 0.1 fusion.51
  66.4 1.6 %collective-permute-start.3 = (f32[32,109]{1,0:T(8,128)S(1)}, f32[32,109]{1,0:T(8,128)S(1)}, u32[]{:S(2)}, u32[]{:S(2)}) collective-permute-start(f32[32,109]{1,0:T(8,128)S(1)} %fusion.51), channel_id=1, source_target_pairs={{0,8},{4,12},{8,0},{12,4},{16,24},{20,28},{24,16},{28,20},{1,9},{5... | collective-permute-start | bytes 41864 | tf_op jit(solution)/shard_map/ppermute | solution.py:20
  68.0 2.2 %collective-permute-done.3 = f32[32,109]{1,0:T(8,128)S(1)} collective-permute-done((f32[32,109]{1,0:T(8,128)S(1)}, f32[32,109]{1,0:T(8,128)S(1)}, u32[]{:S(2)}, u32[]{:S(2)}) %collective-permute-start.3) | collective-permute-done | bytes 13984 | tf_op jit(solution)/shard_map/ppermute | solution.py:20
  70.1 2.6 %collective-permute-start.4 = (f32[32,109]{1,0:T(8,128)S(1)}, f32[32,109]{1,0:T(8,128)S(1)}, u32[]{:S(2)}, u32[]{:S(2)}) collective-permute-start(f32[32,109]{1,0:T(8,128)S(1)} %add.92), channel_id=1, source_target_pairs={{0,16},{4,20},{8,24},{12,28},{16,0},{20,4},{24,8},{28,12},{1,17},{... | collective-permute-start | bytes 41864 | tf_op jit(solution)/shard_map/ppermute | solution.py:20
  72.7 2.0 %collective-permute-done.4 = f32[32,109]{1,0:T(8,128)S(1)} collective-permute-done((f32[32,109]{1,0:T(8,128)S(1)}, f32[32,109]{1,0:T(8,128)S(1)}, u32[]{:S(2)}, u32[]{:S(2)}) %collective-permute-start.4) | collective-permute-done | bytes 13984 | tf_op jit(solution)/shard_map/ppermute | solution.py:20
  74.8 0.0 collective-permute-start.5
  74.8 1.2 %collective-permute-done.5 = f32[32,109]{1,0:T(8,128)S(1)} collective-permute-done((f32[32,109]{1,0:T(8,128)S(1)}, f32[32,109]{1,0:T(8,128)S(1)}, u32[]{:S(2)}, u32[]{:S(2)}) %collective-permute-start.5) | collective-permute-done | bytes 13984 | tf_op jit(solution)/shard_map/ppermute | solution.py:20
  76.0 0.4 collective-permute-start.6
  76.4 1.0 %copy.79 = bf16[8,4,64,128]{3,2,1,0:T(8,128)(2,1)} copy(bf16[8,4,64,128]{3,0,1,2:T(8,128)(2,1)S(1)} %get-tuple-element.19) | data formatting | bytes 1048576
  77.4 2.4 %collective-permute-done.6 = f32[32,109]{1,0:T(8,128)S(1)} collective-permute-done((f32[32,109]{1,0:T(8,128)S(1)}, f32[32,109]{1,0:T(8,128)S(1)}, u32[]{:S(2)}, u32[]{:S(2)}) %collective-permute-start.6) | collective-permute-done | bytes 13984 | tf_op jit(solution)/shard_map/ppermute | solution.py:20
  79.7 0.7 slice_reduce_fusion
  80.4 0.0 copy-done.1
  (27 shorter events, 0.5 us)
Async XLA Ops:
  1.5 15.6 %collective-permute-start = (bf16[4,32,256]{2,1,0:T(8,128)(2,1)S(1)}, bf16[4,32,256]{2,1,0:T(8,128)(2,1)S(1)}, u32[]{:S(2)}, u32[]{:S(2)}) collective-permute-start(bf16[4,32,256]{2,1,0:T(8,128)(2,1)S(1)} %slice_bitcast_fusion), channel_id=1, source_target_pairs={{0,4},{4,8},{8,12},{12,16},{16,20},{20,24},{24,28},{1,5},{5,9},{9,... | collective-permute-start | bytes 196616 | tf_op jit(solution)/shard_map/ppermute | solution.py:10
  18.3 2.3 %collective-permute-start.1 = (bf16[4,9,256]{2,0,1:T(4,128)(2,1)S(1)}, bf16[4,9,256]{2,0,1:T(4,128)(2,1)S(1)}, u32[]{:S(2)}, u32[]{:S(2)}) collective-permute-start(bf16[4,9,256]{2,0,1:T(4,128)(2,1)S(1)} %bitcast.124), channel_id=1, source_target_pairs={{0,1},{1,2},{2,3},{4,5},{5,6},{6,7},{8,9},{9,10},{10,11},{12,13},{... | collective-permute-start | bytes 55304 | tf_op jit(solution)/shard_map/ppermute | solution.py:10
  29.1 0.7 copy-start.2
  32.2 14.4 %all-to-all-start = ((bf16[32,4,16,128]{3,2,1,0:T(8,128)(2,1)}), bf16[32,4,16,128]{3,2,1,0:T(8,128)(2,1)S(1)}, u32[]{:S(2)}, u32[]{:S(2)}) async-start(bf16[32,4,16,128]{3,2,1,0:T(8,128)(2,1)} %copy.72), calls=%async_computation | async-start | bytes 1048576 | tf_op jit(solution)/shard_map/all_to_all | solution.py:81
  46.6 1.0 %copy-start = (bf16[8,4,64,128]{3,2,1,0:T(8,128)(2,1)S(1)}, bf16[8,4,64,128]{3,2,1,0:T(8,128)(2,1)}, u32[]{:S(2)}) copy-start(bf16[8,4,64,128]{3,2,1,0:T(8,128)(2,1)} %param.11) | copy-start | bytes 1572868
  62.6 3.8 %collective-permute-start.2 = (f32[32,109]{1,0:T(8,128)S(1)}, f32[32,109]{1,0:T(8,128)S(1)}, u32[]{:S(2)}, u32[]{:S(2)}) collective-permute-start(f32[32,109]{1,0:T(8,128)S(1)} %pad_maximum_fusion.1), channel_id=1, source_target_pairs={{0,4},{4,0},{8,12},{12,8},{16,20},{20,16},{24,28},{28,24},{1,5},{5... | collective-permute-start | bytes 41864 | tf_op jit(solution)/shard_map/ppermute | solution.py:20
  66.4 3.7 %collective-permute-start.3 = (f32[32,109]{1,0:T(8,128)S(1)}, f32[32,109]{1,0:T(8,128)S(1)}, u32[]{:S(2)}, u32[]{:S(2)}) collective-permute-start(f32[32,109]{1,0:T(8,128)S(1)} %fusion.51), channel_id=1, source_target_pairs={{0,8},{4,12},{8,0},{12,4},{16,24},{20,28},{24,16},{28,20},{1,9},{5... | collective-permute-start | bytes 41864 | tf_op jit(solution)/shard_map/ppermute | solution.py:20
  70.1 4.6 %collective-permute-start.4 = (f32[32,109]{1,0:T(8,128)S(1)}, f32[32,109]{1,0:T(8,128)S(1)}, u32[]{:S(2)}, u32[]{:S(2)}) collective-permute-start(f32[32,109]{1,0:T(8,128)S(1)} %add.92), channel_id=1, source_target_pairs={{0,16},{4,20},{8,24},{12,28},{16,0},{20,4},{24,8},{28,12},{1,17},{... | collective-permute-start | bytes 41864 | tf_op jit(solution)/shard_map/ppermute | solution.py:20
  74.8 1.2 %collective-permute-start.5 = (f32[32,109]{1,0:T(8,128)S(1)}, f32[32,109]{1,0:T(8,128)S(1)}, u32[]{:S(2)}, u32[]{:S(2)}) collective-permute-start(f32[32,109]{1,0:T(8,128)S(1)} %add.93), channel_id=1, source_target_pairs={{0,1},{1,0},{2,3},{3,2},{4,5},{5,4},{6,7},{7,6},{8,9},{9,8},{10,11... | collective-permute-start | bytes 41864 | tf_op jit(solution)/shard_map/ppermute | solution.py:20
  76.0 3.7 %collective-permute-start.6 = (f32[32,109]{1,0:T(8,128)S(1)}, f32[32,109]{1,0:T(8,128)S(1)}, u32[]{:S(2)}, u32[]{:S(2)}) collective-permute-start(f32[32,109]{1,0:T(8,128)S(1)} %add.94), channel_id=1, source_target_pairs={{0,2},{1,3},{2,0},{3,1},{4,6},{5,7},{6,4},{7,5},{8,10},{9,11},{10,... | collective-permute-start | bytes 41864 | tf_op jit(solution)/shard_map/ppermute | solution.py:20
  79.7 0.7 copy-start.1

commit v4 on v3

--- a/solution.py
+++ b/solution.py
@@ -53,6 +53,7 @@
     half_z = depth // 2
     out_chans = weight.shape[0]
     tiles_y = lax.axis_size("gy")
+    cell_grad = lax.all_to_all(grad_out, "gy", split_axis=2, concat_axis=0, tiled=True)
     row_count = rows_live[lax.axis_index("gx")]
     above = from_behind(fields[:, cap_x - 1], "gx", 1)
     ext_rows = extend(fields, above, row_count, 1)
@@ -78,15 +79,12 @@
     col_ok = jnp.arange(half_y, dtype=jnp.int32) >= half_y - col_count // 2
     live = (row_ok[:, None] & col_ok[None, :]).reshape(1, half_x, half_y, 1)
     pre_local = jnp.where(live, conv, 0.0).astype(jnp.bfloat16)
-    regrouped = lax.all_to_all(pre_local, "gy", split_axis=0, concat_axis=2, tiled=True)
-    pre_wide = regrouped.astype(jnp.float32)
+    pre_wide = pre_local.astype(jnp.float32)
     sigma = jax.nn.sigmoid(pre_wide)
-    stem = (pre_wide * sigma).astype(jnp.bfloat16)
-    wide_cols = jnp.arange(half_y, dtype=jnp.int32)[None, :] >= half_y - (cols_live // 2)[:, None]
-    wide_live = row_ok.reshape(1, half_x, 1, 1) & wide_cols.reshape(1, 1, tiles_y * half_y, 1)
+    stem_local = (pre_wide * sigma).astype(jnp.bfloat16)
     slope = sigma * (1.0 + pre_wide * (1.0 - sigma))
-    grad_pre = jnp.where(wide_live, grad_out.astype(jnp.float32) * slope, 0.0).astype(jnp.bfloat16)
-    returned = lax.all_to_all(grad_pre, "gy", split_axis=2, concat_axis=0, tiled=True)
+    returned = jnp.where(live, cell_grad.astype(jnp.float32) * slope, 0.0).astype(jnp.bfloat16)
+    stem = lax.all_to_all(stem_local, "gy", split_axis=0, concat_axis=2, tiled=True)
     grads = []
     for off_z in range(3):
         part = stacked[..., off_z * half_z : (off_z + 1) * half_z]

time: 81 us -> 60.6 us (0.75)
  waiting for transfers between devices: 19 us -> 7.62 us
  blocking collectives: 11.2 us -> 0 us
  starting transfers between devices: 18 us -> 23.8 us
  other arithmetic: 4.26 us -> 0.43 us
  matrix products: 3.46 us -> 4.69 us
  local copies, waits for them, and re-layouts: 16.9 us -> 16 us
    all_to_all x1 -> x0, blocking collectives: 11.2 us -> none  [local(): lax.all_to_all(grad_pre, 'gy', split_axis=2, concat_axis=0, tiled=True)]
    all_to_all x1 -> x2, waiting for transfers between devices: 8.57 us -> 0.01 us  [the longest x1 0.01 us: local(): lax.all_to_all(grad_out, 'gy', split_axis=2, concat_axis=0, tiled=True)]
    all_to_all x1 -> x2, starting transfers between devices: 5.58 us -> 8.6 us  [the longest x1 5.13 us: local(): lax.all_to_all(stem_local, 'gy', split_axis=0, concat_axis=2, tiled=True)]
    ppermute x5, waiting for transfers between devices: 9.92 us -> 7.08 us  [butterfly_sum(): value = value + lax.ppermute(value, axis, swap)]
    ppermute x5, starting transfers between devices: 6.12 us -> 7.97 us  [butterfly_sum(): value = value + lax.ppermute(value, axis, swap)]
    convert_element_type x2 -> x0, other arithmetic: 1.78 us -> none  [the longest x1 1.67 us: local(): jnp.where(wide_live, grad_out.astype(jnp.float32) * slope, 0.0)]
    dot_general x3, matrix products: 1.36 us -> 2.71 us  [local(): jnp.einsum('ok,kpqr->opqr', kernel[:, :, off_z], part, preferred_element_...]
    select_n x1, other arithmetic: 1.18 us -> 0.14 us  [extend(): return jnp.where(places == edge_at, border_wide, kept)]
  transfers between devices with their start and end apart: 8 -> 9, of which waited for: 7 -> 5; matrix products, arithmetic and copies ran while one was open for 7% -> 26% of each run, Pallas kernels for 0% -> 0%
where the time goes in v4:
time: 60.6 us; the launch traced here: 60.1 us
  starting transfers between devices  23.8 us (39%)
  local copies, waits for them, and re-layouts  16 us (26%)
  waiting for transfers between devices  7.62 us (13%)
  between operations  7.56 us (12%)
  matrix products  4.69 us (8%)
    ppermute x5, starting transfers between devices, butterfly_sum(): value = value + lax.ppermute(value, axis, swap)  7.97 us
    slice x9, local copies, waits for them, and re-layouts, local(): ztaps[:, off_x:off_x + 2 * half_x - 1:2, off_y:off_y + 2 * half_y - 1:2]  7.27 us
    ppermute x2, starting transfers between devices, from_behind(): return lax.ppermute(block, axis, route)  7.22 us
    ppermute x5, waiting for transfers between devices, butterfly_sum(): value = value + lax.ppermute(value, axis, swap)  7.08 us
    all_to_all x1, starting transfers between devices, local(): lax.all_to_all(stem_local, 'gy', split_axis=0, concat_axis=2, tiled=True)  5.13 us
    all_to_all x1, starting transfers between devices, local(): lax.all_to_all(grad_out, 'gy', split_axis=2, concat_axis=0, tiled=True)  3.47 us
    unnamed x27, local copies, waits for them, and re-layouts  2.98 us
    dot_general x3, matrix products, local(): jnp.einsum('ok,kpqr->opqr', kernel[:, :, off_z], part, preferred_element_...  2.71 us
  transfers between devices with their start and end apart: 9, of which 5 were waited for; matrix products, arithmetic and copies ran while one was open for 26% of the time, Pallas kernels for 0%

profile of v4, /device:TPU:0, one launch (start us, length us, event | category | flops | bytes accessed | tf_op | source)
XLA Modules:
  0.0 60.1 jit_solution(6326356600531906668)
XLA Ops:
  0.6 0.0 copy-start
  0.6 0.0 copy-start.5
  0.7 0.0 copy-start.6
  0.7 0.0 copy-start.3
  0.7 0.9 %slice_bitcast_fusion = bf16[4,32,256]{2,1,0:T(8,128)(2,1)S(1)} fusion(bf16[4,8,32,256]{3,2,1,0:T(8,128)(2,1)} %param.6), kind=kLoop, calls=%fused_computation.43 | loop fusion | bytes 131072 | tf_op jit(solution)/shard_map/squeeze | solution.py:58
  1.6 4.9 %collective-permute-start = (bf16[4,32,256]{2,1,0:T(8,128)(2,1)S(1)}, bf16[4,32,256]{2,1,0:T(8,128)(2,1)S(1)}, u32[]{:S(2)}, u32[]{:S(2)}) collective-permute-start(bf16[4,32,256]{2,1,0:T(8,128)(2,1)S(1)} %slice_bitcast_fusion), channel_id=1, source_target_pairs={{0,4},{4,8},{8,12},{12,16},{16,20},{20,24},{24,28},{1,5},{5,9},{9,... | collective-permute-start | bytes 196616 | tf_op jit(solution)/shard_map/ppermute | solution.py:10
  6.4 2.2 %copy.72 = bf16[8,4,64,128]{3,0,1,2:T(8,128)(2,1)} copy(bf16[8,4,64,128]{3,2,1,0:T(8,128)(2,1)} %param.11) | data formatting | bytes 1048576 | tf_op args[5]
  8.6 3.5 %all-to-all-start.1 = ((bf16[8,4,64,128]{3,0,1,2:T(8,128)(2,1)}), bf16[8,4,64,128]{3,0,1,2:T(8,128)(2,1)S(1)}, u32[]{:S(2)}, u32[]{:S(2)}) async-start(bf16[8,4,64,128]{3,0,1,2:T(8,128)(2,1)} %copy.72), calls=%async_computation.1 | async-start | bytes 1048576 | tf_op jit(solution)/shard_map/all_to_all | solution.py:56
  12.1 0.0 copy-done.5
  12.1 0.6 dynamic_slice.10
  15.3 0.0 copy-done.6
  15.3 0.6 dynamic_slice.9
  19.9 0.1 copy.64
  20.1 0.1 broadcast_and_fusion
  20.2 0.0 collective-permute-done
  20.2 0.0 copy-done
  20.2 0.1 select_select_fusion
  20.4 2.4 %collective-permute-start.1 = (bf16[4,9,256]{2,0,1:T(4,128)(2,1)S(1)}, bf16[4,9,256]{2,0,1:T(4,128)(2,1)S(1)}, u32[]{:S(2)}, u32[]{:S(2)}) collective-permute-start(bf16[4,9,256]{2,0,1:T(4,128)(2,1)S(1)} %bitcast.103), channel_id=1, source_target_pairs={{0,1},{1,2},{2,3},{4,5},{5,6},{6,7},{8,9},{9,10},{10,11},{12,13},{... | collective-permute-start | bytes 55304 | tf_op jit(solution)/shard_map/ppermute | solution.py:10
  22.8 0.1 copy.85
  22.9 0.1 copy.87
  23.0 0.1 copy.89
  23.1 0.5 collective-permute-done.1
  23.6 0.6 convolution_convert_fusion
  24.2 0.6 %slice.62 = bf16[4,4,16,384]{3,2,1,0:T(8,128)(2,1)S(1)} slice(bf16[4,9,33,384]{3,2,1,0:T(8,128)(2,1)S(1)} %convolution_convert_fusion), slice={[0:4:1], [0:7:2], [0:31:2], [0:384:1]} | slice | bytes 393216 | tf_op jit(solution)/shard_map/slice | solution.py:72
  24.8 0.6 %slice.63 = bf16[4,4,16,384]{3,2,1,0:T(8,128)(2,1)S(1)} slice(bf16[4,9,33,384]{3,2,1,0:T(8,128)(2,1)S(1)} %convolution_convert_fusion), slice={[0:4:1], [0:7:2], [1:32:2], [0:384:1]} | slice | bytes 393216 | tf_op jit(solution)/shard_map/slice | solution.py:72
  25.4 0.7 %slice.64 = bf16[4,4,16,384]{3,2,1,0:T(8,128)(2,1)S(1)} slice(bf16[4,9,33,384]{3,2,1,0:T(8,128)(2,1)S(1)} %convolution_convert_fusion), slice={[0:4:1], [0:7:2], [2:33:2], [0:384:1]} | slice | bytes 393216 | tf_op jit(solution)/shard_map/slice | solution.py:72
  26.2 0.6 %slice.65 = bf16[4,4,16,384]{3,2,1,0:T(8,128)(2,1)S(1)} slice(bf16[4,9,33,384]{3,2,1,0:T(8,128)(2,1)S(1)} %convolution_convert_fusion), slice={[0:4:1], [1:8:2], [0:31:2], [0:384:1]} | slice | bytes 393216 | tf_op jit(solution)/shard_map/slice | solution.py:72
  26.8 0.6 %slice.66 = bf16[4,4,16,384]{3,2,1,0:T(8,128)(2,1)S(1)} slice(bf16[4,9,33,384]{3,2,1,0:T(8,128)(2,1)S(1)} %convolution_convert_fusion), slice={[0:4:1], [1:8:2], [1:32:2], [0:384:1]} | slice | bytes 393216 | tf_op jit(solution)/shard_map/slice | solution.py:72
  27.4 0.7 %slice.67 = bf16[4,4,16,384]{3,2,1,0:T(8,128)(2,1)S(1)} slice(bf16[4,9,33,384]{3,2,1,0:T(8,128)(2,1)S(1)} %convolution_convert_fusion), slice={[0:4:1], [1:8:2], [2:33:2], [0:384:1]} | slice | bytes 393216 | tf_op jit(solution)/shard_map/slice | solution.py:72
  28.1 1.0 %slice.68 = bf16[4,4,16,384]{3,2,1,0:T(8,128)(2,1)S(1)} slice(bf16[4,9,33,384]{3,2,1,0:T(8,128)(2,1)S(1)} %convolution_convert_fusion), slice={[0:4:1], [2:9:2], [0:31:2], [0:384:1]} | slice | bytes 393216 | tf_op jit(solution)/shard_map/slice | solution.py:72
  29.2 1.0 %slice.69 = bf16[4,4,16,384]{3,2,1,0:T(8,128)(2,1)S(1)} slice(bf16[4,9,33,384]{3,2,1,0:T(8,128)(2,1)S(1)} %convolution_convert_fusion), slice={[0:4:1], [2:9:2], [1:32:2], [0:384:1]} | slice | bytes 393216 | tf_op jit(solution)/shard_map/slice | solution.py:72
  30.2 1.4 %slice.70 = bf16[4,4,16,384]{3,2,1,0:T(8,128)(2,1)S(1)} slice(bf16[4,9,33,384]{3,2,1,0:T(8,128)(2,1)S(1)} %convolution_convert_fusion), slice={[0:4:1], [2:9:2], [2:33:2], [0:384:1]} | slice | bytes 393216 | tf_op jit(solution)/shard_map/slice | solution.py:72
  31.9 0.2 copy.62
  32.1 0.0 copy-start.4
  32.1 0.5 fusion.37
  32.6 0.1 copy-done.4
  32.8 0.4 convolution_add_fusion.2
  33.2 0.5 convolution_add_fusion.1
  33.7 0.0 all-to-all-done.1
  33.7 1.8 %convert_reduce_fusion = (f32[32]{0:T(128)S(1)}, bf16[32,4,16,128]{3,0,2,1:T(8,128)(2,1)S(1)}, bf16[32,4,16,128]{3,0,2,1:T(8,128)(2,1)}) fusion(pred[4,16]{1,0:T(4,128)(4,1)S(1)} %broadcast_and_fusion, f32[4,16,128,32]{2,3,1,0:T(8,128)S(1)} %convolution_add_fusion.1, bf16[32,36,1]{1,0,2:T(8,128)(2,1)S(1)} %copy.89, ...), kind=kOutput, calls=%fused_computation.14 | convolution fusion | flops 23855072 | bytes 3213760 | tf_op jit(solution)/shard_map/ok,kpqr->opqr/dot_general | solution.py:78
  35.5 0.5 convolution_bitcast_fusion
  36.0 0.0 copy-start.1
  36.0 0.5 convolution_bitcast_fusion.1
  36.4 0.5 convolution_bitcast_fusion.2
  36.9 0.1 copy.76
  37.0 0.1 copy.74
  37.1 0.1 copy.75
  37.2 0.1 pad_maximum_fusion.1
  37.3 1.6 %collective-permute-start.2 = (f32[32,109]{1,0:T(8,128)S(1)}, f32[32,109]{1,0:T(8,128)S(1)}, u32[]{:S(2)}, u32[]{:S(2)}) collective-permute-start(f32[32,109]{1,0:T(8,128)S(1)} %pad_maximum_fusion.1), channel_id=1, source_target_pairs={{0,4},{4,0},{8,12},{12,8},{16,20},{20,16},{24,28},{28,24},{1,5},{5... | collective-permute-start | bytes 41864 | tf_op jit(solution)/shard_map/ppermute | solution.py:20
  38.9 1.0 %copy.70 = bf16[32,4,16,128]{3,2,1,0:T(8,128)(2,1)} copy(bf16[32,4,16,128]{3,0,2,1:T(8,128)(2,1)S(1)} %copy-done.1) | data formatting | bytes 1048576 | tf_op jit(solution)/shard_map/convert_element_type | solution.py:84
  39.9 5.1 %all-to-all-start = ((bf16[32,4,16,128]{3,2,1,0:T(8,128)(2,1)}), bf16[32,4,16,128]{3,2,1,0:T(8,128)(2,1)S(1)}, u32[]{:S(2)}, u32[]{:S(2)}) async-start(bf16[32,4,16,128]{3,2,1,0:T(8,128)(2,1)} %copy.70), calls=%async_computation | async-start | bytes 1048576 | tf_op jit(solution)/shard_map/all_to_all | solution.py:87
  45.0 0.0 collective-permute-done.2
  45.0 0.1 fusion.42
  45.1 1.6 %collective-permute-start.3 = (f32[32,109]{1,0:T(8,128)S(1)}, f32[32,109]{1,0:T(8,128)S(1)}, u32[]{:S(2)}, u32[]{:S(2)}) collective-permute-start(f32[32,109]{1,0:T(8,128)S(1)} %fusion.42), channel_id=1, source_target_pairs={{0,8},{4,12},{8,0},{12,4},{16,24},{20,28},{24,16},{28,20},{1,9},{5... | collective-permute-start | bytes 41864 | tf_op jit(solution)/shard_map/ppermute | solution.py:20
  46.6 2.2 %collective-permute-done.3 = f32[32,109]{1,0:T(8,128)S(1)} collective-permute-done((f32[32,109]{1,0:T(8,128)S(1)}, f32[32,109]{1,0:T(8,128)S(1)}, u32[]{:S(2)}, u32[]{:S(2)}) %collective-permute-start.3) | collective-permute-done | bytes 13984 | tf_op jit(solution)/shard_map/ppermute | solution.py:20
  48.8 2.6 %collective-permute-start.4 = (f32[32,109]{1,0:T(8,128)S(1)}, f32[32,109]{1,0:T(8,128)S(1)}, u32[]{:S(2)}, u32[]{:S(2)}) collective-permute-start(f32[32,109]{1,0:T(8,128)S(1)} %add.91), channel_id=1, source_target_pairs={{0,16},{4,20},{8,24},{12,28},{16,0},{20,4},{24,8},{28,12},{1,17},{... | collective-permute-start | bytes 41864 | tf_op jit(solution)/shard_map/ppermute | solution.py:20
  51.4 2.0 %collective-permute-done.4 = f32[32,109]{1,0:T(8,128)S(1)} collective-permute-done((f32[32,109]{1,0:T(8,128)S(1)}, f32[32,109]{1,0:T(8,128)S(1)}, u32[]{:S(2)}, u32[]{:S(2)}) %collective-permute-start.4) | collective-permute-done | bytes 13984 | tf_op jit(solution)/shard_map/ppermute | solution.py:20
  53.5 0.0 collective-permute-start.5
  53.5 1.2 %collective-permute-done.5 = f32[32,109]{1,0:T(8,128)S(1)} collective-permute-done((f32[32,109]{1,0:T(8,128)S(1)}, f32[32,109]{1,0:T(8,128)S(1)}, u32[]{:S(2)}, u32[]{:S(2)}) %collective-permute-start.5) | collective-permute-done | bytes 13984 | tf_op jit(solution)/shard_map/ppermute | solution.py:20
  54.6 2.2 %collective-permute-start.6 = (f32[32,109]{1,0:T(8,128)S(1)}, f32[32,109]{1,0:T(8,128)S(1)}, u32[]{:S(2)}, u32[]{:S(2)}) collective-permute-start(f32[32,109]{1,0:T(8,128)S(1)} %add.93), channel_id=1, source_target_pairs={{0,2},{1,3},{2,0},{3,1},{4,6},{5,7},{6,4},{7,5},{8,10},{9,11},{10,... | collective-permute-start | bytes 41864 | tf_op jit(solution)/shard_map/ppermute | solution.py:20
  56.9 1.7 %collective-permute-done.6 = f32[32,109]{1,0:T(8,128)S(1)} collective-permute-done((f32[32,109]{1,0:T(8,128)S(1)}, f32[32,109]{1,0:T(8,128)S(1)}, u32[]{:S(2)}, u32[]{:S(2)}) %collective-permute-start.6) | collective-permute-done | bytes 13984 | tf_op jit(solution)/shard_map/ppermute | solution.py:20
  58.6 0.7 %slice_reduce_fusion = f32[8]{0:T(128)} fusion(f32[8,109]{1,0:T(8,128)S(1)} %dynamic-slice_add_fusion), kind=kLoop, calls=%fused_computation.51 | loop fusion | bytes 64 | tf_op jit(solution)/shard_map/slice | solution.py:98
  59.3 0.0 all-to-all-done
  59.3 0.9 %copy.71 = bf16[8,4,4,16,128]{4,3,2,1,0:T(8,128)(2,1)} copy(bf16[8,4,4,16,128]{4,3,1,0,2:T(8,128)(2,1)S(1)} %bitcast.101) | data formatting | bytes 1048576 | tf_op jit(solution)/shard_map/all_to_all | solution.py:87
  (29 shorter events, 0.5 us)
Async XLA Ops:
  0.6 19.5 %copy-start = (bf16[4,8,32,256]{3,2,1,0:T(8,128)(2,1)S(1)}, bf16[4,8,32,256]{3,2,1,0:T(8,128)(2,1)}, u32[]{:S(2)}) copy-start(bf16[4,8,32,256]{3,2,1,0:T(8,128)(2,1)} %param.6) | copy-start | bytes 1572868
  0.6 11.5 %copy-start.5 = (s32[4]{0:T(128)S(1)}, s32[4]{0:T(128)}, u32[]{:S(2)}) copy-start(s32[4]{0:T(128)} %param.8) | copy-start | bytes 52
  0.7 14.6 %copy-start.6 = (s32[8]{0:T(128)S(1)}, s32[8]{0:T(128)}, u32[]{:S(2)}) copy-start(s32[8]{0:T(128)} %param.7) | copy-start | bytes 100
  0.7 19.2 %copy-start.3 = (bf16[32,108]{1,0:T(8,128)(2,1)S(1)}, bf16[32,108]{1,0:T(8,128)(2,1)}, u32[]{:S(2)}) copy-start(bf16[32,108]{1,0:T(8,128)(2,1)} %param.9) | copy-start | bytes 20740
  1.6 18.6 %collective-permute-start = (bf16[4,32,256]{2,1,0:T(8,128)(2,1)S(1)}, bf16[4,32,256]{2,1,0:T(8,128)(2,1)S(1)}, u32[]{:S(2)}, u32[]{:S(2)}) collective-permute-start(bf16[4,32,256]{2,1,0:T(8,128)(2,1)S(1)} %slice_bitcast_fusion), channel_id=1, source_target_pairs={{0,4},{4,8},{8,12},{12,16},{16,20},{20,24},{24,28},{1,5},{5,9},{9,... | collective-permute-start | bytes 196616 | tf_op jit(solution)/shard_map/ppermute | solution.py:10
  8.6 25.1 %all-to-all-start.1 = ((bf16[8,4,64,128]{3,0,1,2:T(8,128)(2,1)}), bf16[8,4,64,128]{3,0,1,2:T(8,128)(2,1)S(1)}, u32[]{:S(2)}, u32[]{:S(2)}) async-start(bf16[8,4,64,128]{3,0,1,2:T(8,128)(2,1)} %copy.72), calls=%async_computation.1 | async-start | bytes 1048576 | tf_op jit(solution)/shard_map/all_to_all | solution.py:56
  20.4 3.2 %collective-permute-start.1 = (bf16[4,9,256]{2,0,1:T(4,128)(2,1)S(1)}, bf16[4,9,256]{2,0,1:T(4,128)(2,1)S(1)}, u32[]{:S(2)}, u32[]{:S(2)}) collective-permute-start(bf16[4,9,256]{2,0,1:T(4,128)(2,1)S(1)} %bitcast.103), channel_id=1, source_target_pairs={{0,1},{1,2},{2,3},{4,5},{5,6},{6,7},{8,9},{9,10},{10,11},{12,13},{... | collective-permute-start | bytes 55304 | tf_op jit(solution)/shard_map/ppermute | solution.py:10
  32.1 0.7 %copy-start.4 = (f32[32]{0:T(128)S(1)}, f32[32]{0:T(128)}, u32[]{:S(2)}) copy-start(f32[32]{0:T(128)} %param.10) | copy-start | bytes 388
  36.0 2.9 %copy-start.1 = (bf16[32,4,16,128]{3,0,2,1:T(8,128)(2,1)S(1)}, bf16[32,4,16,128]{3,0,2,1:T(8,128)(2,1)}, u32[]{:S(2)}) copy-start(bf16[32,4,16,128]{3,0,2,1:T(8,128)(2,1)} %get-tuple-element.11) | copy-start | bytes 1572868
  37.3 7.7 %collective-permute-start.2 = (f32[32,109]{1,0:T(8,128)S(1)}, f32[32,109]{1,0:T(8,128)S(1)}, u32[]{:S(2)}, u32[]{:S(2)}) collective-permute-start(f32[32,109]{1,0:T(8,128)S(1)} %pad_maximum_fusion.1), channel_id=1, source_target_pairs={{0,4},{4,0},{8,12},{12,8},{16,20},{20,16},{24,28},{28,24},{1,5},{5... | collective-permute-start | bytes 41864 | tf_op jit(solution)/shard_map/ppermute | solution.py:20
  39.9 19.4 %all-to-all-start = ((bf16[32,4,16,128]{3,2,1,0:T(8,128)(2,1)}), bf16[32,4,16,128]{3,2,1,0:T(8,128)(2,1)S(1)}, u32[]{:S(2)}, u32[]{:S(2)}) async-start(bf16[32,4,16,128]{3,2,1,0:T(8,128)(2,1)} %copy.70), calls=%async_computation | async-start | bytes 1048576 | tf_op jit(solution)/shard_map/all_to_all | solution.py:87
  45.1 3.7 %collective-permute-start.3 = (f32[32,109]{1,0:T(8,128)S(1)}, f32[32,109]{1,0:T(8,128)S(1)}, u32[]{:S(2)}, u32[]{:S(2)}) collective-permute-start(f32[32,109]{1,0:T(8,128)S(1)} %fusion.42), channel_id=1, source_target_pairs={{0,8},{4,12},{8,0},{12,4},{16,24},{20,28},{24,16},{28,20},{1,9},{5... | collective-permute-start | bytes 41864 | tf_op jit(solution)/shard_map/ppermute | solution.py:20
  48.8 4.6 %collective-permute-start.4 = (f32[32,109]{1,0:T(8,128)S(1)}, f32[32,109]{1,0:T(8,128)S(1)}, u32[]{:S(2)}, u32[]{:S(2)}) collective-permute-start(f32[32,109]{1,0:T(8,128)S(1)} %add.91), channel_id=1, source_target_pairs={{0,16},{4,20},{8,24},{12,28},{16,0},{20,4},{24,8},{28,12},{1,17},{... | collective-permute-start | bytes 41864 | tf_op jit(solution)/shard_map/ppermute | solution.py:20
  53.5 1.2 %collective-permute-start.5 = (f32[32,109]{1,0:T(8,128)S(1)}, f32[32,109]{1,0:T(8,128)S(1)}, u32[]{:S(2)}, u32[]{:S(2)}) collective-permute-start(f32[32,109]{1,0:T(8,128)S(1)} %add.92), channel_id=1, source_target_pairs={{0,1},{1,0},{2,3},{3,2},{4,5},{5,4},{6,7},{7,6},{8,9},{9,8},{10,11... | collective-permute-start | bytes 41864 | tf_op jit(solution)/shard_map/ppermute | solution.py:20
  54.6 3.9 %collective-permute-start.6 = (f32[32,109]{1,0:T(8,128)S(1)}, f32[32,109]{1,0:T(8,128)S(1)}, u32[]{:S(2)}, u32[]{:S(2)}) collective-permute-start(f32[32,109]{1,0:T(8,128)S(1)} %add.93), channel_id=1, source_target_pairs={{0,2},{1,3},{2,0},{3,1},{4,6},{5,7},{6,4},{7,5},{8,10},{9,11},{10,... | collective-permute-start | bytes 41864 | tf_op jit(solution)/shard_map/ppermute | solution.py:20
  58.6 1.6 %copy-start.2 = (f32[8,109]{1,0:T(8,128)}, f32[8,109]{1,0:T(8,128)S(1)}, u32[]{:S(2)}) copy-start(f32[8,109]{1,0:T(8,128)S(1)} %dynamic-slice_add_fusion) | copy-start | bytes 10468

commit v5 on v4

--- a/solution.py
+++ b/solution.py
@@ -78,8 +78,7 @@
         conv = conv + jnp.einsum("ok,kpqr->opqr", kernel[:, :, off_z], part, preferred_element_type=jnp.float32)
     col_ok = jnp.arange(half_y, dtype=jnp.int32) >= half_y - col_count // 2
     live = (row_ok[:, None] & col_ok[None, :]).reshape(1, half_x, half_y, 1)
-    pre_local = jnp.where(live, conv, 0.0).astype(jnp.bfloat16)
-    pre_wide = pre_local.astype(jnp.float32)
+    pre_wide = lax.reduce_precision(jnp.where(live, conv, 0.0), exponent_bits=8, mantissa_bits=7)
     sigma = jax.nn.sigmoid(pre_wide)
     stem_local = (pre_wide * sigma).astype(jnp.bfloat16)
     slope = sigma * (1.0 + pre_wide * (1.0 - sigma))

time: 60.6 us -> 60.6 us (level)
  no operation moved by 1% of the time
where the time goes in v5:
time: 60.6 us; the launch traced here: 60.2 us
  starting transfers between devices  23.8 us (39%)
  local copies, waits for them, and re-layouts  16 us (26%)
  waiting for transfers between devices  7.61 us (13%)
  between operations  7.56 us (12%)
  matrix products  4.73 us (8%)
    ppermute x5, starting transfers between devices, butterfly_sum(): value = value + lax.ppermute(value, axis, swap)  7.97 us
    slice x9, local copies, waits for them, and re-layouts, local(): ztaps[:, off_x:off_x + 2 * half_x - 1:2, off_y:off_y + 2 * half_y - 1:2]  7.27 us
    ppermute x2, starting transfers between devices, from_behind(): return lax.ppermute(block, axis, route)  7.22 us
    ppermute x5, waiting for transfers between devices, butterfly_sum(): value = value + lax.ppermute(value, axis, swap)  7.08 us
    all_to_all x1, starting transfers between devices, local(): lax.all_to_all(stem_local, 'gy', split_axis=0, concat_axis=2, tiled=True)  5.12 us
    all_to_all x1, starting transfers between devices, local(): lax.all_to_all(grad_out, 'gy', split_axis=2, concat_axis=0, tiled=True)  3.47 us
    unnamed x27, local copies, waits for them, and re-layouts  2.98 us
    dot_general x3, matrix products, local(): jnp.einsum('ok,kpqr->opqr', kernel[:, :, off_z], part, preferred_element_...  2.76 us
  transfers between devices with their start and end apart: 9, of which 5 were waited for; matrix products, arithmetic and copies ran while one was open for 26% of the time, Pallas kernels for 0%

profile of v5, /device:TPU:0, one launch (start us, length us, event | category | flops | bytes accessed | tf_op | source)
XLA Modules:
  0.0 60.2 jit_solution(17281578985451194577)
XLA Ops:
  0.6 0.0 copy-start
  0.6 0.0 copy-start.5
  0.7 0.0 copy-start.6
  0.7 0.0 copy-start.3
  0.7 0.9 %slice_bitcast_fusion = bf16[4,32,256]{2,1,0:T(8,128)(2,1)S(1)} fusion(bf16[4,8,32,256]{3,2,1,0:T(8,128)(2,1)} %param.6), kind=kLoop, calls=%fused_computation.42 | loop fusion | bytes 131072 | tf_op jit(solution)/shard_map/squeeze | solution.py:58
  1.6 4.9 %collective-permute-start = (bf16[4,32,256]{2,1,0:T(8,128)(2,1)S(1)}, bf16[4,32,256]{2,1,0:T(8,128)(2,1)S(1)}, u32[]{:S(2)}, u32[]{:S(2)}) collective-permute-start(bf16[4,32,256]{2,1,0:T(8,128)(2,1)S(1)} %slice_bitcast_fusion), channel_id=1, source_target_pairs={{0,4},{4,8},{8,12},{12,16},{16,20},{20,24},{24,28},{1,5},{5,9},{9,... | collective-permute-start | bytes 196616 | tf_op jit(solution)/shard_map/ppermute | solution.py:10
  6.4 2.2 %copy.72 = bf16[8,4,64,128]{3,0,1,2:T(8,128)(2,1)} copy(bf16[8,4,64,128]{3,2,1,0:T(8,128)(2,1)} %param.11) | data formatting | bytes 1048576 | tf_op args[5]
  8.6 3.5 %all-to-all-start.1 = ((bf16[8,4,64,128]{3,0,1,2:T(8,128)(2,1)}), bf16[8,4,64,128]{3,0,1,2:T(8,128)(2,1)S(1)}, u32[]{:S(2)}, u32[]{:S(2)}) async-start(bf16[8,4,64,128]{3,0,1,2:T(8,128)(2,1)} %copy.72), calls=%async_computation.1 | async-start | bytes 1048576 | tf_op jit(solution)/shard_map/all_to_all | solution.py:56
  12.1 0.0 copy-done.5
  12.1 0.6 dynamic_slice.10
  15.3 0.0 copy-done.6
  15.3 0.6 dynamic_slice.9
  19.9 0.1 copy.64
  20.1 0.1 broadcast_and_fusion
  20.2 0.0 collective-permute-done
  20.2 0.1 select_select_fusion
  20.4 2.4 %collective-permute-start.1 = (bf16[4,9,256]{2,0,1:T(4,128)(2,1)S(1)}, bf16[4,9,256]{2,0,1:T(4,128)(2,1)S(1)}, u32[]{:S(2)}, u32[]{:S(2)}) collective-permute-start(bf16[4,9,256]{2,0,1:T(4,128)(2,1)S(1)} %bitcast.103), channel_id=1, source_target_pairs={{0,1},{1,2},{2,3},{4,5},{5,6},{6,7},{8,9},{9,10},{10,11},{12,13},{... | collective-permute-start | bytes 55304 | tf_op jit(solution)/shard_map/ppermute | solution.py:10
  22.8 0.1 copy.85
  22.9 0.1 copy.87
  23.0 0.1 copy.89
  23.1 0.5 collective-permute-done.1
  23.6 0.6 convolution_convert_fusion
  24.2 0.6 %slice.62 = bf16[4,4,16,384]{3,2,1,0:T(8,128)(2,1)S(1)} slice(bf16[4,9,33,384]{3,2,1,0:T(8,128)(2,1)S(1)} %convolution_convert_fusion), slice={[0:4:1], [0:7:2], [0:31:2], [0:384:1]} | slice | bytes 393216 | tf_op jit(solution)/shard_map/slice | solution.py:72
  24.8 0.6 %slice.63 = bf16[4,4,16,384]{3,2,1,0:T(8,128)(2,1)S(1)} slice(bf16[4,9,33,384]{3,2,1,0:T(8,128)(2,1)S(1)} %convolution_convert_fusion), slice={[0:4:1], [0:7:2], [1:32:2], [0:384:1]} | slice | bytes 393216 | tf_op jit(solution)/shard_map/slice | solution.py:72
  25.4 0.7 %slice.64 = bf16[4,4,16,384]{3,2,1,0:T(8,128)(2,1)S(1)} slice(bf16[4,9,33,384]{3,2,1,0:T(8,128)(2,1)S(1)} %convolution_convert_fusion), slice={[0:4:1], [0:7:2], [2:33:2], [0:384:1]} | slice | bytes 393216 | tf_op jit(solution)/shard_map/slice | solution.py:72
  26.2 0.6 %slice.65 = bf16[4,4,16,384]{3,2,1,0:T(8,128)(2,1)S(1)} slice(bf16[4,9,33,384]{3,2,1,0:T(8,128)(2,1)S(1)} %convolution_convert_fusion), slice={[0:4:1], [1:8:2], [0:31:2], [0:384:1]} | slice | bytes 393216 | tf_op jit(solution)/shard_map/slice | solution.py:72
  26.8 0.6 %slice.66 = bf16[4,4,16,384]{3,2,1,0:T(8,128)(2,1)S(1)} slice(bf16[4,9,33,384]{3,2,1,0:T(8,128)(2,1)S(1)} %convolution_convert_fusion), slice={[0:4:1], [1:8:2], [1:32:2], [0:384:1]} | slice | bytes 393216 | tf_op jit(solution)/shard_map/slice | solution.py:72
  27.4 0.7 %slice.67 = bf16[4,4,16,384]{3,2,1,0:T(8,128)(2,1)S(1)} slice(bf16[4,9,33,384]{3,2,1,0:T(8,128)(2,1)S(1)} %convolution_convert_fusion), slice={[0:4:1], [1:8:2], [2:33:2], [0:384:1]} | slice | bytes 393216 | tf_op jit(solution)/shard_map/slice | solution.py:72
  28.1 1.0 %slice.68 = bf16[4,4,16,384]{3,2,1,0:T(8,128)(2,1)S(1)} slice(bf16[4,9,33,384]{3,2,1,0:T(8,128)(2,1)S(1)} %convolution_convert_fusion), slice={[0:4:1], [2:9:2], [0:31:2], [0:384:1]} | slice | bytes 393216 | tf_op jit(solution)/shard_map/slice | solution.py:72
  29.2 1.0 %slice.69 = bf16[4,4,16,384]{3,2,1,0:T(8,128)(2,1)S(1)} slice(bf16[4,9,33,384]{3,2,1,0:T(8,128)(2,1)S(1)} %convolution_convert_fusion), slice={[0:4:1], [2:9:2], [1:32:2], [0:384:1]} | slice | bytes 393216 | tf_op jit(solution)/shard_map/slice | solution.py:72
  30.2 1.4 %slice.70 = bf16[4,4,16,384]{3,2,1,0:T(8,128)(2,1)S(1)} slice(bf16[4,9,33,384]{3,2,1,0:T(8,128)(2,1)S(1)} %convolution_convert_fusion), slice={[0:4:1], [2:9:2], [2:33:2], [0:384:1]} | slice | bytes 393216 | tf_op jit(solution)/shard_map/slice | solution.py:72
  31.9 0.2 copy.62
  32.1 0.0 copy-start.4
  32.1 0.5 fusion.36
  32.6 0.1 copy-done.4
  32.8 0.4 convolution_add_fusion.2
  33.2 0.5 convolution_add_fusion.1
  33.7 0.0 all-to-all-done.1
  33.7 1.9 %convert_reduce_fusion = (f32[32]{0:T(128)S(1)}, bf16[32,4,16,128]{3,0,2,1:T(8,128)(2,1)S(1)}, bf16[32,4,16,128]{3,0,2,1:T(8,128)(2,1)}) fusion(pred[4,16]{1,0:T(4,128)(4,1)S(1)} %broadcast_and_fusion, f32[4,16,128,32]{2,3,1,0:T(8,128)S(1)} %convolution_add_fusion.1, bf16[32,36,1]{1,0,2:T(8,128)(2,1)S(1)} %copy.89, ...), kind=kOutput, calls=%fused_computation.13 | convolution fusion | flops 23592928 | bytes 3213760 | tf_op jit(solution)/shard_map/ok,kpqr->opqr/dot_general | solution.py:78
  35.5 0.5 convolution_bitcast_fusion
  36.0 0.0 copy-start.1
  36.0 0.5 convolution_bitcast_fusion.1
  36.5 0.5 convolution_bitcast_fusion.2
  36.9 0.1 copy.76
  37.0 0.1 copy.74
  37.2 0.1 copy.75
  37.3 0.1 pad_maximum_fusion.1
  37.3 1.6 %collective-permute-start.2 = (f32[32,109]{1,0:T(8,128)S(1)}, f32[32,109]{1,0:T(8,128)S(1)}, u32[]{:S(2)}, u32[]{:S(2)}) collective-permute-start(f32[32,109]{1,0:T(8,128)S(1)} %pad_maximum_fusion.1), channel_id=1, source_target_pairs={{0,4},{4,0},{8,12},{12,8},{16,20},{20,16},{24,28},{28,24},{1,5},{5... | collective-permute-start | bytes 41864 | tf_op jit(solution)/shard_map/ppermute | solution.py:20
  38.9 1.0 %copy.70 = bf16[32,4,16,128]{3,2,1,0:T(8,128)(2,1)} copy(bf16[32,4,16,128]{3,0,2,1:T(8,128)(2,1)S(1)} %copy-done.1) | data formatting | bytes 1048576 | tf_op jit(solution)/shard_map/convert_element_type | solution.py:83
  39.9 5.1 %all-to-all-start = ((bf16[32,4,16,128]{3,2,1,0:T(8,128)(2,1)}), bf16[32,4,16,128]{3,2,1,0:T(8,128)(2,1)S(1)}, u32[]{:S(2)}, u32[]{:S(2)}) async-start(bf16[32,4,16,128]{3,2,1,0:T(8,128)(2,1)} %copy.70), calls=%async_computation | async-start | bytes 1048576 | tf_op jit(solution)/shard_map/all_to_all | solution.py:86
  45.0 0.0 collective-permute-done.2
  45.0 0.1 fusion.41
  45.1 1.6 %collective-permute-start.3 = (f32[32,109]{1,0:T(8,128)S(1)}, f32[32,109]{1,0:T(8,128)S(1)}, u32[]{:S(2)}, u32[]{:S(2)}) collective-permute-start(f32[32,109]{1,0:T(8,128)S(1)} %fusion.41), channel_id=1, source_target_pairs={{0,8},{4,12},{8,0},{12,4},{16,24},{20,28},{24,16},{28,20},{1,9},{5... | collective-permute-start | bytes 41864 | tf_op jit(solution)/shard_map/ppermute | solution.py:20
  46.7 2.2 %collective-permute-done.3 = f32[32,109]{1,0:T(8,128)S(1)} collective-permute-done((f32[32,109]{1,0:T(8,128)S(1)}, f32[32,109]{1,0:T(8,128)S(1)}, u32[]{:S(2)}, u32[]{:S(2)}) %collective-permute-start.3) | collective-permute-done | bytes 13984 | tf_op jit(solution)/shard_map/ppermute | solution.py:20
  48.9 2.6 %collective-permute-start.4 = (f32[32,109]{1,0:T(8,128)S(1)}, f32[32,109]{1,0:T(8,128)S(1)}, u32[]{:S(2)}, u32[]{:S(2)}) collective-permute-start(f32[32,109]{1,0:T(8,128)S(1)} %add.91), channel_id=1, source_target_pairs={{0,16},{4,20},{8,24},{12,28},{16,0},{20,4},{24,8},{28,12},{1,17},{... | collective-permute-start | bytes 41864 | tf_op jit(solution)/shard_map/ppermute | solution.py:20
  51.5 2.0 %collective-permute-done.4 = f32[32,109]{1,0:T(8,128)S(1)} collective-permute-done((f32[32,109]{1,0:T(8,128)S(1)}, f32[32,109]{1,0:T(8,128)S(1)}, u32[]{:S(2)}, u32[]{:S(2)}) %collective-permute-start.4) | collective-permute-done | bytes 13984 | tf_op jit(solution)/shard_map/ppermute | solution.py:20
  53.5 0.0 collective-permute-start.5
  53.5 1.2 %collective-permute-done.5 = f32[32,109]{1,0:T(8,128)S(1)} collective-permute-done((f32[32,109]{1,0:T(8,128)S(1)}, f32[32,109]{1,0:T(8,128)S(1)}, u32[]{:S(2)}, u32[]{:S(2)}) %collective-permute-start.5) | collective-permute-done | bytes 13984 | tf_op jit(solution)/shard_map/ppermute | solution.py:20
  54.7 2.2 %collective-permute-start.6 = (f32[32,109]{1,0:T(8,128)S(1)}, f32[32,109]{1,0:T(8,128)S(1)}, u32[]{:S(2)}, u32[]{:S(2)}) collective-permute-start(f32[32,109]{1,0:T(8,128)S(1)} %add.93), channel_id=1, source_target_pairs={{0,2},{1,3},{2,0},{3,1},{4,6},{5,7},{6,4},{7,5},{8,10},{9,11},{10,... | collective-permute-start | bytes 41864 | tf_op jit(solution)/shard_map/ppermute | solution.py:20
  56.9 1.7 %collective-permute-done.6 = f32[32,109]{1,0:T(8,128)S(1)} collective-permute-done((f32[32,109]{1,0:T(8,128)S(1)}, f32[32,109]{1,0:T(8,128)S(1)}, u32[]{:S(2)}, u32[]{:S(2)}) %collective-permute-start.6) | collective-permute-done | bytes 13984 | tf_op jit(solution)/shard_map/ppermute | solution.py:20
  58.6 0.7 %slice_reduce_fusion = f32[8]{0:T(128)} fusion(f32[8,109]{1,0:T(8,128)S(1)} %dynamic-slice_add_fusion), kind=kLoop, calls=%fused_computation.50 | loop fusion | bytes 64 | tf_op jit(solution)/shard_map/slice | solution.py:97
  59.3 0.0 all-to-all-done
  59.3 0.9 %copy.71 = bf16[8,4,4,16,128]{4,3,2,1,0:T(8,128)(2,1)} copy(bf16[8,4,4,16,128]{4,3,1,0,2:T(8,128)(2,1)S(1)} %bitcast.101) | data formatting | bytes 1048576 | tf_op jit(solution)/shard_map/all_to_all | solution.py:86
  60.2 0.0 copy-done.2
  (29 shorter events, 0.5 us)
Async XLA Ops:
  0.6 19.5 %copy-start = (bf16[4,8,32,256]{3,2,1,0:T(8,128)(2,1)S(1)}, bf16[4,8,32,256]{3,2,1,0:T(8,128)(2,1)}, u32[]{:S(2)}) copy-start(bf16[4,8,32,256]{3,2,1,0:T(8,128)(2,1)} %param.6) | copy-start | bytes 1572868
  0.6 11.5 %copy-start.5 = (s32[4]{0:T(128)S(1)}, s32[4]{0:T(128)}, u32[]{:S(2)}) copy-start(s32[4]{0:T(128)} %param.8) | copy-start | bytes 52
  0.7 14.6 %copy-start.6 = (s32[8]{0:T(128)S(1)}, s32[8]{0:T(128)}, u32[]{:S(2)}) copy-start(s32[8]{0:T(128)} %param.7) | copy-start | bytes 100
  0.7 19.2 %copy-start.3 = (bf16[32,108]{1,0:T(8,128)(2,1)S(1)}, bf16[32,108]{1,0:T(8,128)(2,1)}, u32[]{:S(2)}) copy-start(bf16[32,108]{1,0:T(8,128)(2,1)} %param.9) | copy-start | bytes 20740
  1.6 18.6 %collective-permute-start = (bf16[4,32,256]{2,1,0:T(8,128)(2,1)S(1)}, bf16[4,32,256]{2,1,0:T(8,128)(2,1)S(1)}, u32[]{:S(2)}, u32[]{:S(2)}) collective-permute-start(bf16[4,32,256]{2,1,0:T(8,128)(2,1)S(1)} %slice_bitcast_fusion), channel_id=1, source_target_pairs={{0,4},{4,8},{8,12},{12,16},{16,20},{20,24},{24,28},{1,5},{5,9},{9,... | collective-permute-start | bytes 196616 | tf_op jit(solution)/shard_map/ppermute | solution.py:10
  8.6 25.1 %all-to-all-start.1 = ((bf16[8,4,64,128]{3,0,1,2:T(8,128)(2,1)}), bf16[8,4,64,128]{3,0,1,2:T(8,128)(2,1)S(1)}, u32[]{:S(2)}, u32[]{:S(2)}) async-start(bf16[8,4,64,128]{3,0,1,2:T(8,128)(2,1)} %copy.72), calls=%async_computation.1 | async-start | bytes 1048576 | tf_op jit(solution)/shard_map/all_to_all | solution.py:56
  20.4 3.2 %collective-permute-start.1 = (bf16[4,9,256]{2,0,1:T(4,128)(2,1)S(1)}, bf16[4,9,256]{2,0,1:T(4,128)(2,1)S(1)}, u32[]{:S(2)}, u32[]{:S(2)}) collective-permute-start(bf16[4,9,256]{2,0,1:T(4,128)(2,1)S(1)} %bitcast.103), channel_id=1, source_target_pairs={{0,1},{1,2},{2,3},{4,5},{5,6},{6,7},{8,9},{9,10},{10,11},{12,13},{... | collective-permute-start | bytes 55304 | tf_op jit(solution)/shard_map/ppermute | solution.py:10
  32.1 0.7 %copy-start.4 = (f32[32]{0:T(128)S(1)}, f32[32]{0:T(128)}, u32[]{:S(2)}) copy-start(f32[32]{0:T(128)} %param.10) | copy-start | bytes 388
  36.0 2.9 %copy-start.1 = (bf16[32,4,16,128]{3,0,2,1:T(8,128)(2,1)S(1)}, bf16[32,4,16,128]{3,0,2,1:T(8,128)(2,1)}, u32[]{:S(2)}) copy-start(bf16[32,4,16,128]{3,0,2,1:T(8,128)(2,1)} %get-tuple-element.11) | copy-start | bytes 1572868
  37.3 7.7 %collective-permute-start.2 = (f32[32,109]{1,0:T(8,128)S(1)}, f32[32,109]{1,0:T(8,128)S(1)}, u32[]{:S(2)}, u32[]{:S(2)}) collective-permute-start(f32[32,109]{1,0:T(8,128)S(1)} %pad_maximum_fusion.1), channel_id=1, source_target_pairs={{0,4},{4,0},{8,12},{12,8},{16,20},{20,16},{24,28},{28,24},{1,5},{5... | collective-permute-start | bytes 41864 | tf_op jit(solution)/shard_map/ppermute | solution.py:20
  39.9 19.4 %all-to-all-start = ((bf16[32,4,16,128]{3,2,1,0:T(8,128)(2,1)}), bf16[32,4,16,128]{3,2,1,0:T(8,128)(2,1)S(1)}, u32[]{:S(2)}, u32[]{:S(2)}) async-start(bf16[32,4,16,128]{3,2,1,0:T(8,128)(2,1)} %copy.70), calls=%async_computation | async-start | bytes 1048576 | tf_op jit(solution)/shard_map/all_to_all | solution.py:86
  45.1 3.7 %collective-permute-start.3 = (f32[32,109]{1,0:T(8,128)S(1)}, f32[32,109]{1,0:T(8,128)S(1)}, u32[]{:S(2)}, u32[]{:S(2)}) collective-permute-start(f32[32,109]{1,0:T(8,128)S(1)} %fusion.41), channel_id=1, source_target_pairs={{0,8},{4,12},{8,0},{12,4},{16,24},{20,28},{24,16},{28,20},{1,9},{5... | collective-permute-start | bytes 41864 | tf_op jit(solution)/shard_map/ppermute | solution.py:20
  48.9 4.6 %collective-permute-start.4 = (f32[32,109]{1,0:T(8,128)S(1)}, f32[32,109]{1,0:T(8,128)S(1)}, u32[]{:S(2)}, u32[]{:S(2)}) collective-permute-start(f32[32,109]{1,0:T(8,128)S(1)} %add.91), channel_id=1, source_target_pairs={{0,16},{4,20},{8,24},{12,28},{16,0},{20,4},{24,8},{28,12},{1,17},{... | collective-permute-start | bytes 41864 | tf_op jit(solution)/shard_map/ppermute | solution.py:20
  53.5 1.2 %collective-permute-start.5 = (f32[32,109]{1,0:T(8,128)S(1)}, f32[32,109]{1,0:T(8,128)S(1)}, u32[]{:S(2)}, u32[]{:S(2)}) collective-permute-start(f32[32,109]{1,0:T(8,128)S(1)} %add.92), channel_id=1, source_target_pairs={{0,1},{1,0},{2,3},{3,2},{4,5},{5,4},{6,7},{7,6},{8,9},{9,8},{10,11... | collective-permute-start | bytes 41864 | tf_op jit(solution)/shard_map/ppermute | solution.py:20
  54.7 3.9 %collective-permute-start.6 = (f32[32,109]{1,0:T(8,128)S(1)}, f32[32,109]{1,0:T(8,128)S(1)}, u32[]{:S(2)}, u32[]{:S(2)}) collective-permute-start(f32[32,109]{1,0:T(8,128)S(1)} %add.93), channel_id=1, source_target_pairs={{0,2},{1,3},{2,0},{3,1},{4,6},{5,7},{6,4},{7,5},{8,10},{9,11},{10,... | collective-permute-start | bytes 41864 | tf_op jit(solution)/shard_map/ppermute | solution.py:20
  58.6 1.6 %copy-start.2 = (f32[8,109]{1,0:T(8,128)}, f32[8,109]{1,0:T(8,128)S(1)}, u32[]{:S(2)}) copy-start(f32[8,109]{1,0:T(8,128)S(1)} %dynamic-slice_add_fusion) | copy-start | bytes 10468

commit v6 on v5

--- a/solution.py
+++ b/solution.py
@@ -8,6 +8,17 @@
     devices = range(lax.axis_size(axis))
     route = [(i - distance, i) for i in devices if i - distance in devices]
     return lax.ppermute(block, axis, route)
+
+
+def from_diagonal(block):
+    nx, ny = lax.axis_size("gx"), lax.axis_size("gy")
+    route = [((i - 1) * ny + j - 1, i * ny + j) for i in range(1, nx) for j in range(1, ny)]
+    return lax.ppermute(block, ("gx", "gy"), route)
+
+
+def pick_count(counts, axis):
+    here = jnp.arange(counts.shape[0], dtype=jnp.int32) == lax.axis_index(axis)
+    return jnp.sum(jnp.where(here, counts, 0))
 
 
 def butterfly_sum(value, axis):
@@ -54,12 +65,14 @@
     out_chans = weight.shape[0]
     tiles_y = lax.axis_size("gy")
     cell_grad = lax.all_to_all(grad_out, "gy", split_axis=2, concat_axis=0, tiled=True)
-    row_count = rows_live[lax.axis_index("gx")]
+    row_count = pick_count(rows_live, "gx")
+    col_count = pick_count(cols_live, "gy")
     above = from_behind(fields[:, cap_x - 1], "gx", 1)
+    side = from_behind(fields[:, :, cap_y - 1], "gy", 1)
+    corner = from_diagonal(fields[:, cap_x - 1, cap_y - 1])
     ext_rows = extend(fields, above, row_count, 1)
+    beside = extend(side, corner, row_count, 1)
     row_ok = jnp.arange(half_x, dtype=jnp.int32) >= half_x - row_count // 2
-    col_count = cols_live[lax.axis_index("gy")]
-    beside = from_behind(ext_rows[:, :, cap_y - 1], "gy", 1)
     ext_full = extend(ext_rows, beside, col_count, 2)
     lanes = jnp.arange(3 * half_z, dtype=jnp.int32)
     source = 2 * (lanes % half_z) + lanes // half_z - 1
@@ -82,14 +95,16 @@
     sigma = jax.nn.sigmoid(pre_wide)
     stem_local = (pre_wide * sigma).astype(jnp.bfloat16)
     slope = sigma * (1.0 + pre_wide * (1.0 - sigma))
-    returned = jnp.where(live, cell_grad.astype(jnp.float32) * slope, 0.0).astype(jnp.bfloat16)
+    grad_wide = jnp.where(live, cell_grad.astype(jnp.float32) * slope, 0.0)
+    grad_wide = lax.reduce_precision(grad_wide, exponent_bits=8, mantissa_bits=7)
+    returned = grad_wide.astype(jnp.bfloat16)
     stem = lax.all_to_all(stem_local, "gy", split_axis=0, concat_axis=2, tiled=True)
     grads = []
     for off_z in range(3):
         part = stacked[..., off_z * half_z : (off_z + 1) * half_z]
         grads.append(jnp.einsum("opqr,kpqr->ok", returned, part, preferred_element_type=jnp.float32))
     weight_full = jnp.stack(grads, axis=-1).reshape(out_chans, -1)
-    bias_full = jnp.sum(returned.astype(jnp.float32), axis=(1, 2, 3))
+    bias_full = jnp.sum(grad_wide, axis=(1, 2, 3))
     packed = jnp.concatenate([weight_full, bias_full[:, None]], axis=1)
     total = butterfly_sum(butterfly_sum(packed, "gx"), "gy")
     rows = out_chans // tiles_y

time: 60.6 us -> 64.4 us (1.063)
  starting transfers between devices: 23.8 us -> 26.1 us
  other arithmetic: 0.43 us -> 1.77 us
    ppermute x0 -> x1, starting transfers between devices: none -> 5.14 us  [from_diagonal(): return lax.ppermute(block, ('gx', 'gy'), route)]
    all_to_all x1, starting transfers between devices: 5.12 us -> 3.47 us  [local(): lax.all_to_all(stem_local, 'gy', split_axis=0, concat_axis=2, tiled=True)]
    slice x2, local copies, waits for them, and re-layouts: 0.05 us -> 1.67 us  [the longest x1 0.94 us: local(): side = from_behind(fields[:, :, cap_y - 1], 'gy', 1)]
    reduce_sum x0 -> x2, other arithmetic: none -> 1.26 us  [pick_count(): return jnp.sum(jnp.where(here, counts, 0))]
    dynamic_slice x2 -> x0, local copies, waits for them, and re-layouts: 1.17 us -> none  [the longest x1 0.59 us: local(): col_count = cols_live[lax.axis_index('gy')]]
    ppermute x2, starting transfers between devices: 7.22 us -> 6.32 us  [from_behind(): return lax.ppermute(block, axis, route)]
    unnamed x27 -> x29, local copies, waits for them, and re-layouts: 2.98 us -> 3 us
  transfers between devices with their start and end apart: 9 -> 10, of which waited for: 5 -> 4; matrix products, arithmetic and copies ran while one was open for 26% -> 27% of each run, Pallas kernels for 0% -> 0%
where the time goes in v6:
time: 64.4 us; the launch traced here: 63.8 us
  starting transfers between devices  26.1 us (41%)
  local copies, waits for them, and re-layouts  16.5 us (26%)
  between operations  7.59 us (12%)
  waiting for transfers between devices  7.17 us (11%)
  matrix products  4.76 us (7%)
  other arithmetic  1.77 us (3%)
    ppermute x5, starting transfers between devices, butterfly_sum(): value = value + lax.ppermute(value, axis, swap)  7.65 us
    slice x9, local copies, waits for them, and re-layouts, local(): ztaps[:, off_x:off_x + 2 * half_x - 1:2, off_y:off_y + 2 * half_y - 1:2]  7.27 us
    ppermute x5, waiting for transfers between devices, butterfly_sum(): value = value + lax.ppermute(value, axis, swap)  7.16 us
    ppermute x2, starting transfers between devices, from_behind(): return lax.ppermute(block, axis, route)  6.32 us
    ppermute x1, starting transfers between devices, from_diagonal(): return lax.ppermute(block, ('gx', 'gy'), route)  5.14 us
    all_to_all x1, starting transfers between devices, local(): lax.all_to_all(grad_out, 'gy', split_axis=2, concat_axis=0, tiled=True)  3.47 us
    all_to_all x1, starting transfers between devices, local(): lax.all_to_all(stem_local, 'gy', split_axis=0, concat_axis=2, tiled=True)  3.47 us
    unnamed x29, local copies, waits for them, and re-layouts  3 us
  transfers between devices with their start and end apart: 10, of which 4 were waited for; matrix products, arithmetic and copies ran while one was open for 27% of the time, Pallas kernels for 0%

profile of v6, /device:TPU:0, one launch (start us, length us, event | category | flops | bytes accessed | tf_op | source)
XLA Modules:
  0.0 63.8 jit_solution(7571755628594108016)
XLA Ops:
  0.6 0.0 copy-start
  0.7 0.9 %slice_bitcast_fusion = bf16[4,32,256]{2,1,0:T(8,128)(2,1)S(1)} fusion(bf16[4,8,32,256]{3,2,1,0:T(8,128)(2,1)} %param.6), kind=kLoop, calls=%fused_computation.41 | loop fusion | bytes 131072 | tf_op jit(solution)/shard_map/squeeze | solution.py:70
  1.6 4.9 %collective-permute-start.2 = (bf16[4,32,256]{2,1,0:T(8,128)(2,1)S(1)}, bf16[4,32,256]{2,1,0:T(8,128)(2,1)S(1)}, u32[]{:S(2)}, u32[]{:S(2)}) collective-permute-start(bf16[4,32,256]{2,1,0:T(8,128)(2,1)S(1)} %slice_bitcast_fusion), channel_id=1, source_target_pairs={{0,4},{4,8},{8,12},{12,16},{16,20},{20,24},{24,28},{1,5},{5,9},{9,... | collective-permute-start | bytes 196616 | tf_op jit(solution)/shard_map/ppermute | solution.py:10
  6.4 0.9 %slice.64 = bf16[4,8,1,256]{3,2,1,0:T(2,128)(2,1)S(1)} slice(bf16[4,8,32,256]{3,2,1,0:T(8,128)(2,1)} %param.6), slice={[0:4], [0:8], [31:32], [0:256]} | slice | bytes 32768 | tf_op jit(solution)/shard_map/slice | solution.py:71
  7.4 1.5 %collective-permute-start.1 = (bf16[4,8,256]{2,1,0:T(8,128)(2,1)S(1)}, bf16[4,8,256]{2,1,0:T(8,128)(2,1)S(1)}, u32[]{:S(2)}, u32[]{:S(2)}) collective-permute-start(bf16[4,8,256]{2,1,0:T(8,128)(2,1)S(1)} %bitcast.104), channel_id=1, source_target_pairs={{0,1},{1,2},{2,3},{4,5},{5,6},{6,7},{8,9},{9,10},{10,11},{12,13},{... | collective-permute-start | bytes 49160 | tf_op jit(solution)/shard_map/ppermute | solution.py:10
  8.9 0.7 %slice.63 = bf16[4,1,1,256]{3,2,1,0:T(2,128)(2,1)S(1)} slice(bf16[4,8,32,256]{3,2,1,0:T(8,128)(2,1)} %param.6), slice={[0:4], [7:8], [31:32], [0:256]} | slice | bytes 4096 | tf_op jit(solution)/shard_map/slice | solution.py:72
  9.6 5.1 %collective-permute-start = (bf16[4,256]{1,0:T(4,128)(2,1)S(1)}, bf16[4,256]{1,0:T(4,128)(2,1)S(1)}, u32[]{:S(2)}, u32[]{:S(2)}) collective-permute-start(bf16[4,256]{1,0:T(4,128)(2,1)S(1)} %bitcast.106), channel_id=1, source_target_pairs={{0,5},{1,6},{2,7},{4,9},{5,10},{6,11},{8,13},{9,14},{10,15},{12,17... | collective-permute-start | bytes 6152 | tf_op jit(solution)/shard_map/ppermute | solution.py:16
  14.8 2.2 %copy.68 = bf16[8,4,64,128]{3,0,1,2:T(8,128)(2,1)} copy(bf16[8,4,64,128]{3,2,1,0:T(8,128)(2,1)} %param.11) | data formatting | bytes 1048576 | tf_op args[5]
  16.9 3.5 %all-to-all-start.1 = ((bf16[8,4,64,128]{3,0,1,2:T(8,128)(2,1)}), bf16[8,4,64,128]{3,0,1,2:T(8,128)(2,1)S(1)}, u32[]{:S(2)}, u32[]{:S(2)}) async-start(bf16[8,4,64,128]{3,0,1,2:T(8,128)(2,1)} %copy.68), calls=%async_computation.1 | async-start | bytes 1048576 | tf_op jit(solution)/shard_map/all_to_all | solution.py:67
  20.4 0.6 fusion.35
  23.7 0.6 fusion.34
  28.3 0.1 copy.60
  28.5 0.1 broadcast_and_fusion
  28.6 0.1 copy.83
  28.7 0.1 copy.85
  28.8 0.1 copy.87
  28.9 0.0 collective-permute-done
  28.9 0.0 collective-permute-done.1
  28.9 0.1 select_select_fusion.1
  29.0 0.0 collective-permute-done.2
  29.0 0.1 select_select_fusion
  29.1 0.6 convolution_convert_fusion
  29.7 0.6 slice.66
  30.3 0.6 slice.67
  31.0 0.7 %slice.68 = bf16[4,4,16,384]{3,2,1,0:T(8,128)(2,1)S(1)} slice(bf16[4,9,33,384]{3,2,1,0:T(8,128)(2,1)S(1)} %convolution_convert_fusion), slice={[0:4:1], [0:7:2], [2:33:2], [0:384:1]} | slice | bytes 393216 | tf_op jit(solution)/shard_map/slice | solution.py:85
  31.7 0.6 slice.69
  32.3 0.6 slice.70
  32.9 0.7 %slice.71 = bf16[4,4,16,384]{3,2,1,0:T(8,128)(2,1)S(1)} slice(bf16[4,9,33,384]{3,2,1,0:T(8,128)(2,1)S(1)} %convolution_convert_fusion), slice={[0:4:1], [1:8:2], [2:33:2], [0:384:1]} | slice | bytes 393216 | tf_op jit(solution)/shard_map/slice | solution.py:85
  33.7 1.0 %slice.72 = bf16[4,4,16,384]{3,2,1,0:T(8,128)(2,1)S(1)} slice(bf16[4,9,33,384]{3,2,1,0:T(8,128)(2,1)S(1)} %convolution_convert_fusion), slice={[0:4:1], [2:9:2], [0:31:2], [0:384:1]} | slice | bytes 393216 | tf_op jit(solution)/shard_map/slice | solution.py:85
  34.7 1.0 %slice.73 = bf16[4,4,16,384]{3,2,1,0:T(8,128)(2,1)S(1)} slice(bf16[4,9,33,384]{3,2,1,0:T(8,128)(2,1)S(1)} %convolution_convert_fusion), slice={[0:4:1], [2:9:2], [1:32:2], [0:384:1]} | slice | bytes 393216 | tf_op jit(solution)/shard_map/slice | solution.py:85
  35.7 1.4 %slice.74 = bf16[4,4,16,384]{3,2,1,0:T(8,128)(2,1)S(1)} slice(bf16[4,9,33,384]{3,2,1,0:T(8,128)(2,1)S(1)} %convolution_convert_fusion), slice={[0:4:1], [2:9:2], [2:33:2], [0:384:1]} | slice | bytes 393216 | tf_op jit(solution)/shard_map/slice | solution.py:85
  37.4 0.2 copy.58
  37.6 0.0 copy-start.4
  37.6 0.5 fusion.42
  38.2 0.1 copy-done.4
  38.3 0.4 convolution_add_fusion.2
  38.7 0.5 convolution_add_fusion.1
  39.2 0.0 all-to-all-done.1
  39.2 1.9 %fusion.40 = (f32[32]{0:T(128)S(1)}, bf16[32,4,16,128]{3,0,2,1:T(8,128)(2,1)S(1)}, bf16[32,4,16,128]{3,0,2,1:T(8,128)(2,1)}) fusion(pred[4,16]{1,0:T(4,128)(4,1)S(1)} %broadcast_and_fusion, f32[4,16,128,32]{2,3,1,0:T(8,128)S(1)} %convolution_add_fusion.1, bf16[32,36,1]{1,0,2:T(8,128)(2,1)S(1)} %copy.87, bf16[36,4,16,128]{3,2,1,0:T(8,128)(2,1)S(1)} %get-tuple-element.8, ...), kind=kOutput, calls=%fused_computation.81 | convolution fusion | flops 23592928 | bytes 3213760 | tf_op jit(solution)/shard_map/ok,kpqr->opqr/dot_general | solution.py:91
  41.1 0.5 convolution_bitcast_fusion
  41.6 0.0 copy-start.1
  41.6 0.5 convolution_bitcast_fusion.1
  42.0 0.5 convolution_bitcast_fusion.2
  42.5 0.1 copy.72
  42.6 0.1 copy.70
  42.7 0.1 copy.71
  42.8 0.1 pad_maximum_fusion.1
  42.9 1.5 %collective-permute-start.3 = (f32[32,109]{1,0:T(8,128)S(1)}, f32[32,109]{1,0:T(8,128)S(1)}, u32[]{:S(2)}, u32[]{:S(2)}) collective-permute-start(f32[32,109]{1,0:T(8,128)S(1)} %pad_maximum_fusion.1), channel_id=1, source_target_pairs={{0,4},{4,0},{8,12},{12,8},{16,20},{20,16},{24,28},{28,24},{1,5},{5... | collective-permute-start | bytes 41864 | tf_op jit(solution)/shard_map/ppermute | solution.py:31
  44.4 0.0 copy-done.1
  44.4 1.0 %copy.66 = bf16[32,4,16,128]{3,2,1,0:T(8,128)(2,1)} copy(bf16[32,4,16,128]{3,0,2,1:T(8,128)(2,1)S(1)} %copy-done.1) | data formatting | bytes 1048576 | tf_op jit(solution)/shard_map/convert_element_type | solution.py:96
  45.4 3.5 %all-to-all-start = ((bf16[32,4,16,128]{3,2,1,0:T(8,128)(2,1)}), bf16[32,4,16,128]{3,2,1,0:T(8,128)(2,1)S(1)}, u32[]{:S(2)}, u32[]{:S(2)}) async-start(bf16[32,4,16,128]{3,2,1,0:T(8,128)(2,1)} %copy.66), calls=%async_computation | async-start | bytes 1048576 | tf_op jit(solution)/shard_map/all_to_all | solution.py:101
  48.9 0.0 collective-permute-done.3
  48.9 0.1 fusion.47
  49.0 1.6 %collective-permute-start.4 = (f32[32,109]{1,0:T(8,128)S(1)}, f32[32,109]{1,0:T(8,128)S(1)}, u32[]{:S(2)}, u32[]{:S(2)}) collective-permute-start(f32[32,109]{1,0:T(8,128)S(1)} %fusion.47), channel_id=1, source_target_pairs={{0,8},{4,12},{8,0},{12,4},{16,24},{20,28},{24,16},{28,20},{1,9},{5... | collective-permute-start | bytes 41864 | tf_op jit(solution)/shard_map/ppermute | solution.py:31
  50.5 2.2 %collective-permute-done.4 = f32[32,109]{1,0:T(8,128)S(1)} collective-permute-done((f32[32,109]{1,0:T(8,128)S(1)}, f32[32,109]{1,0:T(8,128)S(1)}, u32[]{:S(2)}, u32[]{:S(2)}) %collective-permute-start.4) | collective-permute-done | bytes 13984 | tf_op jit(solution)/shard_map/ppermute | solution.py:31
  52.7 2.6 %collective-permute-start.5 = (f32[32,109]{1,0:T(8,128)S(1)}, f32[32,109]{1,0:T(8,128)S(1)}, u32[]{:S(2)}, u32[]{:S(2)}) collective-permute-start(f32[32,109]{1,0:T(8,128)S(1)} %add.85), channel_id=1, source_target_pairs={{0,16},{4,20},{8,24},{12,28},{16,0},{20,4},{24,8},{28,12},{1,17},{... | collective-permute-start | bytes 41864 | tf_op jit(solution)/shard_map/ppermute | solution.py:31
  55.3 2.1 %collective-permute-done.5 = f32[32,109]{1,0:T(8,128)S(1)} collective-permute-done((f32[32,109]{1,0:T(8,128)S(1)}, f32[32,109]{1,0:T(8,128)S(1)}, u32[]{:S(2)}, u32[]{:S(2)}) %collective-permute-start.5) | collective-permute-done | bytes 13984 | tf_op jit(solution)/shard_map/ppermute | solution.py:31
  57.4 0.0 collective-permute-start.6
  57.4 1.2 %collective-permute-done.6 = f32[32,109]{1,0:T(8,128)S(1)} collective-permute-done((f32[32,109]{1,0:T(8,128)S(1)}, f32[32,109]{1,0:T(8,128)S(1)}, u32[]{:S(2)}, u32[]{:S(2)}) %collective-permute-start.6) | collective-permute-done | bytes 13984 | tf_op jit(solution)/shard_map/ppermute | solution.py:31
  58.5 2.0 %collective-permute-start.7 = (f32[32,109]{1,0:T(8,128)S(1)}, f32[32,109]{1,0:T(8,128)S(1)}, u32[]{:S(2)}, u32[]{:S(2)}) collective-permute-start(f32[32,109]{1,0:T(8,128)S(1)} %add.87), channel_id=1, source_target_pairs={{0,2},{1,3},{2,0},{3,1},{4,6},{5,7},{6,4},{7,5},{8,10},{9,11},{10,... | collective-permute-start | bytes 41864 | tf_op jit(solution)/shard_map/ppermute | solution.py:31
  60.5 1.8 %collective-permute-done.7 = f32[32,109]{1,0:T(8,128)S(1)} collective-permute-done((f32[32,109]{1,0:T(8,128)S(1)}, f32[32,109]{1,0:T(8,128)S(1)}, u32[]{:S(2)}, u32[]{:S(2)}) %collective-permute-start.7) | collective-permute-done | bytes 13984 | tf_op jit(solution)/shard_map/ppermute | solution.py:31
  62.3 0.7 %slice_reduce_fusion = f32[8]{0:T(128)} fusion(f32[8,109]{1,0:T(8,128)S(1)} %dynamic-slice_add_fusion), kind=kLoop, calls=%fused_computation.50 | loop fusion | bytes 64 | tf_op jit(solution)/shard_map/slice | solution.py:112
  63.0 0.0 all-to-all-done
  63.0 0.9 %copy.67 = bf16[8,4,4,16,128]{4,3,2,1,0:T(8,128)(2,1)} copy(bf16[8,4,4,16,128]{4,3,1,0,2:T(8,128)(2,1)S(1)} %bitcast.102) | data formatting | bytes 1048576 | tf_op jit(solution)/shard_map/all_to_all | solution.py:101
  (33 shorter events, 0.5 us)
Async XLA Ops:
  0.6 28.3 %copy-start = (bf16[4,8,32,256]{3,2,1,0:T(8,128)(2,1)S(1)}, bf16[4,8,32,256]{3,2,1,0:T(8,128)(2,1)}, u32[]{:S(2)}) copy-start(bf16[4,8,32,256]{3,2,1,0:T(8,128)(2,1)} %param.6) | copy-start | bytes 1572868
  0.6 19.8 %copy-start.5 = (s32[4]{0:T(128)S(1)}, s32[4]{0:T(128)}, u32[]{:S(2)}) copy-start(s32[4]{0:T(128)} %param.8) | copy-start | bytes 52
  0.7 23.0 %copy-start.6 = (s32[8]{0:T(128)S(1)}, s32[8]{0:T(128)}, u32[]{:S(2)}) copy-start(s32[8]{0:T(128)} %param.7) | copy-start | bytes 100
  0.7 27.6 %copy-start.3 = (bf16[32,108]{1,0:T(8,128)(2,1)S(1)}, bf16[32,108]{1,0:T(8,128)(2,1)}, u32[]{:S(2)}) copy-start(bf16[32,108]{1,0:T(8,128)(2,1)} %param.9) | copy-start | bytes 20740
  1.6 27.4 %collective-permute-start.2 = (bf16[4,32,256]{2,1,0:T(8,128)(2,1)S(1)}, bf16[4,32,256]{2,1,0:T(8,128)(2,1)S(1)}, u32[]{:S(2)}, u32[]{:S(2)}) collective-permute-start(bf16[4,32,256]{2,1,0:T(8,128)(2,1)S(1)} %slice_bitcast_fusion), channel_id=1, source_target_pairs={{0,4},{4,8},{8,12},{12,16},{16,20},{20,24},{24,28},{1,5},{5,9},{9,... | collective-permute-start | bytes 196616 | tf_op jit(solution)/shard_map/ppermute | solution.py:10
  7.4 21.5 %collective-permute-start.1 = (bf16[4,8,256]{2,1,0:T(8,128)(2,1)S(1)}, bf16[4,8,256]{2,1,0:T(8,128)(2,1)S(1)}, u32[]{:S(2)}, u32[]{:S(2)}) collective-permute-start(bf16[4,8,256]{2,1,0:T(8,128)(2,1)S(1)} %bitcast.104), channel_id=1, source_target_pairs={{0,1},{1,2},{2,3},{4,5},{5,6},{6,7},{8,9},{9,10},{10,11},{12,13},{... | collective-permute-start | bytes 49160 | tf_op jit(solution)/shard_map/ppermute | solution.py:10
  9.6 19.3 %collective-permute-start = (bf16[4,256]{1,0:T(4,128)(2,1)S(1)}, bf16[4,256]{1,0:T(4,128)(2,1)S(1)}, u32[]{:S(2)}, u32[]{:S(2)}) collective-permute-start(bf16[4,256]{1,0:T(4,128)(2,1)S(1)} %bitcast.106), channel_id=1, source_target_pairs={{0,5},{1,6},{2,7},{4,9},{5,10},{6,11},{8,13},{9,14},{10,15},{12,17... | collective-permute-start | bytes 6152 | tf_op jit(solution)/shard_map/ppermute | solution.py:16
  16.9 22.3 %all-to-all-start.1 = ((bf16[8,4,64,128]{3,0,1,2:T(8,128)(2,1)}), bf16[8,4,64,128]{3,0,1,2:T(8,128)(2,1)S(1)}, u32[]{:S(2)}, u32[]{:S(2)}) async-start(bf16[8,4,64,128]{3,0,1,2:T(8,128)(2,1)} %copy.68), calls=%async_computation.1 | async-start | bytes 1048576 | tf_op jit(solution)/shard_map/all_to_all | solution.py:67
  37.6 0.7 %copy-start.4 = (f32[32]{0:T(128)S(1)}, f32[32]{0:T(128)}, u32[]{:S(2)}) copy-start(f32[32]{0:T(128)} %param.10) | copy-start | bytes 388
  41.6 2.8 %copy-start.1 = (bf16[32,4,16,128]{3,0,2,1:T(8,128)(2,1)S(1)}, bf16[32,4,16,128]{3,0,2,1:T(8,128)(2,1)}, u32[]{:S(2)}) copy-start(bf16[32,4,16,128]{3,0,2,1:T(8,128)(2,1)} %get-tuple-element.11) | copy-start | bytes 1572868
  42.9 6.0 %collective-permute-start.3 = (f32[32,109]{1,0:T(8,128)S(1)}, f32[32,109]{1,0:T(8,128)S(1)}, u32[]{:S(2)}, u32[]{:S(2)}) collective-permute-start(f32[32,109]{1,0:T(8,128)S(1)} %pad_maximum_fusion.1), channel_id=1, source_target_pairs={{0,4},{4,0},{8,12},{12,8},{16,20},{20,16},{24,28},{28,24},{1,5},{5... | collective-permute-start | bytes 41864 | tf_op jit(solution)/shard_map/ppermute | solution.py:31
  45.4 17.6 %all-to-all-start = ((bf16[32,4,16,128]{3,2,1,0:T(8,128)(2,1)}), bf16[32,4,16,128]{3,2,1,0:T(8,128)(2,1)S(1)}, u32[]{:S(2)}, u32[]{:S(2)}) async-start(bf16[32,4,16,128]{3,2,1,0:T(8,128)(2,1)} %copy.66), calls=%async_computation | async-start | bytes 1048576 | tf_op jit(solution)/shard_map/all_to_all | solution.py:101
  49.0 3.7 %collective-permute-start.4 = (f32[32,109]{1,0:T(8,128)S(1)}, f32[32,109]{1,0:T(8,128)S(1)}, u32[]{:S(2)}, u32[]{:S(2)}) collective-permute-start(f32[32,109]{1,0:T(8,128)S(1)} %fusion.47), channel_id=1, source_target_pairs={{0,8},{4,12},{8,0},{12,4},{16,24},{20,28},{24,16},{28,20},{1,9},{5... | collective-permute-start | bytes 41864 | tf_op jit(solution)/shard_map/ppermute | solution.py:31
  52.7 4.6 %collective-permute-start.5 = (f32[32,109]{1,0:T(8,128)S(1)}, f32[32,109]{1,0:T(8,128)S(1)}, u32[]{:S(2)}, u32[]{:S(2)}) collective-permute-start(f32[32,109]{1,0:T(8,128)S(1)} %add.85), channel_id=1, source_target_pairs={{0,16},{4,20},{8,24},{12,28},{16,0},{20,4},{24,8},{28,12},{1,17},{... | collective-permute-start | bytes 41864 | tf_op jit(solution)/shard_map/ppermute | solution.py:31
  57.4 1.2 %collective-permute-start.6 = (f32[32,109]{1,0:T(8,128)S(1)}, f32[32,109]{1,0:T(8,128)S(1)}, u32[]{:S(2)}, u32[]{:S(2)}) collective-permute-start(f32[32,109]{1,0:T(8,128)S(1)} %add.86), channel_id=1, source_target_pairs={{0,1},{1,0},{2,3},{3,2},{4,5},{5,4},{6,7},{7,6},{8,9},{9,8},{10,11... | collective-permute-start | bytes 41864 | tf_op jit(solution)/shard_map/ppermute | solution.py:31
  58.5 3.7 %collective-permute-start.7 = (f32[32,109]{1,0:T(8,128)S(1)}, f32[32,109]{1,0:T(8,128)S(1)}, u32[]{:S(2)}, u32[]{:S(2)}) collective-permute-start(f32[32,109]{1,0:T(8,128)S(1)} %add.87), channel_id=1, source_target_pairs={{0,2},{1,3},{2,0},{3,1},{4,6},{5,7},{6,4},{7,5},{8,10},{9,11},{10,... | collective-permute-start | bytes 41864 | tf_op jit(solution)/shard_map/ppermute | solution.py:31
  62.3 1.6 %copy-start.2 = (f32[8,109]{1,0:T(8,128)}, f32[8,109]{1,0:T(8,128)S(1)}, u32[]{:S(2)}) copy-start(f32[8,109]{1,0:T(8,128)S(1)} %dynamic-slice_add_fusion) | copy-start | bytes 10468

commit v7 on v5

--- a/solution.py
+++ b/solution.py
@@ -22,16 +22,25 @@
     return value
 
 
-def extend(data, border, count, dim):
+def extend(data, border, keep, at, dim):
     length = data.shape[dim]
     border_wide = jnp.expand_dims(border, dim)
     joined = jnp.concatenate([jnp.zeros_like(border_wide), data], axis=dim)
     shape = [1] * joined.ndim
     shape[dim] = length + 1
-    places = jnp.arange(length + 1, dtype=jnp.int32).reshape(shape)
-    edge_at = length - count
-    kept = jnp.where(places > edge_at, joined, jnp.zeros_like(joined))
-    return jnp.where(places == edge_at, border_wide, kept)
+    kept = jnp.where(keep.reshape(shape), joined, jnp.zeros_like(joined))
+    return jnp.where(at.reshape(shape), border_wide, kept)
+
+
+def count_masks(counts, axis, length):
+    here = (jnp.arange(counts.shape[0], dtype=jnp.int32) == lax.axis_index(axis))[:, None]
+    places = jnp.arange(length + 1, dtype=jnp.int32)[None, :]
+    edge = (length - counts)[:, None]
+    keep = jnp.any(here & (places > edge), axis=0)
+    at = jnp.any(here & (places == edge), axis=0)
+    half = jnp.arange(length // 2, dtype=jnp.int32)[None, :]
+    ok = jnp.any(here & (half >= length // 2 - (counts // 2)[:, None]), axis=0)
+    return keep, at, ok
 
 
 def taps(padded, axes, halves):
@@ -54,13 +63,12 @@
     out_chans = weight.shape[0]
     tiles_y = lax.axis_size("gy")
     cell_grad = lax.all_to_all(grad_out, "gy", split_axis=2, concat_axis=0, tiled=True)
-    row_count = rows_live[lax.axis_index("gx")]
+    row_keep, row_at, row_ok = count_masks(rows_live, "gx", cap_x)
+    col_keep, col_at, col_ok = count_masks(cols_live, "gy", cap_y)
     above = from_behind(fields[:, cap_x - 1], "gx", 1)
-    ext_rows = extend(fields, above, row_count, 1)
-    row_ok = jnp.arange(half_x, dtype=jnp.int32) >= half_x - row_count // 2
-    col_count = cols_live[lax.axis_index("gy")]
+    ext_rows = extend(fields, above, row_keep, row_at, 1)
     beside = from_behind(ext_rows[:, :, cap_y - 1], "gy", 1)
-    ext_full = extend(ext_rows, beside, col_count, 2)
+    ext_full = extend(ext_rows, beside, col_keep, col_at, 2)
     lanes = jnp.arange(3 * half_z, dtype=jnp.int32)
     source = 2 * (lanes % half_z) + lanes // half_z - 1
     pick = (jnp.arange(depth, dtype=jnp.int32)[:, None] == source[None, :]).astype(fields.dtype)
@@ -76,20 +84,21 @@
     for off_z in range(3):
         part = stacked[..., off_z * half_z : (off_z + 1) * half_z]
         conv = conv + jnp.einsum("ok,kpqr->opqr", kernel[:, :, off_z], part, preferred_element_type=jnp.float32)
-    col_ok = jnp.arange(half_y, dtype=jnp.int32) >= half_y - col_count // 2
     live = (row_ok[:, None] & col_ok[None, :]).reshape(1, half_x, half_y, 1)
     pre_wide = lax.reduce_precision(jnp.where(live, conv, 0.0), exponent_bits=8, mantissa_bits=7)
     sigma = jax.nn.sigmoid(pre_wide)
     stem_local = (pre_wide * sigma).astype(jnp.bfloat16)
     slope = sigma * (1.0 + pre_wide * (1.0 - sigma))
-    returned = jnp.where(live, cell_grad.astype(jnp.float32) * slope, 0.0).astype(jnp.bfloat16)
+    grad_wide = jnp.where(live, cell_grad.astype(jnp.float32) * slope, 0.0)
+    grad_wide = lax.reduce_precision(grad_wide, exponent_bits=8, mantissa_bits=7)
+    returned = grad_wide.astype(jnp.bfloat16)
     stem = lax.all_to_all(stem_local, "gy", split_axis=0, concat_axis=2, tiled=True)
     grads = []
     for off_z in range(3):
         part = stacked[..., off_z * half_z : (off_z + 1) * half_z]
         grads.append(jnp.einsum("opqr,kpqr->ok", returned, part, preferred_element_type=jnp.float32))
     weight_full = jnp.stack(grads, axis=-1).reshape(out_chans, -1)
-    bias_full = jnp.sum(returned.astype(jnp.float32), axis=(1, 2, 3))
+    bias_full = jnp.sum(grad_wide, axis=(1, 2, 3))
     packed = jnp.concatenate([weight_full, bias_full[:, None]], axis=1)
     total = butterfly_sum(butterfly_sum(packed, "gx"), "gy")
     rows = out_chans // tiles_y

time: 60.6 us -> 54.6 us (0.901)
  between operations: 7.56 us -> 1.03 us
  starting transfers between devices: 23.8 us -> 25.1 us
  local copies, waits for them, and re-layouts: 16 us -> 14.9 us
    all_to_all x1, starting transfers between devices: 5.12 us -> 6.46 us  [local(): lax.all_to_all(stem_local, 'gy', split_axis=0, concat_axis=2, tiled=True)]
    dynamic_slice x2 -> x0, local copies, waits for them, and re-layouts: 1.17 us -> none  [the longest x1 0.59 us: local(): col_count = cols_live[lax.axis_index('gy')]]
  transfers between devices with their start and end apart: 9 -> 9, of which waited for: 5 -> 5; matrix products, arithmetic and copies ran while one was open for 26% -> 28% of each run, Pallas kernels for 0% -> 0%
where the time goes in v7:
time: 54.6 us; the launch traced here: 54.2 us
  starting transfers between devices  25.1 us (46%)
  local copies, waits for them, and re-layouts  14.9 us (27%)
  waiting for transfers between devices  7.68 us (14%)
  matrix products  4.76 us (9%)
  between operations  1.03 us (2%)
  other arithmetic  0.83 us (2%)
    ppermute x5, starting transfers between devices, butterfly_sum(): value = value + lax.ppermute(value, axis, swap)  7.91 us
    slice x9, local copies, waits for them, and re-layouts, local(): ztaps[:, off_x:off_x + 2 * half_x - 1:2, off_y:off_y + 2 * half_y - 1:2]  7.27 us
    ppermute x2, starting transfers between devices, from_behind(): return lax.ppermute(block, axis, route)  7.22 us
    ppermute x5, waiting for transfers between devices, butterfly_sum(): value = value + lax.ppermute(value, axis, swap)  7.14 us
    all_to_all x1, starting transfers between devices, local(): lax.all_to_all(stem_local, 'gy', split_axis=0, concat_axis=2, tiled=True)  6.46 us
    all_to_all x1, starting transfers between devices, local(): lax.all_to_all(grad_out, 'gy', split_axis=2, concat_axis=0, tiled=True)  3.47 us
    unnamed x27, local copies, waits for them, and re-layouts  2.98 us
    dot_general x3, matrix products, local(): jnp.einsum('ok,kpqr->opqr', kernel[:, :, off_z], part, preferred_element_...  2.79 us
  transfers between devices with their start and end apart: 9, of which 5 were waited for; matrix products, arithmetic and copies ran while one was open for 28% of the time, Pallas kernels for 0%

profile of v7, /device:TPU:0, one launch (start us, length us, event | category | flops | bytes accessed | tf_op | source)
XLA Modules:
  0.0 54.2 jit_solution(8380855208119864923)
XLA Ops:
  0.6 0.0 copy-start
  0.6 0.0 copy-start.5
  0.7 0.0 copy-start.6
  0.7 0.0 copy-start.3
  0.7 0.9 %slice_bitcast_fusion = bf16[4,32,256]{2,1,0:T(8,128)(2,1)S(1)} fusion(bf16[4,8,32,256]{3,2,1,0:T(8,128)(2,1)} %param.6), kind=kLoop, calls=%fused_computation.41 | loop fusion | bytes 131072 | tf_op jit(solution)/shard_map/squeeze | solution.py:68
  1.6 4.9 %collective-permute-start = (bf16[4,32,256]{2,1,0:T(8,128)(2,1)S(1)}, bf16[4,32,256]{2,1,0:T(8,128)(2,1)S(1)}, u32[]{:S(2)}, u32[]{:S(2)}) collective-permute-start(bf16[4,32,256]{2,1,0:T(8,128)(2,1)S(1)} %slice_bitcast_fusion), channel_id=1, source_target_pairs={{0,4},{4,8},{8,12},{12,16},{16,20},{20,24},{24,28},{1,5},{5,9},{9,... | collective-permute-start | bytes 196616 | tf_op jit(solution)/shard_map/ppermute | solution.py:10
  6.4 2.2 %copy.89 = bf16[8,4,64,128]{3,0,1,2:T(8,128)(2,1)} copy(bf16[8,4,64,128]{3,2,1,0:T(8,128)(2,1)} %param.11) | data formatting | bytes 1048576 | tf_op args[5]
  8.6 3.5 %all-to-all-start.1 = ((bf16[8,4,64,128]{3,0,1,2:T(8,128)(2,1)}), bf16[8,4,64,128]{3,0,1,2:T(8,128)(2,1)S(1)}, u32[]{:S(2)}, u32[]{:S(2)}) async-start(bf16[8,4,64,128]{3,0,1,2:T(8,128)(2,1)} %copy.89), calls=%async_computation.1 | async-start | bytes 1048576 | tf_op jit(solution)/shard_map/all_to_all | solution.py:65
  12.2 0.1 fusion.39
  12.3 0.1 fusion.29
  12.4 0.0 copy-done.3
  12.4 0.1 copy.81
  12.6 0.1 fusion.41
  12.7 0.1 broadcast_and_fusion
  12.8 0.1 fusion.43
  12.9 0.0 collective-permute-done
  12.9 0.1 select_select_fusion
  13.1 2.4 %collective-permute-start.1 = (bf16[4,9,256]{2,0,1:T(4,128)(2,1)S(1)}, bf16[4,9,256]{2,0,1:T(4,128)(2,1)S(1)}, u32[]{:S(2)}, u32[]{:S(2)}) collective-permute-start(bf16[4,9,256]{2,0,1:T(4,128)(2,1)S(1)} %bitcast.101), channel_id=1, source_target_pairs={{0,1},{1,2},{2,3},{4,5},{5,6},{6,7},{8,9},{9,10},{10,11},{12,13},{... | collective-permute-start | bytes 55304 | tf_op jit(solution)/shard_map/ppermute | solution.py:10
  15.5 0.1 copy.102
  15.6 0.1 copy.104
  15.7 0.1 copy.106
  15.8 0.5 collective-permute-done.1
  16.3 0.6 %convolution_convert_fusion = bf16[4,9,33,384]{3,2,1,0:T(8,128)(2,1)S(1)} fusion(bf16[4,9,32,256]{3,2,1,0:T(8,128)(2,1)S(1)} %select_select_fusion, pred[33]{0:T(512)(128)(4,1)S(1)} %get-tuple-element.7, pred[33]{0:T(512)(128)(4,1)S(1)} %get-tuple-element.6, bf16[4,9,256]{2,1,0:T(8,128)(2,1)S(1)} %copy.78, s32[384]{0:T(512)S(1)} %fusion.33), kind=kOutput, calls=%fused_computation | convolution fusion | flops 234733056 | bytes 1522242 | tf_op jit(solution)/shard_map/cxyz,zk->cxyk/dot_general | solution.py:75
  16.9 0.6 %slice.62 = bf16[4,4,16,384]{3,2,1,0:T(8,128)(2,1)S(1)} slice(bf16[4,9,33,384]{3,2,1,0:T(8,128)(2,1)S(1)} %convolution_convert_fusion), slice={[0:4:1], [0:7:2], [0:31:2], [0:384:1]} | slice | bytes 393216 | tf_op jit(solution)/shard_map/slice | solution.py:80
  17.5 0.6 %slice.63 = bf16[4,4,16,384]{3,2,1,0:T(8,128)(2,1)S(1)} slice(bf16[4,9,33,384]{3,2,1,0:T(8,128)(2,1)S(1)} %convolution_convert_fusion), slice={[0:4:1], [0:7:2], [1:32:2], [0:384:1]} | slice | bytes 393216 | tf_op jit(solution)/shard_map/slice | solution.py:80
  18.1 0.7 %slice.64 = bf16[4,4,16,384]{3,2,1,0:T(8,128)(2,1)S(1)} slice(bf16[4,9,33,384]{3,2,1,0:T(8,128)(2,1)S(1)} %convolution_convert_fusion), slice={[0:4:1], [0:7:2], [2:33:2], [0:384:1]} | slice | bytes 393216 | tf_op jit(solution)/shard_map/slice | solution.py:80
  18.9 0.6 %slice.65 = bf16[4,4,16,384]{3,2,1,0:T(8,128)(2,1)S(1)} slice(bf16[4,9,33,384]{3,2,1,0:T(8,128)(2,1)S(1)} %convolution_convert_fusion), slice={[0:4:1], [1:8:2], [0:31:2], [0:384:1]} | slice | bytes 393216 | tf_op jit(solution)/shard_map/slice | solution.py:80
  19.5 0.6 %slice.66 = bf16[4,4,16,384]{3,2,1,0:T(8,128)(2,1)S(1)} slice(bf16[4,9,33,384]{3,2,1,0:T(8,128)(2,1)S(1)} %convolution_convert_fusion), slice={[0:4:1], [1:8:2], [1:32:2], [0:384:1]} | slice | bytes 393216 | tf_op jit(solution)/shard_map/slice | solution.py:80
  20.1 0.7 %slice.67 = bf16[4,4,16,384]{3,2,1,0:T(8,128)(2,1)S(1)} slice(bf16[4,9,33,384]{3,2,1,0:T(8,128)(2,1)S(1)} %convolution_convert_fusion), slice={[0:4:1], [1:8:2], [2:33:2], [0:384:1]} | slice | bytes 393216 | tf_op jit(solution)/shard_map/slice | solution.py:80
  20.9 1.0 %slice.68 = bf16[4,4,16,384]{3,2,1,0:T(8,128)(2,1)S(1)} slice(bf16[4,9,33,384]{3,2,1,0:T(8,128)(2,1)S(1)} %convolution_convert_fusion), slice={[0:4:1], [2:9:2], [0:31:2], [0:384:1]} | slice | bytes 393216 | tf_op jit(solution)/shard_map/slice | solution.py:80
  21.9 1.0 %slice.69 = bf16[4,4,16,384]{3,2,1,0:T(8,128)(2,1)S(1)} slice(bf16[4,9,33,384]{3,2,1,0:T(8,128)(2,1)S(1)} %convolution_convert_fusion), slice={[0:4:1], [2:9:2], [1:32:2], [0:384:1]} | slice | bytes 393216 | tf_op jit(solution)/shard_map/slice | solution.py:80
  22.9 1.4 %slice.70 = bf16[4,4,16,384]{3,2,1,0:T(8,128)(2,1)S(1)} slice(bf16[4,9,33,384]{3,2,1,0:T(8,128)(2,1)S(1)} %convolution_convert_fusion), slice={[0:4:1], [2:9:2], [2:33:2], [0:384:1]} | slice | bytes 393216 | tf_op jit(solution)/shard_map/slice | solution.py:80
  24.6 0.2 copy.79
  24.8 0.0 copy-start.4
  24.8 0.5 fusion.54
  25.3 0.1 copy-done.4
  25.5 0.4 convolution_add_fusion.2
  25.9 0.5 convolution_add_fusion.1
  26.4 0.0 all-to-all-done.1
  26.4 1.9 %fusion.52 = (f32[32]{0:T(128)S(1)}, bf16[32,4,16,128]{3,0,2,1:T(8,128)(2,1)S(1)}, bf16[32,4,16,128]{3,0,2,1:T(8,128)(2,1)}) fusion(pred[4,16]{1,0:T(4,128)(4,1)S(1)} %broadcast_and_fusion, f32[4,16,128,32]{2,3,1,0:T(8,128)S(1)} %convolution_add_fusion.1, bf16[32,36,1]{1,0,2:T(8,128)(2,1)S(1)} %copy.106, ...), kind=kOutput, calls=%fused_computation.101 | convolution fusion | flops 23592928 | bytes 3213760 | tf_op jit(solution)/shard_map/ok,kpqr->opqr/dot_general | solution.py:86
  28.3 0.5 convolution_bitcast_fusion
  28.7 0.0 copy-start.1
  28.7 0.5 convolution_bitcast_fusion.1
  29.2 0.5 convolution_bitcast_fusion.2
  29.7 0.1 copy.93
  29.8 0.1 copy.91
  29.9 0.1 copy.92
  30.0 0.1 pad_maximum_fusion.1
  30.1 1.6 %collective-permute-start.2 = (f32[32,109]{1,0:T(8,128)S(1)}, f32[32,109]{1,0:T(8,128)S(1)}, u32[]{:S(2)}, u32[]{:S(2)}) collective-permute-start(f32[32,109]{1,0:T(8,128)S(1)} %pad_maximum_fusion.1), channel_id=1, source_target_pairs={{0,4},{4,0},{8,12},{12,8},{16,20},{20,16},{24,28},{28,24},{1,5},{5... | collective-permute-start | bytes 41864 | tf_op jit(solution)/shard_map/ppermute | solution.py:20
  31.6 1.0 %copy.87 = bf16[32,4,16,128]{3,2,1,0:T(8,128)(2,1)} copy(bf16[32,4,16,128]{3,0,2,1:T(8,128)(2,1)S(1)} %copy-done.1) | data formatting | bytes 1048576 | tf_op jit(solution)/shard_map/convert_element_type | solution.py:90
  32.6 6.5 %all-to-all-start = ((bf16[32,4,16,128]{3,2,1,0:T(8,128)(2,1)}), bf16[32,4,16,128]{3,2,1,0:T(8,128)(2,1)S(1)}, u32[]{:S(2)}, u32[]{:S(2)}) async-start(bf16[32,4,16,128]{3,2,1,0:T(8,128)(2,1)} %copy.87), calls=%async_computation | async-start | bytes 1048576 | tf_op jit(solution)/shard_map/all_to_all | solution.py:95
  39.1 0.0 collective-permute-done.2
  39.1 0.1 fusion.59
  39.2 1.6 %collective-permute-start.3 = (f32[32,109]{1,0:T(8,128)S(1)}, f32[32,109]{1,0:T(8,128)S(1)}, u32[]{:S(2)}, u32[]{:S(2)}) collective-permute-start(f32[32,109]{1,0:T(8,128)S(1)} %fusion.59), channel_id=1, source_target_pairs={{0,8},{4,12},{8,0},{12,4},{16,24},{20,28},{24,16},{28,20},{1,9},{5... | collective-permute-start | bytes 41864 | tf_op jit(solution)/shard_map/ppermute | solution.py:20
  40.7 2.2 %collective-permute-done.3 = f32[32,109]{1,0:T(8,128)S(1)} collective-permute-done((f32[32,109]{1,0:T(8,128)S(1)}, f32[32,109]{1,0:T(8,128)S(1)}, u32[]{:S(2)}, u32[]{:S(2)}) %collective-permute-start.3) | collective-permute-done | bytes 13984 | tf_op jit(solution)/shard_map/ppermute | solution.py:20
  42.9 2.6 %collective-permute-start.4 = (f32[32,109]{1,0:T(8,128)S(1)}, f32[32,109]{1,0:T(8,128)S(1)}, u32[]{:S(2)}, u32[]{:S(2)}) collective-permute-start(f32[32,109]{1,0:T(8,128)S(1)} %add.83), channel_id=1, source_target_pairs={{0,16},{4,20},{8,24},{12,28},{16,0},{20,4},{24,8},{28,12},{1,17},{... | collective-permute-start | bytes 41864 | tf_op jit(solution)/shard_map/ppermute | solution.py:20
  45.5 2.1 %collective-permute-done.4 = f32[32,109]{1,0:T(8,128)S(1)} collective-permute-done((f32[32,109]{1,0:T(8,128)S(1)}, f32[32,109]{1,0:T(8,128)S(1)}, u32[]{:S(2)}, u32[]{:S(2)}) %collective-permute-start.4) | collective-permute-done | bytes 13984 | tf_op jit(solution)/shard_map/ppermute | solution.py:20
  47.5 0.0 collective-permute-start.5
  47.6 1.2 %collective-permute-done.5 = f32[32,109]{1,0:T(8,128)S(1)} collective-permute-done((f32[32,109]{1,0:T(8,128)S(1)}, f32[32,109]{1,0:T(8,128)S(1)}, u32[]{:S(2)}, u32[]{:S(2)}) %collective-permute-start.5) | collective-permute-done | bytes 13984 | tf_op jit(solution)/shard_map/ppermute | solution.py:20
  48.7 2.2 %collective-permute-start.6 = (f32[32,109]{1,0:T(8,128)S(1)}, f32[32,109]{1,0:T(8,128)S(1)}, u32[]{:S(2)}, u32[]{:S(2)}) collective-permute-start(f32[32,109]{1,0:T(8,128)S(1)} %add.85), channel_id=1, source_target_pairs={{0,2},{1,3},{2,0},{3,1},{4,6},{5,7},{6,4},{7,5},{8,10},{9,11},{10,... | collective-permute-start | bytes 41864 | tf_op jit(solution)/shard_map/ppermute | solution.py:20
  51.0 1.7 %collective-permute-done.6 = f32[32,109]{1,0:T(8,128)S(1)} collective-permute-done((f32[32,109]{1,0:T(8,128)S(1)}, f32[32,109]{1,0:T(8,128)S(1)}, u32[]{:S(2)}, u32[]{:S(2)}) %collective-permute-start.6) | collective-permute-done | bytes 13984 | tf_op jit(solution)/shard_map/ppermute | solution.py:20
  52.7 0.7 %slice_reduce_fusion = f32[8]{0:T(128)} fusion(f32[8,109]{1,0:T(8,128)S(1)} %dynamic-slice_add_fusion), kind=kLoop, calls=%fused_computation.49 | loop fusion | bytes 64 | tf_op jit(solution)/shard_map/slice | solution.py:106
  53.4 0.0 all-to-all-done
  53.4 0.9 %copy.88 = bf16[8,4,4,16,128]{4,3,2,1,0:T(8,128)(2,1)} copy(bf16[8,4,4,16,128]{4,3,1,0,2:T(8,128)(2,1)S(1)} %bitcast.99) | data formatting | bytes 1048576 | tf_op jit(solution)/shard_map/all_to_all | solution.py:95
  (31 shorter events, 0.5 us)
Async XLA Ops:
  0.6 12.2 %copy-start = (bf16[4,8,32,256]{3,2,1,0:T(8,128)(2,1)S(1)}, bf16[4,8,32,256]{3,2,1,0:T(8,128)(2,1)}, u32[]{:S(2)}) copy-start(bf16[4,8,32,256]{3,2,1,0:T(8,128)(2,1)} %param.6) | copy-start | bytes 1572868
  0.6 11.5 %copy-start.5 = (s32[4]{0:T(128)S(1)}, s32[4]{0:T(128)}, u32[]{:S(2)}) copy-start(s32[4]{0:T(128)} %param.8) | copy-start | bytes 52
  0.7 11.5 %copy-start.6 = (s32[8]{0:T(128)S(1)}, s32[8]{0:T(128)}, u32[]{:S(2)}) copy-start(s32[8]{0:T(128)} %param.7) | copy-start | bytes 100
  0.7 11.7 %copy-start.3 = (bf16[32,108]{1,0:T(8,128)(2,1)S(1)}, bf16[32,108]{1,0:T(8,128)(2,1)}, u32[]{:S(2)}) copy-start(bf16[32,108]{1,0:T(8,128)(2,1)} %param.9) | copy-start | bytes 20740
  1.6 11.3 %collective-permute-start = (bf16[4,32,256]{2,1,0:T(8,128)(2,1)S(1)}, bf16[4,32,256]{2,1,0:T(8,128)(2,1)S(1)}, u32[]{:S(2)}, u32[]{:S(2)}) collective-permute-start(bf16[4,32,256]{2,1,0:T(8,128)(2,1)S(1)} %slice_bitcast_fusion), channel_id=1, source_target_pairs={{0,4},{4,8},{8,12},{12,16},{16,20},{20,24},{24,28},{1,5},{5,9},{9,... | collective-permute-start | bytes 196616 | tf_op jit(solution)/shard_map/ppermute | solution.py:10
  8.6 17.8 %all-to-all-start.1 = ((bf16[8,4,64,128]{3,0,1,2:T(8,128)(2,1)}), bf16[8,4,64,128]{3,0,1,2:T(8,128)(2,1)S(1)}, u32[]{:S(2)}, u32[]{:S(2)}) async-start(bf16[8,4,64,128]{3,0,1,2:T(8,128)(2,1)} %copy.89), calls=%async_computation.1 | async-start | bytes 1048576 | tf_op jit(solution)/shard_map/all_to_all | solution.py:65
  13.1 3.2 %collective-permute-start.1 = (bf16[4,9,256]{2,0,1:T(4,128)(2,1)S(1)}, bf16[4,9,256]{2,0,1:T(4,128)(2,1)S(1)}, u32[]{:S(2)}, u32[]{:S(2)}) collective-permute-start(bf16[4,9,256]{2,0,1:T(4,128)(2,1)S(1)} %bitcast.101), channel_id=1, source_target_pairs={{0,1},{1,2},{2,3},{4,5},{5,6},{6,7},{8,9},{9,10},{10,11},{12,13},{... | collective-permute-start | bytes 55304 | tf_op jit(solution)/shard_map/ppermute | solution.py:10
  24.8 0.7 %copy-start.4 = (f32[32]{0:T(128)S(1)}, f32[32]{0:T(128)}, u32[]{:S(2)}) copy-start(f32[32]{0:T(128)} %param.10) | copy-start | bytes 388
  28.7 2.9 %copy-start.1 = (bf16[32,4,16,128]{3,0,2,1:T(8,128)(2,1)S(1)}, bf16[32,4,16,128]{3,0,2,1:T(8,128)(2,1)}, u32[]{:S(2)}) copy-start(bf16[32,4,16,128]{3,0,2,1:T(8,128)(2,1)} %get-tuple-element.15) | copy-start | bytes 1572868
  30.1 9.0 %collective-permute-start.2 = (f32[32,109]{1,0:T(8,128)S(1)}, f32[32,109]{1,0:T(8,128)S(1)}, u32[]{:S(2)}, u32[]{:S(2)}) collective-permute-start(f32[32,109]{1,0:T(8,128)S(1)} %pad_maximum_fusion.1), channel_id=1, source_target_pairs={{0,4},{4,0},{8,12},{12,8},{16,20},{20,16},{24,28},{28,24},{1,5},{5... | collective-permute-start | bytes 41864 | tf_op jit(solution)/shard_map/ppermute | solution.py:20
  32.6 20.7 %all-to-all-start = ((bf16[32,4,16,128]{3,2,1,0:T(8,128)(2,1)}), bf16[32,4,16,128]{3,2,1,0:T(8,128)(2,1)S(1)}, u32[]{:S(2)}, u32[]{:S(2)}) async-start(bf16[32,4,16,128]{3,2,1,0:T(8,128)(2,1)} %copy.87), calls=%async_computation | async-start | bytes 1048576 | tf_op jit(solution)/shard_map/all_to_all | solution.py:95
  39.2 3.7 %collective-permute-start.3 = (f32[32,109]{1,0:T(8,128)S(1)}, f32[32,109]{1,0:T(8,128)S(1)}, u32[]{:S(2)}, u32[]{:S(2)}) collective-permute-start(f32[32,109]{1,0:T(8,128)S(1)} %fusion.59), channel_id=1, source_target_pairs={{0,8},{4,12},{8,0},{12,4},{16,24},{20,28},{24,16},{28,20},{1,9},{5... | collective-permute-start | bytes 41864 | tf_op jit(solution)/shard_map/ppermute | solution.py:20
  42.9 4.6 %collective-permute-start.4 = (f32[32,109]{1,0:T(8,128)S(1)}, f32[32,109]{1,0:T(8,128)S(1)}, u32[]{:S(2)}, u32[]{:S(2)}) collective-permute-start(f32[32,109]{1,0:T(8,128)S(1)} %add.83), channel_id=1, source_target_pairs={{0,16},{4,20},{8,24},{12,28},{16,0},{20,4},{24,8},{28,12},{1,17},{... | collective-permute-start | bytes 41864 | tf_op jit(solution)/shard_map/ppermute | solution.py:20
  47.5 1.2 %collective-permute-start.5 = (f32[32,109]{1,0:T(8,128)S(1)}, f32[32,109]{1,0:T(8,128)S(1)}, u32[]{:S(2)}, u32[]{:S(2)}) collective-permute-start(f32[32,109]{1,0:T(8,128)S(1)} %add.84), channel_id=1, source_target_pairs={{0,1},{1,0},{2,3},{3,2},{4,5},{5,4},{6,7},{7,6},{8,9},{9,8},{10,11... | collective-permute-start | bytes 41864 | tf_op jit(solution)/shard_map/ppermute | solution.py:20
  48.7 3.9 %collective-permute-start.6 = (f32[32,109]{1,0:T(8,128)S(1)}, f32[32,109]{1,0:T(8,128)S(1)}, u32[]{:S(2)}, u32[]{:S(2)}) collective-permute-start(f32[32,109]{1,0:T(8,128)S(1)} %add.85), channel_id=1, source_target_pairs={{0,2},{1,3},{2,0},{3,1},{4,6},{5,7},{6,4},{7,5},{8,10},{9,11},{10,... | collective-permute-start | bytes 41864 | tf_op jit(solution)/shard_map/ppermute | solution.py:20
  52.7 1.6 %copy-start.2 = (f32[8,109]{1,0:T(8,128)}, f32[8,109]{1,0:T(8,128)S(1)}, u32[]{:S(2)}) copy-start(f32[8,109]{1,0:T(8,128)S(1)} %dynamic-slice_add_fusion) | copy-start | bytes 10468

commit v8 on v7

--- a/solution.py
+++ b/solution.py
@@ -74,10 +74,16 @@
     pick = (jnp.arange(depth, dtype=jnp.int32)[:, None] == source[None, :]).astype(fields.dtype)
     ztaps = jnp.einsum("cxyz,zk->cxyk", ext_full, pick, preferred_element_type=jnp.float32)
     ztaps = ztaps.astype(fields.dtype)
+    rows = jnp.arange(3 * half_y, dtype=jnp.int32)
+    row_source = 2 * (rows % half_y) + rows // half_y
+    row_pick = (row_source[:, None] == jnp.arange(cap_y + 1, dtype=jnp.int32)[None, :]).astype(fields.dtype)
+    row_pick = jnp.broadcast_to(row_pick, (in_chans, cap_x + 1) + row_pick.shape)
+    yztaps = jnp.einsum("cxjy,cxyk->cxjk", row_pick, ztaps, preferred_element_type=jnp.float32)
+    yztaps = yztaps.astype(fields.dtype)
     blocks = []
     for off_x in range(3):
         for off_y in range(3):
-            blocks.append(ztaps[:, off_x : off_x + 2 * half_x - 1 : 2, off_y : off_y + 2 * half_y - 1 : 2])
+            blocks.append(yztaps[:, off_x : off_x + 2 * half_x - 1 : 2, off_y * half_y : (off_y + 1) * half_y])
     stacked = jnp.stack(blocks, axis=1).reshape(in_chans * 9, half_x, half_y, 3 * half_z)
     kernel = weight.reshape(out_chans, in_chans * 9, 3)
     conv = bias[:, None, None, None]
@@ -101,8 +107,8 @@
     bias_full = jnp.sum(grad_wide, axis=(1, 2, 3))
     packed = jnp.concatenate([weight_full, bias_full[:, None]], axis=1)
     total = butterfly_sum(butterfly_sum(packed, "gx"), "gy")
-    rows = out_chans // tiles_y
-    mine = lax.dynamic_slice_in_dim(total, lax.axis_index("gy") * rows, rows, 0)
+    share = out_chans // tiles_y
+    mine = lax.dynamic_slice_in_dim(total, lax.axis_index("gy") * share, share, 0)
     weight_grad, bias_grad = mine[:, :-1], mine[:, -1]
     return (stem, weight_grad, bias_grad)
 

time: 54.6 us -> 47.7 us (0.87)
  local copies, waits for them, and re-layouts: 14.9 us -> 7.6 us
  starting transfers between devices: 25.1 us -> 23.7 us
  waiting for transfers between devices: 7.68 us -> 9.02 us
    slice x9 -> x0, local copies, waits for them, and re-layouts: 7.27 us -> none  [local(): ztaps[:, off_x:off_x + 2 * half_x - 1:2, off_y:off_y + 2 * half_y - 1:2]]
    all_to_all x1, starting transfers between devices: 6.46 us -> 5.07 us  [local(): lax.all_to_all(stem_local, 'gy', split_axis=0, concat_axis=2, tiled=True)]
    all_to_all x1, waiting for transfers between devices: 0.01 us -> 1.37 us  [local(): lax.all_to_all(grad_out, 'gy', split_axis=2, concat_axis=0, tiled=True)]
  transfers between devices with their start and end apart: 9 -> 9, of which waited for: 5 -> 6; matrix products, arithmetic and copies ran while one was open for 28% -> 17% of each run, Pallas kernels for 0% -> 0%
where the time goes in v8:
time: 47.7 us; the launch traced here: 47.3 us
  starting transfers between devices  23.7 us (50%)
  waiting for transfers between devices  9.02 us (19%)
  local copies, waits for them, and re-layouts  7.6 us (16%)
  matrix products  5.23 us (11%)
  between operations  0.97 us (2%)
  other arithmetic  0.84 us (2%)
    ppermute x5, starting transfers between devices, butterfly_sum(): value = value + lax.ppermute(value, axis, swap)  7.93 us
    ppermute x2, starting transfers between devices, from_behind(): return lax.ppermute(block, axis, route)  7.21 us
    ppermute x5, waiting for transfers between devices, butterfly_sum(): value = value + lax.ppermute(value, axis, swap)  7.12 us
    all_to_all x1, starting transfers between devices, local(): lax.all_to_all(stem_local, 'gy', split_axis=0, concat_axis=2, tiled=True)  5.07 us
    all_to_all x1, starting transfers between devices, local(): lax.all_to_all(grad_out, 'gy', split_axis=2, concat_axis=0, tiled=True)  3.47 us
    unnamed x27, local copies, waits for them, and re-layouts  2.98 us
    dot_general x3, matrix products, local(): jnp.einsum('ok,kpqr->opqr', kernel[:, :, off_z], part, preferred_element_...  2.78 us
    dot_general x3, matrix products, local(): jnp.einsum('opqr,kpqr->ok', returned, part, preferred_element_type=jnp.fl...  1.37 us
  transfers between devices with their start and end apart: 9, of which 6 were waited for; matrix products, arithmetic and copies ran while one was open for 17% of the time, Pallas kernels for 0%

profile of v8, /device:TPU:0, one launch (start us, length us, event | category | flops | bytes accessed | tf_op | source)
XLA Modules:
  0.0 47.3 jit_solution(3558924180177803312)
XLA Ops:
  0.6 0.0 copy-start
  0.6 0.0 copy-start.5
  0.7 0.0 copy-start.6
  0.7 0.0 copy-start.3
  0.7 0.9 %slice_bitcast_fusion = bf16[4,32,256]{2,1,0:T(8,128)(2,1)S(1)} fusion(bf16[4,8,32,256]{3,2,1,0:T(8,128)(2,1)} %param.6), kind=kLoop, calls=%fused_computation.43 | loop fusion | bytes 131072 | tf_op jit(solution)/shard_map/squeeze | solution.py:68
  1.6 4.9 %collective-permute-start = (bf16[4,32,256]{2,1,0:T(8,128)(2,1)S(1)}, bf16[4,32,256]{2,1,0:T(8,128)(2,1)S(1)}, u32[]{:S(2)}, u32[]{:S(2)}) collective-permute-start(bf16[4,32,256]{2,1,0:T(8,128)(2,1)S(1)} %slice_bitcast_fusion), channel_id=1, source_target_pairs={{0,4},{4,8},{8,12},{12,16},{16,20},{20,24},{24,28},{1,5},{5,9},{9,... | collective-permute-start | bytes 196616 | tf_op jit(solution)/shard_map/ppermute | solution.py:10
  6.4 2.2 %copy.89 = bf16[8,4,64,128]{3,0,1,2:T(8,128)(2,1)} copy(bf16[8,4,64,128]{3,2,1,0:T(8,128)(2,1)} %param.11) | data formatting | bytes 1048576 | tf_op args[5]
  8.6 3.5 %all-to-all-start.1 = ((bf16[8,4,64,128]{3,0,1,2:T(8,128)(2,1)}), bf16[8,4,64,128]{3,0,1,2:T(8,128)(2,1)S(1)}, u32[]{:S(2)}, u32[]{:S(2)}) async-start(bf16[8,4,64,128]{3,0,1,2:T(8,128)(2,1)} %copy.89), calls=%async_computation.1 | async-start | bytes 1048576 | tf_op jit(solution)/shard_map/all_to_all | solution.py:65
  12.1 0.0 copy-done.5
  12.2 0.0 copy-done.6
  12.2 0.1 fusion.50
  12.3 0.1 fusion.40
  12.4 0.0 copy-done.3
  12.4 0.1 copy.81
  12.6 0.1 fusion.52
  12.7 0.1 broadcast_and_fusion
  12.8 0.1 fusion.54
  12.9 0.0 collective-permute-done
  12.9 0.0 copy-done
  12.9 0.1 select_select_fusion
  13.1 2.4 %collective-permute-start.1 = (bf16[4,9,256]{2,0,1:T(4,128)(2,1)S(1)}, bf16[4,9,256]{2,0,1:T(4,128)(2,1)S(1)}, u32[]{:S(2)}, u32[]{:S(2)}) collective-permute-start(bf16[4,9,256]{2,0,1:T(4,128)(2,1)S(1)} %bitcast.102), channel_id=1, source_target_pairs={{0,1},{1,2},{2,3},{4,5},{5,6},{6,7},{8,9},{9,10},{10,11},{12,13},{... | collective-permute-start | bytes 55304 | tf_op jit(solution)/shard_map/ppermute | solution.py:10
  15.5 0.1 copy.102
  15.6 0.1 copy.104
  15.7 0.1 copy.106
  15.8 0.5 %collective-permute-done.1 = bf16[4,9,256]{2,0,1:T(4,128)(2,1)S(1)} collective-permute-done((bf16[4,9,256]{2,0,1:T(4,128)(2,1)S(1)}, bf16[4,9,256]{2,0,1:T(4,128)(2,1)S(1)}, u32[]{:S(2)}, u32[]{:S(2)}) %collective-permute-start.1) | collective-permute-done | bytes 18464 | tf_op jit(solution)/shard_map/ppermute | solution.py:10
  16.3 1.1 %convolution_convert_fusion = bf16[4,9,48,384]{3,2,1,0:T(8,128)(2,1)S(1)} fusion(bf16[4,9,32,256]{3,2,1,0:T(8,128)(2,1)S(1)} %select_select_fusion, pred[33]{0:T(512)(128)(4,1)S(1)} %get-tuple-element.7, pred[33]{0:T(512)(128)(4,1)S(1)} %get-tuple-element.6, bf16[4,9,256]{2,1,0:T(8,128)(2,1)S(1)} %copy.78, s32[384]{0:T(512)S(1)} %fusion.44, ...), kind=kOutput, calls=%fused_computation | convolution fusion | flops 279191040 | bytes 1940130 | tf_op jit(solution)/shard_map/cxjy,cxyk->cxjk/dot_general | solution.py:81
  17.7 0.2 copy.79
  17.9 0.0 copy-start.4
  18.0 0.5 %fusion.68 = (bf16[36,4,16,128]{3,2,1,0:T(8,128)(2,1)S(1)}, bf16[36,4,16,128]{3,2,1,0:T(8,128)(2,1)S(1)}, bf16[36,4,16,128]{3,2,1,0:T(8,128)(2,1)S(1)}) fusion(bf16[36,4,16,384]{3,2,1,0:T(8,128)(2,1)S(1)} %bitcast.99), kind=kLoop, calls=%fused_computation.113 | loop fusion | bytes 3538944 | tf_op jit(solution)/shard_map/slice | solution.py:91
  18.5 0.1 copy-done.4
  18.6 0.4 convolution_add_fusion.2
  19.1 0.5 convolution_add_fusion.1
  19.5 1.4 %all-to-all-done.1 = bf16[8,4,64,128]{3,0,1,2:T(8,128)(2,1)S(1)} async-done(((bf16[8,4,64,128]{3,0,1,2:T(8,128)(2,1)}), bf16[8,4,64,128]{3,0,1,2:T(8,128)(2,1)S(1)}, u32[]{:S(2)}, u32[]{:S(2)}) %all-to-all-start.1) | async-done | bytes 524320 | tf_op jit(solution)/shard_map/all_to_all | solution.py:65
  20.9 1.9 %fusion.66 = (f32[32]{0:T(128)S(1)}, bf16[32,4,16,128]{3,0,2,1:T(8,128)(2,1)S(1)}, bf16[32,4,16,128]{3,0,2,1:T(8,128)(2,1)}) fusion(pred[4,16]{1,0:T(4,128)(4,1)S(1)} %broadcast_and_fusion, f32[4,16,128,32]{2,3,1,0:T(8,128)S(1)} %convolution_add_fusion.1, bf16[32,36,1]{1,0,2:T(8,128)(2,1)S(1)} %copy.106, ...), kind=kOutput, calls=%fused_computation.112 | convolution fusion | flops 23592928 | bytes 3213760 | tf_op jit(solution)/shard_map/ok,kpqr->opqr/dot_general | solution.py:92
  22.8 0.5 convolution_bitcast_fusion
  23.2 0.0 copy-start.1
  23.2 0.5 convolution_bitcast_fusion.1
  23.7 0.5 convolution_bitcast_fusion.2
  24.2 0.1 copy.93
  24.3 0.1 copy.91
  24.4 0.1 copy.92
  24.5 0.1 pad_maximum_fusion.1
  24.6 1.6 %collective-permute-start.2 = (f32[32,109]{1,0:T(8,128)S(1)}, f32[32,109]{1,0:T(8,128)S(1)}, u32[]{:S(2)}, u32[]{:S(2)}) collective-permute-start(f32[32,109]{1,0:T(8,128)S(1)} %pad_maximum_fusion.1), channel_id=1, source_target_pairs={{0,4},{4,0},{8,12},{12,8},{16,20},{20,16},{24,28},{28,24},{1,5},{5... | collective-permute-start | bytes 41864 | tf_op jit(solution)/shard_map/ppermute | solution.py:20
  26.1 0.0 copy-done.1
  26.1 1.0 %copy.87 = bf16[32,4,16,128]{3,2,1,0:T(8,128)(2,1)} copy(bf16[32,4,16,128]{3,0,2,1:T(8,128)(2,1)S(1)} %copy-done.1) | data formatting | bytes 1048576 | tf_op jit(solution)/shard_map/convert_element_type | solution.py:96
  27.1 5.1 %all-to-all-start = ((bf16[32,4,16,128]{3,2,1,0:T(8,128)(2,1)}), bf16[32,4,16,128]{3,2,1,0:T(8,128)(2,1)S(1)}, u32[]{:S(2)}, u32[]{:S(2)}) async-start(bf16[32,4,16,128]{3,2,1,0:T(8,128)(2,1)} %copy.87), calls=%async_computation | async-start | bytes 1048576 | tf_op jit(solution)/shard_map/all_to_all | solution.py:101
  32.2 0.0 collective-permute-done.2
  32.2 0.1 fusion.73
  32.3 1.6 %collective-permute-start.3 = (f32[32,109]{1,0:T(8,128)S(1)}, f32[32,109]{1,0:T(8,128)S(1)}, u32[]{:S(2)}, u32[]{:S(2)}) collective-permute-start(f32[32,109]{1,0:T(8,128)S(1)} %fusion.73), channel_id=1, source_target_pairs={{0,8},{4,12},{8,0},{12,4},{16,24},{20,28},{24,16},{28,20},{1,9},{5... | collective-permute-start | bytes 41864 | tf_op jit(solution)/shard_map/ppermute | solution.py:20
  33.8 2.2 %collective-permute-done.3 = f32[32,109]{1,0:T(8,128)S(1)} collective-permute-done((f32[32,109]{1,0:T(8,128)S(1)}, f32[32,109]{1,0:T(8,128)S(1)}, u32[]{:S(2)}, u32[]{:S(2)}) %collective-permute-start.3) | collective-permute-done | bytes 13984 | tf_op jit(solution)/shard_map/ppermute | solution.py:20
  36.0 2.6 %collective-permute-start.4 = (f32[32,109]{1,0:T(8,128)S(1)}, f32[32,109]{1,0:T(8,128)S(1)}, u32[]{:S(2)}, u32[]{:S(2)}) collective-permute-start(f32[32,109]{1,0:T(8,128)S(1)} %add.107), channel_id=1, source_target_pairs={{0,16},{4,20},{8,24},{12,28},{16,0},{20,4},{24,8},{28,12},{1,17},{... | collective-permute-start | bytes 41864 | tf_op jit(solution)/shard_map/ppermute | solution.py:20
  38.6 2.1 %collective-permute-done.4 = f32[32,109]{1,0:T(8,128)S(1)} collective-permute-done((f32[32,109]{1,0:T(8,128)S(1)}, f32[32,109]{1,0:T(8,128)S(1)}, u32[]{:S(2)}, u32[]{:S(2)}) %collective-permute-start.4) | collective-permute-done | bytes 13984 | tf_op jit(solution)/shard_map/ppermute | solution.py:20
  40.7 0.0 collective-permute-start.5
  40.7 1.2 %collective-permute-done.5 = f32[32,109]{1,0:T(8,128)S(1)} collective-permute-done((f32[32,109]{1,0:T(8,128)S(1)}, f32[32,109]{1,0:T(8,128)S(1)}, u32[]{:S(2)}, u32[]{:S(2)}) %collective-permute-start.5) | collective-permute-done | bytes 13984 | tf_op jit(solution)/shard_map/ppermute | solution.py:20
  41.8 2.2 %collective-permute-start.6 = (f32[32,109]{1,0:T(8,128)S(1)}, f32[32,109]{1,0:T(8,128)S(1)}, u32[]{:S(2)}, u32[]{:S(2)}) collective-permute-start(f32[32,109]{1,0:T(8,128)S(1)} %add.109), channel_id=1, source_target_pairs={{0,2},{1,3},{2,0},{3,1},{4,6},{5,7},{6,4},{7,5},{8,10},{9,11},{10,... | collective-permute-start | bytes 41864 | tf_op jit(solution)/shard_map/ppermute | solution.py:20
  44.1 1.7 %collective-permute-done.6 = f32[32,109]{1,0:T(8,128)S(1)} collective-permute-done((f32[32,109]{1,0:T(8,128)S(1)}, f32[32,109]{1,0:T(8,128)S(1)}, u32[]{:S(2)}, u32[]{:S(2)}) %collective-permute-start.6) | collective-permute-done | bytes 13984 | tf_op jit(solution)/shard_map/ppermute | solution.py:20
  45.8 0.0 copy-start.2
  45.8 0.7 %slice_reduce_fusion = f32[8]{0:T(128)} fusion(f32[8,109]{1,0:T(8,128)S(1)} %dynamic-slice_add_fusion), kind=kLoop, calls=%fused_computation.53 | loop fusion | bytes 64 | tf_op jit(solution)/shard_map/slice | solution.py:112
  46.5 0.0 all-to-all-done
  46.5 0.9 %copy.88 = bf16[8,4,4,16,128]{4,3,2,1,0:T(8,128)(2,1)} copy(bf16[8,4,4,16,128]{4,3,1,0,2:T(8,128)(2,1)S(1)} %bitcast.100) | data formatting | bytes 1048576 | tf_op jit(solution)/shard_map/all_to_all | solution.py:101
  47.3 0.0 copy-done.2
  (27 shorter events, 0.5 us)
Async XLA Ops:
  0.6 12.3 %copy-start = (bf16[4,8,32,256]{3,2,1,0:T(8,128)(2,1)S(1)}, bf16[4,8,32,256]{3,2,1,0:T(8,128)(2,1)}, u32[]{:S(2)}) copy-start(bf16[4,8,32,256]{3,2,1,0:T(8,128)(2,1)} %param.6) | copy-start | bytes 1572868
  0.6 11.5 %copy-start.5 = (s32[4]{0:T(128)S(1)}, s32[4]{0:T(128)}, u32[]{:S(2)}) copy-start(s32[4]{0:T(128)} %param.8) | copy-start | bytes 52
  0.7 11.5 %copy-start.6 = (s32[8]{0:T(128)S(1)}, s32[8]{0:T(128)}, u32[]{:S(2)}) copy-start(s32[8]{0:T(128)} %param.7) | copy-start | bytes 100
  0.7 11.8 %copy-start.3 = (bf16[32,108]{1,0:T(8,128)(2,1)S(1)}, bf16[32,108]{1,0:T(8,128)(2,1)}, u32[]{:S(2)}) copy-start(bf16[32,108]{1,0:T(8,128)(2,1)} %param.9) | copy-start | bytes 20740
  1.6 11.3 %collective-permute-start = (bf16[4,32,256]{2,1,0:T(8,128)(2,1)S(1)}, bf16[4,32,256]{2,1,0:T(8,128)(2,1)S(1)}, u32[]{:S(2)}, u32[]{:S(2)}) collective-permute-start(bf16[4,32,256]{2,1,0:T(8,128)(2,1)S(1)} %slice_bitcast_fusion), channel_id=1, source_target_pairs={{0,4},{4,8},{8,12},{12,16},{16,20},{20,24},{24,28},{1,5},{5,9},{9,... | collective-permute-start | bytes 196616 | tf_op jit(solution)/shard_map/ppermute | solution.py:10
  8.6 12.3 %all-to-all-start.1 = ((bf16[8,4,64,128]{3,0,1,2:T(8,128)(2,1)}), bf16[8,4,64,128]{3,0,1,2:T(8,128)(2,1)S(1)}, u32[]{:S(2)}, u32[]{:S(2)}) async-start(bf16[8,4,64,128]{3,0,1,2:T(8,128)(2,1)} %copy.89), calls=%async_computation.1 | async-start | bytes 1048576 | tf_op jit(solution)/shard_map/all_to_all | solution.py:65
  13.1 3.2 %collective-permute-start.1 = (bf16[4,9,256]{2,0,1:T(4,128)(2,1)S(1)}, bf16[4,9,256]{2,0,1:T(4,128)(2,1)S(1)}, u32[]{:S(2)}, u32[]{:S(2)}) collective-permute-start(bf16[4,9,256]{2,0,1:T(4,128)(2,1)S(1)} %bitcast.102), channel_id=1, source_target_pairs={{0,1},{1,2},{2,3},{4,5},{5,6},{6,7},{8,9},{9,10},{10,11},{12,13},{... | collective-permute-start | bytes 55304 | tf_op jit(solution)/shard_map/ppermute | solution.py:10
  17.9 0.7 %copy-start.4 = (f32[32]{0:T(128)S(1)}, f32[32]{0:T(128)}, u32[]{:S(2)}) copy-start(f32[32]{0:T(128)} %param.10) | copy-start | bytes 388
  23.2 2.9 %copy-start.1 = (bf16[32,4,16,128]{3,0,2,1:T(8,128)(2,1)S(1)}, bf16[32,4,16,128]{3,0,2,1:T(8,128)(2,1)}, u32[]{:S(2)}) copy-start(bf16[32,4,16,128]{3,0,2,1:T(8,128)(2,1)} %get-tuple-element.15) | copy-start | bytes 1572868
  24.6 7.6 %collective-permute-start.2 = (f32[32,109]{1,0:T(8,128)S(1)}, f32[32,109]{1,0:T(8,128)S(1)}, u32[]{:S(2)}, u32[]{:S(2)}) collective-permute-start(f32[32,109]{1,0:T(8,128)S(1)} %pad_maximum_fusion.1), channel_id=1, source_target_pairs={{0,4},{4,0},{8,12},{12,8},{16,20},{20,16},{24,28},{28,24},{1,5},{5... | collective-permute-start | bytes 41864 | tf_op jit(solution)/shard_map/ppermute | solution.py:20
  27.1 19.4 %all-to-all-start = ((bf16[32,4,16,128]{3,2,1,0:T(8,128)(2,1)}), bf16[32,4,16,128]{3,2,1,0:T(8,128)(2,1)S(1)}, u32[]{:S(2)}, u32[]{:S(2)}) async-start(bf16[32,4,16,128]{3,2,1,0:T(8,128)(2,1)} %copy.87), calls=%async_computation | async-start | bytes 1048576 | tf_op jit(solution)/shard_map/all_to_all | solution.py:101
  32.3 3.7 %collective-permute-start.3 = (f32[32,109]{1,0:T(8,128)S(1)}, f32[32,109]{1,0:T(8,128)S(1)}, u32[]{:S(2)}, u32[]{:S(2)}) collective-permute-start(f32[32,109]{1,0:T(8,128)S(1)} %fusion.73), channel_id=1, source_target_pairs={{0,8},{4,12},{8,0},{12,4},{16,24},{20,28},{24,16},{28,20},{1,9},{5... | collective-permute-start | bytes 41864 | tf_op jit(solution)/shard_map/ppermute | solution.py:20
  36.0 4.6 %collective-permute-start.4 = (f32[32,109]{1,0:T(8,128)S(1)}, f32[32,109]{1,0:T(8,128)S(1)}, u32[]{:S(2)}, u32[]{:S(2)}) collective-permute-start(f32[32,109]{1,0:T(8,128)S(1)} %add.107), channel_id=1, source_target_pairs={{0,16},{4,20},{8,24},{12,28},{16,0},{20,4},{24,8},{28,12},{1,17},{... | collective-permute-start | bytes 41864 | tf_op jit(solution)/shard_map/ppermute | solution.py:20
  40.7 1.2 %collective-permute-start.5 = (f32[32,109]{1,0:T(8,128)S(1)}, f32[32,109]{1,0:T(8,128)S(1)}, u32[]{:S(2)}, u32[]{:S(2)}) collective-permute-start(f32[32,109]{1,0:T(8,128)S(1)} %add.108), channel_id=1, source_target_pairs={{0,1},{1,0},{2,3},{3,2},{4,5},{5,4},{6,7},{7,6},{8,9},{9,8},{10,11... | collective-permute-start | bytes 41864 | tf_op jit(solution)/shard_map/ppermute | solution.py:20
  41.8 3.9 %collective-permute-start.6 = (f32[32,109]{1,0:T(8,128)S(1)}, f32[32,109]{1,0:T(8,128)S(1)}, u32[]{:S(2)}, u32[]{:S(2)}) collective-permute-start(f32[32,109]{1,0:T(8,128)S(1)} %add.109), channel_id=1, source_target_pairs={{0,2},{1,3},{2,0},{3,1},{4,6},{5,7},{6,4},{7,5},{8,10},{9,11},{10,... | collective-permute-start | bytes 41864 | tf_op jit(solution)/shard_map/ppermute | solution.py:20
  45.8 1.6 %copy-start.2 = (f32[8,109]{1,0:T(8,128)}, f32[8,109]{1,0:T(8,128)S(1)}, u32[]{:S(2)}) copy-start(f32[8,109]{1,0:T(8,128)S(1)} %dynamic-slice_add_fusion) | copy-start | bytes 10468

commit v9 on v8

--- a/solution.py
+++ b/solution.py
@@ -62,7 +62,11 @@
     half_z = depth // 2
     out_chans = weight.shape[0]
     tiles_y = lax.axis_size("gy")
-    cell_grad = lax.all_to_all(grad_out, "gy", split_axis=2, concat_axis=0, tiled=True)
+    chans, rows_x, cols_all, lanes_z = grad_out.shape
+    out_parts = grad_out.reshape(chans, rows_x, tiles_y, cols_all // tiles_y, lanes_z).transpose(2, 0, 1, 3, 4)
+    out_parts = out_parts.reshape(tiles_y, chans * rows_x, cols_all // tiles_y, lanes_z)
+    cell_grad = lax.all_to_all(out_parts, "gy", split_axis=0, concat_axis=0, tiled=True)
+    cell_grad = cell_grad.reshape(tiles_y * chans, rows_x, cols_all // tiles_y, lanes_z)
     row_keep, row_at, row_ok = count_masks(rows_live, "gx", cap_x)
     col_keep, col_at, col_ok = count_masks(cols_live, "gy", cap_y)
     above = from_behind(fields[:, cap_x - 1], "gx", 1)
@@ -98,7 +102,10 @@
     grad_wide = jnp.where(live, cell_grad.astype(jnp.float32) * slope, 0.0)
     grad_wide = lax.reduce_precision(grad_wide, exponent_bits=8, mantissa_bits=7)
     returned = grad_wide.astype(jnp.bfloat16)
-    stem = lax.all_to_all(stem_local, "gy", split_axis=0, concat_axis=2, tiled=True)
+    stem_parts = stem_local.reshape(tiles_y, chans * rows_x, cols_all // tiles_y, lanes_z)
+    stem = lax.all_to_all(stem_parts, "gy", split_axis=0, concat_axis=0, tiled=True)
+    stem = stem.reshape(tiles_y, chans, rows_x, cols_all // tiles_y, lanes_z)
+    stem = stem.transpose(1, 2, 0, 3, 4).reshape(chans, rows_x, cols_all, lanes_z)
     grads = []
     for off_z in range(3):
         part = stacked[..., off_z * half_z : (off_z + 1) * half_z]

time: 47.7 us -> 47.4 us (level)
    unnamed x27 -> x24, local copies, waits for them, and re-layouts: 2.98 us -> 0.8 us
    reshape x0 -> x1, local copies, waits for them, and re-layouts: none -> 1.9 us  [local(): grad_out.reshape(chans, rows_x, tiles_y, cols_all // tiles_y, lanes_z)]
    all_to_all x1 -> x0, local copies, waits for them, and re-layouts: 0.86 us -> none  [local(): lax.all_to_all(stem_local, 'gy', split_axis=0, concat_axis=2, tiled=True)]
    transpose x0 -> x1, local copies, waits for them, and re-layouts: none -> 0.86 us  [local(): stem.transpose(1, 2, 0, 3, 4).reshape(chans, rows_x, cols_all, lanes_z)]
where the time goes in v9:
time: 47.4 us; the launch traced here: 47 us
  starting transfers between devices  23.7 us (50%)
  waiting for transfers between devices  9 us (19%)
  local copies, waits for them, and re-layouts  7.31 us (15%)
  matrix products  5.08 us (11%)
  between operations  0.98 us (2%)
  other arithmetic  0.95 us (2%)
    ppermute x5, starting transfers between devices, butterfly_sum(): value = value + lax.ppermute(value, axis, swap)  7.94 us
    ppermute x2, starting transfers between devices, from_behind(): return lax.ppermute(block, axis, route)  7.22 us
    ppermute x5, waiting for transfers between devices, butterfly_sum(): value = value + lax.ppermute(value, axis, swap)  7.11 us
    all_to_all x1, starting transfers between devices, local(): lax.all_to_all(stem_parts, 'gy', split_axis=0, concat_axis=0, tiled=True)  5.07 us
    all_to_all x1, starting transfers between devices, local(): lax.all_to_all(out_parts, 'gy', split_axis=0, concat_axis=0, tiled=True)  3.47 us
    dot_general x3, matrix products, local(): jnp.einsum('ok,kpqr->opqr', kernel[:, :, off_z], part, preferred_element_...  2.59 us
    reshape x1, local copies, waits for them, and re-layouts, local(): grad_out.reshape(chans, rows_x, tiles_y, cols_all // tiles_y, lanes_z)  1.9 us
    dot_general x3, matrix products, local(): jnp.einsum('opqr,kpqr->ok', returned, part, preferred_element_type=jnp.fl...  1.43 us
  transfers between devices with their start and end apart: 9, of which 6 were waited for; matrix products, arithmetic and copies ran while one was open for 17% of the time, Pallas kernels for 0%

profile of v9, /device:TPU:0, one launch (start us, length us, event | category | flops | bytes accessed | tf_op | source)
XLA Modules:
  0.0 47.0 jit_solution(15706954593850203835)
XLA Ops:
  0.6 0.0 copy-start
  0.6 0.0 copy-start.4
  0.7 0.0 copy-start.5
  0.7 0.0 copy-start.2
  0.7 0.9 %slice_bitcast_fusion = bf16[4,32,256]{2,1,0:T(8,128)(2,1)S(1)} fusion(bf16[4,8,32,256]{3,2,1,0:T(8,128)(2,1)} %param.6), kind=kLoop, calls=%fused_computation.43 | loop fusion | bytes 131072 | tf_op jit(solution)/shard_map/squeeze | solution.py:72
  1.6 4.9 %collective-permute-start = (bf16[4,32,256]{2,1,0:T(8,128)(2,1)S(1)}, bf16[4,32,256]{2,1,0:T(8,128)(2,1)S(1)}, u32[]{:S(2)}, u32[]{:S(2)}) collective-permute-start(bf16[4,32,256]{2,1,0:T(8,128)(2,1)S(1)} %slice_bitcast_fusion), channel_id=1, source_target_pairs={{0,4},{4,8},{8,12},{12,16},{16,20},{20,24},{24,28},{1,5},{5,9},{9,... | collective-permute-start | bytes 196616 | tf_op jit(solution)/shard_map/ppermute | solution.py:10
  6.4 1.9 %copy.72 = bf16[8,4,4,16,128]{4,3,1,0,2:T(8,128)(2,1)} copy(bf16[8,4,4,16,128]{4,3,2,1,0:T(8,128)(2,1)} %bitcast.96) | data formatting | bytes 1048576 | tf_op jit(solution)/shard_map/reshape | solution.py:66
  8.3 3.5 %all-to-all-start.1 = ((bf16[4,32,16,128]{3,2,1,0:T(8,128)(2,1)}), bf16[4,32,16,128]{3,2,1,0:T(8,128)(2,1)S(1)}, u32[]{:S(2)}, u32[]{:S(2)}) async-start(bf16[4,32,16,128]{3,2,1,0:T(8,128)(2,1)} %bitcast.30), calls=%async_computation.1 | async-start | bytes 1048576 | tf_op jit(solution)/shard_map/all_to_all | solution.py:68
  11.9 0.0 copy-done.4
  11.9 0.0 copy-done.5
  11.9 0.0 copy-done.2
  11.9 0.1 copy.64
  12.2 0.1 fusion.40
  12.2 0.1 fusion.50
  12.4 0.1 fusion.52
  12.5 0.1 broadcast_and_fusion
  12.5 0.1 fusion.54
  12.6 0.0 collective-permute-done
  12.6 0.0 copy-done
  12.6 0.1 select_select_fusion
  12.9 2.4 %collective-permute-start.1 = (bf16[4,9,256]{2,0,1:T(4,128)(2,1)S(1)}, bf16[4,9,256]{2,0,1:T(4,128)(2,1)S(1)}, u32[]{:S(2)}, u32[]{:S(2)}) collective-permute-start(bf16[4,9,256]{2,0,1:T(4,128)(2,1)S(1)} %bitcast.98), channel_id=1, source_target_pairs={{0,1},{1,2},{2,3},{4,5},{5,6},{6,7},{8,9},{9,10},{10,11},{12,13},{... | collective-permute-start | bytes 55304 | tf_op jit(solution)/shard_map/ppermute | solution.py:10
  15.2 0.1 copy.85
  15.3 0.1 copy.87
  15.4 0.1 copy.89
  15.5 0.5 %collective-permute-done.1 = bf16[4,9,256]{2,0,1:T(4,128)(2,1)S(1)} collective-permute-done((bf16[4,9,256]{2,0,1:T(4,128)(2,1)S(1)}, bf16[4,9,256]{2,0,1:T(4,128)(2,1)S(1)}, u32[]{:S(2)}, u32[]{:S(2)}) %collective-permute-start.1) | collective-permute-done | bytes 18464 | tf_op jit(solution)/shard_map/ppermute | solution.py:10
  16.0 1.1 %convolution_convert_fusion = bf16[4,9,48,384]{3,2,1,0:T(8,128)(2,1)S(1)} fusion(bf16[4,9,32,256]{3,2,1,0:T(8,128)(2,1)S(1)} %select_select_fusion, pred[33]{0:T(512)(128)(4,1)S(1)} %get-tuple-element.7, pred[33]{0:T(512)(128)(4,1)S(1)} %get-tuple-element.6, bf16[4,9,256]{2,1,0:T(8,128)(2,1)S(1)} %copy.61, s32[384]{0:T(512)S(1)} %fusion.44, ...), kind=kOutput, calls=%fused_computation | convolution fusion | flops 279191040 | bytes 1940130 | tf_op jit(solution)/shard_map/cxjy,cxyk->cxjk/dot_general | solution.py:85
  17.5 0.2 copy.62
  17.7 0.0 copy-start.3
  17.7 0.5 %fusion.68 = (bf16[36,4,16,128]{3,2,1,0:T(8,128)(2,1)S(1)}, bf16[36,4,16,128]{3,2,1,0:T(8,128)(2,1)S(1)}, bf16[36,4,16,128]{3,2,1,0:T(8,128)(2,1)S(1)}) fusion(bf16[36,4,16,384]{3,2,1,0:T(8,128)(2,1)S(1)} %bitcast.93), kind=kLoop, calls=%fused_computation.113 | loop fusion | bytes 3538944 | tf_op jit(solution)/shard_map/slice | solution.py:95
  18.2 0.1 copy-done.3
  18.3 0.4 convolution_add_fusion.2
  18.8 0.5 convolution_add_fusion.1
  19.2 1.4 %all-to-all-done.1 = bf16[4,32,16,128]{3,2,1,0:T(8,128)(2,1)S(1)} async-done(((bf16[4,32,16,128]{3,2,1,0:T(8,128)(2,1)}), bf16[4,32,16,128]{3,2,1,0:T(8,128)(2,1)S(1)}, u32[]{:S(2)}, u32[]{:S(2)}) %all-to-all-start.1) | async-done | bytes 524320 | tf_op jit(solution)/shard_map/all_to_all | solution.py:68
  20.6 0.1 convert.1
  20.7 1.7 %fusion.66 = (f32[32]{0:T(128)S(1)}, bf16[32,4,16,128]{3,0,2,1:T(8,128)(2,1)S(1)}, bf16[32,4,16,128]{3,0,2,1:T(8,128)(2,1)S(1)}) fusion(f32[32,4,16,128]{3,2,1,0:T(8,128)S(1)} %convert.1, pred[4,16]{1,0:T(4,128)(4,1)S(1)} %broadcast_and_fusion, f32[4,16,128,32]{2,3,1,0:T(8,128)S(1)} %convolution_add_fusion.1, bf16[32,36,1]{1,0,2:T(8,128)(2,1)S(1)} %copy.89, ...), kind=kOutput, calls=%fused_computation.112 | convolution fusion | flops 23330784 | bytes 3738048 | tf_op jit(solution)/shard_map/ok,kpqr->opqr/dot_general | solution.py:96
  22.4 0.5 %convolution_bitcast_fusion.2 = f32[32,36,1]{1,0,2:T(8,128)S(1)} fusion(bf16[36,4,16,128]{3,2,1,0:T(8,128)(2,1)S(1)} %get-tuple-element.14, bf16[32,4,16,128]{3,0,2,1:T(8,128)(2,1)S(1)} %get-tuple-element.11), kind=kOutput, calls=%fused_computation.10 | convolution fusion | flops 18874368 | bytes 1118720 | tf_op jit(solution)/shard_map/opqr,kpqr->ok/dot_general | solution.py:112
  22.9 0.5 %convolution_bitcast_fusion.1 = f32[32,36,1]{1,0,2:T(8,128)S(1)} fusion(bf16[36,4,16,128]{3,2,1,0:T(8,128)(2,1)S(1)} %get-tuple-element.13, bf16[32,4,16,128]{3,0,2,1:T(8,128)(2,1)S(1)} %get-tuple-element.11), kind=kOutput, calls=%fused_computation.9 | convolution fusion | flops 18874368 | bytes 1118720 | tf_op jit(solution)/shard_map/opqr,kpqr->ok/dot_general | solution.py:112
  23.4 0.5 %convolution_bitcast_fusion = f32[32,36,1]{1,0,2:T(8,128)S(1)} fusion(bf16[36,4,16,128]{3,2,1,0:T(8,128)(2,1)S(1)} %get-tuple-element.12, bf16[32,4,16,128]{3,0,2,1:T(8,128)(2,1)S(1)} %get-tuple-element.11), kind=kOutput, calls=%fused_computation.8 | convolution fusion | flops 18874368 | bytes 1118720 | tf_op jit(solution)/shard_map/opqr,kpqr->ok/dot_general | solution.py:112
  23.9 0.1 copy.74
  24.0 0.1 copy.75
  24.1 0.1 copy.76
  24.2 0.1 pad_maximum_fusion.1
  24.2 1.6 %collective-permute-start.2 = (f32[32,109]{1,0:T(8,128)S(1)}, f32[32,109]{1,0:T(8,128)S(1)}, u32[]{:S(2)}, u32[]{:S(2)}) collective-permute-start(f32[32,109]{1,0:T(8,128)S(1)} %pad_maximum_fusion.1), channel_id=1, source_target_pairs={{0,4},{4,0},{8,12},{12,8},{16,20},{20,16},{24,28},{28,24},{1,5},{5... | collective-permute-start | bytes 41864 | tf_op jit(solution)/shard_map/ppermute | solution.py:20
  25.8 1.0 %copy.70 = bf16[32,4,16,128]{3,2,1,0:T(8,128)(2,1)} copy(bf16[32,4,16,128]{3,0,2,1:T(8,128)(2,1)S(1)} %get-tuple-element.15) | data formatting | bytes 1048576 | tf_op jit(solution)/shard_map/convert_element_type | solution.py:100
  26.8 5.1 %all-to-all-start = ((bf16[4,32,16,128]{3,2,1,0:T(8,128)(2,1)}), bf16[4,32,16,128]{3,2,1,0:T(8,128)(2,1)S(1)}, u32[]{:S(2)}, u32[]{:S(2)}) async-start(bf16[4,32,16,128]{3,2,1,0:T(8,128)(2,1)} %bitcast.24), calls=%async_computation | async-start | bytes 1048576 | tf_op jit(solution)/shard_map/all_to_all | solution.py:106
  31.9 0.0 collective-permute-done.2
  31.9 0.1 fusion.73
  31.9 1.6 %collective-permute-start.3 = (f32[32,109]{1,0:T(8,128)S(1)}, f32[32,109]{1,0:T(8,128)S(1)}, u32[]{:S(2)}, u32[]{:S(2)}) collective-permute-start(f32[32,109]{1,0:T(8,128)S(1)} %fusion.73), channel_id=1, source_target_pairs={{0,8},{4,12},{8,0},{12,4},{16,24},{20,28},{24,16},{28,20},{1,9},{5... | collective-permute-start | bytes 41864 | tf_op jit(solution)/shard_map/ppermute | solution.py:20
  33.5 2.2 %collective-permute-done.3 = f32[32,109]{1,0:T(8,128)S(1)} collective-permute-done((f32[32,109]{1,0:T(8,128)S(1)}, f32[32,109]{1,0:T(8,128)S(1)}, u32[]{:S(2)}, u32[]{:S(2)}) %collective-permute-start.3) | collective-permute-done | bytes 13984 | tf_op jit(solution)/shard_map/ppermute | solution.py:20
  35.7 2.6 %collective-permute-start.4 = (f32[32,109]{1,0:T(8,128)S(1)}, f32[32,109]{1,0:T(8,128)S(1)}, u32[]{:S(2)}, u32[]{:S(2)}) collective-permute-start(f32[32,109]{1,0:T(8,128)S(1)} %add.107), channel_id=1, source_target_pairs={{0,16},{4,20},{8,24},{12,28},{16,0},{20,4},{24,8},{28,12},{1,17},{... | collective-permute-start | bytes 41864 | tf_op jit(solution)/shard_map/ppermute | solution.py:20
  38.3 2.1 %collective-permute-done.4 = f32[32,109]{1,0:T(8,128)S(1)} collective-permute-done((f32[32,109]{1,0:T(8,128)S(1)}, f32[32,109]{1,0:T(8,128)S(1)}, u32[]{:S(2)}, u32[]{:S(2)}) %collective-permute-start.4) | collective-permute-done | bytes 13984 | tf_op jit(solution)/shard_map/ppermute | solution.py:20
  40.3 0.0 collective-permute-start.5
  40.3 1.2 %collective-permute-done.5 = f32[32,109]{1,0:T(8,128)S(1)} collective-permute-done((f32[32,109]{1,0:T(8,128)S(1)}, f32[32,109]{1,0:T(8,128)S(1)}, u32[]{:S(2)}, u32[]{:S(2)}) %collective-permute-start.5) | collective-permute-done | bytes 13984 | tf_op jit(solution)/shard_map/ppermute | solution.py:20
  41.5 2.2 %collective-permute-start.6 = (f32[32,109]{1,0:T(8,128)S(1)}, f32[32,109]{1,0:T(8,128)S(1)}, u32[]{:S(2)}, u32[]{:S(2)}) collective-permute-start(f32[32,109]{1,0:T(8,128)S(1)} %add.109), channel_id=1, source_target_pairs={{0,2},{1,3},{2,0},{3,1},{4,6},{5,7},{6,4},{7,5},{8,10},{9,11},{10,... | collective-permute-start | bytes 41864 | tf_op jit(solution)/shard_map/ppermute | solution.py:20
  43.7 1.7 %collective-permute-done.6 = f32[32,109]{1,0:T(8,128)S(1)} collective-permute-done((f32[32,109]{1,0:T(8,128)S(1)}, f32[32,109]{1,0:T(8,128)S(1)}, u32[]{:S(2)}, u32[]{:S(2)}) %collective-permute-start.6) | collective-permute-done | bytes 13984 | tf_op jit(solution)/shard_map/ppermute | solution.py:20
  45.5 0.0 copy-start.1
  45.5 0.7 %slice_reduce_fusion = f32[8]{0:T(128)} fusion(f32[8,109]{1,0:T(8,128)S(1)} %dynamic-slice_add_fusion), kind=kLoop, calls=%fused_computation.53 | loop fusion | bytes 64 | tf_op jit(solution)/shard_map/slice | solution.py:119
  46.2 0.0 all-to-all-done
  46.2 0.9 %copy.71 = bf16[8,4,4,16,128]{4,3,2,1,0:T(8,128)(2,1)} copy(bf16[8,4,4,16,128]{4,3,1,0,2:T(8,128)(2,1)S(1)} %bitcast.95) | data formatting | bytes 1048576 | tf_op jit(solution)/shard_map/transpose | solution.py:108
  47.0 0.0 copy-done.1
  (27 shorter events, 0.5 us)
Async XLA Ops:
  0.6 12.0 %copy-start = (bf16[4,8,32,256]{3,2,1,0:T(8,128)(2,1)S(1)}, bf16[4,8,32,256]{3,2,1,0:T(8,128)(2,1)}, u32[]{:S(2)}) copy-start(bf16[4,8,32,256]{3,2,1,0:T(8,128)(2,1)} %param.6) | copy-start | bytes 1572868
  0.6 11.2 %copy-start.4 = (s32[8]{0:T(128)S(1)}, s32[8]{0:T(128)}, u32[]{:S(2)}) copy-start(s32[8]{0:T(128)} %param.7) | copy-start | bytes 100
  0.7 11.2 %copy-start.5 = (s32[4]{0:T(128)S(1)}, s32[4]{0:T(128)}, u32[]{:S(2)}) copy-start(s32[4]{0:T(128)} %param.8) | copy-start | bytes 52
  0.7 11.3 %copy-start.2 = (bf16[32,108]{1,0:T(8,128)(2,1)S(1)}, bf16[32,108]{1,0:T(8,128)(2,1)}, u32[]{:S(2)}) copy-start(bf16[32,108]{1,0:T(8,128)(2,1)} %param.9) | copy-start | bytes 20740
  1.6 11.1 %collective-permute-start = (bf16[4,32,256]{2,1,0:T(8,128)(2,1)S(1)}, bf16[4,32,256]{2,1,0:T(8,128)(2,1)S(1)}, u32[]{:S(2)}, u32[]{:S(2)}) collective-permute-start(bf16[4,32,256]{2,1,0:T(8,128)(2,1)S(1)} %slice_bitcast_fusion), channel_id=1, source_target_pairs={{0,4},{4,8},{8,12},{12,16},{16,20},{20,24},{24,28},{1,5},{5,9},{9,... | collective-permute-start | bytes 196616 | tf_op jit(solution)/shard_map/ppermute | solution.py:10
  8.3 12.3 %all-to-all-start.1 = ((bf16[4,32,16,128]{3,2,1,0:T(8,128)(2,1)}), bf16[4,32,16,128]{3,2,1,0:T(8,128)(2,1)S(1)}, u32[]{:S(2)}, u32[]{:S(2)}) async-start(bf16[4,32,16,128]{3,2,1,0:T(8,128)(2,1)} %bitcast.30), calls=%async_computation.1 | async-start | bytes 1048576 | tf_op jit(solution)/shard_map/all_to_all | solution.py:68
  12.9 3.2 %collective-permute-start.1 = (bf16[4,9,256]{2,0,1:T(4,128)(2,1)S(1)}, bf16[4,9,256]{2,0,1:T(4,128)(2,1)S(1)}, u32[]{:S(2)}, u32[]{:S(2)}) collective-permute-start(bf16[4,9,256]{2,0,1:T(4,128)(2,1)S(1)} %bitcast.98), channel_id=1, source_target_pairs={{0,1},{1,2},{2,3},{4,5},{5,6},{6,7},{8,9},{9,10},{10,11},{12,13},{... | collective-permute-start | bytes 55304 | tf_op jit(solution)/shard_map/ppermute | solution.py:10
  17.7 0.7 %copy-start.3 = (f32[32]{0:T(128)S(1)}, f32[32]{0:T(128)}, u32[]{:S(2)}) copy-start(f32[32]{0:T(128)} %param.10) | copy-start | bytes 388
  24.2 7.6 %collective-permute-start.2 = (f32[32,109]{1,0:T(8,128)S(1)}, f32[32,109]{1,0:T(8,128)S(1)}, u32[]{:S(2)}, u32[]{:S(2)}) collective-permute-start(f32[32,109]{1,0:T(8,128)S(1)} %pad_maximum_fusion.1), channel_id=1, source_target_pairs={{0,4},{4,0},{8,12},{12,8},{16,20},{20,16},{24,28},{28,24},{1,5},{5... | collective-permute-start | bytes 41864 | tf_op jit(solution)/shard_map/ppermute | solution.py:20
  26.8 19.4 %all-to-all-start = ((bf16[4,32,16,128]{3,2,1,0:T(8,128)(2,1)}), bf16[4,32,16,128]{3,2,1,0:T(8,128)(2,1)S(1)}, u32[]{:S(2)}, u32[]{:S(2)}) async-start(bf16[4,32,16,128]{3,2,1,0:T(8,128)(2,1)} %bitcast.24), calls=%async_computation | async-start | bytes 1048576 | tf_op jit(solution)/shard_map/all_to_all | solution.py:106
  31.9 3.7 %collective-permute-start.3 = (f32[32,109]{1,0:T(8,128)S(1)}, f32[32,109]{1,0:T(8,128)S(1)}, u32[]{:S(2)}, u32[]{:S(2)}) collective-permute-start(f32[32,109]{1,0:T(8,128)S(1)} %fusion.73), channel_id=1, source_target_pairs={{0,8},{4,12},{8,0},{12,4},{16,24},{20,28},{24,16},{28,20},{1,9},{5... | collective-permute-start | bytes 41864 | tf_op jit(solution)/shard_map/ppermute | solution.py:20
  35.7 4.6 %collective-permute-start.4 = (f32[32,109]{1,0:T(8,128)S(1)}, f32[32,109]{1,0:T(8,128)S(1)}, u32[]{:S(2)}, u32[]{:S(2)}) collective-permute-start(f32[32,109]{1,0:T(8,128)S(1)} %add.107), channel_id=1, source_target_pairs={{0,16},{4,20},{8,24},{12,28},{16,0},{20,4},{24,8},{28,12},{1,17},{... | collective-permute-start | bytes 41864 | tf_op jit(solution)/shard_map/ppermute | solution.py:20
  40.3 1.2 %collective-permute-start.5 = (f32[32,109]{1,0:T(8,128)S(1)}, f32[32,109]{1,0:T(8,128)S(1)}, u32[]{:S(2)}, u32[]{:S(2)}) collective-permute-start(f32[32,109]{1,0:T(8,128)S(1)} %add.108), channel_id=1, source_target_pairs={{0,1},{1,0},{2,3},{3,2},{4,5},{5,4},{6,7},{7,6},{8,9},{9,8},{10,11... | collective-permute-start | bytes 41864 | tf_op jit(solution)/shard_map/ppermute | solution.py:20
  41.5 3.9 %collective-permute-start.6 = (f32[32,109]{1,0:T(8,128)S(1)}, f32[32,109]{1,0:T(8,128)S(1)}, u32[]{:S(2)}, u32[]{:S(2)}) collective-permute-start(f32[32,109]{1,0:T(8,128)S(1)} %add.109), channel_id=1, source_target_pairs={{0,2},{1,3},{2,0},{3,1},{4,6},{5,7},{6,4},{7,5},{8,10},{9,11},{10,... | collective-permute-start | bytes 41864 | tf_op jit(solution)/shard_map/ppermute | solution.py:20
  45.5 1.6 %copy-start.1 = (f32[8,109]{1,0:T(8,128)}, f32[8,109]{1,0:T(8,128)S(1)}, u32[]{:S(2)}) copy-start(f32[8,109]{1,0:T(8,128)S(1)} %dynamic-slice_add_fusion) | copy-start | bytes 10468

commit v10 on v9

--- a/solution.py
+++ b/solution.py
@@ -14,11 +14,11 @@
     size = lax.axis_size(axis)
     if size & (size - 1):
         return lax.psum(value, axis)
-    step = 1
-    while step < size:
+    step = size // 2
+    while step:
         swap = [(i, i ^ step) for i in range(size)]
         value = value + lax.ppermute(value, axis, swap)
-        step *= 2
+        step //= 2
     return value
 
 

time: 47.4 us -> 47.5 us (level)
  no operation moved by 1% of the time
where the time goes in v10:
time: 47.5 us; the launch traced here: 47.2 us
  starting transfers between devices  23.7 us (50%)
  waiting for transfers between devices  9.14 us (19%)
  local copies, waits for them, and re-layouts  7.31 us (15%)
  matrix products  5.08 us (11%)
  between operations  0.98 us (2%)
  other arithmetic  0.95 us (2%)
    ppermute x5, starting transfers between devices, butterfly_sum(): value = value + lax.ppermute(value, axis, swap)  7.94 us
    ppermute x5, waiting for transfers between devices, butterfly_sum(): value = value + lax.ppermute(value, axis, swap)  7.24 us
    ppermute x2, starting transfers between devices, from_behind(): return lax.ppermute(block, axis, route)  7.22 us
    all_to_all x1, starting transfers between devices, local(): lax.all_to_all(stem_parts, 'gy', split_axis=0, concat_axis=0, tiled=True)  5.06 us
    all_to_all x1, starting transfers between devices, local(): lax.all_to_all(out_parts, 'gy', split_axis=0, concat_axis=0, tiled=True)  3.47 us
    dot_general x3, matrix products, local(): jnp.einsum('ok,kpqr->opqr', kernel[:, :, off_z], part, preferred_element_...  2.59 us
    reshape x1, local copies, waits for them, and re-layouts, local(): grad_out.reshape(chans, rows_x, tiles_y, cols_all // tiles_y, lanes_z)  1.9 us
    dot_general x3, matrix products, local(): jnp.einsum('opqr,kpqr->ok', returned, part, preferred_element_type=jnp.fl...  1.43 us
  transfers between devices with their start and end apart: 9, of which 6 were waited for; matrix products, arithmetic and copies ran while one was open for 17% of the time, Pallas kernels for 0%

profile of v10, /device:TPU:0, one launch (start us, length us, event | category | flops | bytes accessed | tf_op | source)
XLA Modules:
  0.0 47.2 jit_solution(14127078386887279975)
XLA Ops:
  0.6 0.0 copy-start
  0.6 0.0 copy-start.4
  0.7 0.0 copy-start.5
  0.7 0.0 copy-start.2
  0.7 0.9 %slice_bitcast_fusion = bf16[4,32,256]{2,1,0:T(8,128)(2,1)S(1)} fusion(bf16[4,8,32,256]{3,2,1,0:T(8,128)(2,1)} %param.6), kind=kLoop, calls=%fused_computation.43 | loop fusion | bytes 131072 | tf_op jit(solution)/shard_map/squeeze | solution.py:72
  1.6 4.9 %collective-permute-start = (bf16[4,32,256]{2,1,0:T(8,128)(2,1)S(1)}, bf16[4,32,256]{2,1,0:T(8,128)(2,1)S(1)}, u32[]{:S(2)}, u32[]{:S(2)}) collective-permute-start(bf16[4,32,256]{2,1,0:T(8,128)(2,1)S(1)} %slice_bitcast_fusion), channel_id=1, source_target_pairs={{0,4},{4,8},{8,12},{12,16},{16,20},{20,24},{24,28},{1,5},{5,9},{9,... | collective-permute-start | bytes 196616 | tf_op jit(solution)/shard_map/ppermute | solution.py:10
  6.4 1.9 %copy.72 = bf16[8,4,4,16,128]{4,3,1,0,2:T(8,128)(2,1)} copy(bf16[8,4,4,16,128]{4,3,2,1,0:T(8,128)(2,1)} %bitcast.96) | data formatting | bytes 1048576 | tf_op jit(solution)/shard_map/reshape | solution.py:66
  8.3 3.5 %all-to-all-start.1 = ((bf16[4,32,16,128]{3,2,1,0:T(8,128)(2,1)}), bf16[4,32,16,128]{3,2,1,0:T(8,128)(2,1)S(1)}, u32[]{:S(2)}, u32[]{:S(2)}) async-start(bf16[4,32,16,128]{3,2,1,0:T(8,128)(2,1)} %bitcast.30), calls=%async_computation.1 | async-start | bytes 1048576 | tf_op jit(solution)/shard_map/all_to_all | solution.py:68
  11.9 0.0 copy-done.4
  11.9 0.0 copy-done.5
  11.9 0.0 copy-done.2
  11.9 0.1 copy.64
  12.2 0.1 fusion.40
  12.2 0.1 fusion.50
  12.4 0.1 fusion.52
  12.5 0.1 broadcast_and_fusion
  12.5 0.1 fusion.54
  12.6 0.0 collective-permute-done
  12.6 0.0 copy-done
  12.6 0.1 select_select_fusion
  12.9 2.4 %collective-permute-start.1 = (bf16[4,9,256]{2,0,1:T(4,128)(2,1)S(1)}, bf16[4,9,256]{2,0,1:T(4,128)(2,1)S(1)}, u32[]{:S(2)}, u32[]{:S(2)}) collective-permute-start(bf16[4,9,256]{2,0,1:T(4,128)(2,1)S(1)} %bitcast.98), channel_id=1, source_target_pairs={{0,1},{1,2},{2,3},{4,5},{5,6},{6,7},{8,9},{9,10},{10,11},{12,13},{... | collective-permute-start | bytes 55304 | tf_op jit(solution)/shard_map/ppermute | solution.py:10
  15.2 0.1 copy.85
  15.3 0.1 copy.87
  15.4 0.1 copy.89
  15.5 0.5 %collective-permute-done.1 = bf16[4,9,256]{2,0,1:T(4,128)(2,1)S(1)} collective-permute-done((bf16[4,9,256]{2,0,1:T(4,128)(2,1)S(1)}, bf16[4,9,256]{2,0,1:T(4,128)(2,1)S(1)}, u32[]{:S(2)}, u32[]{:S(2)}) %collective-permute-start.1) | collective-permute-done | bytes 18464 | tf_op jit(solution)/shard_map/ppermute | solution.py:10
  16.0 1.1 %convolution_convert_fusion = bf16[4,9,48,384]{3,2,1,0:T(8,128)(2,1)S(1)} fusion(bf16[4,9,32,256]{3,2,1,0:T(8,128)(2,1)S(1)} %select_select_fusion, pred[33]{0:T(512)(128)(4,1)S(1)} %get-tuple-element.7, pred[33]{0:T(512)(128)(4,1)S(1)} %get-tuple-element.6, bf16[4,9,256]{2,1,0:T(8,128)(2,1)S(1)} %copy.61, s32[384]{0:T(512)S(1)} %fusion.44, ...), kind=kOutput, calls=%fused_computation | convolution fusion | flops 279191040 | bytes 1940130 | tf_op jit(solution)/shard_map/cxjy,cxyk->cxjk/dot_general | solution.py:85
  17.5 0.2 copy.62
  17.7 0.0 copy-start.3
  17.7 0.5 %fusion.68 = (bf16[36,4,16,128]{3,2,1,0:T(8,128)(2,1)S(1)}, bf16[36,4,16,128]{3,2,1,0:T(8,128)(2,1)S(1)}, bf16[36,4,16,128]{3,2,1,0:T(8,128)(2,1)S(1)}) fusion(bf16[36,4,16,384]{3,2,1,0:T(8,128)(2,1)S(1)} %bitcast.93), kind=kLoop, calls=%fused_computation.113 | loop fusion | bytes 3538944 | tf_op jit(solution)/shard_map/slice | solution.py:95
  18.2 0.1 copy-done.3
  18.3 0.4 convolution_add_fusion.2
  18.8 0.5 convolution_add_fusion.1
  19.2 1.4 %all-to-all-done.1 = bf16[4,32,16,128]{3,2,1,0:T(8,128)(2,1)S(1)} async-done(((bf16[4,32,16,128]{3,2,1,0:T(8,128)(2,1)}), bf16[4,32,16,128]{3,2,1,0:T(8,128)(2,1)S(1)}, u32[]{:S(2)}, u32[]{:S(2)}) %all-to-all-start.1) | async-done | bytes 524320 | tf_op jit(solution)/shard_map/all_to_all | solution.py:68
  20.6 0.1 convert.1
  20.7 1.7 %fusion.66 = (f32[32]{0:T(128)S(1)}, bf16[32,4,16,128]{3,0,2,1:T(8,128)(2,1)S(1)}, bf16[32,4,16,128]{3,0,2,1:T(8,128)(2,1)S(1)}) fusion(f32[32,4,16,128]{3,2,1,0:T(8,128)S(1)} %convert.1, pred[4,16]{1,0:T(4,128)(4,1)S(1)} %broadcast_and_fusion, f32[4,16,128,32]{2,3,1,0:T(8,128)S(1)} %convolution_add_fusion.1, bf16[32,36,1]{1,0,2:T(8,128)(2,1)S(1)} %copy.89, ...), kind=kOutput, calls=%fused_computation.112 | convolution fusion | flops 23330784 | bytes 3738048 | tf_op jit(solution)/shard_map/ok,kpqr->opqr/dot_general | solution.py:96
  22.4 0.5 %convolution_bitcast_fusion.2 = f32[32,36,1]{1,0,2:T(8,128)S(1)} fusion(bf16[36,4,16,128]{3,2,1,0:T(8,128)(2,1)S(1)} %get-tuple-element.14, bf16[32,4,16,128]{3,0,2,1:T(8,128)(2,1)S(1)} %get-tuple-element.11), kind=kOutput, calls=%fused_computation.10 | convolution fusion | flops 18874368 | bytes 1118720 | tf_op jit(solution)/shard_map/opqr,kpqr->ok/dot_general | solution.py:112
  22.9 0.5 %convolution_bitcast_fusion.1 = f32[32,36,1]{1,0,2:T(8,128)S(1)} fusion(bf16[36,4,16,128]{3,2,1,0:T(8,128)(2,1)S(1)} %get-tuple-element.13, bf16[32,4,16,128]{3,0,2,1:T(8,128)(2,1)S(1)} %get-tuple-element.11), kind=kOutput, calls=%fused_computation.9 | convolution fusion | flops 18874368 | bytes 1118720 | tf_op jit(solution)/shard_map/opqr,kpqr->ok/dot_general | solution.py:112
  23.4 0.5 %convolution_bitcast_fusion = f32[32,36,1]{1,0,2:T(8,128)S(1)} fusion(bf16[36,4,16,128]{3,2,1,0:T(8,128)(2,1)S(1)} %get-tuple-element.12, bf16[32,4,16,128]{3,0,2,1:T(8,128)(2,1)S(1)} %get-tuple-element.11), kind=kOutput, calls=%fused_computation.8 | convolution fusion | flops 18874368 | bytes 1118720 | tf_op jit(solution)/shard_map/opqr,kpqr->ok/dot_general | solution.py:112
  23.9 0.1 copy.74
  24.0 0.1 copy.75
  24.1 0.1 copy.76
  24.2 0.1 pad_maximum_fusion.1
  24.2 2.6 %collective-permute-start.2 = (f32[32,109]{1,0:T(8,128)S(1)}, f32[32,109]{1,0:T(8,128)S(1)}, u32[]{:S(2)}, u32[]{:S(2)}) collective-permute-start(f32[32,109]{1,0:T(8,128)S(1)} %pad_maximum_fusion.1), channel_id=1, source_target_pairs={{0,16},{4,20},{8,24},{12,28},{16,0},{20,4},{24,8},{28,12},{1,17},{... | collective-permute-start | bytes 41864 | tf_op jit(solution)/shard_map/ppermute | solution.py:20
  26.8 1.0 %copy.70 = bf16[32,4,16,128]{3,2,1,0:T(8,128)(2,1)} copy(bf16[32,4,16,128]{3,0,2,1:T(8,128)(2,1)S(1)} %get-tuple-element.15) | data formatting | bytes 1048576 | tf_op jit(solution)/shard_map/convert_element_type | solution.py:100
  27.8 5.1 %all-to-all-start = ((bf16[4,32,16,128]{3,2,1,0:T(8,128)(2,1)}), bf16[4,32,16,128]{3,2,1,0:T(8,128)(2,1)S(1)}, u32[]{:S(2)}, u32[]{:S(2)}) async-start(bf16[4,32,16,128]{3,2,1,0:T(8,128)(2,1)} %bitcast.24), calls=%async_computation | async-start | bytes 1048576 | tf_op jit(solution)/shard_map/all_to_all | solution.py:106
  32.9 0.0 collective-permute-done.2
  32.9 0.1 fusion.73
  33.0 1.6 %collective-permute-start.3 = (f32[32,109]{1,0:T(8,128)S(1)}, f32[32,109]{1,0:T(8,128)S(1)}, u32[]{:S(2)}, u32[]{:S(2)}) collective-permute-start(f32[32,109]{1,0:T(8,128)S(1)} %fusion.73), channel_id=1, source_target_pairs={{0,8},{4,12},{8,0},{12,4},{16,24},{20,28},{24,16},{28,20},{1,9},{5... | collective-permute-start | bytes 41864 | tf_op jit(solution)/shard_map/ppermute | solution.py:20
  34.6 2.2 %collective-permute-done.3 = f32[32,109]{1,0:T(8,128)S(1)} collective-permute-done((f32[32,109]{1,0:T(8,128)S(1)}, f32[32,109]{1,0:T(8,128)S(1)}, u32[]{:S(2)}, u32[]{:S(2)}) %collective-permute-start.3) | collective-permute-done | bytes 13984 | tf_op jit(solution)/shard_map/ppermute | solution.py:20
  36.7 1.5 %collective-permute-start.4 = (f32[32,109]{1,0:T(8,128)S(1)}, f32[32,109]{1,0:T(8,128)S(1)}, u32[]{:S(2)}, u32[]{:S(2)}) collective-permute-start(f32[32,109]{1,0:T(8,128)S(1)} %add.107), channel_id=1, source_target_pairs={{0,4},{4,0},{8,12},{12,8},{16,20},{20,16},{24,28},{28,24},{1,5},{5... | collective-permute-start | bytes 41864 | tf_op jit(solution)/shard_map/ppermute | solution.py:20
  38.3 2.2 %collective-permute-done.4 = f32[32,109]{1,0:T(8,128)S(1)} collective-permute-done((f32[32,109]{1,0:T(8,128)S(1)}, f32[32,109]{1,0:T(8,128)S(1)}, u32[]{:S(2)}, u32[]{:S(2)}) %collective-permute-start.4) | collective-permute-done | bytes 13984 | tf_op jit(solution)/shard_map/ppermute | solution.py:20
  40.5 2.2 %collective-permute-start.5 = (f32[32,109]{1,0:T(8,128)S(1)}, f32[32,109]{1,0:T(8,128)S(1)}, u32[]{:S(2)}, u32[]{:S(2)}) collective-permute-start(f32[32,109]{1,0:T(8,128)S(1)} %add.108), channel_id=1, source_target_pairs={{0,2},{1,3},{2,0},{3,1},{4,6},{5,7},{6,4},{7,5},{8,10},{9,11},{10,... | collective-permute-start | bytes 41864 | tf_op jit(solution)/shard_map/ppermute | solution.py:20
  42.7 1.7 %collective-permute-done.5 = f32[32,109]{1,0:T(8,128)S(1)} collective-permute-done((f32[32,109]{1,0:T(8,128)S(1)}, f32[32,109]{1,0:T(8,128)S(1)}, u32[]{:S(2)}, u32[]{:S(2)}) %collective-permute-start.5) | collective-permute-done | bytes 13984 | tf_op jit(solution)/shard_map/ppermute | solution.py:20
  44.4 0.0 collective-permute-start.6
  44.4 1.2 %collective-permute-done.6 = f32[32,109]{1,0:T(8,128)S(1)} collective-permute-done((f32[32,109]{1,0:T(8,128)S(1)}, f32[32,109]{1,0:T(8,128)S(1)}, u32[]{:S(2)}, u32[]{:S(2)}) %collective-permute-start.6) | collective-permute-done | bytes 13984 | tf_op jit(solution)/shard_map/ppermute | solution.py:20
  45.6 0.0 copy-start.1
  45.6 0.7 %slice_reduce_fusion = f32[8]{0:T(128)} fusion(f32[8,109]{1,0:T(8,128)S(1)} %dynamic-slice_add_fusion), kind=kLoop, calls=%fused_computation.53 | loop fusion | bytes 64 | tf_op jit(solution)/shard_map/slice | solution.py:119
  46.3 0.0 all-to-all-done
  46.3 0.9 %copy.71 = bf16[8,4,4,16,128]{4,3,2,1,0:T(8,128)(2,1)} copy(bf16[8,4,4,16,128]{4,3,1,0,2:T(8,128)(2,1)S(1)} %bitcast.95) | data formatting | bytes 1048576 | tf_op jit(solution)/shard_map/transpose | solution.py:108
  47.2 0.0 copy-done.1
  (27 shorter events, 0.5 us)
Async XLA Ops:
  0.6 12.0 %copy-start = (bf16[4,8,32,256]{3,2,1,0:T(8,128)(2,1)S(1)}, bf16[4,8,32,256]{3,2,1,0:T(8,128)(2,1)}, u32[]{:S(2)}) copy-start(bf16[4,8,32,256]{3,2,1,0:T(8,128)(2,1)} %param.6) | copy-start | bytes 1572868
  0.6 11.2 %copy-start.4 = (s32[8]{0:T(128)S(1)}, s32[8]{0:T(128)}, u32[]{:S(2)}) copy-start(s32[8]{0:T(128)} %param.7) | copy-start | bytes 100
  0.7 11.2 %copy-start.5 = (s32[4]{0:T(128)S(1)}, s32[4]{0:T(128)}, u32[]{:S(2)}) copy-start(s32[4]{0:T(128)} %param.8) | copy-start | bytes 52
  0.7 11.3 %copy-start.2 = (bf16[32,108]{1,0:T(8,128)(2,1)S(1)}, bf16[32,108]{1,0:T(8,128)(2,1)}, u32[]{:S(2)}) copy-start(bf16[32,108]{1,0:T(8,128)(2,1)} %param.9) | copy-start | bytes 20740
  1.6 11.1 %collective-permute-start = (bf16[4,32,256]{2,1,0:T(8,128)(2,1)S(1)}, bf16[4,32,256]{2,1,0:T(8,128)(2,1)S(1)}, u32[]{:S(2)}, u32[]{:S(2)}) collective-permute-start(bf16[4,32,256]{2,1,0:T(8,128)(2,1)S(1)} %slice_bitcast_fusion), channel_id=1, source_target_pairs={{0,4},{4,8},{8,12},{12,16},{16,20},{20,24},{24,28},{1,5},{5,9},{9,... | collective-permute-start | bytes 196616 | tf_op jit(solution)/shard_map/ppermute | solution.py:10
  8.3 12.3 %all-to-all-start.1 = ((bf16[4,32,16,128]{3,2,1,0:T(8,128)(2,1)}), bf16[4,32,16,128]{3,2,1,0:T(8,128)(2,1)S(1)}, u32[]{:S(2)}, u32[]{:S(2)}) async-start(bf16[4,32,16,128]{3,2,1,0:T(8,128)(2,1)} %bitcast.30), calls=%async_computation.1 | async-start | bytes 1048576 | tf_op jit(solution)/shard_map/all_to_all | solution.py:68
  12.9 3.2 %collective-permute-start.1 = (bf16[4,9,256]{2,0,1:T(4,128)(2,1)S(1)}, bf16[4,9,256]{2,0,1:T(4,128)(2,1)S(1)}, u32[]{:S(2)}, u32[]{:S(2)}) collective-permute-start(bf16[4,9,256]{2,0,1:T(4,128)(2,1)S(1)} %bitcast.98), channel_id=1, source_target_pairs={{0,1},{1,2},{2,3},{4,5},{5,6},{6,7},{8,9},{9,10},{10,11},{12,13},{... | collective-permute-start | bytes 55304 | tf_op jit(solution)/shard_map/ppermute | solution.py:10
  17.7 0.7 %copy-start.3 = (f32[32]{0:T(128)S(1)}, f32[32]{0:T(128)}, u32[]{:S(2)}) copy-start(f32[32]{0:T(128)} %param.10) | copy-start | bytes 388
  24.2 8.7 %collective-permute-start.2 = (f32[32,109]{1,0:T(8,128)S(1)}, f32[32,109]{1,0:T(8,128)S(1)}, u32[]{:S(2)}, u32[]{:S(2)}) collective-permute-start(f32[32,109]{1,0:T(8,128)S(1)} %pad_maximum_fusion.1), channel_id=1, source_target_pairs={{0,16},{4,20},{8,24},{12,28},{16,0},{20,4},{24,8},{28,12},{1,17},{... | collective-permute-start | bytes 41864 | tf_op jit(solution)/shard_map/ppermute | solution.py:20
  27.8 18.5 %all-to-all-start = ((bf16[4,32,16,128]{3,2,1,0:T(8,128)(2,1)}), bf16[4,32,16,128]{3,2,1,0:T(8,128)(2,1)S(1)}, u32[]{:S(2)}, u32[]{:S(2)}) async-start(bf16[4,32,16,128]{3,2,1,0:T(8,128)(2,1)} %bitcast.24), calls=%async_computation | async-start | bytes 1048576 | tf_op jit(solution)/shard_map/all_to_all | solution.py:106
  33.0 3.7 %collective-permute-start.3 = (f32[32,109]{1,0:T(8,128)S(1)}, f32[32,109]{1,0:T(8,128)S(1)}, u32[]{:S(2)}, u32[]{:S(2)}) collective-permute-start(f32[32,109]{1,0:T(8,128)S(1)} %fusion.73), channel_id=1, source_target_pairs={{0,8},{4,12},{8,0},{12,4},{16,24},{20,28},{24,16},{28,20},{1,9},{5... | collective-permute-start | bytes 41864 | tf_op jit(solution)/shard_map/ppermute | solution.py:20
  36.7 3.7 %collective-permute-start.4 = (f32[32,109]{1,0:T(8,128)S(1)}, f32[32,109]{1,0:T(8,128)S(1)}, u32[]{:S(2)}, u32[]{:S(2)}) collective-permute-start(f32[32,109]{1,0:T(8,128)S(1)} %add.107), channel_id=1, source_target_pairs={{0,4},{4,0},{8,12},{12,8},{16,20},{20,16},{24,28},{28,24},{1,5},{5... | collective-permute-start | bytes 41864 | tf_op jit(solution)/shard_map/ppermute | solution.py:20
  40.5 3.9 %collective-permute-start.5 = (f32[32,109]{1,0:T(8,128)S(1)}, f32[32,109]{1,0:T(8,128)S(1)}, u32[]{:S(2)}, u32[]{:S(2)}) collective-permute-start(f32[32,109]{1,0:T(8,128)S(1)} %add.108), channel_id=1, source_target_pairs={{0,2},{1,3},{2,0},{3,1},{4,6},{5,7},{6,4},{7,5},{8,10},{9,11},{10,... | collective-permute-start | bytes 41864 | tf_op jit(solution)/shard_map/ppermute | solution.py:20
  44.4 1.2 %collective-permute-start.6 = (f32[32,109]{1,0:T(8,128)S(1)}, f32[32,109]{1,0:T(8,128)S(1)}, u32[]{:S(2)}, u32[]{:S(2)}) collective-permute-start(f32[32,109]{1,0:T(8,128)S(1)} %add.109), channel_id=1, source_target_pairs={{0,1},{1,0},{2,3},{3,2},{4,5},{5,4},{6,7},{7,6},{8,9},{9,8},{10,11... | collective-permute-start | bytes 41864 | tf_op jit(solution)/shard_map/ppermute | solution.py:20
  45.6 1.6 %copy-start.1 = (f32[8,109]{1,0:T(8,128)}, f32[8,109]{1,0:T(8,128)S(1)}, u32[]{:S(2)}) copy-start(f32[8,109]{1,0:T(8,128)S(1)} %dynamic-slice_add_fusion) | copy-start | bytes 10468

commit v11 on v10

--- a/solution.py
+++ b/solution.py
@@ -102,10 +102,6 @@
     grad_wide = jnp.where(live, cell_grad.astype(jnp.float32) * slope, 0.0)
     grad_wide = lax.reduce_precision(grad_wide, exponent_bits=8, mantissa_bits=7)
     returned = grad_wide.astype(jnp.bfloat16)
-    stem_parts = stem_local.reshape(tiles_y, chans * rows_x, cols_all // tiles_y, lanes_z)
-    stem = lax.all_to_all(stem_parts, "gy", split_axis=0, concat_axis=0, tiled=True)
-    stem = stem.reshape(tiles_y, chans, rows_x, cols_all // tiles_y, lanes_z)
-    stem = stem.transpose(1, 2, 0, 3, 4).reshape(chans, rows_x, cols_all, lanes_z)
     grads = []
     for off_z in range(3):
         part = stacked[..., off_z * half_z : (off_z + 1) * half_z]
@@ -113,10 +109,25 @@
     weight_full = jnp.stack(grads, axis=-1).reshape(out_chans, -1)
     bias_full = jnp.sum(grad_wide, axis=(1, 2, 3))
     packed = jnp.concatenate([weight_full, bias_full[:, None]], axis=1)
-    total = butterfly_sum(butterfly_sum(packed, "gx"), "gy")
     share = out_chans // tiles_y
-    mine = lax.dynamic_slice_in_dim(total, lax.axis_index("gy") * share, share, 0)
-    weight_grad, bias_grad = mine[:, :-1], mine[:, -1]
+    high = packed.astype(jnp.bfloat16)
+    low = (packed - high.astype(jnp.float32)).astype(jnp.bfloat16)
+    coded = jnp.stack([high, low]).reshape(2, tiles_y, -1).transpose(1, 0, 2).reshape(tiles_y, -1)
+    tile = (cols_all // tiles_y) * lanes_z
+    extra = -(-coded.shape[1] // tile)
+    coded = jnp.pad(coded, ((0, 0), (0, extra * tile - coded.shape[1])))
+    coded = coded.reshape(tiles_y, extra, cols_all // tiles_y, lanes_z)
+    stem_parts = stem_local.reshape(tiles_y, chans * rows_x, cols_all // tiles_y, lanes_z)
+    sent = jnp.concatenate([stem_parts, coded], axis=1)
+    got = lax.all_to_all(sent, "gy", split_axis=0, concat_axis=0, tiled=True)
+    stem = got[:, : chans * rows_x].reshape(tiles_y, chans, rows_x, cols_all // tiles_y, lanes_z)
+    stem = stem.transpose(1, 2, 0, 3, 4).reshape(chans, rows_x, cols_all, lanes_z)
+    width = packed.shape[1]
+    pieces = got[:, chans * rows_x :].reshape(tiles_y, -1)[:, : 2 * share * width]
+    pieces = pieces.reshape(tiles_y, 2, share, width).astype(jnp.float32)
+    part = jnp.sum(pieces[:, 0] + pieces[:, 1], axis=0)
+    total = butterfly_sum(part, "gx")
+    weight_grad, bias_grad = total[:, :-1], total[:, -1]
     return (stem, weight_grad, bias_grad)
 
 

time: 47.5 us -> 51.6 us (1.086)
  blocking collectives: 0 us -> 13.9 us
  starting transfers between devices: 23.7 us -> 16.5 us
  waiting for transfers between devices: 9.14 us -> 7 us
    all_to_all x0 -> x1, blocking collectives: none -> 13.9 us  [local(): got = lax.all_to_all(sent, 'gy', split_axis=0, concat_axis=0, tiled=True)]
    all_to_all x1 -> x0, starting transfers between devices: 5.06 us -> none  [local(): lax.all_to_all(stem_parts, 'gy', split_axis=0, concat_axis=0, tiled=True)]
    ppermute x5 -> x3, starting transfers between devices: 7.94 us -> 5.78 us  [butterfly_sum(): value = value + lax.ppermute(value, axis, swap)]
    ppermute x5 -> x3, waiting for transfers between devices: 7.24 us -> 5.11 us  [butterfly_sum(): value = value + lax.ppermute(value, axis, swap)]
    convert_element_type x1, local copies, waits for them, and re-layouts: 1 us -> 0.21 us  [local(): stem_local = (pre_wide * sigma).astype(jnp.bfloat16)]
  transfers between devices with their start and end apart: 9 -> 6, of which waited for: 6 -> 5; matrix products, arithmetic and copies ran while one was open for 17% -> 14% of each run, Pallas kernels for 0% -> 0%
where the time goes in v11:
time: 51.6 us; the launch traced here: 51.3 us
  starting transfers between devices  16.5 us (32%)
  blocking collectives  13.9 us (27%)
  waiting for transfers between devices  7 us (14%)
  local copies, waits for them, and re-layouts  6.88 us (13%)
  matrix products  5.09 us (10%)
  between operations  1.05 us (2%)
  other arithmetic  0.95 us (2%)
    all_to_all x1, blocking collectives, local(): got = lax.all_to_all(sent, 'gy', split_axis=0, concat_axis=0, tiled=True)  13.9 us
    ppermute x2, starting transfers between devices, from_behind(): return lax.ppermute(block, axis, route)  7.22 us
    ppermute x3, starting transfers between devices, butterfly_sum(): value = value + lax.ppermute(value, axis, swap)  5.78 us
    ppermute x3, waiting for transfers between devices, butterfly_sum(): value = value + lax.ppermute(value, axis, swap)  5.11 us
    all_to_all x1, starting transfers between devices, local(): lax.all_to_all(out_parts, 'gy', split_axis=0, concat_axis=0, tiled=True)  3.47 us
    dot_general x3, matrix products, local(): jnp.einsum('ok,kpqr->opqr', kernel[:, :, off_z], part, preferred_element_...  2.59 us
    reshape x1, local copies, waits for them, and re-layouts, local(): grad_out.reshape(chans, rows_x, tiles_y, cols_all // tiles_y, lanes_z)  1.9 us
    dot_general x3, matrix products, local(): jnp.einsum('opqr,kpqr->ok', returned, part, preferred_element_type=jnp.fl...  1.43 us
  transfers between devices with their start and end apart: 6, of which 5 were waited for; matrix products, arithmetic and copies ran while one was open for 14% of the time, Pallas kernels for 0%

profile of v11, /device:TPU:0, one launch (start us, length us, event | category | flops | bytes accessed | tf_op | source)
XLA Modules:
  0.0 51.3 jit_solution(3745314251762752293)
XLA Ops:
  0.6 0.0 copy-start
  0.6 0.0 copy-start.4
  0.7 0.0 copy-start.5
  0.7 0.0 copy-start.2
  0.7 0.9 %slice_bitcast_fusion = bf16[4,32,256]{2,1,0:T(8,128)(2,1)S(1)} fusion(bf16[4,8,32,256]{3,2,1,0:T(8,128)(2,1)} %param.6), kind=kLoop, calls=%fused_computation.44 | loop fusion | bytes 131072 | tf_op jit(solution)/shard_map/squeeze | solution.py:72
  1.6 4.9 %collective-permute-start = (bf16[4,32,256]{2,1,0:T(8,128)(2,1)S(1)}, bf16[4,32,256]{2,1,0:T(8,128)(2,1)S(1)}, u32[]{:S(2)}, u32[]{:S(2)}) collective-permute-start(bf16[4,32,256]{2,1,0:T(8,128)(2,1)S(1)} %slice_bitcast_fusion), channel_id=1, source_target_pairs={{0,4},{4,8},{8,12},{12,16},{16,20},{20,24},{24,28},{1,5},{5,9},{9,... | collective-permute-start | bytes 196616 | tf_op jit(solution)/shard_map/ppermute | solution.py:10
  6.4 1.9 %copy.87 = bf16[8,4,4,16,128]{4,3,1,0,2:T(8,128)(2,1)} copy(bf16[8,4,4,16,128]{4,3,2,1,0:T(8,128)(2,1)} %bitcast.111) | data formatting | bytes 1048576 | tf_op jit(solution)/shard_map/reshape | solution.py:66
  8.3 3.5 %all-to-all-start = ((bf16[4,32,16,128]{3,2,1,0:T(8,128)(2,1)}), bf16[4,32,16,128]{3,2,1,0:T(8,128)(2,1)S(1)}, u32[]{:S(2)}, u32[]{:S(2)}) async-start(bf16[4,32,16,128]{3,2,1,0:T(8,128)(2,1)} %bitcast.27), calls=%async_computation | async-start | bytes 1048576 | tf_op jit(solution)/shard_map/all_to_all | solution.py:68
  11.9 0.0 copy-done.4
  11.9 0.0 copy-done.5
  11.9 0.0 copy-done.2
  11.9 0.1 copy.80
  12.2 0.1 fusion.41
  12.3 0.1 fusion.51
  12.4 0.1 fusion.53
  12.5 0.1 broadcast_and_fusion
  12.5 0.1 fusion.55
  12.6 0.0 collective-permute-done
  12.6 0.0 copy-done
  12.6 0.1 select_select_fusion
  12.9 2.4 %collective-permute-start.1 = (bf16[4,9,256]{2,0,1:T(4,128)(2,1)S(1)}, bf16[4,9,256]{2,0,1:T(4,128)(2,1)S(1)}, u32[]{:S(2)}, u32[]{:S(2)}) collective-permute-start(bf16[4,9,256]{2,0,1:T(4,128)(2,1)S(1)} %bitcast.115), channel_id=1, source_target_pairs={{0,1},{1,2},{2,3},{4,5},{5,6},{6,7},{8,9},{9,10},{10,11},{12,13},{... | collective-permute-start | bytes 55304 | tf_op jit(solution)/shard_map/ppermute | solution.py:10
  15.2 0.1 copy.102
  15.3 0.1 copy.104
  15.4 0.1 copy.106
  15.5 0.5 %collective-permute-done.1 = bf16[4,9,256]{2,0,1:T(4,128)(2,1)S(1)} collective-permute-done((bf16[4,9,256]{2,0,1:T(4,128)(2,1)S(1)}, bf16[4,9,256]{2,0,1:T(4,128)(2,1)S(1)}, u32[]{:S(2)}, u32[]{:S(2)}) %collective-permute-start.1) | collective-permute-done | bytes 18464 | tf_op jit(solution)/shard_map/ppermute | solution.py:10
  16.0 1.1 %convolution_convert_fusion = bf16[4,9,48,384]{3,2,1,0:T(8,128)(2,1)S(1)} fusion(bf16[4,9,32,256]{3,2,1,0:T(8,128)(2,1)S(1)} %select_select_fusion, pred[33]{0:T(512)(128)(4,1)S(1)} %get-tuple-element.4, pred[33]{0:T(512)(128)(4,1)S(1)} %get-tuple-element.3, bf16[4,9,256]{2,1,0:T(8,128)(2,1)S(1)} %copy.77, s32[384]{0:T(512)S(1)} %fusion.45, ...), kind=kOutput, calls=%fused_computation | convolution fusion | flops 279191040 | bytes 1940130 | tf_op jit(solution)/shard_map/cxjy,cxyk->cxjk/dot_general | solution.py:85
  17.5 0.2 copy.78
  17.7 0.0 copy-start.3
  17.7 0.5 %fusion.69 = (bf16[36,4,16,128]{3,2,1,0:T(8,128)(2,1)S(1)}, bf16[36,4,16,128]{3,2,1,0:T(8,128)(2,1)S(1)}, bf16[36,4,16,128]{3,2,1,0:T(8,128)(2,1)S(1)}) fusion(bf16[36,4,16,384]{3,2,1,0:T(8,128)(2,1)S(1)} %bitcast.107), kind=kLoop, calls=%fused_computation.122 | loop fusion | bytes 3538944 | tf_op jit(solution)/shard_map/slice | solution.py:95
  18.2 0.1 copy-done.3
  18.3 0.4 convolution_add_fusion.2
  18.8 0.5 convolution_add_fusion.1
  19.3 1.4 %all-to-all-done = bf16[4,32,16,128]{3,2,1,0:T(8,128)(2,1)S(1)} async-done(((bf16[4,32,16,128]{3,2,1,0:T(8,128)(2,1)}), bf16[4,32,16,128]{3,2,1,0:T(8,128)(2,1)S(1)}, u32[]{:S(2)}, u32[]{:S(2)}) %all-to-all-start) | async-done | bytes 524320 | tf_op jit(solution)/shard_map/all_to_all | solution.py:68
  20.6 0.1 convert.2
  20.7 1.7 %fusion.67 = (f32[32]{0:T(128)S(1)}, bf16[32,4,16,128]{3,0,2,1:T(8,128)(2,1)S(1)}, bf16[32,4,16,128]{3,0,2,1:T(8,128)(2,1)S(1)}) fusion(f32[32,4,16,128]{3,2,1,0:T(8,128)S(1)} %convert.2, pred[4,16]{1,0:T(4,128)(4,1)S(1)} %broadcast_and_fusion, f32[4,16,128,32]{2,3,1,0:T(8,128)S(1)} %convolution_add_fusion.1, bf16[32,36,1]{1,0,2:T(8,128)(2,1)S(1)} %copy.106, ...), kind=kOutput, calls=%fused_computation.121 | convolution fusion | flops 23330784 | bytes 3738048 | tf_op jit(solution)/shard_map/ok,kpqr->opqr/dot_general | solution.py:96
  22.4 0.5 convolution_bitcast_fusion.2
  22.9 0.5 convolution_bitcast_fusion.1
  23.4 0.5 convolution_bitcast_fusion
  23.8 0.2 copy.86
  24.1 0.1 copy.89
  24.2 0.1 copy.90
  24.3 0.1 copy.91
  24.4 0.1 pad_maximum_fusion.2
  24.5 0.1 concatenate.26
  24.6 0.1 reshape.189
  24.7 0.1 pad_maximum_fusion
  24.8 13.9 %all_to_all.10 = bf16[4,33,16,128]{3,2,1,0:T(8,128)(2,1)S(1)} all-to-all(bf16[4,33,16,128]{3,2,1,0:T(8,128)(2,1)S(1)} %pad_maximum_fusion), channel_id=1, replica_groups=mesh['gx'=8,'gy'=4] {'gy'}, dimensions={0} | all-to-all | bytes 1081344 | tf_op jit(solution)/shard_map/all_to_all | solution.py:122
  38.7 0.1 reshape.195
  38.8 2.7 %collective-permute-start.2 = (f32[8,109]{1,0:T(8,128)S(1)}, f32[8,109]{1,0:T(8,128)S(1)}, u32[]{:S(2)}, u32[]{:S(2)}) collective-permute-start(f32[8,109]{1,0:T(8,128)S(1)} %fusion.32), channel_id=1, source_target_pairs={{0,16},{4,20},{8,24},{12,28},{16,0},{20,4},{24,8},{28,12},{1,17},{... | collective-permute-start | bytes 10472 | tf_op jit(solution)/shard_map/ppermute | solution.py:20
  41.4 1.9 %collective-permute-done.2 = f32[8,109]{1,0:T(8,128)S(1)} collective-permute-done((f32[8,109]{1,0:T(8,128)S(1)}, f32[8,109]{1,0:T(8,128)S(1)}, u32[]{:S(2)}, u32[]{:S(2)}) %collective-permute-start.2) | collective-permute-done | bytes 3520 | tf_op jit(solution)/shard_map/ppermute | solution.py:20
  43.4 1.6 %collective-permute-start.3 = (f32[8,109]{1,0:T(8,128)S(1)}, f32[8,109]{1,0:T(8,128)S(1)}, u32[]{:S(2)}, u32[]{:S(2)}) collective-permute-start(f32[8,109]{1,0:T(8,128)S(1)} %add.104), channel_id=1, source_target_pairs={{0,8},{4,12},{8,0},{12,4},{16,24},{20,28},{24,16},{28,20},{1,9},{5... | collective-permute-start | bytes 10472 | tf_op jit(solution)/shard_map/ppermute | solution.py:20
  44.9 2.0 %collective-permute-done.3 = f32[8,109]{1,0:T(8,128)S(1)} collective-permute-done((f32[8,109]{1,0:T(8,128)S(1)}, f32[8,109]{1,0:T(8,128)S(1)}, u32[]{:S(2)}, u32[]{:S(2)}) %collective-permute-start.3) | collective-permute-done | bytes 3520 | tf_op jit(solution)/shard_map/ppermute | solution.py:20
  47.0 1.5 %collective-permute-start.4 = (f32[8,109]{1,0:T(8,128)S(1)}, f32[8,109]{1,0:T(8,128)S(1)}, u32[]{:S(2)}, u32[]{:S(2)}) collective-permute-start(f32[8,109]{1,0:T(8,128)S(1)} %add.105), channel_id=1, source_target_pairs={{0,4},{4,0},{8,12},{12,8},{16,20},{20,16},{24,28},{28,24},{1,5},{5... | collective-permute-start | bytes 10472 | tf_op jit(solution)/shard_map/ppermute | solution.py:20
  48.6 0.9 %copy.93 = bf16[8,4,4,16,128]{4,3,2,1,0:T(8,128)(2,1)} copy(bf16[8,4,4,16,128]{4,3,1,0,2:T(8,128)(2,1)S(1)} %bitcast.110) | data formatting | bytes 1048576 | tf_op jit(solution)/shard_map/transpose | solution.py:124
  49.4 1.2 %collective-permute-done.4 = f32[8,109]{1,0:T(8,128)S(1)} collective-permute-done((f32[8,109]{1,0:T(8,128)S(1)}, f32[8,109]{1,0:T(8,128)S(1)}, u32[]{:S(2)}, u32[]{:S(2)}) %collective-permute-start.4) | collective-permute-done | bytes 3520 | tf_op jit(solution)/shard_map/ppermute | solution.py:20
  50.6 0.0 copy-start.1
  50.6 0.7 %slice_reduce_fusion = f32[8]{0:T(128)} fusion(f32[8,109]{1,0:T(8,128)S(1)} %add.106), kind=kLoop, calls=%fused_computation.62 | loop fusion | bytes 64 | tf_op jit(solution)/shard_map/slice | solution.py:130
  51.3 0.0 copy-done.1
  (36 shorter events, 0.6 us)
Async XLA Ops:
  0.6 12.0 %copy-start = (bf16[4,8,32,256]{3,2,1,0:T(8,128)(2,1)S(1)}, bf16[4,8,32,256]{3,2,1,0:T(8,128)(2,1)}, u32[]{:S(2)}) copy-start(bf16[4,8,32,256]{3,2,1,0:T(8,128)(2,1)} %param.6) | copy-start | bytes 1572868
  0.6 11.2 %copy-start.4 = (s32[8]{0:T(128)S(1)}, s32[8]{0:T(128)}, u32[]{:S(2)}) copy-start(s32[8]{0:T(128)} %param.7) | copy-start | bytes 100
  0.7 11.2 %copy-start.5 = (s32[4]{0:T(128)S(1)}, s32[4]{0:T(128)}, u32[]{:S(2)}) copy-start(s32[4]{0:T(128)} %param.8) | copy-start | bytes 52
  0.7 11.3 %copy-start.2 = (bf16[32,108]{1,0:T(8,128)(2,1)S(1)}, bf16[32,108]{1,0:T(8,128)(2,1)}, u32[]{:S(2)}) copy-start(bf16[32,108]{1,0:T(8,128)(2,1)} %param.9) | copy-start | bytes 20740
  1.6 11.1 %collective-permute-start = (bf16[4,32,256]{2,1,0:T(8,128)(2,1)S(1)}, bf16[4,32,256]{2,1,0:T(8,128)(2,1)S(1)}, u32[]{:S(2)}, u32[]{:S(2)}) collective-permute-start(bf16[4,32,256]{2,1,0:T(8,128)(2,1)S(1)} %slice_bitcast_fusion), channel_id=1, source_target_pairs={{0,4},{4,8},{8,12},{12,16},{16,20},{20,24},{24,28},{1,5},{5,9},{9,... | collective-permute-start | bytes 196616 | tf_op jit(solution)/shard_map/ppermute | solution.py:10
  8.3 12.3 %all-to-all-start = ((bf16[4,32,16,128]{3,2,1,0:T(8,128)(2,1)}), bf16[4,32,16,128]{3,2,1,0:T(8,128)(2,1)S(1)}, u32[]{:S(2)}, u32[]{:S(2)}) async-start(bf16[4,32,16,128]{3,2,1,0:T(8,128)(2,1)} %bitcast.27), calls=%async_computation | async-start | bytes 1048576 | tf_op jit(solution)/shard_map/all_to_all | solution.py:68
  12.9 3.2 %collective-permute-start.1 = (bf16[4,9,256]{2,0,1:T(4,128)(2,1)S(1)}, bf16[4,9,256]{2,0,1:T(4,128)(2,1)S(1)}, u32[]{:S(2)}, u32[]{:S(2)}) collective-permute-start(bf16[4,9,256]{2,0,1:T(4,128)(2,1)S(1)} %bitcast.115), channel_id=1, source_target_pairs={{0,1},{1,2},{2,3},{4,5},{5,6},{6,7},{8,9},{9,10},{10,11},{12,13},{... | collective-permute-start | bytes 55304 | tf_op jit(solution)/shard_map/ppermute | solution.py:10
  17.7 0.7 %copy-start.3 = (f32[32]{0:T(128)S(1)}, f32[32]{0:T(128)}, u32[]{:S(2)}) copy-start(f32[32]{0:T(128)} %param.10) | copy-start | bytes 388
  38.8 4.6 %collective-permute-start.2 = (f32[8,109]{1,0:T(8,128)S(1)}, f32[8,109]{1,0:T(8,128)S(1)}, u32[]{:S(2)}, u32[]{:S(2)}) collective-permute-start(f32[8,109]{1,0:T(8,128)S(1)} %fusion.32), channel_id=1, source_target_pairs={{0,16},{4,20},{8,24},{12,28},{16,0},{20,4},{24,8},{28,12},{1,17},{... | collective-permute-start | bytes 10472 | tf_op jit(solution)/shard_map/ppermute | solution.py:20
  43.4 3.6 %collective-permute-start.3 = (f32[8,109]{1,0:T(8,128)S(1)}, f32[8,109]{1,0:T(8,128)S(1)}, u32[]{:S(2)}, u32[]{:S(2)}) collective-permute-start(f32[8,109]{1,0:T(8,128)S(1)} %add.104), channel_id=1, source_target_pairs={{0,8},{4,12},{8,0},{12,4},{16,24},{20,28},{24,16},{28,20},{1,9},{5... | collective-permute-start | bytes 10472 | tf_op jit(solution)/shard_map/ppermute | solution.py:20
  47.0 3.6 %collective-permute-start.4 = (f32[8,109]{1,0:T(8,128)S(1)}, f32[8,109]{1,0:T(8,128)S(1)}, u32[]{:S(2)}, u32[]{:S(2)}) collective-permute-start(f32[8,109]{1,0:T(8,128)S(1)} %add.105), channel_id=1, source_target_pairs={{0,4},{4,0},{8,12},{12,8},{16,20},{20,16},{24,28},{28,24},{1,5},{5... | collective-permute-start | bytes 10472 | tf_op jit(solution)/shard_map/ppermute | solution.py:20
  50.6 0.7 %copy-start.1 = (f32[8,109]{1,0:T(8,128)}, f32[8,109]{1,0:T(8,128)S(1)}, u32[]{:S(2)}) copy-start(f32[8,109]{1,0:T(8,128)S(1)} %add.106) | copy-start | bytes 10468

commit v12 on v8

--- a/solution.py
+++ b/solution.py
@@ -14,11 +14,16 @@
     size = lax.axis_size(axis)
     if size & (size - 1):
         return lax.psum(value, axis)
-    step = 1
-    while step < size:
-        swap = [(i, i ^ step) for i in range(size)]
-        value = value + lax.ppermute(value, axis, swap)
-        step *= 2
+    bits = size.bit_length() - 1
+    while bits:
+        low = max(bits - 2, 0)
+        spans = [(1 << low) * t for t in range(1, 1 << (bits - low))]
+        got = [lax.ppermute(value, axis, [(i, i ^ t) for i in range(size)]) for t in spans]
+        if len(got) == 1:
+            value = value + got[0]
+        else:
+            value = (value + got[0]) + (got[1] + got[2])
+        bits = low
     return value
 
 

time: 47.7 us -> 46.2 us (0.969)
  waiting for transfers between devices: 9.02 us -> 7.66 us
    ppermute x5 -> x7, waiting for transfers between devices: 7.12 us -> 5.76 us  [butterfly_sum(): lax.ppermute(value, axis, [(i, i ^ t) for i in range(size)])]
    ppermute x5 -> x7, starting transfers between devices: 7.93 us -> 7.84 us  [butterfly_sum(): lax.ppermute(value, axis, [(i, i ^ t) for i in range(size)])]
  transfers between devices with their start and end apart: 9 -> 11, of which waited for: 6 -> 5; matrix products, arithmetic and copies ran while one was open for 17% -> 18% of each run, Pallas kernels for 0% -> 0%
where the time goes in v12:
time: 46.2 us; the launch traced here: 45.9 us
  starting transfers between devices  23.6 us (51%)
  waiting for transfers between devices  7.66 us (17%)
  local copies, waits for them, and re-layouts  7.6 us (16%)
  matrix products  5.23 us (11%)
  between operations  0.98 us (2%)
  other arithmetic  0.84 us (2%)
    ppermute x7, starting transfers between devices, butterfly_sum(): lax.ppermute(value, axis, [(i, i ^ t) for i in range(size)])  7.84 us
    ppermute x2, starting transfers between devices, from_behind(): return lax.ppermute(block, axis, route)  7.21 us
    ppermute x7, waiting for transfers between devices, butterfly_sum(): lax.ppermute(value, axis, [(i, i ^ t) for i in range(size)])  5.76 us
    all_to_all x1, starting transfers between devices, local(): lax.all_to_all(stem_local, 'gy', split_axis=0, concat_axis=2, tiled=True)  5.07 us
    all_to_all x1, starting transfers between devices, local(): lax.all_to_all(grad_out, 'gy', split_axis=2, concat_axis=0, tiled=True)  3.47 us
    unnamed x27, local copies, waits for them, and re-layouts  2.99 us
    dot_general x3, matrix products, local(): jnp.einsum('ok,kpqr->opqr', kernel[:, :, off_z], part, preferred_element_...  2.78 us
    dot_general x3, matrix products, local(): jnp.einsum('opqr,kpqr->ok', returned, part, preferred_element_type=jnp.fl...  1.37 us
  transfers between devices with their start and end apart: 11, of which 5 were waited for; matrix products, arithmetic and copies ran while one was open for 18% of the time, Pallas kernels for 0%

profile of v12, /device:TPU:0, one launch (start us, length us, event | category | flops | bytes accessed | tf_op | source)
XLA Modules:
  0.0 45.9 jit_solution(15572663622242711832)
XLA Ops:
  0.6 0.0 copy-start
  0.6 0.0 copy-start.5
  0.7 0.0 copy-start.6
  0.7 0.0 copy-start.3
  0.7 0.9 %slice_bitcast_fusion = bf16[4,32,256]{2,1,0:T(8,128)(2,1)S(1)} fusion(bf16[4,8,32,256]{3,2,1,0:T(8,128)(2,1)} %param.6), kind=kLoop, calls=%fused_computation.43 | loop fusion | bytes 131072 | tf_op jit(solution)/shard_map/squeeze | solution.py:73
  1.6 4.9 %collective-permute-start = (bf16[4,32,256]{2,1,0:T(8,128)(2,1)S(1)}, bf16[4,32,256]{2,1,0:T(8,128)(2,1)S(1)}, u32[]{:S(2)}, u32[]{:S(2)}) collective-permute-start(bf16[4,32,256]{2,1,0:T(8,128)(2,1)S(1)} %slice_bitcast_fusion), channel_id=1, source_target_pairs={{0,4},{4,8},{8,12},{12,16},{16,20},{20,24},{24,28},{1,5},{5,9},{9,... | collective-permute-start | bytes 196616 | tf_op jit(solution)/shard_map/ppermute | solution.py:10
  6.4 2.2 %copy.89 = bf16[8,4,64,128]{3,0,1,2:T(8,128)(2,1)} copy(bf16[8,4,64,128]{3,2,1,0:T(8,128)(2,1)} %param.11) | data formatting | bytes 1048576 | tf_op args[5]
  8.6 3.5 %all-to-all-start.1 = ((bf16[8,4,64,128]{3,0,1,2:T(8,128)(2,1)}), bf16[8,4,64,128]{3,0,1,2:T(8,128)(2,1)S(1)}, u32[]{:S(2)}, u32[]{:S(2)}) async-start(bf16[8,4,64,128]{3,0,1,2:T(8,128)(2,1)} %copy.89), calls=%async_computation.1 | async-start | bytes 1048576 | tf_op jit(solution)/shard_map/all_to_all | solution.py:70
  12.1 0.0 copy-done.5
  12.2 0.0 copy-done.6
  12.2 0.1 fusion.51
  12.3 0.1 fusion.41
  12.4 0.0 copy-done.3
  12.4 0.1 copy.81
  12.6 0.1 fusion.53
  12.7 0.1 broadcast_and_fusion
  12.8 0.1 fusion.55
  12.9 0.0 collective-permute-done
  12.9 0.1 select_select_fusion
  13.1 2.4 %collective-permute-start.1 = (bf16[4,9,256]{2,0,1:T(4,128)(2,1)S(1)}, bf16[4,9,256]{2,0,1:T(4,128)(2,1)S(1)}, u32[]{:S(2)}, u32[]{:S(2)}) collective-permute-start(bf16[4,9,256]{2,0,1:T(4,128)(2,1)S(1)} %bitcast.102), channel_id=1, source_target_pairs={{0,1},{1,2},{2,3},{4,5},{5,6},{6,7},{8,9},{9,10},{10,11},{12,13},{... | collective-permute-start | bytes 55304 | tf_op jit(solution)/shard_map/ppermute | solution.py:10
  15.5 0.1 copy.102
  15.6 0.1 copy.104
  15.7 0.1 copy.106
  15.8 0.5 %collective-permute-done.1 = bf16[4,9,256]{2,0,1:T(4,128)(2,1)S(1)} collective-permute-done((bf16[4,9,256]{2,0,1:T(4,128)(2,1)S(1)}, bf16[4,9,256]{2,0,1:T(4,128)(2,1)S(1)}, u32[]{:S(2)}, u32[]{:S(2)}) %collective-permute-start.1) | collective-permute-done | bytes 18464 | tf_op jit(solution)/shard_map/ppermute | solution.py:10
  16.3 1.1 %convolution_convert_fusion = bf16[4,9,48,384]{3,2,1,0:T(8,128)(2,1)S(1)} fusion(bf16[4,9,32,256]{3,2,1,0:T(8,128)(2,1)S(1)} %select_select_fusion, pred[33]{0:T(512)(128)(4,1)S(1)} %get-tuple-element.7, pred[33]{0:T(512)(128)(4,1)S(1)} %get-tuple-element.6, bf16[4,9,256]{2,1,0:T(8,128)(2,1)S(1)} %copy.78, s32[384]{0:T(512)S(1)} %fusion.45, ...), kind=kOutput, calls=%fused_computation | convolution fusion | flops 279191040 | bytes 1940130 | tf_op jit(solution)/shard_map/cxjy,cxyk->cxjk/dot_general | solution.py:86
  17.7 0.2 copy.79
  17.9 0.0 copy-start.4
  18.0 0.5 %fusion.69 = (bf16[36,4,16,128]{3,2,1,0:T(8,128)(2,1)S(1)}, bf16[36,4,16,128]{3,2,1,0:T(8,128)(2,1)S(1)}, bf16[36,4,16,128]{3,2,1,0:T(8,128)(2,1)S(1)}) fusion(bf16[36,4,16,384]{3,2,1,0:T(8,128)(2,1)S(1)} %bitcast.99), kind=kLoop, calls=%fused_computation.116 | loop fusion | bytes 3538944 | tf_op jit(solution)/shard_map/slice | solution.py:96
  18.5 0.1 copy-done.4
  18.6 0.4 convolution_add_fusion.2
  19.1 0.5 convolution_add_fusion.1
  19.5 1.4 %all-to-all-done.1 = bf16[8,4,64,128]{3,0,1,2:T(8,128)(2,1)S(1)} async-done(((bf16[8,4,64,128]{3,0,1,2:T(8,128)(2,1)}), bf16[8,4,64,128]{3,0,1,2:T(8,128)(2,1)S(1)}, u32[]{:S(2)}, u32[]{:S(2)}) %all-to-all-start.1) | async-done | bytes 524320 | tf_op jit(solution)/shard_map/all_to_all | solution.py:70
  20.9 1.9 %fusion.67 = (f32[32]{0:T(128)S(1)}, bf16[32,4,16,128]{3,0,2,1:T(8,128)(2,1)S(1)}, bf16[32,4,16,128]{3,0,2,1:T(8,128)(2,1)}) fusion(pred[4,16]{1,0:T(4,128)(4,1)S(1)} %broadcast_and_fusion, f32[4,16,128,32]{2,3,1,0:T(8,128)S(1)} %convolution_add_fusion.1, bf16[32,36,1]{1,0,2:T(8,128)(2,1)S(1)} %copy.106, ...), kind=kOutput, calls=%fused_computation.115 | convolution fusion | flops 23592928 | bytes 3213760 | tf_op jit(solution)/shard_map/ok,kpqr->opqr/dot_general | solution.py:97
  22.8 0.5 convolution_bitcast_fusion
  23.2 0.0 copy-start.1
  23.2 0.5 convolution_bitcast_fusion.1
  23.7 0.5 %convolution_bitcast_fusion.2 = f32[32,36,1]{1,0,2:T(8,128)S(1)} fusion(bf16[36,4,16,128]{3,2,1,0:T(8,128)(2,1)S(1)} %get-tuple-element.14, bf16[32,4,16,128]{3,0,2,1:T(8,128)(2,1)S(1)} %get-tuple-element.11), kind=kOutput, calls=%fused_computation.10 | convolution fusion | flops 18874368 | bytes 1118720 | tf_op jit(solution)/shard_map/opqr,kpqr->ok/dot_general | solution.py:110
  24.2 0.1 copy.93
  24.3 0.1 copy.91
  24.4 0.1 copy.92
  24.5 0.1 pad_maximum_fusion.1
  24.6 2.6 %collective-permute-start.3 = (f32[32,109]{1,0:T(8,128)S(1)}, f32[32,109]{1,0:T(8,128)S(1)}, u32[]{:S(2)}, u32[]{:S(2)}) collective-permute-start(f32[32,109]{1,0:T(8,128)S(1)} %pad_maximum_fusion.1), channel_id=1, source_target_pairs={{0,16},{4,20},{8,24},{12,28},{16,0},{20,4},{24,8},{28,12},{1,17},{... | collective-permute-start | bytes 41864 | tf_op jit(solution)/shard_map/ppermute | solution.py:21
  27.2 1.3 %collective-permute-start.4 = (f32[32,109]{1,0:T(8,128)S(1)}, f32[32,109]{1,0:T(8,128)S(1)}, u32[]{:S(2)}, u32[]{:S(2)}) collective-permute-start(f32[32,109]{1,0:T(8,128)S(1)} %pad_maximum_fusion.1), channel_id=1, source_target_pairs={{0,24},{4,28},{8,16},{12,20},{16,8},{20,12},{24,0},{28,4},{1,25},{... | collective-permute-start | bytes 41864 | tf_op jit(solution)/shard_map/ppermute | solution.py:21
  28.5 0.2 collective-permute-start.2
  28.7 0.0 copy-done.1
  28.7 1.0 %copy.87 = bf16[32,4,16,128]{3,2,1,0:T(8,128)(2,1)} copy(bf16[32,4,16,128]{3,0,2,1:T(8,128)(2,1)S(1)} %copy-done.1) | data formatting | bytes 1048576 | tf_op jit(solution)/shard_map/convert_element_type | solution.py:101
  29.7 5.1 %all-to-all-start = ((bf16[32,4,16,128]{3,2,1,0:T(8,128)(2,1)}), bf16[32,4,16,128]{3,2,1,0:T(8,128)(2,1)S(1)}, u32[]{:S(2)}, u32[]{:S(2)}) async-start(bf16[32,4,16,128]{3,2,1,0:T(8,128)(2,1)} %copy.87), calls=%async_computation | async-start | bytes 1048576 | tf_op jit(solution)/shard_map/all_to_all | solution.py:106
  34.8 0.0 collective-permute-done.3
  34.8 0.0 collective-permute-done.4
  34.8 0.0 collective-permute-done.2
  34.8 0.1 add_add_fusion
  34.9 1.3 %collective-permute-start.5 = (f32[32,109]{1,0:T(8,128)S(1)}, f32[32,109]{1,0:T(8,128)S(1)}, u32[]{:S(2)}, u32[]{:S(2)}) collective-permute-start(f32[32,109]{1,0:T(8,128)S(1)} %add_add_fusion), channel_id=1, source_target_pairs={{0,4},{4,0},{8,12},{12,8},{16,20},{20,16},{24,28},{28,24},{1,5},{5... | collective-permute-start | bytes 41864 | tf_op jit(solution)/shard_map/ppermute | solution.py:21
  36.2 2.4 %collective-permute-done.5 = f32[32,109]{1,0:T(8,128)S(1)} collective-permute-done((f32[32,109]{1,0:T(8,128)S(1)}, f32[32,109]{1,0:T(8,128)S(1)}, u32[]{:S(2)}, u32[]{:S(2)}) %collective-permute-start.5) | collective-permute-done | bytes 13984 | tf_op jit(solution)/shard_map/ppermute | solution.py:21
  38.7 0.9 %collective-permute-start.8 = (f32[32,109]{1,0:T(8,128)S(1)}, f32[32,109]{1,0:T(8,128)S(1)}, u32[]{:S(2)}, u32[]{:S(2)}) collective-permute-start(f32[32,109]{1,0:T(8,128)S(1)} %add.115), channel_id=1, source_target_pairs={{0,3},{1,2},{2,1},{3,0},{4,7},{5,6},{6,5},{7,4},{8,11},{9,10},{10,... | collective-permute-start | bytes 41864 | tf_op jit(solution)/shard_map/ppermute | solution.py:21
  39.5 1.4 %collective-permute-start.7 = (f32[32,109]{1,0:T(8,128)S(1)}, f32[32,109]{1,0:T(8,128)S(1)}, u32[]{:S(2)}, u32[]{:S(2)}) collective-permute-start(f32[32,109]{1,0:T(8,128)S(1)} %add.115), channel_id=1, source_target_pairs={{0,2},{1,3},{2,0},{3,1},{4,6},{5,7},{6,4},{7,5},{8,10},{9,11},{10,... | collective-permute-start | bytes 41864 | tf_op jit(solution)/shard_map/ppermute | solution.py:21
  40.9 0.0 collective-permute-start.6
  41.0 2.2 %collective-permute-done.8 = f32[32,109]{1,0:T(8,128)S(1)} collective-permute-done((f32[32,109]{1,0:T(8,128)S(1)}, f32[32,109]{1,0:T(8,128)S(1)}, u32[]{:S(2)}, u32[]{:S(2)}) %collective-permute-start.8) | collective-permute-done | bytes 13984 | tf_op jit(solution)/shard_map/ppermute | solution.py:21
  43.2 1.1 %collective-permute-done.7 = f32[32,109]{1,0:T(8,128)S(1)} collective-permute-done((f32[32,109]{1,0:T(8,128)S(1)}, f32[32,109]{1,0:T(8,128)S(1)}, u32[]{:S(2)}, u32[]{:S(2)}) %collective-permute-start.7) | collective-permute-done | bytes 13984 | tf_op jit(solution)/shard_map/ppermute | solution.py:21
  44.3 0.0 collective-permute-done.6
  44.3 0.0 copy-start.2
  44.3 0.7 %slice_reduce_fusion = f32[8]{0:T(128)} fusion(f32[8,109]{1,0:T(8,128)S(1)} %fusion.35), kind=kLoop, calls=%fused_computation.56 | loop fusion | bytes 64 | tf_op jit(solution)/shard_map/slice | solution.py:117
  45.0 0.0 all-to-all-done
  45.0 0.9 %copy.88 = bf16[8,4,4,16,128]{4,3,2,1,0:T(8,128)(2,1)} copy(bf16[8,4,4,16,128]{4,3,1,0,2:T(8,128)(2,1)S(1)} %bitcast.100) | data formatting | bytes 1048576 | tf_op jit(solution)/shard_map/all_to_all | solution.py:106
  45.9 0.0 copy-done.2
  (26 shorter events, 0.5 us)
Async XLA Ops:
  0.6 12.3 %copy-start = (bf16[4,8,32,256]{3,2,1,0:T(8,128)(2,1)S(1)}, bf16[4,8,32,256]{3,2,1,0:T(8,128)(2,1)}, u32[]{:S(2)}) copy-start(bf16[4,8,32,256]{3,2,1,0:T(8,128)(2,1)} %param.6) | copy-start | bytes 1572868
  0.6 11.5 %copy-start.5 = (s32[4]{0:T(128)S(1)}, s32[4]{0:T(128)}, u32[]{:S(2)}) copy-start(s32[4]{0:T(128)} %param.8) | copy-start | bytes 52
  0.7 11.5 %copy-start.6 = (s32[8]{0:T(128)S(1)}, s32[8]{0:T(128)}, u32[]{:S(2)}) copy-start(s32[8]{0:T(128)} %param.7) | copy-start | bytes 100
  0.7 11.8 %copy-start.3 = (bf16[32,108]{1,0:T(8,128)(2,1)S(1)}, bf16[32,108]{1,0:T(8,128)(2,1)}, u32[]{:S(2)}) copy-start(bf16[32,108]{1,0:T(8,128)(2,1)} %param.9) | copy-start | bytes 20740
  1.6 11.3 %collective-permute-start = (bf16[4,32,256]{2,1,0:T(8,128)(2,1)S(1)}, bf16[4,32,256]{2,1,0:T(8,128)(2,1)S(1)}, u32[]{:S(2)}, u32[]{:S(2)}) collective-permute-start(bf16[4,32,256]{2,1,0:T(8,128)(2,1)S(1)} %slice_bitcast_fusion), channel_id=1, source_target_pairs={{0,4},{4,8},{8,12},{12,16},{16,20},{20,24},{24,28},{1,5},{5,9},{9,... | collective-permute-start | bytes 196616 | tf_op jit(solution)/shard_map/ppermute | solution.py:10
  8.6 12.3 %all-to-all-start.1 = ((bf16[8,4,64,128]{3,0,1,2:T(8,128)(2,1)}), bf16[8,4,64,128]{3,0,1,2:T(8,128)(2,1)S(1)}, u32[]{:S(2)}, u32[]{:S(2)}) async-start(bf16[8,4,64,128]{3,0,1,2:T(8,128)(2,1)} %copy.89), calls=%async_computation.1 | async-start | bytes 1048576 | tf_op jit(solution)/shard_map/all_to_all | solution.py:70
  13.1 3.2 %collective-permute-start.1 = (bf16[4,9,256]{2,0,1:T(4,128)(2,1)S(1)}, bf16[4,9,256]{2,0,1:T(4,128)(2,1)S(1)}, u32[]{:S(2)}, u32[]{:S(2)}) collective-permute-start(bf16[4,9,256]{2,0,1:T(4,128)(2,1)S(1)} %bitcast.102), channel_id=1, source_target_pairs={{0,1},{1,2},{2,3},{4,5},{5,6},{6,7},{8,9},{9,10},{10,11},{12,13},{... | collective-permute-start | bytes 55304 | tf_op jit(solution)/shard_map/ppermute | solution.py:10
  17.9 0.7 %copy-start.4 = (f32[32]{0:T(128)S(1)}, f32[32]{0:T(128)}, u32[]{:S(2)}) copy-start(f32[32]{0:T(128)} %param.10) | copy-start | bytes 388
  23.2 5.5 %copy-start.1 = (bf16[32,4,16,128]{3,0,2,1:T(8,128)(2,1)S(1)}, bf16[32,4,16,128]{3,0,2,1:T(8,128)(2,1)}, u32[]{:S(2)}) copy-start(bf16[32,4,16,128]{3,0,2,1:T(8,128)(2,1)} %get-tuple-element.15) | copy-start | bytes 1572868
  24.6 10.2 %collective-permute-start.3 = (f32[32,109]{1,0:T(8,128)S(1)}, f32[32,109]{1,0:T(8,128)S(1)}, u32[]{:S(2)}, u32[]{:S(2)}) collective-permute-start(f32[32,109]{1,0:T(8,128)S(1)} %pad_maximum_fusion.1), channel_id=1, source_target_pairs={{0,16},{4,20},{8,24},{12,28},{16,0},{20,4},{24,8},{28,12},{1,17},{... | collective-permute-start | bytes 41864 | tf_op jit(solution)/shard_map/ppermute | solution.py:21
  27.2 7.7 %collective-permute-start.4 = (f32[32,109]{1,0:T(8,128)S(1)}, f32[32,109]{1,0:T(8,128)S(1)}, u32[]{:S(2)}, u32[]{:S(2)}) collective-permute-start(f32[32,109]{1,0:T(8,128)S(1)} %pad_maximum_fusion.1), channel_id=1, source_target_pairs={{0,24},{4,28},{8,16},{12,20},{16,8},{20,12},{24,0},{28,4},{1,25},{... | collective-permute-start | bytes 41864 | tf_op jit(solution)/shard_map/ppermute | solution.py:21
  28.5 6.3 %collective-permute-start.2 = (f32[32,109]{1,0:T(8,128)S(1)}, f32[32,109]{1,0:T(8,128)S(1)}, u32[]{:S(2)}, u32[]{:S(2)}) collective-permute-start(f32[32,109]{1,0:T(8,128)S(1)} %pad_maximum_fusion.1), channel_id=1, source_target_pairs={{0,8},{4,12},{8,0},{12,4},{16,24},{20,28},{24,16},{28,20},{1,9},{5... | collective-permute-start | bytes 41864 | tf_op jit(solution)/shard_map/ppermute | solution.py:21
  29.7 15.3 %all-to-all-start = ((bf16[32,4,16,128]{3,2,1,0:T(8,128)(2,1)}), bf16[32,4,16,128]{3,2,1,0:T(8,128)(2,1)S(1)}, u32[]{:S(2)}, u32[]{:S(2)}) async-start(bf16[32,4,16,128]{3,2,1,0:T(8,128)(2,1)} %copy.87), calls=%async_computation | async-start | bytes 1048576 | tf_op jit(solution)/shard_map/all_to_all | solution.py:106
  34.9 3.7 %collective-permute-start.5 = (f32[32,109]{1,0:T(8,128)S(1)}, f32[32,109]{1,0:T(8,128)S(1)}, u32[]{:S(2)}, u32[]{:S(2)}) collective-permute-start(f32[32,109]{1,0:T(8,128)S(1)} %add_add_fusion), channel_id=1, source_target_pairs={{0,4},{4,0},{8,12},{12,8},{16,20},{20,16},{24,28},{28,24},{1,5},{5... | collective-permute-start | bytes 41864 | tf_op jit(solution)/shard_map/ppermute | solution.py:21
  38.7 4.6 %collective-permute-start.8 = (f32[32,109]{1,0:T(8,128)S(1)}, f32[32,109]{1,0:T(8,128)S(1)}, u32[]{:S(2)}, u32[]{:S(2)}) collective-permute-start(f32[32,109]{1,0:T(8,128)S(1)} %add.115), channel_id=1, source_target_pairs={{0,3},{1,2},{2,1},{3,0},{4,7},{5,6},{6,5},{7,4},{8,11},{9,10},{10,... | collective-permute-start | bytes 41864 | tf_op jit(solution)/shard_map/ppermute | solution.py:21
  39.5 4.8 %collective-permute-start.7 = (f32[32,109]{1,0:T(8,128)S(1)}, f32[32,109]{1,0:T(8,128)S(1)}, u32[]{:S(2)}, u32[]{:S(2)}) collective-permute-start(f32[32,109]{1,0:T(8,128)S(1)} %add.115), channel_id=1, source_target_pairs={{0,2},{1,3},{2,0},{3,1},{4,6},{5,7},{6,4},{7,5},{8,10},{9,11},{10,... | collective-permute-start | bytes 41864 | tf_op jit(solution)/shard_map/ppermute | solution.py:21
  40.9 3.4 %collective-permute-start.6 = (f32[32,109]{1,0:T(8,128)S(1)}, f32[32,109]{1,0:T(8,128)S(1)}, u32[]{:S(2)}, u32[]{:S(2)}) collective-permute-start(f32[32,109]{1,0:T(8,128)S(1)} %add.115), channel_id=1, source_target_pairs={{0,1},{1,0},{2,3},{3,2},{4,5},{5,4},{6,7},{7,6},{8,9},{9,8},{10,11... | collective-permute-start | bytes 41864 | tf_op jit(solution)/shard_map/ppermute | solution.py:21
  44.3 1.6 %copy-start.2 = (f32[8,109]{1,0:T(8,128)}, f32[8,109]{1,0:T(8,128)S(1)}, u32[]{:S(2)}) copy-start(f32[8,109]{1,0:T(8,128)S(1)} %fusion.35) | copy-start | bytes 10468

commit v13 on v12

--- a/solution.py
+++ b/solution.py
@@ -16,13 +16,12 @@
         return lax.psum(value, axis)
     bits = size.bit_length() - 1
     while bits:
-        low = max(bits - 2, 0)
+        low = max(bits - 3, 0)
         spans = [(1 << low) * t for t in range(1, 1 << (bits - low))]
-        got = [lax.ppermute(value, axis, [(i, i ^ t) for i in range(size)]) for t in spans]
-        if len(got) == 1:
-            value = value + got[0]
-        else:
-            value = (value + got[0]) + (got[1] + got[2])
+        vals = [value] + [lax.ppermute(value, axis, [(i, i ^ t) for i in range(size)]) for t in spans]
+        while len(vals) > 1:
+            vals = [vals[k] + vals[k + 1] for k in range(0, len(vals), 2)]
+        value = vals[0]
         bits = low
     return value
 

time: 46.2 us -> 53.2 us (1.15)
  starting transfers between devices: 23.6 us -> 29.2 us
  waiting for transfers between devices: 7.66 us -> 8.98 us
    ppermute x7 -> x10, starting transfers between devices: 7.84 us -> 13.5 us  [butterfly_sum(): lax.ppermute(value, axis, [(i, i ^ t) for i in range(size)])]
    ppermute x7 -> x10, waiting for transfers between devices: 5.76 us -> 7.07 us  [butterfly_sum(): lax.ppermute(value, axis, [(i, i ^ t) for i in range(size)])]
  transfers between devices with their start and end apart: 11 -> 14, of which waited for: 5 -> 4; matrix products, arithmetic and copies ran while one was open for 18% -> 15% of each run, Pallas kernels for 0% -> 0%
where the time goes in v13:
time: 53.2 us; the launch traced here: 52.9 us
  starting transfers between devices  29.2 us (55%)
  waiting for transfers between devices  8.98 us (17%)
  local copies, waits for them, and re-layouts  7.6 us (14%)
  matrix products  5.23 us (10%)
  between operations  1 us (2%)
  other arithmetic  0.84 us (2%)
    ppermute x10, starting transfers between devices, butterfly_sum(): lax.ppermute(value, axis, [(i, i ^ t) for i in range(size)])  13.5 us
    ppermute x2, starting transfers between devices, from_behind(): return lax.ppermute(block, axis, route)  7.21 us
    ppermute x10, waiting for transfers between devices, butterfly_sum(): lax.ppermute(value, axis, [(i, i ^ t) for i in range(size)])  7.07 us
    all_to_all x1, starting transfers between devices, local(): lax.all_to_all(stem_local, 'gy', split_axis=0, concat_axis=2, tiled=True)  5.07 us
    all_to_all x1, starting transfers between devices, local(): lax.all_to_all(grad_out, 'gy', split_axis=2, concat_axis=0, tiled=True)  3.47 us
    unnamed x27, local copies, waits for them, and re-layouts  2.99 us
    dot_general x3, matrix products, local(): jnp.einsum('ok,kpqr->opqr', kernel[:, :, off_z], part, preferred_element_...  2.78 us
    dot_general x3, matrix products, local(): jnp.einsum('opqr,kpqr->ok', returned, part, preferred_element_type=jnp.fl...  1.37 us
  transfers between devices with their start and end apart: 14, of which 4 were waited for; matrix products, arithmetic and copies ran while one was open for 15% of the time, Pallas kernels for 0%

profile of v13, /device:TPU:0, one launch (start us, length us, event | category | flops | bytes accessed | tf_op | source)
XLA Modules:
  0.0 52.9 jit_solution(8396129027970953828)
XLA Ops:
  0.6 0.0 copy-start
  0.6 0.0 copy-start.5
  0.7 0.9 %slice_bitcast_fusion = bf16[4,32,256]{2,1,0:T(8,128)(2,1)S(1)} fusion(bf16[4,8,32,256]{3,2,1,0:T(8,128)(2,1)} %param.6), kind=kLoop, calls=%fused_computation.43 | loop fusion | bytes 131072 | tf_op jit(solution)/shard_map/squeeze | solution.py:72
  1.6 4.9 %collective-permute-start = (bf16[4,32,256]{2,1,0:T(8,128)(2,1)S(1)}, bf16[4,32,256]{2,1,0:T(8,128)(2,1)S(1)}, u32[]{:S(2)}, u32[]{:S(2)}) collective-permute-start(bf16[4,32,256]{2,1,0:T(8,128)(2,1)S(1)} %slice_bitcast_fusion), channel_id=1, source_target_pairs={{0,4},{4,8},{8,12},{12,16},{16,20},{20,24},{24,28},{1,5},{5,9},{9,... | collective-permute-start | bytes 196616 | tf_op jit(solution)/shard_map/ppermute | solution.py:10
  6.4 2.2 %copy.89 = bf16[8,4,64,128]{3,0,1,2:T(8,128)(2,1)} copy(bf16[8,4,64,128]{3,2,1,0:T(8,128)(2,1)} %param.11) | data formatting | bytes 1048576 | tf_op args[5]
  8.6 3.5 %all-to-all-start.1 = ((bf16[8,4,64,128]{3,0,1,2:T(8,128)(2,1)}), bf16[8,4,64,128]{3,0,1,2:T(8,128)(2,1)S(1)}, u32[]{:S(2)}, u32[]{:S(2)}) async-start(bf16[8,4,64,128]{3,0,1,2:T(8,128)(2,1)} %copy.89), calls=%async_computation.1 | async-start | bytes 1048576 | tf_op jit(solution)/shard_map/all_to_all | solution.py:69
  12.2 0.1 fusion.51
  12.3 0.1 fusion.41
  12.4 0.1 copy.81
  12.6 0.1 fusion.53
  12.7 0.1 broadcast_and_fusion
  12.8 0.1 fusion.55
  12.9 0.0 collective-permute-done
  12.9 0.0 copy-done
  12.9 0.1 select_select_fusion
  13.1 2.4 %collective-permute-start.1 = (bf16[4,9,256]{2,0,1:T(4,128)(2,1)S(1)}, bf16[4,9,256]{2,0,1:T(4,128)(2,1)S(1)}, u32[]{:S(2)}, u32[]{:S(2)}) collective-permute-start(bf16[4,9,256]{2,0,1:T(4,128)(2,1)S(1)} %bitcast.102), channel_id=1, source_target_pairs={{0,1},{1,2},{2,3},{4,5},{5,6},{6,7},{8,9},{9,10},{10,11},{12,13},{... | collective-permute-start | bytes 55304 | tf_op jit(solution)/shard_map/ppermute | solution.py:10
  15.5 0.1 copy.102
  15.6 0.1 copy.104
  15.7 0.1 copy.106
  15.8 0.5 %collective-permute-done.1 = bf16[4,9,256]{2,0,1:T(4,128)(2,1)S(1)} collective-permute-done((bf16[4,9,256]{2,0,1:T(4,128)(2,1)S(1)}, bf16[4,9,256]{2,0,1:T(4,128)(2,1)S(1)}, u32[]{:S(2)}, u32[]{:S(2)}) %collective-permute-start.1) | collective-permute-done | bytes 18464 | tf_op jit(solution)/shard_map/ppermute | solution.py:10
  16.3 1.1 %convolution_convert_fusion = bf16[4,9,48,384]{3,2,1,0:T(8,128)(2,1)S(1)} fusion(bf16[4,9,32,256]{3,2,1,0:T(8,128)(2,1)S(1)} %select_select_fusion, pred[33]{0:T(512)(128)(4,1)S(1)} %get-tuple-element.7, pred[33]{0:T(512)(128)(4,1)S(1)} %get-tuple-element.6, bf16[4,9,256]{2,1,0:T(8,128)(2,1)S(1)} %copy.78, s32[384]{0:T(512)S(1)} %fusion.45, ...), kind=kOutput, calls=%fused_computation | convolution fusion | flops 279191040 | bytes 1940130 | tf_op jit(solution)/shard_map/cxjy,cxyk->cxjk/dot_general | solution.py:85
  17.7 0.2 copy.79
  17.9 0.0 copy-start.4
  18.0 0.5 fusion.69
  18.5 0.1 copy-done.4
  18.6 0.4 convolution_add_fusion.2
  19.1 0.5 convolution_add_fusion.1
  19.5 1.4 %all-to-all-done.1 = bf16[8,4,64,128]{3,0,1,2:T(8,128)(2,1)S(1)} async-done(((bf16[8,4,64,128]{3,0,1,2:T(8,128)(2,1)}), bf16[8,4,64,128]{3,0,1,2:T(8,128)(2,1)S(1)}, u32[]{:S(2)}, u32[]{:S(2)}) %all-to-all-start.1) | async-done | bytes 524320 | tf_op jit(solution)/shard_map/all_to_all | solution.py:69
  20.9 1.9 %fusion.67 = (f32[32]{0:T(128)S(1)}, bf16[32,4,16,128]{3,0,2,1:T(8,128)(2,1)S(1)}, bf16[32,4,16,128]{3,0,2,1:T(8,128)(2,1)}) fusion(pred[4,16]{1,0:T(4,128)(4,1)S(1)} %broadcast_and_fusion, f32[4,16,128,32]{2,3,1,0:T(8,128)S(1)} %convolution_add_fusion.1, bf16[32,36,1]{1,0,2:T(8,128)(2,1)S(1)} %copy.106, ...), kind=kOutput, calls=%fused_computation.115 | convolution fusion | flops 23592928 | bytes 3213760 | tf_op jit(solution)/shard_map/ok,kpqr->opqr/dot_general | solution.py:96
  22.8 0.5 convolution_bitcast_fusion
  23.2 0.0 copy-start.1
  23.2 0.5 convolution_bitcast_fusion.1
  23.7 0.5 convolution_bitcast_fusion.2
  24.2 0.1 copy.93
  24.3 0.1 copy.91
  24.4 0.1 copy.92
  24.5 0.1 pad_maximum_fusion.1
  24.6 3.6 %collective-permute-start.7 = (f32[32,109]{1,0:T(8,128)S(1)}, f32[32,109]{1,0:T(8,128)S(1)}, u32[]{:S(2)}, u32[]{:S(2)}) collective-permute-start(f32[32,109]{1,0:T(8,128)S(1)} %pad_maximum_fusion.1), channel_id=1, source_target_pairs={{0,24},{4,28},{8,16},{12,20},{16,8},{20,12},{24,0},{28,4},{1,25},{... | collective-permute-start | bytes 41864 | tf_op jit(solution)/shard_map/ppermute | solution.py:21
  28.2 1.2 %collective-permute-start.8 = (f32[32,109]{1,0:T(8,128)S(1)}, f32[32,109]{1,0:T(8,128)S(1)}, u32[]{:S(2)}, u32[]{:S(2)}) collective-permute-start(f32[32,109]{1,0:T(8,128)S(1)} %pad_maximum_fusion.1), channel_id=1, source_target_pairs={{0,28},{4,24},{8,20},{12,16},{16,12},{20,8},{24,4},{28,0},{1,29},{... | collective-permute-start | bytes 41864 | tf_op jit(solution)/shard_map/ppermute | solution.py:21
  29.4 0.8 %collective-permute-start.5 = (f32[32,109]{1,0:T(8,128)S(1)}, f32[32,109]{1,0:T(8,128)S(1)}, u32[]{:S(2)}, u32[]{:S(2)}) collective-permute-start(f32[32,109]{1,0:T(8,128)S(1)} %pad_maximum_fusion.1), channel_id=1, source_target_pairs={{0,16},{4,20},{8,24},{12,28},{16,0},{20,4},{24,8},{28,12},{1,17},{... | collective-permute-start | bytes 41864 | tf_op jit(solution)/shard_map/ppermute | solution.py:21
  30.2 2.0 %collective-permute-start.6 = (f32[32,109]{1,0:T(8,128)S(1)}, f32[32,109]{1,0:T(8,128)S(1)}, u32[]{:S(2)}, u32[]{:S(2)}) collective-permute-start(f32[32,109]{1,0:T(8,128)S(1)} %pad_maximum_fusion.1), channel_id=1, source_target_pairs={{0,20},{4,16},{8,28},{12,24},{16,4},{20,0},{24,12},{28,8},{1,21},{... | collective-permute-start | bytes 41864 | tf_op jit(solution)/shard_map/ppermute | solution.py:21
  32.2 1.2 %collective-permute-start.3 = (f32[32,109]{1,0:T(8,128)S(1)}, f32[32,109]{1,0:T(8,128)S(1)}, u32[]{:S(2)}, u32[]{:S(2)}) collective-permute-start(f32[32,109]{1,0:T(8,128)S(1)} %pad_maximum_fusion.1), channel_id=1, source_target_pairs={{0,8},{4,12},{8,0},{12,4},{16,24},{20,28},{24,16},{28,20},{1,9},{5... | collective-permute-start | bytes 41864 | tf_op jit(solution)/shard_map/ppermute | solution.py:21
  33.5 0.0 collective-permute-done.7
  33.5 1.8 %collective-permute-start.4 = (f32[32,109]{1,0:T(8,128)S(1)}, f32[32,109]{1,0:T(8,128)S(1)}, u32[]{:S(2)}, u32[]{:S(2)}) collective-permute-start(f32[32,109]{1,0:T(8,128)S(1)} %pad_maximum_fusion.1), channel_id=1, source_target_pairs={{0,12},{4,8},{8,4},{12,0},{16,28},{20,24},{24,20},{28,16},{1,13},{... | collective-permute-start | bytes 41864 | tf_op jit(solution)/shard_map/ppermute | solution.py:21
  35.2 0.0 collective-permute-done.8
  35.2 0.5 collective-permute-start.2
  35.7 1.0 %copy.87 = bf16[32,4,16,128]{3,2,1,0:T(8,128)(2,1)} copy(bf16[32,4,16,128]{3,0,2,1:T(8,128)(2,1)S(1)} %copy-done.1) | data formatting | bytes 1048576 | tf_op jit(solution)/shard_map/convert_element_type | solution.py:100
  36.7 5.1 %all-to-all-start = ((bf16[32,4,16,128]{3,2,1,0:T(8,128)(2,1)}), bf16[32,4,16,128]{3,2,1,0:T(8,128)(2,1)S(1)}, u32[]{:S(2)}, u32[]{:S(2)}) async-start(bf16[32,4,16,128]{3,2,1,0:T(8,128)(2,1)} %copy.87), calls=%async_computation | async-start | bytes 1048576 | tf_op jit(solution)/shard_map/all_to_all | solution.py:105
  41.8 0.0 collective-permute-done.5
  41.8 0.0 collective-permute-done.6
  41.8 0.0 collective-permute-done.3
  41.8 0.0 collective-permute-done.4
  41.8 0.0 collective-permute-done.2
  41.8 0.1 add_add_fusion
  41.9 1.7 %collective-permute-start.11 = (f32[32,109]{1,0:T(8,128)S(1)}, f32[32,109]{1,0:T(8,128)S(1)}, u32[]{:S(2)}, u32[]{:S(2)}) collective-permute-start(f32[32,109]{1,0:T(8,128)S(1)} %add_add_fusion), channel_id=1, source_target_pairs={{0,3},{1,2},{2,1},{3,0},{4,7},{5,6},{6,5},{7,4},{8,11},{9,10},{10,... | collective-permute-start | bytes 41864 | tf_op jit(solution)/shard_map/ppermute | solution.py:21
  43.7 0.6 %collective-permute-start.10 = (f32[32,109]{1,0:T(8,128)S(1)}, f32[32,109]{1,0:T(8,128)S(1)}, u32[]{:S(2)}, u32[]{:S(2)}) collective-permute-start(f32[32,109]{1,0:T(8,128)S(1)} %add_add_fusion), channel_id=1, source_target_pairs={{0,2},{1,3},{2,0},{3,1},{4,6},{5,7},{6,4},{7,5},{8,10},{9,11},{10,... | collective-permute-start | bytes 41864 | tf_op jit(solution)/shard_map/ppermute | solution.py:21
  44.2 0.0 collective-permute-start.9
  44.2 6.0 %collective-permute-done.11 = f32[32,109]{1,0:T(8,128)S(1)} collective-permute-done((f32[32,109]{1,0:T(8,128)S(1)}, f32[32,109]{1,0:T(8,128)S(1)}, u32[]{:S(2)}, u32[]{:S(2)}) %collective-permute-start.11) | collective-permute-done | bytes 13984 | tf_op jit(solution)/shard_map/ppermute | solution.py:21
  50.2 1.1 %collective-permute-done.10 = f32[32,109]{1,0:T(8,128)S(1)} collective-permute-done((f32[32,109]{1,0:T(8,128)S(1)}, f32[32,109]{1,0:T(8,128)S(1)}, u32[]{:S(2)}, u32[]{:S(2)}) %collective-permute-start.10) | collective-permute-done | bytes 13984 | tf_op jit(solution)/shard_map/ppermute | solution.py:21
  51.3 0.0 collective-permute-done.9
  51.3 0.0 copy-start.2
  51.3 0.7 %slice_reduce_fusion = f32[8]{0:T(128)} fusion(f32[8,109]{1,0:T(8,128)S(1)} %fusion.35), kind=kLoop, calls=%fused_computation.56 | loop fusion | bytes 64 | tf_op jit(solution)/shard_map/slice | solution.py:116
  52.0 0.0 all-to-all-done
  52.0 0.9 %copy.88 = bf16[8,4,4,16,128]{4,3,2,1,0:T(8,128)(2,1)} copy(bf16[8,4,4,16,128]{4,3,1,0,2:T(8,128)(2,1)S(1)} %bitcast.100) | data formatting | bytes 1048576 | tf_op jit(solution)/shard_map/all_to_all | solution.py:105
  (31 shorter events, 0.5 us)
Async XLA Ops:
  0.6 12.3 %copy-start = (bf16[4,8,32,256]{3,2,1,0:T(8,128)(2,1)S(1)}, bf16[4,8,32,256]{3,2,1,0:T(8,128)(2,1)}, u32[]{:S(2)}) copy-start(bf16[4,8,32,256]{3,2,1,0:T(8,128)(2,1)} %param.6) | copy-start | bytes 1572868
  0.6 11.5 %copy-start.5 = (s32[4]{0:T(128)S(1)}, s32[4]{0:T(128)}, u32[]{:S(2)}) copy-start(s32[4]{0:T(128)} %param.8) | copy-start | bytes 52
  0.7 11.5 %copy-start.6 = (s32[8]{0:T(128)S(1)}, s32[8]{0:T(128)}, u32[]{:S(2)}) copy-start(s32[8]{0:T(128)} %param.7) | copy-start | bytes 100
  0.7 11.8 %copy-start.3 = (bf16[32,108]{1,0:T(8,128)(2,1)S(1)}, bf16[32,108]{1,0:T(8,128)(2,1)}, u32[]{:S(2)}) copy-start(bf16[32,108]{1,0:T(8,128)(2,1)} %param.9) | copy-start | bytes 20740
  1.6 11.3 %collective-permute-start = (bf16[4,32,256]{2,1,0:T(8,128)(2,1)S(1)}, bf16[4,32,256]{2,1,0:T(8,128)(2,1)S(1)}, u32[]{:S(2)}, u32[]{:S(2)}) collective-permute-start(bf16[4,32,256]{2,1,0:T(8,128)(2,1)S(1)} %slice_bitcast_fusion), channel_id=1, source_target_pairs={{0,4},{4,8},{8,12},{12,16},{16,20},{20,24},{24,28},{1,5},{5,9},{9,... | collective-permute-start | bytes 196616 | tf_op jit(solution)/shard_map/ppermute | solution.py:10
  8.6 12.3 %all-to-all-start.1 = ((bf16[8,4,64,128]{3,0,1,2:T(8,128)(2,1)}), bf16[8,4,64,128]{3,0,1,2:T(8,128)(2,1)S(1)}, u32[]{:S(2)}, u32[]{:S(2)}) async-start(bf16[8,4,64,128]{3,0,1,2:T(8,128)(2,1)} %copy.89), calls=%async_computation.1 | async-start | bytes 1048576 | tf_op jit(solution)/shard_map/all_to_all | solution.py:69
  13.1 3.2 %collective-permute-start.1 = (bf16[4,9,256]{2,0,1:T(4,128)(2,1)S(1)}, bf16[4,9,256]{2,0,1:T(4,128)(2,1)S(1)}, u32[]{:S(2)}, u32[]{:S(2)}) collective-permute-start(bf16[4,9,256]{2,0,1:T(4,128)(2,1)S(1)} %bitcast.102), channel_id=1, source_target_pairs={{0,1},{1,2},{2,3},{4,5},{5,6},{6,7},{8,9},{9,10},{10,11},{12,13},{... | collective-permute-start | bytes 55304 | tf_op jit(solution)/shard_map/ppermute | solution.py:10
  17.9 0.7 %copy-start.4 = (f32[32]{0:T(128)S(1)}, f32[32]{0:T(128)}, u32[]{:S(2)}) copy-start(f32[32]{0:T(128)} %param.10) | copy-start | bytes 388
  23.2 12.5 %copy-start.1 = (bf16[32,4,16,128]{3,0,2,1:T(8,128)(2,1)S(1)}, bf16[32,4,16,128]{3,0,2,1:T(8,128)(2,1)}, u32[]{:S(2)}) copy-start(bf16[32,4,16,128]{3,0,2,1:T(8,128)(2,1)} %get-tuple-element.15) | copy-start | bytes 1572868
  24.6 8.9 %collective-permute-start.7 = (f32[32,109]{1,0:T(8,128)S(1)}, f32[32,109]{1,0:T(8,128)S(1)}, u32[]{:S(2)}, u32[]{:S(2)}) collective-permute-start(f32[32,109]{1,0:T(8,128)S(1)} %pad_maximum_fusion.1), channel_id=1, source_target_pairs={{0,24},{4,28},{8,16},{12,20},{16,8},{20,12},{24,0},{28,4},{1,25},{... | collective-permute-start | bytes 41864 | tf_op jit(solution)/shard_map/ppermute | solution.py:21
  28.2 7.1 %collective-permute-start.8 = (f32[32,109]{1,0:T(8,128)S(1)}, f32[32,109]{1,0:T(8,128)S(1)}, u32[]{:S(2)}, u32[]{:S(2)}) collective-permute-start(f32[32,109]{1,0:T(8,128)S(1)} %pad_maximum_fusion.1), channel_id=1, source_target_pairs={{0,28},{4,24},{8,20},{12,16},{16,12},{20,8},{24,4},{28,0},{1,29},{... | collective-permute-start | bytes 41864 | tf_op jit(solution)/shard_map/ppermute | solution.py:21
  29.4 12.4 %collective-permute-start.5 = (f32[32,109]{1,0:T(8,128)S(1)}, f32[32,109]{1,0:T(8,128)S(1)}, u32[]{:S(2)}, u32[]{:S(2)}) collective-permute-start(f32[32,109]{1,0:T(8,128)S(1)} %pad_maximum_fusion.1), channel_id=1, source_target_pairs={{0,16},{4,20},{8,24},{12,28},{16,0},{20,4},{24,8},{28,12},{1,17},{... | collective-permute-start | bytes 41864 | tf_op jit(solution)/shard_map/ppermute | solution.py:21
  30.2 11.6 %collective-permute-start.6 = (f32[32,109]{1,0:T(8,128)S(1)}, f32[32,109]{1,0:T(8,128)S(1)}, u32[]{:S(2)}, u32[]{:S(2)}) collective-permute-start(f32[32,109]{1,0:T(8,128)S(1)} %pad_maximum_fusion.1), channel_id=1, source_target_pairs={{0,20},{4,16},{8,28},{12,24},{16,4},{20,0},{24,12},{28,8},{1,21},{... | collective-permute-start | bytes 41864 | tf_op jit(solution)/shard_map/ppermute | solution.py:21
  32.2 9.6 %collective-permute-start.3 = (f32[32,109]{1,0:T(8,128)S(1)}, f32[32,109]{1,0:T(8,128)S(1)}, u32[]{:S(2)}, u32[]{:S(2)}) collective-permute-start(f32[32,109]{1,0:T(8,128)S(1)} %pad_maximum_fusion.1), channel_id=1, source_target_pairs={{0,8},{4,12},{8,0},{12,4},{16,24},{20,28},{24,16},{28,20},{1,9},{5... | collective-permute-start | bytes 41864 | tf_op jit(solution)/shard_map/ppermute | solution.py:21
  33.5 8.3 %collective-permute-start.4 = (f32[32,109]{1,0:T(8,128)S(1)}, f32[32,109]{1,0:T(8,128)S(1)}, u32[]{:S(2)}, u32[]{:S(2)}) collective-permute-start(f32[32,109]{1,0:T(8,128)S(1)} %pad_maximum_fusion.1), channel_id=1, source_target_pairs={{0,12},{4,8},{8,4},{12,0},{16,28},{20,24},{24,20},{28,16},{1,13},{... | collective-permute-start | bytes 41864 | tf_op jit(solution)/shard_map/ppermute | solution.py:21
  35.2 6.6 %collective-permute-start.2 = (f32[32,109]{1,0:T(8,128)S(1)}, f32[32,109]{1,0:T(8,128)S(1)}, u32[]{:S(2)}, u32[]{:S(2)}) collective-permute-start(f32[32,109]{1,0:T(8,128)S(1)} %pad_maximum_fusion.1), channel_id=1, source_target_pairs={{0,4},{4,0},{8,12},{12,8},{16,20},{20,16},{24,28},{28,24},{1,5},{5... | collective-permute-start | bytes 41864 | tf_op jit(solution)/shard_map/ppermute | solution.py:21
  36.7 15.3 %all-to-all-start = ((bf16[32,4,16,128]{3,2,1,0:T(8,128)(2,1)}), bf16[32,4,16,128]{3,2,1,0:T(8,128)(2,1)S(1)}, u32[]{:S(2)}, u32[]{:S(2)}) async-start(bf16[32,4,16,128]{3,2,1,0:T(8,128)(2,1)} %copy.87), calls=%async_computation | async-start | bytes 1048576 | tf_op jit(solution)/shard_map/all_to_all | solution.py:105
  41.9 8.3 %collective-permute-start.11 = (f32[32,109]{1,0:T(8,128)S(1)}, f32[32,109]{1,0:T(8,128)S(1)}, u32[]{:S(2)}, u32[]{:S(2)}) collective-permute-start(f32[32,109]{1,0:T(8,128)S(1)} %add_add_fusion), channel_id=1, source_target_pairs={{0,3},{1,2},{2,1},{3,0},{4,7},{5,6},{6,5},{7,4},{8,11},{9,10},{10,... | collective-permute-start | bytes 41864 | tf_op jit(solution)/shard_map/ppermute | solution.py:21
  43.7 7.6 %collective-permute-start.10 = (f32[32,109]{1,0:T(8,128)S(1)}, f32[32,109]{1,0:T(8,128)S(1)}, u32[]{:S(2)}, u32[]{:S(2)}) collective-permute-start(f32[32,109]{1,0:T(8,128)S(1)} %add_add_fusion), channel_id=1, source_target_pairs={{0,2},{1,3},{2,0},{3,1},{4,6},{5,7},{6,4},{7,5},{8,10},{9,11},{10,... | collective-permute-start | bytes 41864 | tf_op jit(solution)/shard_map/ppermute | solution.py:21
  44.2 7.1 %collective-permute-start.9 = (f32[32,109]{1,0:T(8,128)S(1)}, f32[32,109]{1,0:T(8,128)S(1)}, u32[]{:S(2)}, u32[]{:S(2)}) collective-permute-start(f32[32,109]{1,0:T(8,128)S(1)} %add_add_fusion), channel_id=1, source_target_pairs={{0,1},{1,0},{2,3},{3,2},{4,5},{5,4},{6,7},{7,6},{8,9},{9,8},{10,11... | collective-permute-start | bytes 41864 | tf_op jit(solution)/shard_map/ppermute | solution.py:21
  51.3 1.6 %copy-start.2 = (f32[8,109]{1,0:T(8,128)}, f32[8,109]{1,0:T(8,128)S(1)}, u32[]{:S(2)}) copy-start(f32[8,109]{1,0:T(8,128)S(1)} %fusion.35) | copy-start | bytes 10468

commit v14 on v12

--- a/solution.py
+++ b/solution.py
@@ -111,7 +111,7 @@
     weight_full = jnp.stack(grads, axis=-1).reshape(out_chans, -1)
     bias_full = jnp.sum(grad_wide, axis=(1, 2, 3))
     packed = jnp.concatenate([weight_full, bias_full[:, None]], axis=1)
-    total = butterfly_sum(butterfly_sum(packed, "gx"), "gy")
+    total = butterfly_sum(butterfly_sum(packed, "gy"), "gx")
     share = out_chans // tiles_y
     mine = lax.dynamic_slice_in_dim(total, lax.axis_index("gy") * share, share, 0)
     weight_grad, bias_grad = mine[:, :-1], mine[:, -1]

time: 46.2 us -> 50.2 us (1.087)
  waiting for transfers between devices: 7.66 us -> 11.5 us
    all_to_all x1, waiting for transfers between devices: 0.01 us -> 4.23 us  [local(): lax.all_to_all(stem_local, 'gy', split_axis=0, concat_axis=2, tiled=True)]
    ppermute x7, starting transfers between devices: 7.84 us -> 9.56 us  [butterfly_sum(): lax.ppermute(value, axis, [(i, i ^ t) for i in range(size)])]
    all_to_all x1, starting transfers between devices: 5.07 us -> 3.47 us  [local(): lax.all_to_all(stem_local, 'gy', split_axis=0, concat_axis=2, tiled=True)]
  transfers between devices with their start and end apart: 11 -> 11, of which waited for: 5 -> 6; matrix products, arithmetic and copies ran while one was open for 18% -> 16% of each run, Pallas kernels for 0% -> 0%
where the time goes in v14:
time: 50.2 us; the launch traced here: 49.9 us
  starting transfers between devices  23.7 us (47%)
  waiting for transfers between devices  11.5 us (23%)
  local copies, waits for them, and re-layouts  7.6 us (15%)
  matrix products  5.23 us (10%)
  between operations  1 us (2%)
  other arithmetic  0.84 us (2%)
    ppermute x7, starting transfers between devices, butterfly_sum(): lax.ppermute(value, axis, [(i, i ^ t) for i in range(size)])  9.56 us
    ppermute x2, starting transfers between devices, from_behind(): return lax.ppermute(block, axis, route)  7.21 us
    ppermute x7, waiting for transfers between devices, butterfly_sum(): lax.ppermute(value, axis, [(i, i ^ t) for i in range(size)])  5.4 us
    all_to_all x1, waiting for transfers between devices, local(): lax.all_to_all(stem_local, 'gy', split_axis=0, concat_axis=2, tiled=True)  4.23 us
    all_to_all x1, starting transfers between devices, local(): lax.all_to_all(grad_out, 'gy', split_axis=2, concat_axis=0, tiled=True)  3.47 us
    all_to_all x1, starting transfers between devices, local(): lax.all_to_all(stem_local, 'gy', split_axis=0, concat_axis=2, tiled=True)  3.47 us
    unnamed x27, local copies, waits for them, and re-layouts  2.98 us
    dot_general x3, matrix products, local(): jnp.einsum('ok,kpqr->opqr', kernel[:, :, off_z], part, preferred_element_...  2.78 us
  transfers between devices with their start and end apart: 11, of which 6 were waited for; matrix products, arithmetic and copies ran while one was open for 16% of the time, Pallas kernels for 0%

profile of v14, /device:TPU:0, one launch (start us, length us, event | category | flops | bytes accessed | tf_op | source)
XLA Modules:
  0.0 49.9 jit_solution(14878217840909026422)
XLA Ops:
  0.6 0.0 copy-start
  0.6 0.0 copy-start.5
  0.7 0.0 copy-start.6
  0.7 0.0 copy-start.3
  0.7 0.9 %slice_bitcast_fusion = bf16[4,32,256]{2,1,0:T(8,128)(2,1)S(1)} fusion(bf16[4,8,32,256]{3,2,1,0:T(8,128)(2,1)} %param.6), kind=kLoop, calls=%fused_computation.43 | loop fusion | bytes 131072 | tf_op jit(solution)/shard_map/squeeze | solution.py:73
  1.6 4.9 %collective-permute-start = (bf16[4,32,256]{2,1,0:T(8,128)(2,1)S(1)}, bf16[4,32,256]{2,1,0:T(8,128)(2,1)S(1)}, u32[]{:S(2)}, u32[]{:S(2)}) collective-permute-start(bf16[4,32,256]{2,1,0:T(8,128)(2,1)S(1)} %slice_bitcast_fusion), channel_id=1, source_target_pairs={{0,4},{4,8},{8,12},{12,16},{16,20},{20,24},{24,28},{1,5},{5,9},{9,... | collective-permute-start | bytes 196616 | tf_op jit(solution)/shard_map/ppermute | solution.py:10
  6.4 2.2 %copy.89 = bf16[8,4,64,128]{3,0,1,2:T(8,128)(2,1)} copy(bf16[8,4,64,128]{3,2,1,0:T(8,128)(2,1)} %param.11) | data formatting | bytes 1048576 | tf_op args[5]
  8.6 3.5 %all-to-all-start.1 = ((bf16[8,4,64,128]{3,0,1,2:T(8,128)(2,1)}), bf16[8,4,64,128]{3,0,1,2:T(8,128)(2,1)S(1)}, u32[]{:S(2)}, u32[]{:S(2)}) async-start(bf16[8,4,64,128]{3,0,1,2:T(8,128)(2,1)} %copy.89), calls=%async_computation.1 | async-start | bytes 1048576 | tf_op jit(solution)/shard_map/all_to_all | solution.py:70
  12.1 0.0 copy-done.5
  12.2 0.0 copy-done.6
  12.2 0.1 fusion.50
  12.3 0.1 fusion.40
  12.4 0.0 copy-done.3
  12.4 0.1 copy.81
  12.6 0.1 fusion.52
  12.7 0.1 broadcast_and_fusion
  12.8 0.1 fusion.54
  12.9 0.0 collective-permute-done
  12.9 0.0 copy-done
  12.9 0.1 select_select_fusion
  13.1 2.4 %collective-permute-start.1 = (bf16[4,9,256]{2,0,1:T(4,128)(2,1)S(1)}, bf16[4,9,256]{2,0,1:T(4,128)(2,1)S(1)}, u32[]{:S(2)}, u32[]{:S(2)}) collective-permute-start(bf16[4,9,256]{2,0,1:T(4,128)(2,1)S(1)} %bitcast.102), channel_id=1, source_target_pairs={{0,1},{1,2},{2,3},{4,5},{5,6},{6,7},{8,9},{9,10},{10,11},{12,13},{... | collective-permute-start | bytes 55304 | tf_op jit(solution)/shard_map/ppermute | solution.py:10
  15.5 0.1 copy.102
  15.6 0.1 copy.104
  15.7 0.1 copy.106
  15.8 0.5 %collective-permute-done.1 = bf16[4,9,256]{2,0,1:T(4,128)(2,1)S(1)} collective-permute-done((bf16[4,9,256]{2,0,1:T(4,128)(2,1)S(1)}, bf16[4,9,256]{2,0,1:T(4,128)(2,1)S(1)}, u32[]{:S(2)}, u32[]{:S(2)}) %collective-permute-start.1) | collective-permute-done | bytes 18464 | tf_op jit(solution)/shard_map/ppermute | solution.py:10
  16.3 1.1 %convolution_convert_fusion = bf16[4,9,48,384]{3,2,1,0:T(8,128)(2,1)S(1)} fusion(bf16[4,9,32,256]{3,2,1,0:T(8,128)(2,1)S(1)} %select_select_fusion, pred[33]{0:T(512)(128)(4,1)S(1)} %get-tuple-element.7, pred[33]{0:T(512)(128)(4,1)S(1)} %get-tuple-element.6, bf16[4,9,256]{2,1,0:T(8,128)(2,1)S(1)} %copy.78, s32[384]{0:T(512)S(1)} %fusion.44, ...), kind=kOutput, calls=%fused_computation | convolution fusion | flops 279191040 | bytes 1940130 | tf_op jit(solution)/shard_map/cxjy,cxyk->cxjk/dot_general | solution.py:86
  17.7 0.2 copy.79
  17.9 0.0 copy-start.4
  18.0 0.5 %fusion.68 = (bf16[36,4,16,128]{3,2,1,0:T(8,128)(2,1)S(1)}, bf16[36,4,16,128]{3,2,1,0:T(8,128)(2,1)S(1)}, bf16[36,4,16,128]{3,2,1,0:T(8,128)(2,1)S(1)}) fusion(bf16[36,4,16,384]{3,2,1,0:T(8,128)(2,1)S(1)} %bitcast.99), kind=kLoop, calls=%fused_computation.115 | loop fusion | bytes 3538944 | tf_op jit(solution)/shard_map/slice | solution.py:96
  18.5 0.1 copy-done.4
  18.6 0.4 convolution_add_fusion.2
  19.1 0.5 convolution_add_fusion.1
  19.5 1.4 %all-to-all-done.1 = bf16[8,4,64,128]{3,0,1,2:T(8,128)(2,1)S(1)} async-done(((bf16[8,4,64,128]{3,0,1,2:T(8,128)(2,1)}), bf16[8,4,64,128]{3,0,1,2:T(8,128)(2,1)S(1)}, u32[]{:S(2)}, u32[]{:S(2)}) %all-to-all-start.1) | async-done | bytes 524320 | tf_op jit(solution)/shard_map/all_to_all | solution.py:70
  20.9 1.9 %fusion.66 = (f32[32]{0:T(128)S(1)}, bf16[32,4,16,128]{3,0,2,1:T(8,128)(2,1)S(1)}, bf16[32,4,16,128]{3,0,2,1:T(8,128)(2,1)}) fusion(pred[4,16]{1,0:T(4,128)(4,1)S(1)} %broadcast_and_fusion, f32[4,16,128,32]{2,3,1,0:T(8,128)S(1)} %convolution_add_fusion.1, bf16[32,36,1]{1,0,2:T(8,128)(2,1)S(1)} %copy.106, ...), kind=kOutput, calls=%fused_computation.114 | convolution fusion | flops 23592928 | bytes 3213760 | tf_op jit(solution)/shard_map/ok,kpqr->opqr/dot_general | solution.py:97
  22.8 0.5 convolution_bitcast_fusion
  23.2 0.0 copy-start.1
  23.2 0.5 convolution_bitcast_fusion.1
  23.7 0.5 convolution_bitcast_fusion.2
  24.2 0.1 copy.93
  24.3 0.1 copy.91
  24.4 0.1 copy.92
  24.5 0.1 pad_maximum_fusion.1
  24.6 3.8 %collective-permute-start.3 = (f32[32,109]{1,0:T(8,128)S(1)}, f32[32,109]{1,0:T(8,128)S(1)}, u32[]{:S(2)}, u32[]{:S(2)}) collective-permute-start(f32[32,109]{1,0:T(8,128)S(1)} %pad_maximum_fusion.1), channel_id=1, source_target_pairs={{0,2},{1,3},{2,0},{3,1},{4,6},{5,7},{6,4},{7,5},{8,10},{9,11},{10,... | collective-permute-start | bytes 41864 | tf_op jit(solution)/shard_map/ppermute | solution.py:21
  28.4 0.0 collective-permute-start.4
  28.4 0.2 collective-permute-start.2
  28.6 1.5 %collective-permute-done.3 = f32[32,109]{1,0:T(8,128)S(1)} collective-permute-done((f32[32,109]{1,0:T(8,128)S(1)}, f32[32,109]{1,0:T(8,128)S(1)}, u32[]{:S(2)}, u32[]{:S(2)}) %collective-permute-start.3) | collective-permute-done | bytes 13984 | tf_op jit(solution)/shard_map/ppermute | solution.py:21
  30.1 1.4 %collective-permute-done.4 = f32[32,109]{1,0:T(8,128)S(1)} collective-permute-done((f32[32,109]{1,0:T(8,128)S(1)}, f32[32,109]{1,0:T(8,128)S(1)}, u32[]{:S(2)}, u32[]{:S(2)}) %collective-permute-start.4) | collective-permute-done | bytes 13984 | tf_op jit(solution)/shard_map/ppermute | solution.py:21
  31.5 0.0 collective-permute-done.2
  31.5 0.1 add_add_fusion.1
  31.6 2.6 %collective-permute-start.6 = (f32[32,109]{1,0:T(8,128)S(1)}, f32[32,109]{1,0:T(8,128)S(1)}, u32[]{:S(2)}, u32[]{:S(2)}) collective-permute-start(f32[32,109]{1,0:T(8,128)S(1)} %add_add_fusion.1), channel_id=1, source_target_pairs={{0,16},{4,20},{8,24},{12,28},{16,0},{20,4},{24,8},{28,12},{1,17},{... | collective-permute-start | bytes 41864 | tf_op jit(solution)/shard_map/ppermute | solution.py:21
  34.2 1.4 %collective-permute-start.7 = (f32[32,109]{1,0:T(8,128)S(1)}, f32[32,109]{1,0:T(8,128)S(1)}, u32[]{:S(2)}, u32[]{:S(2)}) collective-permute-start(f32[32,109]{1,0:T(8,128)S(1)} %add_add_fusion.1), channel_id=1, source_target_pairs={{0,24},{4,28},{8,16},{12,20},{16,8},{20,12},{24,0},{28,4},{1,25},{... | collective-permute-start | bytes 41864 | tf_op jit(solution)/shard_map/ppermute | solution.py:21
  35.6 0.2 collective-permute-start.5
  35.8 0.0 copy-done.1
  35.8 1.0 %copy.87 = bf16[32,4,16,128]{3,2,1,0:T(8,128)(2,1)} copy(bf16[32,4,16,128]{3,0,2,1:T(8,128)(2,1)S(1)} %copy-done.1) | data formatting | bytes 1048576 | tf_op jit(solution)/shard_map/convert_element_type | solution.py:101
  36.8 3.5 %all-to-all-start = ((bf16[32,4,16,128]{3,2,1,0:T(8,128)(2,1)}), bf16[32,4,16,128]{3,2,1,0:T(8,128)(2,1)S(1)}, u32[]{:S(2)}, u32[]{:S(2)}) async-start(bf16[32,4,16,128]{3,2,1,0:T(8,128)(2,1)} %copy.87), calls=%async_computation | async-start | bytes 1048576 | tf_op jit(solution)/shard_map/all_to_all | solution.py:106
  40.3 0.0 collective-permute-done.6
  40.3 0.0 collective-permute-done.7
  40.3 0.0 collective-permute-done.5
  40.3 1.4 %collective-permute-start.8 = (f32[32,109]{1,0:T(8,128)S(1)}, f32[32,109]{1,0:T(8,128)S(1)}, u32[]{:S(2)}, u32[]{:S(2)}) collective-permute-start(f32[32,109]{1,0:T(8,128)S(1)} %add_add_fusion), channel_id=1, source_target_pairs={{0,4},{4,0},{8,12},{12,8},{16,20},{20,16},{24,28},{28,24},{1,5},{5... | collective-permute-start | bytes 41864 | tf_op jit(solution)/shard_map/ppermute | solution.py:21
  41.7 2.4 %collective-permute-done.8 = f32[32,109]{1,0:T(8,128)S(1)} collective-permute-done((f32[32,109]{1,0:T(8,128)S(1)}, f32[32,109]{1,0:T(8,128)S(1)}, u32[]{:S(2)}, u32[]{:S(2)}) %collective-permute-start.8) | collective-permute-done | bytes 13984 | tf_op jit(solution)/shard_map/ppermute | solution.py:21
  44.1 0.7 %slice_reduce_fusion = f32[8]{0:T(128)} fusion(f32[8,109]{1,0:T(8,128)S(1)} %dynamic-slice_add_fusion), kind=kLoop, calls=%fused_computation.55 | loop fusion | bytes 64 | tf_op jit(solution)/shard_map/slice | solution.py:117
  44.8 4.2 %all-to-all-done = bf16[32,4,16,128]{3,2,1,0:T(8,128)(2,1)S(1)} async-done(((bf16[32,4,16,128]{3,2,1,0:T(8,128)(2,1)}), bf16[32,4,16,128]{3,2,1,0:T(8,128)(2,1)S(1)}, u32[]{:S(2)}, u32[]{:S(2)}) %all-to-all-start) | async-done | bytes 524320 | tf_op jit(solution)/shard_map/all_to_all | solution.py:106
  49.0 0.9 %copy.88 = bf16[8,4,4,16,128]{4,3,2,1,0:T(8,128)(2,1)} copy(bf16[8,4,4,16,128]{4,3,1,0,2:T(8,128)(2,1)S(1)} %bitcast.100) | data formatting | bytes 1048576 | tf_op jit(solution)/shard_map/all_to_all | solution.py:106
  49.9 0.0 copy-done.2
  (26 shorter events, 0.5 us)
Async XLA Ops:
  0.6 12.3 %copy-start = (bf16[4,8,32,256]{3,2,1,0:T(8,128)(2,1)S(1)}, bf16[4,8,32,256]{3,2,1,0:T(8,128)(2,1)}, u32[]{:S(2)}) copy-start(bf16[4,8,32,256]{3,2,1,0:T(8,128)(2,1)} %param.6) | copy-start | bytes 1572868
  0.6 11.5 %copy-start.5 = (s32[4]{0:T(128)S(1)}, s32[4]{0:T(128)}, u32[]{:S(2)}) copy-start(s32[4]{0:T(128)} %param.8) | copy-start | bytes 52
  0.7 11.5 %copy-start.6 = (s32[8]{0:T(128)S(1)}, s32[8]{0:T(128)}, u32[]{:S(2)}) copy-start(s32[8]{0:T(128)} %param.7) | copy-start | bytes 100
  0.7 11.8 %copy-start.3 = (bf16[32,108]{1,0:T(8,128)(2,1)S(1)}, bf16[32,108]{1,0:T(8,128)(2,1)}, u32[]{:S(2)}) copy-start(bf16[32,108]{1,0:T(8,128)(2,1)} %param.9) | copy-start | bytes 20740
  1.6 11.3 %collective-permute-start = (bf16[4,32,256]{2,1,0:T(8,128)(2,1)S(1)}, bf16[4,32,256]{2,1,0:T(8,128)(2,1)S(1)}, u32[]{:S(2)}, u32[]{:S(2)}) collective-permute-start(bf16[4,32,256]{2,1,0:T(8,128)(2,1)S(1)} %slice_bitcast_fusion), channel_id=1, source_target_pairs={{0,4},{4,8},{8,12},{12,16},{16,20},{20,24},{24,28},{1,5},{5,9},{9,... | collective-permute-start | bytes 196616 | tf_op jit(solution)/shard_map/ppermute | solution.py:10
  8.6 12.3 %all-to-all-start.1 = ((bf16[8,4,64,128]{3,0,1,2:T(8,128)(2,1)}), bf16[8,4,64,128]{3,0,1,2:T(8,128)(2,1)S(1)}, u32[]{:S(2)}, u32[]{:S(2)}) async-start(bf16[8,4,64,128]{3,0,1,2:T(8,128)(2,1)} %copy.89), calls=%async_computation.1 | async-start | bytes 1048576 | tf_op jit(solution)/shard_map/all_to_all | solution.py:70
  13.1 3.2 %collective-permute-start.1 = (bf16[4,9,256]{2,0,1:T(4,128)(2,1)S(1)}, bf16[4,9,256]{2,0,1:T(4,128)(2,1)S(1)}, u32[]{:S(2)}, u32[]{:S(2)}) collective-permute-start(bf16[4,9,256]{2,0,1:T(4,128)(2,1)S(1)} %bitcast.102), channel_id=1, source_target_pairs={{0,1},{1,2},{2,3},{4,5},{5,6},{6,7},{8,9},{9,10},{10,11},{12,13},{... | collective-permute-start | bytes 55304 | tf_op jit(solution)/shard_map/ppermute | solution.py:10
  17.9 0.7 %copy-start.4 = (f32[32]{0:T(128)S(1)}, f32[32]{0:T(128)}, u32[]{:S(2)}) copy-start(f32[32]{0:T(128)} %param.10) | copy-start | bytes 388
  23.2 12.6 %copy-start.1 = (bf16[32,4,16,128]{3,0,2,1:T(8,128)(2,1)S(1)}, bf16[32,4,16,128]{3,0,2,1:T(8,128)(2,1)}, u32[]{:S(2)}) copy-start(bf16[32,4,16,128]{3,0,2,1:T(8,128)(2,1)} %get-tuple-element.15) | copy-start | bytes 1572868
  24.6 5.5 %collective-permute-start.3 = (f32[32,109]{1,0:T(8,128)S(1)}, f32[32,109]{1,0:T(8,128)S(1)}, u32[]{:S(2)}, u32[]{:S(2)}) collective-permute-start(f32[32,109]{1,0:T(8,128)S(1)} %pad_maximum_fusion.1), channel_id=1, source_target_pairs={{0,2},{1,3},{2,0},{3,1},{4,6},{5,7},{6,4},{7,5},{8,10},{9,11},{10,... | collective-permute-start | bytes 41864 | tf_op jit(solution)/shard_map/ppermute | solution.py:21
  28.4 3.2 %collective-permute-start.4 = (f32[32,109]{1,0:T(8,128)S(1)}, f32[32,109]{1,0:T(8,128)S(1)}, u32[]{:S(2)}, u32[]{:S(2)}) collective-permute-start(f32[32,109]{1,0:T(8,128)S(1)} %pad_maximum_fusion.1), channel_id=1, source_target_pairs={{0,3},{1,2},{2,1},{3,0},{4,7},{5,6},{6,5},{7,4},{8,11},{9,10},{10,... | collective-permute-start | bytes 41864 | tf_op jit(solution)/shard_map/ppermute | solution.py:21
  28.4 3.2 %collective-permute-start.2 = (f32[32,109]{1,0:T(8,128)S(1)}, f32[32,109]{1,0:T(8,128)S(1)}, u32[]{:S(2)}, u32[]{:S(2)}) collective-permute-start(f32[32,109]{1,0:T(8,128)S(1)} %pad_maximum_fusion.1), channel_id=1, source_target_pairs={{0,1},{1,0},{2,3},{3,2},{4,5},{5,4},{6,7},{7,6},{8,9},{9,8},{10,11... | collective-permute-start | bytes 41864 | tf_op jit(solution)/shard_map/ppermute | solution.py:21
  31.6 8.7 %collective-permute-start.6 = (f32[32,109]{1,0:T(8,128)S(1)}, f32[32,109]{1,0:T(8,128)S(1)}, u32[]{:S(2)}, u32[]{:S(2)}) collective-permute-start(f32[32,109]{1,0:T(8,128)S(1)} %add_add_fusion.1), channel_id=1, source_target_pairs={{0,16},{4,20},{8,24},{12,28},{16,0},{20,4},{24,8},{28,12},{1,17},{... | collective-permute-start | bytes 41864 | tf_op jit(solution)/shard_map/ppermute | solution.py:21
  34.2 6.1 %collective-permute-start.7 = (f32[32,109]{1,0:T(8,128)S(1)}, f32[32,109]{1,0:T(8,128)S(1)}, u32[]{:S(2)}, u32[]{:S(2)}) collective-permute-start(f32[32,109]{1,0:T(8,128)S(1)} %add_add_fusion.1), channel_id=1, source_target_pairs={{0,24},{4,28},{8,16},{12,20},{16,8},{20,12},{24,0},{28,4},{1,25},{... | collective-permute-start | bytes 41864 | tf_op jit(solution)/shard_map/ppermute | solution.py:21
  35.6 4.7 %collective-permute-start.5 = (f32[32,109]{1,0:T(8,128)S(1)}, f32[32,109]{1,0:T(8,128)S(1)}, u32[]{:S(2)}, u32[]{:S(2)}) collective-permute-start(f32[32,109]{1,0:T(8,128)S(1)} %add_add_fusion.1), channel_id=1, source_target_pairs={{0,8},{4,12},{8,0},{12,4},{16,24},{20,28},{24,16},{28,20},{1,9},{5... | collective-permute-start | bytes 41864 | tf_op jit(solution)/shard_map/ppermute | solution.py:21
  36.8 12.3 %all-to-all-start = ((bf16[32,4,16,128]{3,2,1,0:T(8,128)(2,1)}), bf16[32,4,16,128]{3,2,1,0:T(8,128)(2,1)S(1)}, u32[]{:S(2)}, u32[]{:S(2)}) async-start(bf16[32,4,16,128]{3,2,1,0:T(8,128)(2,1)} %copy.87), calls=%async_computation | async-start | bytes 1048576 | tf_op jit(solution)/shard_map/all_to_all | solution.py:106
  40.3 3.8 %collective-permute-start.8 = (f32[32,109]{1,0:T(8,128)S(1)}, f32[32,109]{1,0:T(8,128)S(1)}, u32[]{:S(2)}, u32[]{:S(2)}) collective-permute-start(f32[32,109]{1,0:T(8,128)S(1)} %add_add_fusion), channel_id=1, source_target_pairs={{0,4},{4,0},{8,12},{12,8},{16,20},{20,16},{24,28},{28,24},{1,5},{5... | collective-permute-start | bytes 41864 | tf_op jit(solution)/shard_map/ppermute | solution.py:21
  44.1 5.8 %copy-start.2 = (f32[8,109]{1,0:T(8,128)}, f32[8,109]{1,0:T(8,128)S(1)}, u32[]{:S(2)}) copy-start(f32[8,109]{1,0:T(8,128)S(1)} %dynamic-slice_add_fusion) | copy-start | bytes 10468

commit v15 on v8

--- a/solution.py
+++ b/solution.py
@@ -10,15 +10,31 @@
     return lax.ppermute(block, axis, route)
 
 
-def butterfly_sum(value, axis):
-    size = lax.axis_size(axis)
-    if size & (size - 1):
-        return lax.psum(value, axis)
-    step = 1
-    while step < size:
-        swap = [(i, i ^ step) for i in range(size)]
-        value = value + lax.ppermute(value, axis, swap)
-        step *= 2
+def exchange(value, axes, size, spans):
+    vals = [value] + [lax.ppermute(value, axes, [(i, i ^ t) for i in range(size)]) for t in spans]
+    while len(vals) > 1:
+        vals = [vals[k] + vals[k + 1] for k in range(0, len(vals), 2)]
+    return vals[0]
+
+
+def grid_sum(value):
+    nx, ny = lax.axis_size("gx"), lax.axis_size("gy")
+    if nx & (nx - 1) or ny & (ny - 1):
+        return lax.psum(value, ("gx", "gy"))
+    bits_x, bits_y = nx.bit_length() - 1, ny.bit_length() - 1
+    while bits_x >= 2:
+        low = bits_x - 2
+        value = exchange(value, "gx", nx, [(1 << low) * t for t in (1, 2, 3)])
+        bits_x = low
+    if bits_x and bits_y:
+        top = 1 << (bits_y - 1)
+        value = exchange(value, ("gx", "gy"), nx * ny, [top, ny, ny + top])
+        bits_x, bits_y = 0, bits_y - 1
+    if bits_x:
+        value = exchange(value, "gx", nx, [1])
+    while bits_y:
+        bits_y -= 1
+        value = exchange(value, "gy", ny, [1 << bits_y])
     return value
 
 
@@ -106,7 +122,7 @@
     weight_full = jnp.stack(grads, axis=-1).reshape(out_chans, -1)
     bias_full = jnp.sum(grad_wide, axis=(1, 2, 3))
     packed = jnp.concatenate([weight_full, bias_full[:, None]], axis=1)
-    total = butterfly_sum(butterfly_sum(packed, "gx"), "gy")
+    total = grid_sum(packed)
     share = out_chans // tiles_y
     mine = lax.dynamic_slice_in_dim(total, lax.axis_index("gy") * share, share, 0)
     weight_grad, bias_grad = mine[:, :-1], mine[:, -1]

time: 47.7 us -> 52.6 us (1.10)
  waiting for transfers between devices: 9.02 us -> 13.4 us
    all_to_all x1, waiting for transfers between devices: 0.01 us -> 6.54 us  [local(): lax.all_to_all(stem_local, 'gy', split_axis=0, concat_axis=2, tiled=True)]
    ppermute x5 -> x7, waiting for transfers between devices: 7.12 us -> 4.95 us  [exchange(): lax.ppermute(value, axes, [(i, i ^ t) for i in range(size)])]
    ppermute x5 -> x7, starting transfers between devices: 7.93 us -> 10 us  [exchange(): lax.ppermute(value, axes, [(i, i ^ t) for i in range(size)])]
    all_to_all x1, starting transfers between devices: 5.07 us -> 3.47 us  [local(): lax.all_to_all(stem_local, 'gy', split_axis=0, concat_axis=2, tiled=True)]
  transfers between devices with their start and end apart: 9 -> 11, of which waited for: 6 -> 6; matrix products, arithmetic and copies ran while one was open for 17% -> 15% of each run, Pallas kernels for 0% -> 0%
where the time goes in v15:
time: 52.6 us; the launch traced here: 52.2 us
  starting transfers between devices  24.2 us (46%)
  waiting for transfers between devices  13.4 us (25%)
  local copies, waits for them, and re-layouts  7.6 us (14%)
  matrix products  5.23 us (10%)
  between operations  1 us (2%)
  other arithmetic  0.84 us (2%)
    ppermute x7, starting transfers between devices, exchange(): lax.ppermute(value, axes, [(i, i ^ t) for i in range(size)])  10 us
    ppermute x2, starting transfers between devices, from_behind(): return lax.ppermute(block, axis, route)  7.21 us
    all_to_all x1, waiting for transfers between devices, local(): lax.all_to_all(stem_local, 'gy', split_axis=0, concat_axis=2, tiled=True)  6.54 us
    ppermute x7, waiting for transfers between devices, exchange(): lax.ppermute(value, axes, [(i, i ^ t) for i in range(size)])  4.95 us
    all_to_all x1, starting transfers between devices, local(): lax.all_to_all(grad_out, 'gy', split_axis=2, concat_axis=0, tiled=True)  3.47 us
    all_to_all x1, starting transfers between devices, local(): lax.all_to_all(stem_local, 'gy', split_axis=0, concat_axis=2, tiled=True)  3.47 us
    unnamed x27, local copies, waits for them, and re-layouts  2.98 us
    dot_general x3, matrix products, local(): jnp.einsum('ok,kpqr->opqr', kernel[:, :, off_z], part, preferred_element_...  2.78 us
  transfers between devices with their start and end apart: 11, of which 6 were waited for; matrix products, arithmetic and copies ran while one was open for 15% of the time, Pallas kernels for 0%

profile of v15, /device:TPU:0, one launch (start us, length us, event | category | flops | bytes accessed | tf_op | source)
XLA Modules:
  0.0 52.2 jit_solution(3714443823551427366)
XLA Ops:
  0.6 0.0 copy-start
  0.6 0.0 copy-start.5
  0.7 0.0 copy-start.6
  0.7 0.0 copy-start.3
  0.7 0.9 %slice_bitcast_fusion = bf16[4,32,256]{2,1,0:T(8,128)(2,1)S(1)} fusion(bf16[4,8,32,256]{3,2,1,0:T(8,128)(2,1)} %param.6), kind=kLoop, calls=%fused_computation.43 | loop fusion | bytes 131072 | tf_op jit(solution)/shard_map/squeeze | solution.py:84
  1.6 4.9 %collective-permute-start = (bf16[4,32,256]{2,1,0:T(8,128)(2,1)S(1)}, bf16[4,32,256]{2,1,0:T(8,128)(2,1)S(1)}, u32[]{:S(2)}, u32[]{:S(2)}) collective-permute-start(bf16[4,32,256]{2,1,0:T(8,128)(2,1)S(1)} %slice_bitcast_fusion), channel_id=1, source_target_pairs={{0,4},{4,8},{8,12},{12,16},{16,20},{20,24},{24,28},{1,5},{5,9},{9,... | collective-permute-start | bytes 196616 | tf_op jit(solution)/shard_map/ppermute | solution.py:10
  6.4 2.2 %copy.89 = bf16[8,4,64,128]{3,0,1,2:T(8,128)(2,1)} copy(bf16[8,4,64,128]{3,2,1,0:T(8,128)(2,1)} %param.11) | data formatting | bytes 1048576 | tf_op args[5]
  8.6 3.5 %all-to-all-start.1 = ((bf16[8,4,64,128]{3,0,1,2:T(8,128)(2,1)}), bf16[8,4,64,128]{3,0,1,2:T(8,128)(2,1)S(1)}, u32[]{:S(2)}, u32[]{:S(2)}) async-start(bf16[8,4,64,128]{3,0,1,2:T(8,128)(2,1)} %copy.89), calls=%async_computation.1 | async-start | bytes 1048576 | tf_op jit(solution)/shard_map/all_to_all | solution.py:81
  12.1 0.0 copy-done.5
  12.2 0.0 copy-done.6
  12.2 0.1 fusion.50
  12.3 0.1 fusion.40
  12.4 0.0 copy-done.3
  12.4 0.1 copy.81
  12.6 0.1 fusion.52
  12.7 0.1 broadcast_and_fusion
  12.8 0.1 fusion.54
  12.9 0.0 collective-permute-done
  12.9 0.0 copy-done
  12.9 0.1 select_select_fusion
  13.1 2.4 %collective-permute-start.1 = (bf16[4,9,256]{2,0,1:T(4,128)(2,1)S(1)}, bf16[4,9,256]{2,0,1:T(4,128)(2,1)S(1)}, u32[]{:S(2)}, u32[]{:S(2)}) collective-permute-start(bf16[4,9,256]{2,0,1:T(4,128)(2,1)S(1)} %bitcast.102), channel_id=1, source_target_pairs={{0,1},{1,2},{2,3},{4,5},{5,6},{6,7},{8,9},{9,10},{10,11},{12,13},{... | collective-permute-start | bytes 55304 | tf_op jit(solution)/shard_map/ppermute | solution.py:10
  15.5 0.1 copy.102
  15.6 0.1 copy.104
  15.7 0.1 copy.106
  15.8 0.5 %collective-permute-done.1 = bf16[4,9,256]{2,0,1:T(4,128)(2,1)S(1)} collective-permute-done((bf16[4,9,256]{2,0,1:T(4,128)(2,1)S(1)}, bf16[4,9,256]{2,0,1:T(4,128)(2,1)S(1)}, u32[]{:S(2)}, u32[]{:S(2)}) %collective-permute-start.1) | collective-permute-done | bytes 18464 | tf_op jit(solution)/shard_map/ppermute | solution.py:10
  16.3 1.1 %convolution_convert_fusion = bf16[4,9,48,384]{3,2,1,0:T(8,128)(2,1)S(1)} fusion(bf16[4,9,32,256]{3,2,1,0:T(8,128)(2,1)S(1)} %select_select_fusion, pred[33]{0:T(512)(128)(4,1)S(1)} %get-tuple-element.7, pred[33]{0:T(512)(128)(4,1)S(1)} %get-tuple-element.6, bf16[4,9,256]{2,1,0:T(8,128)(2,1)S(1)} %copy.78, s32[384]{0:T(512)S(1)} %fusion.44, ...), kind=kOutput, calls=%fused_computation | convolution fusion | flops 279191040 | bytes 1940130 | tf_op jit(solution)/shard_map/cxjy,cxyk->cxjk/dot_general | solution.py:97
  17.7 0.2 copy.79
  17.9 0.0 copy-start.4
  18.0 0.5 fusion.68
  18.5 0.1 copy-done.4
  18.6 0.4 convolution_add_fusion.2
  19.1 0.5 convolution_add_fusion.1
  19.5 1.4 %all-to-all-done.1 = bf16[8,4,64,128]{3,0,1,2:T(8,128)(2,1)S(1)} async-done(((bf16[8,4,64,128]{3,0,1,2:T(8,128)(2,1)}), bf16[8,4,64,128]{3,0,1,2:T(8,128)(2,1)S(1)}, u32[]{:S(2)}, u32[]{:S(2)}) %all-to-all-start.1) | async-done | bytes 524320 | tf_op jit(solution)/shard_map/all_to_all | solution.py:81
  20.9 1.9 %fusion.66 = (f32[32]{0:T(128)S(1)}, bf16[32,4,16,128]{3,0,2,1:T(8,128)(2,1)S(1)}, bf16[32,4,16,128]{3,0,2,1:T(8,128)(2,1)}) fusion(pred[4,16]{1,0:T(4,128)(4,1)S(1)} %broadcast_and_fusion, f32[4,16,128,32]{2,3,1,0:T(8,128)S(1)} %convolution_add_fusion.1, bf16[32,36,1]{1,0,2:T(8,128)(2,1)S(1)} %copy.106, ...), kind=kOutput, calls=%fused_computation.114 | convolution fusion | flops 23592928 | bytes 3213760 | tf_op jit(solution)/shard_map/ok,kpqr->opqr/dot_general | solution.py:108
  22.8 0.5 convolution_bitcast_fusion
  23.2 0.0 copy-start.1
  23.2 0.5 convolution_bitcast_fusion.1
  23.7 0.5 convolution_bitcast_fusion.2
  24.2 0.1 copy.93
  24.3 0.1 copy.91
  24.4 0.1 copy.92
  24.5 0.1 pad_maximum_fusion.1
  24.6 2.6 %collective-permute-start.3 = (f32[32,109]{1,0:T(8,128)S(1)}, f32[32,109]{1,0:T(8,128)S(1)}, u32[]{:S(2)}, u32[]{:S(2)}) collective-permute-start(f32[32,109]{1,0:T(8,128)S(1)} %pad_maximum_fusion.1), channel_id=1, source_target_pairs={{0,16},{4,20},{8,24},{12,28},{16,0},{20,4},{24,8},{28,12},{1,17},{... | collective-permute-start | bytes 41864 | tf_op jit(solution)/shard_map/ppermute | solution.py:14
  27.2 1.3 %collective-permute-start.4 = (f32[32,109]{1,0:T(8,128)S(1)}, f32[32,109]{1,0:T(8,128)S(1)}, u32[]{:S(2)}, u32[]{:S(2)}) collective-permute-start(f32[32,109]{1,0:T(8,128)S(1)} %pad_maximum_fusion.1), channel_id=1, source_target_pairs={{0,24},{4,28},{8,16},{12,20},{16,8},{20,12},{24,0},{28,4},{1,25},{... | collective-permute-start | bytes 41864 | tf_op jit(solution)/shard_map/ppermute | solution.py:14
  28.5 0.2 collective-permute-start.2
  28.7 0.5 collective-permute-done.3
  29.2 3.5 %collective-permute-done.4 = f32[32,109]{1,0:T(8,128)S(1)} collective-permute-done((f32[32,109]{1,0:T(8,128)S(1)}, f32[32,109]{1,0:T(8,128)S(1)}, u32[]{:S(2)}, u32[]{:S(2)}) %collective-permute-start.4) | collective-permute-done | bytes 13984 | tf_op jit(solution)/shard_map/ppermute | solution.py:14
  32.7 0.0 collective-permute-done.2
  32.7 0.1 add_add_fusion.1
  32.8 1.6 %collective-permute-start.6 = (f32[32,109]{1,0:T(8,128)S(1)}, f32[32,109]{1,0:T(8,128)S(1)}, u32[]{:S(2)}, u32[]{:S(2)}) collective-permute-start(f32[32,109]{1,0:T(8,128)S(1)} %add_add_fusion.1), channel_id=1, source_target_pairs={{0,4},{1,5},{2,6},{3,7},{4,0},{5,1},{6,2},{7,3},{8,12},{9,13},{10,... | collective-permute-start | bytes 41864 | tf_op jit(solution)/shard_map/ppermute | solution.py:14
  34.3 3.7 %collective-permute-start.7 = (f32[32,109]{1,0:T(8,128)S(1)}, f32[32,109]{1,0:T(8,128)S(1)}, u32[]{:S(2)}, u32[]{:S(2)}) collective-permute-start(f32[32,109]{1,0:T(8,128)S(1)} %add_add_fusion.1), channel_id=1, source_target_pairs={{0,6},{1,7},{2,4},{3,5},{4,2},{5,3},{6,0},{7,1},{8,14},{9,15},{10,... | collective-permute-start | bytes 41864 | tf_op jit(solution)/shard_map/ppermute | solution.py:14
  38.0 0.1 collective-permute-start.5
  38.1 0.0 copy-done.1
  38.1 1.0 %copy.87 = bf16[32,4,16,128]{3,2,1,0:T(8,128)(2,1)} copy(bf16[32,4,16,128]{3,0,2,1:T(8,128)(2,1)S(1)} %copy-done.1) | data formatting | bytes 1048576 | tf_op jit(solution)/shard_map/convert_element_type | solution.py:112
  39.1 3.5 %all-to-all-start = ((bf16[32,4,16,128]{3,2,1,0:T(8,128)(2,1)}), bf16[32,4,16,128]{3,2,1,0:T(8,128)(2,1)S(1)}, u32[]{:S(2)}, u32[]{:S(2)}) async-start(bf16[32,4,16,128]{3,2,1,0:T(8,128)(2,1)} %copy.87), calls=%async_computation | async-start | bytes 1048576 | tf_op jit(solution)/shard_map/all_to_all | solution.py:117
  42.6 0.0 collective-permute-done.6
  42.6 0.0 collective-permute-done.7
  42.6 0.0 collective-permute-done.5
  42.7 0.5 collective-permute-start.8
  43.2 1.0 %collective-permute-done.8 = f32[32,109]{1,0:T(8,128)S(1)} collective-permute-done((f32[32,109]{1,0:T(8,128)S(1)}, f32[32,109]{1,0:T(8,128)S(1)}, u32[]{:S(2)}, u32[]{:S(2)}) %collective-permute-start.8) | collective-permute-done | bytes 13984 | tf_op jit(solution)/shard_map/ppermute | solution.py:14
  44.2 0.7 %slice_reduce_fusion = f32[8]{0:T(128)} fusion(f32[8,109]{1,0:T(8,128)S(1)} %dynamic-slice_add_fusion), kind=kLoop, calls=%fused_computation.55 | loop fusion | bytes 64 | tf_op jit(solution)/shard_map/slice | solution.py:128
  44.8 6.5 %all-to-all-done = bf16[32,4,16,128]{3,2,1,0:T(8,128)(2,1)S(1)} async-done(((bf16[32,4,16,128]{3,2,1,0:T(8,128)(2,1)}), bf16[32,4,16,128]{3,2,1,0:T(8,128)(2,1)S(1)}, u32[]{:S(2)}, u32[]{:S(2)}) %all-to-all-start) | async-done | bytes 524320 | tf_op jit(solution)/shard_map/all_to_all | solution.py:117
  51.4 0.9 %copy.88 = bf16[8,4,4,16,128]{4,3,2,1,0:T(8,128)(2,1)} copy(bf16[8,4,4,16,128]{4,3,1,0,2:T(8,128)(2,1)S(1)} %bitcast.100) | data formatting | bytes 1048576 | tf_op jit(solution)/shard_map/all_to_all | solution.py:117
  52.2 0.0 copy-done.2
  (26 shorter events, 0.5 us)
Async XLA Ops:
  0.6 12.3 %copy-start = (bf16[4,8,32,256]{3,2,1,0:T(8,128)(2,1)S(1)}, bf16[4,8,32,256]{3,2,1,0:T(8,128)(2,1)}, u32[]{:S(2)}) copy-start(bf16[4,8,32,256]{3,2,1,0:T(8,128)(2,1)} %param.6) | copy-start | bytes 1572868
  0.6 11.5 %copy-start.5 = (s32[4]{0:T(128)S(1)}, s32[4]{0:T(128)}, u32[]{:S(2)}) copy-start(s32[4]{0:T(128)} %param.8) | copy-start | bytes 52
  0.7 11.5 %copy-start.6 = (s32[8]{0:T(128)S(1)}, s32[8]{0:T(128)}, u32[]{:S(2)}) copy-start(s32[8]{0:T(128)} %param.7) | copy-start | bytes 100
  0.7 11.8 %copy-start.3 = (bf16[32,108]{1,0:T(8,128)(2,1)S(1)}, bf16[32,108]{1,0:T(8,128)(2,1)}, u32[]{:S(2)}) copy-start(bf16[32,108]{1,0:T(8,128)(2,1)} %param.9) | copy-start | bytes 20740
  1.6 11.3 %collective-permute-start = (bf16[4,32,256]{2,1,0:T(8,128)(2,1)S(1)}, bf16[4,32,256]{2,1,0:T(8,128)(2,1)S(1)}, u32[]{:S(2)}, u32[]{:S(2)}) collective-permute-start(bf16[4,32,256]{2,1,0:T(8,128)(2,1)S(1)} %slice_bitcast_fusion), channel_id=1, source_target_pairs={{0,4},{4,8},{8,12},{12,16},{16,20},{20,24},{24,28},{1,5},{5,9},{9,... | collective-permute-start | bytes 196616 | tf_op jit(solution)/shard_map/ppermute | solution.py:10
  8.6 12.3 %all-to-all-start.1 = ((bf16[8,4,64,128]{3,0,1,2:T(8,128)(2,1)}), bf16[8,4,64,128]{3,0,1,2:T(8,128)(2,1)S(1)}, u32[]{:S(2)}, u32[]{:S(2)}) async-start(bf16[8,4,64,128]{3,0,1,2:T(8,128)(2,1)} %copy.89), calls=%async_computation.1 | async-start | bytes 1048576 | tf_op jit(solution)/shard_map/all_to_all | solution.py:81
  13.1 3.2 %collective-permute-start.1 = (bf16[4,9,256]{2,0,1:T(4,128)(2,1)S(1)}, bf16[4,9,256]{2,0,1:T(4,128)(2,1)S(1)}, u32[]{:S(2)}, u32[]{:S(2)}) collective-permute-start(bf16[4,9,256]{2,0,1:T(4,128)(2,1)S(1)} %bitcast.102), channel_id=1, source_target_pairs={{0,1},{1,2},{2,3},{4,5},{5,6},{6,7},{8,9},{9,10},{10,11},{12,13},{... | collective-permute-start | bytes 55304 | tf_op jit(solution)/shard_map/ppermute | solution.py:10
  17.9 0.7 %copy-start.4 = (f32[32]{0:T(128)S(1)}, f32[32]{0:T(128)}, u32[]{:S(2)}) copy-start(f32[32]{0:T(128)} %param.10) | copy-start | bytes 388
  23.2 14.9 %copy-start.1 = (bf16[32,4,16,128]{3,0,2,1:T(8,128)(2,1)S(1)}, bf16[32,4,16,128]{3,0,2,1:T(8,128)(2,1)}, u32[]{:S(2)}) copy-start(bf16[32,4,16,128]{3,0,2,1:T(8,128)(2,1)} %get-tuple-element.15) | copy-start | bytes 1572868
  24.6 4.6 %collective-permute-start.3 = (f32[32,109]{1,0:T(8,128)S(1)}, f32[32,109]{1,0:T(8,128)S(1)}, u32[]{:S(2)}, u32[]{:S(2)}) collective-permute-start(f32[32,109]{1,0:T(8,128)S(1)} %pad_maximum_fusion.1), channel_id=1, source_target_pairs={{0,16},{4,20},{8,24},{12,28},{16,0},{20,4},{24,8},{28,12},{1,17},{... | collective-permute-start | bytes 41864 | tf_op jit(solution)/shard_map/ppermute | solution.py:14
  27.2 5.5 %collective-permute-start.4 = (f32[32,109]{1,0:T(8,128)S(1)}, f32[32,109]{1,0:T(8,128)S(1)}, u32[]{:S(2)}, u32[]{:S(2)}) collective-permute-start(f32[32,109]{1,0:T(8,128)S(1)} %pad_maximum_fusion.1), channel_id=1, source_target_pairs={{0,24},{4,28},{8,16},{12,20},{16,8},{20,12},{24,0},{28,4},{1,25},{... | collective-permute-start | bytes 41864 | tf_op jit(solution)/shard_map/ppermute | solution.py:14
  28.5 4.2 %collective-permute-start.2 = (f32[32,109]{1,0:T(8,128)S(1)}, f32[32,109]{1,0:T(8,128)S(1)}, u32[]{:S(2)}, u32[]{:S(2)}) collective-permute-start(f32[32,109]{1,0:T(8,128)S(1)} %pad_maximum_fusion.1), channel_id=1, source_target_pairs={{0,8},{4,12},{8,0},{12,4},{16,24},{20,28},{24,16},{28,20},{1,9},{5... | collective-permute-start | bytes 41864 | tf_op jit(solution)/shard_map/ppermute | solution.py:14
  32.8 9.8 %collective-permute-start.6 = (f32[32,109]{1,0:T(8,128)S(1)}, f32[32,109]{1,0:T(8,128)S(1)}, u32[]{:S(2)}, u32[]{:S(2)}) collective-permute-start(f32[32,109]{1,0:T(8,128)S(1)} %add_add_fusion.1), channel_id=1, source_target_pairs={{0,4},{1,5},{2,6},{3,7},{4,0},{5,1},{6,2},{7,3},{8,12},{9,13},{10,... | collective-permute-start | bytes 41864 | tf_op jit(solution)/shard_map/ppermute | solution.py:14
  34.3 8.3 %collective-permute-start.7 = (f32[32,109]{1,0:T(8,128)S(1)}, f32[32,109]{1,0:T(8,128)S(1)}, u32[]{:S(2)}, u32[]{:S(2)}) collective-permute-start(f32[32,109]{1,0:T(8,128)S(1)} %add_add_fusion.1), channel_id=1, source_target_pairs={{0,6},{1,7},{2,4},{3,5},{4,2},{5,3},{6,0},{7,1},{8,14},{9,15},{10,... | collective-permute-start | bytes 41864 | tf_op jit(solution)/shard_map/ppermute | solution.py:14
  38.0 4.6 %collective-permute-start.5 = (f32[32,109]{1,0:T(8,128)S(1)}, f32[32,109]{1,0:T(8,128)S(1)}, u32[]{:S(2)}, u32[]{:S(2)}) collective-permute-start(f32[32,109]{1,0:T(8,128)S(1)} %add_add_fusion.1), channel_id=1, source_target_pairs={{0,2},{1,3},{2,0},{3,1},{4,6},{5,7},{6,4},{7,5},{8,10},{9,11},{10,... | collective-permute-start | bytes 41864 | tf_op jit(solution)/shard_map/ppermute | solution.py:14
  39.1 12.3 %all-to-all-start = ((bf16[32,4,16,128]{3,2,1,0:T(8,128)(2,1)}), bf16[32,4,16,128]{3,2,1,0:T(8,128)(2,1)S(1)}, u32[]{:S(2)}, u32[]{:S(2)}) async-start(bf16[32,4,16,128]{3,2,1,0:T(8,128)(2,1)} %copy.87), calls=%async_computation | async-start | bytes 1048576 | tf_op jit(solution)/shard_map/all_to_all | solution.py:117
  42.7 1.5 %collective-permute-start.8 = (f32[32,109]{1,0:T(8,128)S(1)}, f32[32,109]{1,0:T(8,128)S(1)}, u32[]{:S(2)}, u32[]{:S(2)}) collective-permute-start(f32[32,109]{1,0:T(8,128)S(1)} %add_add_fusion), channel_id=1, source_target_pairs={{0,1},{1,0},{2,3},{3,2},{4,5},{5,4},{6,7},{7,6},{8,9},{9,8},{10,11... | collective-permute-start | bytes 41864 | tf_op jit(solution)/shard_map/ppermute | solution.py:14
  44.2 8.1 %copy-start.2 = (f32[8,109]{1,0:T(8,128)}, f32[8,109]{1,0:T(8,128)S(1)}, u32[]{:S(2)}) copy-start(f32[8,109]{1,0:T(8,128)S(1)} %dynamic-slice_add_fusion) | copy-start | bytes 10468

commit v16 on v14

--- a/solution.py
+++ b/solution.py
@@ -10,13 +10,13 @@
     return lax.ppermute(block, axis, route)
 
 
-def butterfly_sum(value, axis):
+def butterfly_sum(value, axis, widest=2):
     size = lax.axis_size(axis)
     if size & (size - 1):
         return lax.psum(value, axis)
     bits = size.bit_length() - 1
     while bits:
-        low = max(bits - 2, 0)
+        low = max(bits - widest, 0)
         spans = [(1 << low) * t for t in range(1, 1 << (bits - low))]
         got = [lax.ppermute(value, axis, [(i, i ^ t) for i in range(size)]) for t in spans]
         if len(got) == 1:
@@ -111,7 +111,7 @@
     weight_full = jnp.stack(grads, axis=-1).reshape(out_chans, -1)
     bias_full = jnp.sum(grad_wide, axis=(1, 2, 3))
     packed = jnp.concatenate([weight_full, bias_full[:, None]], axis=1)
-    total = butterfly_sum(butterfly_sum(packed, "gy"), "gx")
+    total = butterfly_sum(butterfly_sum(packed, "gx"), "gy", 1)
     share = out_chans // tiles_y
     mine = lax.dynamic_slice_in_dim(total, lax.axis_index("gy") * share, share, 0)
     weight_grad, bias_grad = mine[:, :-1], mine[:, -1]

time: 50.2 us -> 47.1 us (0.938)
  waiting for transfers between devices: 11.5 us -> 8.6 us
    all_to_all x1, waiting for transfers between devices: 4.23 us -> 0.01 us  [local(): lax.all_to_all(stem_local, 'gy', split_axis=0, concat_axis=2, tiled=True)]
    ppermute x7 -> x6, starting transfers between devices: 9.56 us -> 7.72 us  [butterfly_sum(): lax.ppermute(value, axis, [(i, i ^ t) for i in range(size)])]
    all_to_all x1, starting transfers between devices: 3.47 us -> 5.07 us  [local(): lax.all_to_all(stem_local, 'gy', split_axis=0, concat_axis=2, tiled=True)]
    ppermute x7 -> x6, waiting for transfers between devices: 5.4 us -> 6.7 us  [butterfly_sum(): lax.ppermute(value, axis, [(i, i ^ t) for i in range(size)])]
  transfers between devices with their start and end apart: 11 -> 10, of which waited for: 6 -> 5; matrix products, arithmetic and copies ran while one was open for 16% -> 17% of each run, Pallas kernels for 0% -> 0%
where the time goes in v16:
time: 47.1 us; the launch traced here: 46.7 us
  starting transfers between devices  23.5 us (50%)
  waiting for transfers between devices  8.6 us (18%)
  local copies, waits for them, and re-layouts  7.6 us (16%)
  matrix products  5.23 us (11%)
  between operations  0.98 us (2%)
  other arithmetic  0.84 us (2%)
    ppermute x6, starting transfers between devices, butterfly_sum(): lax.ppermute(value, axis, [(i, i ^ t) for i in range(size)])  7.72 us
    ppermute x2, starting transfers between devices, from_behind(): return lax.ppermute(block, axis, route)  7.21 us
    ppermute x6, waiting for transfers between devices, butterfly_sum(): lax.ppermute(value, axis, [(i, i ^ t) for i in range(size)])  6.7 us
    all_to_all x1, starting transfers between devices, local(): lax.all_to_all(stem_local, 'gy', split_axis=0, concat_axis=2, tiled=True)  5.07 us
    all_to_all x1, starting transfers between devices, local(): lax.all_to_all(grad_out, 'gy', split_axis=2, concat_axis=0, tiled=True)  3.47 us
    unnamed x27, local copies, waits for them, and re-layouts  2.98 us
    dot_general x3, matrix products, local(): jnp.einsum('ok,kpqr->opqr', kernel[:, :, off_z], part, preferred_element_...  2.78 us
    dot_general x3, matrix products, local(): jnp.einsum('opqr,kpqr->ok', returned, part, preferred_element_type=jnp.fl...  1.37 us
  transfers between devices with their start and end apart: 10, of which 5 were waited for; matrix products, arithmetic and copies ran while one was open for 17% of the time, Pallas kernels for 0%

profile of v16, /device:TPU:0, one launch (start us, length us, event | category | flops | bytes accessed | tf_op | source)
XLA Modules:
  0.0 46.7 jit_solution(2451752089535637933)
XLA Ops:
  0.6 0.0 copy-start
  0.6 0.0 copy-start.5
  0.7 0.0 copy-start.6
  0.7 0.0 copy-start.3
  0.7 0.9 %slice_bitcast_fusion = bf16[4,32,256]{2,1,0:T(8,128)(2,1)S(1)} fusion(bf16[4,8,32,256]{3,2,1,0:T(8,128)(2,1)} %param.6), kind=kLoop, calls=%fused_computation.43 | loop fusion | bytes 131072 | tf_op jit(solution)/shard_map/squeeze | solution.py:73
  1.6 4.9 %collective-permute-start = (bf16[4,32,256]{2,1,0:T(8,128)(2,1)S(1)}, bf16[4,32,256]{2,1,0:T(8,128)(2,1)S(1)}, u32[]{:S(2)}, u32[]{:S(2)}) collective-permute-start(bf16[4,32,256]{2,1,0:T(8,128)(2,1)S(1)} %slice_bitcast_fusion), channel_id=1, source_target_pairs={{0,4},{4,8},{8,12},{12,16},{16,20},{20,24},{24,28},{1,5},{5,9},{9,... | collective-permute-start | bytes 196616 | tf_op jit(solution)/shard_map/ppermute | solution.py:10
  6.4 2.2 %copy.89 = bf16[8,4,64,128]{3,0,1,2:T(8,128)(2,1)} copy(bf16[8,4,64,128]{3,2,1,0:T(8,128)(2,1)} %param.11) | data formatting | bytes 1048576 | tf_op args[5]
  8.6 3.5 %all-to-all-start.1 = ((bf16[8,4,64,128]{3,0,1,2:T(8,128)(2,1)}), bf16[8,4,64,128]{3,0,1,2:T(8,128)(2,1)S(1)}, u32[]{:S(2)}, u32[]{:S(2)}) async-start(bf16[8,4,64,128]{3,0,1,2:T(8,128)(2,1)} %copy.89), calls=%async_computation.1 | async-start | bytes 1048576 | tf_op jit(solution)/shard_map/all_to_all | solution.py:70
  12.1 0.0 copy-done.5
  12.2 0.0 copy-done.6
  12.2 0.1 fusion.50
  12.3 0.1 fusion.40
  12.4 0.0 copy-done.3
  12.4 0.1 copy.81
  12.6 0.1 fusion.52
  12.7 0.1 broadcast_and_fusion
  12.8 0.1 fusion.54
  12.9 0.0 collective-permute-done
  12.9 0.0 copy-done
  12.9 0.1 select_select_fusion
  13.1 2.4 %collective-permute-start.1 = (bf16[4,9,256]{2,0,1:T(4,128)(2,1)S(1)}, bf16[4,9,256]{2,0,1:T(4,128)(2,1)S(1)}, u32[]{:S(2)}, u32[]{:S(2)}) collective-permute-start(bf16[4,9,256]{2,0,1:T(4,128)(2,1)S(1)} %bitcast.102), channel_id=1, source_target_pairs={{0,1},{1,2},{2,3},{4,5},{5,6},{6,7},{8,9},{9,10},{10,11},{12,13},{... | collective-permute-start | bytes 55304 | tf_op jit(solution)/shard_map/ppermute | solution.py:10
  15.5 0.1 copy.102
  15.6 0.1 copy.104
  15.7 0.1 copy.106
  15.8 0.5 %collective-permute-done.1 = bf16[4,9,256]{2,0,1:T(4,128)(2,1)S(1)} collective-permute-done((bf16[4,9,256]{2,0,1:T(4,128)(2,1)S(1)}, bf16[4,9,256]{2,0,1:T(4,128)(2,1)S(1)}, u32[]{:S(2)}, u32[]{:S(2)}) %collective-permute-start.1) | collective-permute-done | bytes 18464 | tf_op jit(solution)/shard_map/ppermute | solution.py:10
  16.3 1.1 %convolution_convert_fusion = bf16[4,9,48,384]{3,2,1,0:T(8,128)(2,1)S(1)} fusion(bf16[4,9,32,256]{3,2,1,0:T(8,128)(2,1)S(1)} %select_select_fusion, pred[33]{0:T(512)(128)(4,1)S(1)} %get-tuple-element.7, pred[33]{0:T(512)(128)(4,1)S(1)} %get-tuple-element.6, bf16[4,9,256]{2,1,0:T(8,128)(2,1)S(1)} %copy.78, s32[384]{0:T(512)S(1)} %fusion.44, ...), kind=kOutput, calls=%fused_computation | convolution fusion | flops 279191040 | bytes 1940130 | tf_op jit(solution)/shard_map/cxjy,cxyk->cxjk/dot_general | solution.py:86
  17.7 0.2 copy.79
  17.9 0.0 copy-start.4
  18.0 0.5 %fusion.68 = (bf16[36,4,16,128]{3,2,1,0:T(8,128)(2,1)S(1)}, bf16[36,4,16,128]{3,2,1,0:T(8,128)(2,1)S(1)}, bf16[36,4,16,128]{3,2,1,0:T(8,128)(2,1)S(1)}) fusion(bf16[36,4,16,384]{3,2,1,0:T(8,128)(2,1)S(1)} %bitcast.99), kind=kLoop, calls=%fused_computation.114 | loop fusion | bytes 3538944 | tf_op jit(solution)/shard_map/slice | solution.py:96
  18.5 0.1 copy-done.4
  18.6 0.4 convolution_add_fusion.2
  19.1 0.5 convolution_add_fusion.1
  19.5 1.4 %all-to-all-done.1 = bf16[8,4,64,128]{3,0,1,2:T(8,128)(2,1)S(1)} async-done(((bf16[8,4,64,128]{3,0,1,2:T(8,128)(2,1)}), bf16[8,4,64,128]{3,0,1,2:T(8,128)(2,1)S(1)}, u32[]{:S(2)}, u32[]{:S(2)}) %all-to-all-start.1) | async-done | bytes 524320 | tf_op jit(solution)/shard_map/all_to_all | solution.py:70
  20.9 1.9 %fusion.66 = (f32[32]{0:T(128)S(1)}, bf16[32,4,16,128]{3,0,2,1:T(8,128)(2,1)S(1)}, bf16[32,4,16,128]{3,0,2,1:T(8,128)(2,1)}) fusion(pred[4,16]{1,0:T(4,128)(4,1)S(1)} %broadcast_and_fusion, f32[4,16,128,32]{2,3,1,0:T(8,128)S(1)} %convolution_add_fusion.1, bf16[32,36,1]{1,0,2:T(8,128)(2,1)S(1)} %copy.106, ...), kind=kOutput, calls=%fused_computation.113 | convolution fusion | flops 23592928 | bytes 3213760 | tf_op jit(solution)/shard_map/ok,kpqr->opqr/dot_general | solution.py:97
  22.8 0.5 convolution_bitcast_fusion
  23.2 0.0 copy-start.1
  23.2 0.5 convolution_bitcast_fusion.1
  23.7 0.5 convolution_bitcast_fusion.2
  24.2 0.1 copy.93
  24.3 0.1 copy.91
  24.4 0.1 copy.92
  24.5 0.1 pad_maximum_fusion.1
  24.6 2.6 %collective-permute-start.3 = (f32[32,109]{1,0:T(8,128)S(1)}, f32[32,109]{1,0:T(8,128)S(1)}, u32[]{:S(2)}, u32[]{:S(2)}) collective-permute-start(f32[32,109]{1,0:T(8,128)S(1)} %pad_maximum_fusion.1), channel_id=1, source_target_pairs={{0,16},{4,20},{8,24},{12,28},{16,0},{20,4},{24,8},{28,12},{1,17},{... | collective-permute-start | bytes 41864 | tf_op jit(solution)/shard_map/ppermute | solution.py:21
  27.2 1.3 %collective-permute-start.4 = (f32[32,109]{1,0:T(8,128)S(1)}, f32[32,109]{1,0:T(8,128)S(1)}, u32[]{:S(2)}, u32[]{:S(2)}) collective-permute-start(f32[32,109]{1,0:T(8,128)S(1)} %pad_maximum_fusion.1), channel_id=1, source_target_pairs={{0,24},{4,28},{8,16},{12,20},{16,8},{20,12},{24,0},{28,4},{1,25},{... | collective-permute-start | bytes 41864 | tf_op jit(solution)/shard_map/ppermute | solution.py:21
  28.5 0.2 collective-permute-start.2
  28.7 0.0 copy-done.1
  28.7 1.0 %copy.87 = bf16[32,4,16,128]{3,2,1,0:T(8,128)(2,1)} copy(bf16[32,4,16,128]{3,0,2,1:T(8,128)(2,1)S(1)} %copy-done.1) | data formatting | bytes 1048576 | tf_op jit(solution)/shard_map/convert_element_type | solution.py:101
  29.7 5.1 %all-to-all-start = ((bf16[32,4,16,128]{3,2,1,0:T(8,128)(2,1)}), bf16[32,4,16,128]{3,2,1,0:T(8,128)(2,1)S(1)}, u32[]{:S(2)}, u32[]{:S(2)}) async-start(bf16[32,4,16,128]{3,2,1,0:T(8,128)(2,1)} %copy.87), calls=%async_computation | async-start | bytes 1048576 | tf_op jit(solution)/shard_map/all_to_all | solution.py:106
  34.8 0.0 collective-permute-done.3
  34.8 0.0 collective-permute-done.4
  34.8 0.0 collective-permute-done.2
  34.8 0.1 add_add_fusion
  34.9 1.3 %collective-permute-start.5 = (f32[32,109]{1,0:T(8,128)S(1)}, f32[32,109]{1,0:T(8,128)S(1)}, u32[]{:S(2)}, u32[]{:S(2)}) collective-permute-start(f32[32,109]{1,0:T(8,128)S(1)} %add_add_fusion), channel_id=1, source_target_pairs={{0,4},{4,0},{8,12},{12,8},{16,20},{20,16},{24,28},{28,24},{1,5},{5... | collective-permute-start | bytes 41864 | tf_op jit(solution)/shard_map/ppermute | solution.py:21
  36.2 2.4 %collective-permute-done.5 = f32[32,109]{1,0:T(8,128)S(1)} collective-permute-done((f32[32,109]{1,0:T(8,128)S(1)}, f32[32,109]{1,0:T(8,128)S(1)}, u32[]{:S(2)}, u32[]{:S(2)}) %collective-permute-start.5) | collective-permute-done | bytes 13984 | tf_op jit(solution)/shard_map/ppermute | solution.py:21
  38.7 2.2 %collective-permute-start.6 = (f32[32,109]{1,0:T(8,128)S(1)}, f32[32,109]{1,0:T(8,128)S(1)}, u32[]{:S(2)}, u32[]{:S(2)}) collective-permute-start(f32[32,109]{1,0:T(8,128)S(1)} %add.112), channel_id=1, source_target_pairs={{0,2},{1,3},{2,0},{3,1},{4,6},{5,7},{6,4},{7,5},{8,10},{9,11},{10,... | collective-permute-start | bytes 41864 | tf_op jit(solution)/shard_map/ppermute | solution.py:21
  40.9 3.1 %collective-permute-done.6 = f32[32,109]{1,0:T(8,128)S(1)} collective-permute-done((f32[32,109]{1,0:T(8,128)S(1)}, f32[32,109]{1,0:T(8,128)S(1)}, u32[]{:S(2)}, u32[]{:S(2)}) %collective-permute-start.6) | collective-permute-done | bytes 13984 | tf_op jit(solution)/shard_map/ppermute | solution.py:21
  44.0 0.0 collective-permute-start.7
  44.0 1.2 %collective-permute-done.7 = f32[32,109]{1,0:T(8,128)S(1)} collective-permute-done((f32[32,109]{1,0:T(8,128)S(1)}, f32[32,109]{1,0:T(8,128)S(1)}, u32[]{:S(2)}, u32[]{:S(2)}) %collective-permute-start.7) | collective-permute-done | bytes 13984 | tf_op jit(solution)/shard_map/ppermute | solution.py:21
  45.2 0.0 copy-start.2
  45.2 0.7 %slice_reduce_fusion = f32[8]{0:T(128)} fusion(f32[8,109]{1,0:T(8,128)S(1)} %dynamic-slice_add_fusion), kind=kLoop, calls=%fused_computation.54 | loop fusion | bytes 64 | tf_op jit(solution)/shard_map/slice | solution.py:117
  45.9 0.0 all-to-all-done
  45.9 0.9 %copy.88 = bf16[8,4,4,16,128]{4,3,2,1,0:T(8,128)(2,1)} copy(bf16[8,4,4,16,128]{4,3,1,0,2:T(8,128)(2,1)S(1)} %bitcast.100) | data formatting | bytes 1048576 | tf_op jit(solution)/shard_map/all_to_all | solution.py:106
  46.7 0.0 copy-done.2
  (26 shorter events, 0.5 us)
Async XLA Ops:
  0.6 12.3 %copy-start = (bf16[4,8,32,256]{3,2,1,0:T(8,128)(2,1)S(1)}, bf16[4,8,32,256]{3,2,1,0:T(8,128)(2,1)}, u32[]{:S(2)}) copy-start(bf16[4,8,32,256]{3,2,1,0:T(8,128)(2,1)} %param.6) | copy-start | bytes 1572868
  0.6 11.5 %copy-start.5 = (s32[4]{0:T(128)S(1)}, s32[4]{0:T(128)}, u32[]{:S(2)}) copy-start(s32[4]{0:T(128)} %param.8) | copy-start | bytes 52
  0.7 11.5 %copy-start.6 = (s32[8]{0:T(128)S(1)}, s32[8]{0:T(128)}, u32[]{:S(2)}) copy-start(s32[8]{0:T(128)} %param.7) | copy-start | bytes 100
  0.7 11.8 %copy-start.3 = (bf16[32,108]{1,0:T(8,128)(2,1)S(1)}, bf16[32,108]{1,0:T(8,128)(2,1)}, u32[]{:S(2)}) copy-start(bf16[32,108]{1,0:T(8,128)(2,1)} %param.9) | copy-start | bytes 20740
  1.6 11.3 %collective-permute-start = (bf16[4,32,256]{2,1,0:T(8,128)(2,1)S(1)}, bf16[4,32,256]{2,1,0:T(8,128)(2,1)S(1)}, u32[]{:S(2)}, u32[]{:S(2)}) collective-permute-start(bf16[4,32,256]{2,1,0:T(8,128)(2,1)S(1)} %slice_bitcast_fusion), channel_id=1, source_target_pairs={{0,4},{4,8},{8,12},{12,16},{16,20},{20,24},{24,28},{1,5},{5,9},{9,... | collective-permute-start | bytes 196616 | tf_op jit(solution)/shard_map/ppermute | solution.py:10
  8.6 12.3 %all-to-all-start.1 = ((bf16[8,4,64,128]{3,0,1,2:T(8,128)(2,1)}), bf16[8,4,64,128]{3,0,1,2:T(8,128)(2,1)S(1)}, u32[]{:S(2)}, u32[]{:S(2)}) async-start(bf16[8,4,64,128]{3,0,1,2:T(8,128)(2,1)} %copy.89), calls=%async_computation.1 | async-start | bytes 1048576 | tf_op jit(solution)/shard_map/all_to_all | solution.py:70
  13.1 3.2 %collective-permute-start.1 = (bf16[4,9,256]{2,0,1:T(4,128)(2,1)S(1)}, bf16[4,9,256]{2,0,1:T(4,128)(2,1)S(1)}, u32[]{:S(2)}, u32[]{:S(2)}) collective-permute-start(bf16[4,9,256]{2,0,1:T(4,128)(2,1)S(1)} %bitcast.102), channel_id=1, source_target_pairs={{0,1},{1,2},{2,3},{4,5},{5,6},{6,7},{8,9},{9,10},{10,11},{12,13},{... | collective-permute-start | bytes 55304 | tf_op jit(solution)/shard_map/ppermute | solution.py:10
  17.9 0.7 %copy-start.4 = (f32[32]{0:T(128)S(1)}, f32[32]{0:T(128)}, u32[]{:S(2)}) copy-start(f32[32]{0:T(128)} %param.10) | copy-start | bytes 388
  23.2 5.5 %copy-start.1 = (bf16[32,4,16,128]{3,0,2,1:T(8,128)(2,1)S(1)}, bf16[32,4,16,128]{3,0,2,1:T(8,128)(2,1)}, u32[]{:S(2)}) copy-start(bf16[32,4,16,128]{3,0,2,1:T(8,128)(2,1)} %get-tuple-element.15) | copy-start | bytes 1572868
  24.6 10.2 %collective-permute-start.3 = (f32[32,109]{1,0:T(8,128)S(1)}, f32[32,109]{1,0:T(8,128)S(1)}, u32[]{:S(2)}, u32[]{:S(2)}) collective-permute-start(f32[32,109]{1,0:T(8,128)S(1)} %pad_maximum_fusion.1), channel_id=1, source_target_pairs={{0,16},{4,20},{8,24},{12,28},{16,0},{20,4},{24,8},{28,12},{1,17},{... | collective-permute-start | bytes 41864 | tf_op jit(solution)/shard_map/ppermute | solution.py:21
  27.2 7.7 %collective-permute-start.4 = (f32[32,109]{1,0:T(8,128)S(1)}, f32[32,109]{1,0:T(8,128)S(1)}, u32[]{:S(2)}, u32[]{:S(2)}) collective-permute-start(f32[32,109]{1,0:T(8,128)S(1)} %pad_maximum_fusion.1), channel_id=1, source_target_pairs={{0,24},{4,28},{8,16},{12,20},{16,8},{20,12},{24,0},{28,4},{1,25},{... | collective-permute-start | bytes 41864 | tf_op jit(solution)/shard_map/ppermute | solution.py:21
  28.5 6.3 %collective-permute-start.2 = (f32[32,109]{1,0:T(8,128)S(1)}, f32[32,109]{1,0:T(8,128)S(1)}, u32[]{:S(2)}, u32[]{:S(2)}) collective-permute-start(f32[32,109]{1,0:T(8,128)S(1)} %pad_maximum_fusion.1), channel_id=1, source_target_pairs={{0,8},{4,12},{8,0},{12,4},{16,24},{20,28},{24,16},{28,20},{1,9},{5... | collective-permute-start | bytes 41864 | tf_op jit(solution)/shard_map/ppermute | solution.py:21
  29.7 16.1 %all-to-all-start = ((bf16[32,4,16,128]{3,2,1,0:T(8,128)(2,1)}), bf16[32,4,16,128]{3,2,1,0:T(8,128)(2,1)S(1)}, u32[]{:S(2)}, u32[]{:S(2)}) async-start(bf16[32,4,16,128]{3,2,1,0:T(8,128)(2,1)} %copy.87), calls=%async_computation | async-start | bytes 1048576 | tf_op jit(solution)/shard_map/all_to_all | solution.py:106
  34.9 3.7 %collective-permute-start.5 = (f32[32,109]{1,0:T(8,128)S(1)}, f32[32,109]{1,0:T(8,128)S(1)}, u32[]{:S(2)}, u32[]{:S(2)}) collective-permute-start(f32[32,109]{1,0:T(8,128)S(1)} %add_add_fusion), channel_id=1, source_target_pairs={{0,4},{4,0},{8,12},{12,8},{16,20},{20,16},{24,28},{28,24},{1,5},{5... | collective-permute-start | bytes 41864 | tf_op jit(solution)/shard_map/ppermute | solution.py:21
  38.7 5.3 %collective-permute-start.6 = (f32[32,109]{1,0:T(8,128)S(1)}, f32[32,109]{1,0:T(8,128)S(1)}, u32[]{:S(2)}, u32[]{:S(2)}) collective-permute-start(f32[32,109]{1,0:T(8,128)S(1)} %add.112), channel_id=1, source_target_pairs={{0,2},{1,3},{2,0},{3,1},{4,6},{5,7},{6,4},{7,5},{8,10},{9,11},{10,... | collective-permute-start | bytes 41864 | tf_op jit(solution)/shard_map/ppermute | solution.py:21
  44.0 1.2 %collective-permute-start.7 = (f32[32,109]{1,0:T(8,128)S(1)}, f32[32,109]{1,0:T(8,128)S(1)}, u32[]{:S(2)}, u32[]{:S(2)}) collective-permute-start(f32[32,109]{1,0:T(8,128)S(1)} %add.113), channel_id=1, source_target_pairs={{0,1},{1,0},{2,3},{3,2},{4,5},{5,4},{6,7},{7,6},{8,9},{9,8},{10,11... | collective-permute-start | bytes 41864 | tf_op jit(solution)/shard_map/ppermute | solution.py:21
  45.2 1.6 %copy-start.2 = (f32[8,109]{1,0:T(8,128)}, f32[8,109]{1,0:T(8,128)S(1)}, u32[]{:S(2)}) copy-start(f32[8,109]{1,0:T(8,128)S(1)} %dynamic-slice_add_fusion) | copy-start | bytes 10468

commit v17 on v12

--- a/solution.py
+++ b/solution.py
@@ -89,12 +89,10 @@
     for off_x in range(3):
         for off_y in range(3):
             blocks.append(yztaps[:, off_x : off_x + 2 * half_x - 1 : 2, off_y * half_y : (off_y + 1) * half_y])
-    stacked = jnp.stack(blocks, axis=1).reshape(in_chans * 9, half_x, half_y, 3 * half_z)
-    kernel = weight.reshape(out_chans, in_chans * 9, 3)
-    conv = bias[:, None, None, None]
-    for off_z in range(3):
-        part = stacked[..., off_z * half_z : (off_z + 1) * half_z]
-        conv = conv + jnp.einsum("ok,kpqr->opqr", kernel[:, :, off_z], part, preferred_element_type=jnp.float32)
+    blocks = [b.reshape(b.shape[:3] + (3, half_z)).transpose(0, 3, 1, 2, 4) for b in blocks]
+    patches = jnp.stack(blocks, axis=1).reshape(in_chans * 27, half_x, half_y, half_z)
+    conv = jnp.einsum("ok,kpqr->opqr", weight, patches, preferred_element_type=jnp.float32)
+    conv = conv + bias[:, None, None, None]
     live = (row_ok[:, None] & col_ok[None, :]).reshape(1, half_x, half_y, 1)
     pre_wide = lax.reduce_precision(jnp.where(live, conv, 0.0), exponent_bits=8, mantissa_bits=7)
     sigma = jax.nn.sigmoid(pre_wide)
@@ -104,11 +102,7 @@
     grad_wide = lax.reduce_precision(grad_wide, exponent_bits=8, mantissa_bits=7)
     returned = grad_wide.astype(jnp.bfloat16)
     stem = lax.all_to_all(stem_local, "gy", split_axis=0, concat_axis=2, tiled=True)
-    grads = []
-    for off_z in range(3):
-        part = stacked[..., off_z * half_z : (off_z + 1) * half_z]
-        grads.append(jnp.einsum("opqr,kpqr->ok", returned, part, preferred_element_type=jnp.float32))
-    weight_full = jnp.stack(grads, axis=-1).reshape(out_chans, -1)
+    weight_full = jnp.einsum("opqr,kpqr->ok", returned, patches, preferred_element_type=jnp.float32)
     bias_full = jnp.sum(grad_wide, axis=(1, 2, 3))
     packed = jnp.concatenate([weight_full, bias_full[:, None]], axis=1)
     total = butterfly_sum(butterfly_sum(packed, "gx"), "gy")

time: 46.2 us -> 55.6 us (1.20)
  local copies, waits for them, and re-layouts: 7.6 us -> 16 us
  other arithmetic: 0.84 us -> 2.14 us
  waiting for transfers between devices: 7.66 us -> 6.58 us
  starting transfers between devices: 23.6 us -> 24.5 us
    unnamed x27 -> x17, local copies, waits for them, and re-layouts: 2.99 us -> 8.7 us
    another operation x3 -> x2, local copies, waits for them, and re-layouts: 0.32 us -> 2.97 us  [local(): jnp.stack(blocks, axis=1).reshape(in_chans * 27, half_x, half_y, half_z)]
    all_to_all x1, waiting for transfers between devices: 1.37 us -> 0.01 us  [local(): lax.all_to_all(grad_out, 'gy', split_axis=2, concat_axis=0, tiled=True)]
    sub x2, other arithmetic: 0.02 us -> 1.33 us  [count_masks(): ok = jnp.any(here & (half >= length // 2 - (counts // 2)[:, None]), axis=0)]
    all_to_all x1, starting transfers between devices: 3.47 us -> 4.13 us  [local(): lax.all_to_all(grad_out, 'gy', split_axis=2, concat_axis=0, tiled=True)]
    dot_general x6 -> x2, matrix products: 4.16 us -> 3.95 us  [the longest x1 2.81 us: local(): jnp.einsum('ok,kpqr->opqr', weight, patches, preferred_element_type=jnp.f...]
  transfers between devices with their start and end apart: 11 -> 11, of which waited for: 5 -> 4; matrix products, arithmetic and copies ran while one was open for 18% -> 31% of each run, Pallas kernels for 0% -> 0%
where the time goes in v17:
time: 55.6 us; the launch traced here: 55.2 us
  starting transfers between devices  24.5 us (44%)
  local copies, waits for them, and re-layouts  16 us (29%)
  waiting for transfers between devices  6.58 us (12%)
  matrix products  5.02 us (9%)
  other arithmetic  2.14 us (4%)
  between operations  0.85 us (2%)
    unnamed x17, local copies, waits for them, and re-layouts  8.7 us
    ppermute x7, starting transfers between devices, butterfly_sum(): lax.ppermute(value, axis, [(i, i ^ t) for i in range(size)])  7.83 us
    ppermute x2, starting transfers between devices, from_behind(): return lax.ppermute(block, axis, route)  7.21 us
    ppermute x7, waiting for transfers between devices, butterfly_sum(): lax.ppermute(value, axis, [(i, i ^ t) for i in range(size)])  5.77 us
    all_to_all x1, starting transfers between devices, local(): lax.all_to_all(stem_local, 'gy', split_axis=0, concat_axis=2, tiled=True)  5.36 us
    all_to_all x1, starting transfers between devices, local(): lax.all_to_all(grad_out, 'gy', split_axis=2, concat_axis=0, tiled=True)  4.13 us
    another operation x2, local copies, waits for them, and re-layouts, local(): jnp.stack(blocks, axis=1).reshape(in_chans * 27, half_x, half_y, half_z)  2.97 us
    dot_general x1, matrix products, local(): jnp.einsum('ok,kpqr->opqr', weight, patches, preferred_element_type=jnp.f...  2.81 us
  transfers between devices with their start and end apart: 11, of which 4 were waited for; matrix products, arithmetic and copies ran while one was open for 31% of the time, Pallas kernels for 0%

profile of v17, /device:TPU:0, one launch (start us, length us, event | category | flops | bytes accessed | tf_op | source)
XLA Modules:
  0.0 55.2 jit_solution(14699968664340894468)
XLA Ops:
  0.6 0.0 copy-start
  0.6 0.0 copy-start.1
  0.7 0.9 %slice_bitcast_fusion = bf16[4,32,256]{2,1,0:T(8,128)(2,1)S(1)} fusion(bf16[4,8,32,256]{3,2,1,0:T(8,128)(2,1)} %param.6), kind=kLoop, calls=%fused_computation.38 | loop fusion | bytes 131072 | tf_op jit(solution)/shard_map/squeeze | solution.py:73
  1.6 4.9 %collective-permute-start = (bf16[4,32,256]{2,1,0:T(8,128)(2,1)S(1)}, bf16[4,32,256]{2,1,0:T(8,128)(2,1)S(1)}, u32[]{:S(2)}, u32[]{:S(2)}) collective-permute-start(bf16[4,32,256]{2,1,0:T(8,128)(2,1)S(1)} %slice_bitcast_fusion), channel_id=1, source_target_pairs={{0,4},{4,8},{8,12},{12,16},{16,20},{20,24},{24,28},{1,5},{5,9},{9,... | collective-permute-start | bytes 196616 | tf_op jit(solution)/shard_map/ppermute | solution.py:10
  6.4 2.2 %copy.47 = bf16[8,4,64,128]{3,0,1,2:T(8,128)(2,1)} copy(bf16[8,4,64,128]{3,2,1,0:T(8,128)(2,1)} %param.11) | data formatting | bytes 1048576 | tf_op args[5]
  8.6 4.1 %all-to-all-start.1 = ((bf16[8,4,64,128]{3,0,1,2:T(8,128)(2,1)}), bf16[8,4,64,128]{3,0,1,2:T(8,128)(2,1)}, u32[]{:S(2)}, u32[]{:S(2)}) async-start(bf16[8,4,64,128]{3,0,1,2:T(8,128)(2,1)} %copy.47), calls=%async_computation.1 | async-start | bytes 1048576 | tf_op jit(solution)/shard_map/all_to_all | solution.py:70
  12.8 0.7 %fusion.69 = (s32[4]{0:T(128)S(1)}, s32[4]{0:T(128)S(1)}) fusion(s32[4]{0:T(128)} %param.8), kind=kLoop, calls=%fused_computation.97 | loop fusion | flops 68 | bytes 48 | tf_op jit(solution)/shard_map/sub | solution.py:47
  13.4 0.7 %fusion.70 = (s32[8]{0:T(128)S(1)}, s32[8]{0:T(128)S(1)}) fusion(s32[8]{0:T(128)} %param.7), kind=kLoop, calls=%fused_computation.99 | loop fusion | flops 136 | bytes 96 | tf_op jit(solution)/shard_map/sub | solution.py:47
  14.1 0.1 fusion.60
  14.2 0.1 fusion.50
  14.3 0.1 fusion.62
  14.4 0.1 broadcast_and_fusion
  14.5 0.1 fusion.64
  14.6 0.0 collective-permute-done
  14.6 0.1 select_select_fusion
  14.8 2.4 %collective-permute-start.1 = (bf16[4,9,256]{2,0,1:T(4,128)(2,1)S(1)}, bf16[4,9,256]{2,0,1:T(4,128)(2,1)S(1)}, u32[]{:S(2)}, u32[]{:S(2)}) collective-permute-start(bf16[4,9,256]{2,0,1:T(4,128)(2,1)S(1)} %bitcast.103), channel_id=1, source_target_pairs={{0,1},{1,2},{2,3},{4,5},{5,6},{6,7},{8,9},{9,10},{10,11},{12,13},{... | collective-permute-start | bytes 55304 | tf_op jit(solution)/shard_map/ppermute | solution.py:10
  17.2 0.8 %collective-permute-done.1 = bf16[4,9,256]{2,0,1:T(4,128)(2,1)S(1)} collective-permute-done((bf16[4,9,256]{2,0,1:T(4,128)(2,1)S(1)}, bf16[4,9,256]{2,0,1:T(4,128)(2,1)S(1)}, u32[]{:S(2)}, u32[]{:S(2)}) %collective-permute-start.1) | collective-permute-done | bytes 18464 | tf_op jit(solution)/shard_map/ppermute | solution.py:10
  18.0 1.1 %convolution_convert_fusion = bf16[4,9,48,384]{3,2,1,0:T(8,128)(2,1)S(1)} fusion(bf16[4,9,32,256]{3,2,1,0:T(8,128)(2,1)S(1)} %select_select_fusion, pred[33]{0:T(512)(128)(4,1)S(1)} %get-tuple-element.4, pred[33]{0:T(512)(128)(4,1)S(1)} %get-tuple-element.3, bf16[4,9,256]{2,1,0:T(8,128)(2,1)S(1)} %copy.42, s32[384]{0:T(512)S(1)} %fusion.54, ...), kind=kOutput, calls=%fused_computation.4 | convolution fusion | flops 279191040 | bytes 1940130 | tf_op jit(solution)/shard_map/cxjy,cxyk->cxjk/dot_general | solution.py:86
  19.1 0.2 fusion.75
  19.3 0.1 reshape.140
  19.4 0.8 %bitcast_dynamic-update-slice_fusion.8 = bf16[4,9,3,4,16,128]{5,2,4,3,0,1:T(4,128)(2,1)} fusion(bf16[4,4,16,3,128]{4,3,2,1,0:T(4,128)(2,1)S(1)} %reshape.140), kind=kLoop, calls=%fused_computation.35 | loop fusion | bytes 458752
  20.2 0.1 reshape.141
  20.2 0.1 reshape.142
  20.3 0.1 reshape.143
  20.4 0.1 reshape.144
  20.4 0.1 reshape.145
  20.5 0.1 reshape.146
  20.6 0.1 reshape.147
  20.6 0.1 reshape.148
  20.7 0.8 %bitcast_dynamic-update-slice_fusion.7 = bf16[4,9,3,4,16,128]{5,2,4,3,0,1:T(4,128)(2,1)} fusion(bf16[4,9,3,4,16,128]{5,2,4,3,0,1:T(4,128)(2,1)} %bitcast_dynamic-update-slice_fusion.8, bf16[4,4,16,3,128]{4,3,2,1,0:T(4,128)(2,1)S(1)} %reshape.141), kind=kLoop, calls=%fused_computation.34 | loop fusion | bytes 458752
  21.5 0.8 %bitcast_dynamic-update-slice_fusion.6 = bf16[4,9,3,4,16,128]{5,2,4,3,0,1:T(4,128)(2,1)} fusion(bf16[4,9,3,4,16,128]{5,2,4,3,0,1:T(4,128)(2,1)} %bitcast_dynamic-update-slice_fusion.7, bf16[4,4,16,3,128]{4,3,2,1,0:T(4,128)(2,1)S(1)} %reshape.142), kind=kLoop, calls=%fused_computation.33 | loop fusion | bytes 458752
  22.3 0.8 %bitcast_dynamic-update-slice_fusion.5 = bf16[4,9,3,4,16,128]{5,2,4,3,0,1:T(4,128)(2,1)} fusion(bf16[4,9,3,4,16,128]{5,2,4,3,0,1:T(4,128)(2,1)} %bitcast_dynamic-update-slice_fusion.6, bf16[4,4,16,3,128]{4,3,2,1,0:T(4,128)(2,1)S(1)} %reshape.143), kind=kLoop, calls=%fused_computation.32 | loop fusion | bytes 458752
  23.1 0.8 %bitcast_dynamic-update-slice_fusion.4 = bf16[4,9,3,4,16,128]{5,2,4,3,0,1:T(4,128)(2,1)} fusion(bf16[4,9,3,4,16,128]{5,2,4,3,0,1:T(4,128)(2,1)} %bitcast_dynamic-update-slice_fusion.5, bf16[4,4,16,3,128]{4,3,2,1,0:T(4,128)(2,1)S(1)} %reshape.144), kind=kLoop, calls=%fused_computation.31 | loop fusion | bytes 458752
  24.0 0.8 %bitcast_dynamic-update-slice_fusion.3 = bf16[4,9,3,4,16,128]{5,2,4,3,0,1:T(4,128)(2,1)} fusion(bf16[4,9,3,4,16,128]{5,2,4,3,0,1:T(4,128)(2,1)} %bitcast_dynamic-update-slice_fusion.4, bf16[4,4,16,3,128]{4,3,2,1,0:T(4,128)(2,1)S(1)} %reshape.145), kind=kLoop, calls=%fused_computation.30 | loop fusion | bytes 458752
  24.8 0.8 %bitcast_dynamic-update-slice_fusion.2 = bf16[4,9,3,4,16,128]{5,2,4,3,0,1:T(4,128)(2,1)} fusion(bf16[4,9,3,4,16,128]{5,2,4,3,0,1:T(4,128)(2,1)} %bitcast_dynamic-update-slice_fusion.3, bf16[4,4,16,3,128]{4,3,2,1,0:T(4,128)(2,1)S(1)} %reshape.146), kind=kLoop, calls=%fused_computation.29 | loop fusion | bytes 458752
  25.6 0.8 %bitcast_dynamic-update-slice_fusion.1 = bf16[4,9,3,4,16,128]{5,2,4,3,0,1:T(4,128)(2,1)} fusion(bf16[4,9,3,4,16,128]{5,2,4,3,0,1:T(4,128)(2,1)} %bitcast_dynamic-update-slice_fusion.2, bf16[4,4,16,3,128]{4,3,2,1,0:T(4,128)(2,1)S(1)} %reshape.147), kind=kLoop, calls=%fused_computation.28 | loop fusion | bytes 458752
  26.4 0.8 %bitcast_dynamic-update-slice_fusion = bf16[4,9,3,4,16,128]{5,2,4,3,0,1:T(4,128)(2,1)} fusion(bf16[4,9,3,4,16,128]{5,2,4,3,0,1:T(4,128)(2,1)} %bitcast_dynamic-update-slice_fusion.1, bf16[4,4,16,3,128]{4,3,2,1,0:T(4,128)(2,1)S(1)} %reshape.148), kind=kLoop, calls=%fused_computation.27 | loop fusion | bytes 458752 | tf_op jit(solution)/shard_map/stack | solution.py:93
  27.2 2.1 %copy.43 = bf16[4,9,3,4,16,128]{5,4,3,2,1,0:T(8,128)(2,1)S(1)} copy(bf16[4,9,3,4,16,128]{5,2,4,3,0,1:T(4,128)(2,1)} %bitcast_dynamic-update-slice_fusion) | data formatting | bytes 3538944 | tf_op jit(solution)/shard_map/stack | solution.py:93
  29.4 0.0 all-to-all-done.1
  29.4 2.8 %fusion.73 = (f32[32]{0:T(128)S(1)}, bf16[32,4,16,128]{3,0,2,1:T(8,128)(2,1)S(1)}, bf16[32,4,16,128]{3,0,2,1:T(8,128)(2,1)S(1)}) fusion(pred[4,16]{1,0:T(4,128)(4,1)S(1)} %broadcast_and_fusion, f32[32]{0:T(128)S(1)} %copy-done.3, bf16[32,108]{1,0:T(8,128)(2,1)S(1)} %copy-done, bf16[108,4,16,128]{3,2,1,0:T(8,128)(2,1)S(1)} %bitcast.99, ...), kind=kOutput, calls=%fused_computation.104 | convolution fusion | flops 61341664 | bytes 3349568 | tf_op jit(solution)/shard_map/ok,kpqr->opqr/dot_general | solution.py:94
  32.2 0.1 copy.50
  32.3 1.1 %fusion.16 = f32[32,108]{1,0:T(8,128)S(1)} fusion(bf16[108,4,16,128]{3,2,1,0:T(8,128)(2,1)S(1)} %bitcast.100, bf16[32,4,16,128]{3,0,2,1:T(8,128)(2,1)S(1)} %get-tuple-element.8), kind=kOutput, calls=%fused_computation.10 | convolution fusion | flops 56623104 | bytes 2307584 | tf_op jit(solution)/shard_map/opqr,kpqr->ok/dot_general | solution.py:105
  33.5 0.1 pad_maximum_fusion
  33.5 2.6 %collective-permute-start.3 = (f32[32,109]{1,0:T(8,128)S(1)}, f32[32,109]{1,0:T(8,128)S(1)}, u32[]{:S(2)}, u32[]{:S(2)}) collective-permute-start(f32[32,109]{1,0:T(8,128)S(1)} %pad_maximum_fusion), channel_id=1, source_target_pairs={{0,16},{4,20},{8,24},{12,28},{16,0},{20,4},{24,8},{28,12},{1,17},{... | collective-permute-start | bytes 41864 | tf_op jit(solution)/shard_map/ppermute | solution.py:21
  36.1 1.4 %collective-permute-start.4 = (f32[32,109]{1,0:T(8,128)S(1)}, f32[32,109]{1,0:T(8,128)S(1)}, u32[]{:S(2)}, u32[]{:S(2)}) collective-permute-start(f32[32,109]{1,0:T(8,128)S(1)} %pad_maximum_fusion), channel_id=1, source_target_pairs={{0,24},{4,28},{8,16},{12,20},{16,8},{20,12},{24,0},{28,4},{1,25},{... | collective-permute-start | bytes 41864 | tf_op jit(solution)/shard_map/ppermute | solution.py:21
  37.5 0.2 collective-permute-start.2
  37.7 1.0 %copy.45 = bf16[32,4,16,128]{3,2,1,0:T(8,128)(2,1)} copy(bf16[32,4,16,128]{3,0,2,1:T(8,128)(2,1)S(1)} %get-tuple-element.18) | data formatting | bytes 1048576 | tf_op jit(solution)/shard_map/convert_element_type | solution.py:99
  38.7 5.4 %all-to-all-start = ((bf16[32,4,16,128]{3,2,1,0:T(8,128)(2,1)}), bf16[32,4,16,128]{3,2,1,0:T(8,128)(2,1)S(1)}, u32[]{:S(2)}, u32[]{:S(2)}) async-start(bf16[32,4,16,128]{3,2,1,0:T(8,128)(2,1)} %copy.45), calls=%async_computation | async-start | bytes 1048576 | tf_op jit(solution)/shard_map/all_to_all | solution.py:104
  44.1 0.0 collective-permute-done.3
  44.1 0.0 collective-permute-done.4
  44.1 0.0 collective-permute-done.2
  44.1 0.1 add_add_fusion
  44.2 1.3 %collective-permute-start.5 = (f32[32,109]{1,0:T(8,128)S(1)}, f32[32,109]{1,0:T(8,128)S(1)}, u32[]{:S(2)}, u32[]{:S(2)}) collective-permute-start(f32[32,109]{1,0:T(8,128)S(1)} %add_add_fusion), channel_id=1, source_target_pairs={{0,4},{4,0},{8,12},{12,8},{16,20},{20,16},{24,28},{28,24},{1,5},{5... | collective-permute-start | bytes 41864 | tf_op jit(solution)/shard_map/ppermute | solution.py:21
  45.5 2.4 %collective-permute-done.5 = f32[32,109]{1,0:T(8,128)S(1)} collective-permute-done((f32[32,109]{1,0:T(8,128)S(1)}, f32[32,109]{1,0:T(8,128)S(1)}, u32[]{:S(2)}, u32[]{:S(2)}) %collective-permute-start.5) | collective-permute-done | bytes 13984 | tf_op jit(solution)/shard_map/ppermute | solution.py:21
  47.9 0.9 %collective-permute-start.8 = (f32[32,109]{1,0:T(8,128)S(1)}, f32[32,109]{1,0:T(8,128)S(1)}, u32[]{:S(2)}, u32[]{:S(2)}) collective-permute-start(f32[32,109]{1,0:T(8,128)S(1)} %add.105), channel_id=1, source_target_pairs={{0,3},{1,2},{2,1},{3,0},{4,7},{5,6},{6,5},{7,4},{8,11},{9,10},{10,... | collective-permute-start | bytes 41864 | tf_op jit(solution)/shard_map/ppermute | solution.py:21
  48.8 1.4 %collective-permute-start.7 = (f32[32,109]{1,0:T(8,128)S(1)}, f32[32,109]{1,0:T(8,128)S(1)}, u32[]{:S(2)}, u32[]{:S(2)}) collective-permute-start(f32[32,109]{1,0:T(8,128)S(1)} %add.105), channel_id=1, source_target_pairs={{0,2},{1,3},{2,0},{3,1},{4,6},{5,7},{6,4},{7,5},{8,10},{9,11},{10,... | collective-permute-start | bytes 41864 | tf_op jit(solution)/shard_map/ppermute | solution.py:21
  50.2 0.0 collective-permute-start.6
  50.3 2.2 %collective-permute-done.8 = f32[32,109]{1,0:T(8,128)S(1)} collective-permute-done((f32[32,109]{1,0:T(8,128)S(1)}, f32[32,109]{1,0:T(8,128)S(1)}, u32[]{:S(2)}, u32[]{:S(2)}) %collective-permute-start.8) | collective-permute-done | bytes 13984 | tf_op jit(solution)/shard_map/ppermute | solution.py:21
  52.5 1.1 %collective-permute-done.7 = f32[32,109]{1,0:T(8,128)S(1)} collective-permute-done((f32[32,109]{1,0:T(8,128)S(1)}, f32[32,109]{1,0:T(8,128)S(1)}, u32[]{:S(2)}, u32[]{:S(2)}) %collective-permute-start.7) | collective-permute-done | bytes 13984 | tf_op jit(solution)/shard_map/ppermute | solution.py:21
  53.6 0.0 collective-permute-done.6
  53.6 0.0 copy-start.2
  53.6 0.7 %slice_reduce_fusion = f32[8]{0:T(128)} fusion(f32[8,109]{1,0:T(8,128)S(1)} %fusion.44), kind=kLoop, calls=%fused_computation.48 | loop fusion | bytes 64 | tf_op jit(solution)/shard_map/slice | solution.py:111
  54.3 0.0 all-to-all-done
  54.3 0.9 %copy.46 = bf16[8,4,4,16,128]{4,3,2,1,0:T(8,128)(2,1)} copy(bf16[8,4,4,16,128]{4,3,1,0,2:T(8,128)(2,1)S(1)} %bitcast.101) | data formatting | bytes 1048576 | tf_op jit(solution)/shard_map/all_to_all | solution.py:104
  (15 shorter events, 0.1 us)
Async XLA Ops:
  0.6 28.8 %copy-start = (bf16[32,108]{1,0:T(8,128)(2,1)S(1)}, bf16[32,108]{1,0:T(8,128)(2,1)}, u32[]{:S(2)}) copy-start(bf16[32,108]{1,0:T(8,128)(2,1)} %param.9) | copy-start | bytes 20740
  0.6 14.0 %copy-start.1 = (bf16[4,8,32,256]{3,2,1,0:T(8,128)(2,1)S(1)}, bf16[4,8,32,256]{3,2,1,0:T(8,128)(2,1)}, u32[]{:S(2)}) copy-start(bf16[4,8,32,256]{3,2,1,0:T(8,128)(2,1)} %param.6) | copy-start | bytes 1572868
  1.6 13.0 %collective-permute-start = (bf16[4,32,256]{2,1,0:T(8,128)(2,1)S(1)}, bf16[4,32,256]{2,1,0:T(8,128)(2,1)S(1)}, u32[]{:S(2)}, u32[]{:S(2)}) collective-permute-start(bf16[4,32,256]{2,1,0:T(8,128)(2,1)S(1)} %slice_bitcast_fusion), channel_id=1, source_target_pairs={{0,4},{4,8},{8,12},{12,16},{16,20},{20,24},{24,28},{1,5},{5,9},{9,... | collective-permute-start | bytes 196616 | tf_op jit(solution)/shard_map/ppermute | solution.py:10
  8.6 20.8 %all-to-all-start.1 = ((bf16[8,4,64,128]{3,0,1,2:T(8,128)(2,1)}), bf16[8,4,64,128]{3,0,1,2:T(8,128)(2,1)}, u32[]{:S(2)}, u32[]{:S(2)}) async-start(bf16[8,4,64,128]{3,0,1,2:T(8,128)(2,1)} %copy.47), calls=%async_computation.1 | async-start | bytes 1048576 | tf_op jit(solution)/shard_map/all_to_all | solution.py:70
  14.8 3.2 %collective-permute-start.1 = (bf16[4,9,256]{2,0,1:T(4,128)(2,1)S(1)}, bf16[4,9,256]{2,0,1:T(4,128)(2,1)S(1)}, u32[]{:S(2)}, u32[]{:S(2)}) collective-permute-start(bf16[4,9,256]{2,0,1:T(4,128)(2,1)S(1)} %bitcast.103), channel_id=1, source_target_pairs={{0,1},{1,2},{2,3},{4,5},{5,6},{6,7},{8,9},{9,10},{10,11},{12,13},{... | collective-permute-start | bytes 55304 | tf_op jit(solution)/shard_map/ppermute | solution.py:10
  26.4 3.0 %copy-start.3 = (f32[32]{0:T(128)S(1)}, f32[32]{0:T(128)}, u32[]{:S(2)}) copy-start(f32[32]{0:T(128)} %param.10) | copy-start | bytes 388
  33.5 10.5 %collective-permute-start.3 = (f32[32,109]{1,0:T(8,128)S(1)}, f32[32,109]{1,0:T(8,128)S(1)}, u32[]{:S(2)}, u32[]{:S(2)}) collective-permute-start(f32[32,109]{1,0:T(8,128)S(1)} %pad_maximum_fusion), channel_id=1, source_target_pairs={{0,16},{4,20},{8,24},{12,28},{16,0},{20,4},{24,8},{28,12},{1,17},{... | collective-permute-start | bytes 41864 | tf_op jit(solution)/shard_map/ppermute | solution.py:21
  36.1 7.9 %collective-permute-start.4 = (f32[32,109]{1,0:T(8,128)S(1)}, f32[32,109]{1,0:T(8,128)S(1)}, u32[]{:S(2)}, u32[]{:S(2)}) collective-permute-start(f32[32,109]{1,0:T(8,128)S(1)} %pad_maximum_fusion), channel_id=1, source_target_pairs={{0,24},{4,28},{8,16},{12,20},{16,8},{20,12},{24,0},{28,4},{1,25},{... | collective-permute-start | bytes 41864 | tf_op jit(solution)/shard_map/ppermute | solution.py:21
  37.5 6.6 %collective-permute-start.2 = (f32[32,109]{1,0:T(8,128)S(1)}, f32[32,109]{1,0:T(8,128)S(1)}, u32[]{:S(2)}, u32[]{:S(2)}) collective-permute-start(f32[32,109]{1,0:T(8,128)S(1)} %pad_maximum_fusion), channel_id=1, source_target_pairs={{0,8},{4,12},{8,0},{12,4},{16,24},{20,28},{24,16},{28,20},{1,9},{5... | collective-permute-start | bytes 41864 | tf_op jit(solution)/shard_map/ppermute | solution.py:21
  38.7 15.6 %all-to-all-start = ((bf16[32,4,16,128]{3,2,1,0:T(8,128)(2,1)}), bf16[32,4,16,128]{3,2,1,0:T(8,128)(2,1)S(1)}, u32[]{:S(2)}, u32[]{:S(2)}) async-start(bf16[32,4,16,128]{3,2,1,0:T(8,128)(2,1)} %copy.45), calls=%async_computation | async-start | bytes 1048576 | tf_op jit(solution)/shard_map/all_to_all | solution.py:104
  44.2 3.7 %collective-permute-start.5 = (f32[32,109]{1,0:T(8,128)S(1)}, f32[32,109]{1,0:T(8,128)S(1)}, u32[]{:S(2)}, u32[]{:S(2)}) collective-permute-start(f32[32,109]{1,0:T(8,128)S(1)} %add_add_fusion), channel_id=1, source_target_pairs={{0,4},{4,0},{8,12},{12,8},{16,20},{20,16},{24,28},{28,24},{1,5},{5... | collective-permute-start | bytes 41864 | tf_op jit(solution)/shard_map/ppermute | solution.py:21
  47.9 4.6 %collective-permute-start.8 = (f32[32,109]{1,0:T(8,128)S(1)}, f32[32,109]{1,0:T(8,128)S(1)}, u32[]{:S(2)}, u32[]{:S(2)}) collective-permute-start(f32[32,109]{1,0:T(8,128)S(1)} %add.105), channel_id=1, source_target_pairs={{0,3},{1,2},{2,1},{3,0},{4,7},{5,6},{6,5},{7,4},{8,11},{9,10},{10,... | collective-permute-start | bytes 41864 | tf_op jit(solution)/shard_map/ppermute | solution.py:21
  48.8 4.8 %collective-permute-start.7 = (f32[32,109]{1,0:T(8,128)S(1)}, f32[32,109]{1,0:T(8,128)S(1)}, u32[]{:S(2)}, u32[]{:S(2)}) collective-permute-start(f32[32,109]{1,0:T(8,128)S(1)} %add.105), channel_id=1, source_target_pairs={{0,2},{1,3},{2,0},{3,1},{4,6},{5,7},{6,4},{7,5},{8,10},{9,11},{10,... | collective-permute-start | bytes 41864 | tf_op jit(solution)/shard_map/ppermute | solution.py:21
  50.2 3.4 %collective-permute-start.6 = (f32[32,109]{1,0:T(8,128)S(1)}, f32[32,109]{1,0:T(8,128)S(1)}, u32[]{:S(2)}, u32[]{:S(2)}) collective-permute-start(f32[32,109]{1,0:T(8,128)S(1)} %add.105), channel_id=1, source_target_pairs={{0,1},{1,0},{2,3},{3,2},{4,5},{5,4},{6,7},{7,6},{8,9},{9,8},{10,11... | collective-permute-start | bytes 41864 | tf_op jit(solution)/shard_map/ppermute | solution.py:21
  53.6 1.6 %copy-start.2 = (f32[8,109]{1,0:T(8,128)}, f32[8,109]{1,0:T(8,128)S(1)}, u32[]{:S(2)}) copy-start(f32[8,109]{1,0:T(8,128)S(1)} %fusion.44) | copy-start | bytes 10468

commit v18 on v12

--- a/solution.py
+++ b/solution.py
@@ -98,7 +98,8 @@
     live = (row_ok[:, None] & col_ok[None, :]).reshape(1, half_x, half_y, 1)
     pre_wide = lax.reduce_precision(jnp.where(live, conv, 0.0), exponent_bits=8, mantissa_bits=7)
     sigma = jax.nn.sigmoid(pre_wide)
-    stem_local = (pre_wide * sigma).astype(jnp.bfloat16)
+    pre_out = lax.reduce_precision(jnp.where(live, lax.optimization_barrier(conv), 0.0), exponent_bits=8, mantissa_bits=7)
+    stem_local = (pre_out * jax.nn.sigmoid(pre_out)).astype(jnp.bfloat16)
     slope = sigma * (1.0 + pre_wide * (1.0 - sigma))
     grad_wide = jnp.where(live, cell_grad.astype(jnp.float32) * slope, 0.0)
     grad_wide = lax.reduce_precision(grad_wide, exponent_bits=8, mantissa_bits=7)

time: 46.2 us -> 46.5 us (level)
  starting transfers between devices: 23.6 us -> 25.3 us
  matrix products: 5.23 us -> 3.85 us
  waiting for transfers between devices: 7.66 us -> 6.75 us
  other arithmetic: 0.84 us -> 1.72 us
    dot_general x3, matrix products: 2.78 us -> 1.35 us  [local(): jnp.einsum('ok,kpqr->opqr', kernel[:, :, off_z], part, preferred_element_...]
    ppermute x7, starting transfers between devices: 7.84 us -> 9.09 us  [butterfly_sum(): lax.ppermute(value, axis, [(i, i ^ t) for i in range(size)])]
    reduce_sum x0 -> x1, other arithmetic: none -> 0.77 us  [local(): bias_full = jnp.sum(grad_wide, axis=(1, 2, 3))]
    all_to_all x1, waiting for transfers between devices: 1.37 us -> 0.9 us  [local(): lax.all_to_all(grad_out, 'gy', split_axis=2, concat_axis=0, tiled=True)]
    unnamed x27 -> x25, local copies, waits for them, and re-layouts: 2.99 us -> 2.97 us
  transfers between devices with their start and end apart: 11 -> 11, of which waited for: 5 -> 5; matrix products, arithmetic and copies ran while one was open for 18% -> 19% of each run, Pallas kernels for 0% -> 0%
where the time goes in v18:
time: 46.5 us; the launch traced here: 46.2 us
  starting transfers between devices  25.3 us (54%)
  local copies, waits for them, and re-layouts  7.59 us (16%)
  waiting for transfers between devices  6.75 us (15%)
  matrix products  3.85 us (8%)
  other arithmetic  1.72 us (4%)
  between operations  1 us (2%)
    ppermute x7, starting transfers between devices, butterfly_sum(): lax.ppermute(value, axis, [(i, i ^ t) for i in range(size)])  9.09 us
    ppermute x2, starting transfers between devices, from_behind(): return lax.ppermute(block, axis, route)  7.22 us
    all_to_all x1, starting transfers between devices, local(): lax.all_to_all(stem_local, 'gy', split_axis=0, concat_axis=2, tiled=True)  5.52 us
    ppermute x7, waiting for transfers between devices, butterfly_sum(): lax.ppermute(value, axis, [(i, i ^ t) for i in range(size)])  5.31 us
    all_to_all x1, starting transfers between devices, local(): lax.all_to_all(grad_out, 'gy', split_axis=2, concat_axis=0, tiled=True)  3.47 us
    unnamed x25, local copies, waits for them, and re-layouts  2.97 us
    dot_general x3, matrix products, local(): jnp.einsum('opqr,kpqr->ok', returned, part, preferred_element_type=jnp.fl...  1.43 us
    dot_general x3, matrix products, local(): jnp.einsum('ok,kpqr->opqr', kernel[:, :, off_z], part, preferred_element_...  1.35 us
  transfers between devices with their start and end apart: 11, of which 5 were waited for; matrix products, arithmetic and copies ran while one was open for 19% of the time, Pallas kernels for 0%

profile of v18, /device:TPU:0, one launch (start us, length us, event | category | flops | bytes accessed | tf_op | source)
XLA Modules:
  0.0 46.2 jit_solution(4903376820159028977)
XLA Ops:
  0.6 0.0 copy-start
  0.6 0.0 copy-start.4
  0.7 0.0 copy-start.5
  0.7 0.0 copy-start.2
  0.7 0.9 %slice_bitcast_fusion = bf16[4,32,256]{2,1,0:T(8,128)(2,1)S(1)} fusion(bf16[4,8,32,256]{3,2,1,0:T(8,128)(2,1)} %param.6), kind=kLoop, calls=%fused_computation.40 | loop fusion | bytes 131072 | tf_op jit(solution)/shard_map/squeeze | solution.py:73
  1.6 4.9 %collective-permute-start = (bf16[4,32,256]{2,1,0:T(8,128)(2,1)S(1)}, bf16[4,32,256]{2,1,0:T(8,128)(2,1)S(1)}, u32[]{:S(2)}, u32[]{:S(2)}) collective-permute-start(bf16[4,32,256]{2,1,0:T(8,128)(2,1)S(1)} %slice_bitcast_fusion), channel_id=1, source_target_pairs={{0,4},{4,8},{8,12},{12,16},{16,20},{20,24},{24,28},{1,5},{5,9},{9,... | collective-permute-start | bytes 196616 | tf_op jit(solution)/shard_map/ppermute | solution.py:10
  6.4 2.2 %copy.89 = bf16[8,4,64,128]{3,0,1,2:T(8,128)(2,1)} copy(bf16[8,4,64,128]{3,2,1,0:T(8,128)(2,1)} %param.11) | data formatting | bytes 1048576 | tf_op args[5]
  8.6 3.5 %all-to-all-start.1 = ((bf16[8,4,64,128]{3,0,1,2:T(8,128)(2,1)}), bf16[8,4,64,128]{3,0,1,2:T(8,128)(2,1)S(1)}, u32[]{:S(2)}, u32[]{:S(2)}) async-start(bf16[8,4,64,128]{3,0,1,2:T(8,128)(2,1)} %copy.89), calls=%async_computation.1 | async-start | bytes 1048576 | tf_op jit(solution)/shard_map/all_to_all | solution.py:70
  12.1 0.0 copy-done.4
  12.2 0.0 copy-done.5
  12.2 0.0 copy-done.2
  12.2 0.1 copy.81
  12.4 0.1 fusion.39
  12.5 0.1 fusion.49
  12.6 0.1 fusion.51
  12.7 0.1 broadcast_and_fusion
  12.8 0.1 fusion.53
  12.9 0.0 collective-permute-done
  12.9 0.0 copy-done
  12.9 0.1 select_select_fusion
  13.1 2.4 %collective-permute-start.1 = (bf16[4,9,256]{2,0,1:T(4,128)(2,1)S(1)}, bf16[4,9,256]{2,0,1:T(4,128)(2,1)S(1)}, u32[]{:S(2)}, u32[]{:S(2)}) collective-permute-start(bf16[4,9,256]{2,0,1:T(4,128)(2,1)S(1)} %bitcast.99), channel_id=1, source_target_pairs={{0,1},{1,2},{2,3},{4,5},{5,6},{6,7},{8,9},{9,10},{10,11},{12,13},{... | collective-permute-start | bytes 55304 | tf_op jit(solution)/shard_map/ppermute | solution.py:10
  15.5 0.1 copy.102
  15.6 0.1 copy.104
  15.7 0.1 copy.106
  15.8 0.5 %collective-permute-done.1 = bf16[4,9,256]{2,0,1:T(4,128)(2,1)S(1)} collective-permute-done((bf16[4,9,256]{2,0,1:T(4,128)(2,1)S(1)}, bf16[4,9,256]{2,0,1:T(4,128)(2,1)S(1)}, u32[]{:S(2)}, u32[]{:S(2)}) %collective-permute-start.1) | collective-permute-done | bytes 18464 | tf_op jit(solution)/shard_map/ppermute | solution.py:10
  16.3 1.1 %convolution_convert_fusion = bf16[4,9,48,384]{3,2,1,0:T(8,128)(2,1)S(1)} fusion(bf16[4,9,32,256]{3,2,1,0:T(8,128)(2,1)S(1)} %select_select_fusion, pred[33]{0:T(512)(128)(4,1)S(1)} %get-tuple-element.7, pred[33]{0:T(512)(128)(4,1)S(1)} %get-tuple-element.6, bf16[4,9,256]{2,1,0:T(8,128)(2,1)S(1)} %copy.78, s32[384]{0:T(512)S(1)} %fusion.43, ...), kind=kOutput, calls=%fused_computation | convolution fusion | flops 279191040 | bytes 1940130 | tf_op jit(solution)/shard_map/cxjy,cxyk->cxjk/dot_general | solution.py:86
  17.8 0.2 copy.79
  17.9 0.0 copy-start.3
  18.0 0.5 %fusion.67 = (bf16[36,4,16,128]{3,2,1,0:T(8,128)(2,1)S(1)}, bf16[36,4,16,128]{3,2,1,0:T(8,128)(2,1)S(1)}, bf16[36,4,16,128]{3,2,1,0:T(8,128)(2,1)S(1)}) fusion(bf16[36,4,16,384]{3,2,1,0:T(8,128)(2,1)S(1)} %bitcast.96), kind=kLoop, calls=%fused_computation.113 | loop fusion | bytes 3538944 | tf_op jit(solution)/shard_map/slice | solution.py:96
  18.5 0.1 copy-done.3
  18.6 0.4 convolution_add_fusion.2
  19.1 0.5 convolution_add_fusion.1
  19.5 0.5 fusion
  20.0 0.9 %all-to-all-done.1 = bf16[8,4,64,128]{3,0,1,2:T(8,128)(2,1)S(1)} async-done(((bf16[8,4,64,128]{3,0,1,2:T(8,128)(2,1)}), bf16[8,4,64,128]{3,0,1,2:T(8,128)(2,1)S(1)}, u32[]{:S(2)}, u32[]{:S(2)}) %all-to-all-start.1) | async-done | bytes 524320 | tf_op jit(solution)/shard_map/all_to_all | solution.py:70
  20.9 0.1 bitcast_convert_fusion
  21.0 0.8 %fusion.65 = (f32[32]{0:T(128)S(1)}, bf16[32,4,16,128]{3,0,2,1:T(8,128)(2,1)S(1)}, bf16[32,4,16,128]{3,0,2,1:T(8,128)(2,1)S(1)}) fusion(f32[32,4,16,128]{3,0,2,1:T(8,128)S(1)} %fusion, f32[8,4,4,16,128]{4,0,1,3,2:T(8,128)S(1)} %bitcast_convert_fusion, pred[4,16]{1,0:T(4,128)(4,1)S(1)} %broadcast_and_fusion), kind=kLoop, calls=%fused_computation.112 | loop fusion | flops 5504992 | bytes 3145920 | tf_op jit(solution)/shard_map/reduce_sum | solution.py:113
  21.8 0.5 %convolution_bitcast_fusion.2 = f32[32,36,1]{1,0,2:T(8,128)S(1)} fusion(bf16[36,4,16,128]{3,2,1,0:T(8,128)(2,1)S(1)} %get-tuple-element.14, bf16[32,4,16,128]{3,0,2,1:T(8,128)(2,1)S(1)} %get-tuple-element.11), kind=kOutput, calls=%fused_computation.8 | convolution fusion | flops 18874368 | bytes 1118720 | tf_op jit(solution)/shard_map/opqr,kpqr->ok/dot_general | solution.py:111
  22.2 0.5 %convolution_bitcast_fusion.1 = f32[32,36,1]{1,0,2:T(8,128)S(1)} fusion(bf16[36,4,16,128]{3,2,1,0:T(8,128)(2,1)S(1)} %get-tuple-element.13, bf16[32,4,16,128]{3,0,2,1:T(8,128)(2,1)S(1)} %get-tuple-element.11), kind=kOutput, calls=%fused_computation.7 | convolution fusion | flops 18874368 | bytes 1118720 | tf_op jit(solution)/shard_map/opqr,kpqr->ok/dot_general | solution.py:111
  22.7 0.5 %convolution_bitcast_fusion = f32[32,36,1]{1,0,2:T(8,128)S(1)} fusion(bf16[36,4,16,128]{3,2,1,0:T(8,128)(2,1)S(1)} %get-tuple-element.12, bf16[32,4,16,128]{3,0,2,1:T(8,128)(2,1)S(1)} %get-tuple-element.11), kind=kOutput, calls=%fused_computation.6 | convolution fusion | flops 18874368 | bytes 1118720 | tf_op jit(solution)/shard_map/opqr,kpqr->ok/dot_general | solution.py:111
  23.2 0.1 copy.91
  23.4 0.1 copy.92
  23.4 0.1 copy.93
  23.5 0.1 pad_maximum_fusion.1
  23.6 1.6 %collective-permute-start.2 = (f32[32,109]{1,0:T(8,128)S(1)}, f32[32,109]{1,0:T(8,128)S(1)}, u32[]{:S(2)}, u32[]{:S(2)}) collective-permute-start(f32[32,109]{1,0:T(8,128)S(1)} %pad_maximum_fusion.1), channel_id=1, source_target_pairs={{0,8},{4,12},{8,0},{12,4},{16,24},{20,28},{24,16},{28,20},{1,9},{5... | collective-permute-start | bytes 41864 | tf_op jit(solution)/shard_map/ppermute | solution.py:21
  25.2 2.6 %collective-permute-start.3 = (f32[32,109]{1,0:T(8,128)S(1)}, f32[32,109]{1,0:T(8,128)S(1)}, u32[]{:S(2)}, u32[]{:S(2)}) collective-permute-start(f32[32,109]{1,0:T(8,128)S(1)} %pad_maximum_fusion.1), channel_id=1, source_target_pairs={{0,16},{4,20},{8,24},{12,28},{16,0},{20,4},{24,8},{28,12},{1,17},{... | collective-permute-start | bytes 41864 | tf_op jit(solution)/shard_map/ppermute | solution.py:21
  27.8 0.2 collective-permute-start.4
  28.0 1.0 %copy.87 = bf16[32,4,16,128]{3,2,1,0:T(8,128)(2,1)} copy(bf16[32,4,16,128]{3,0,2,1:T(8,128)(2,1)S(1)} %get-tuple-element.18) | data formatting | bytes 1048576 | tf_op jit(solution)/shard_map/convert_element_type | solution.py:102
  29.0 5.5 %all-to-all-start = ((bf16[32,4,16,128]{3,2,1,0:T(8,128)(2,1)}), bf16[32,4,16,128]{3,2,1,0:T(8,128)(2,1)S(1)}, u32[]{:S(2)}, u32[]{:S(2)}) async-start(bf16[32,4,16,128]{3,2,1,0:T(8,128)(2,1)} %copy.87), calls=%async_computation | async-start | bytes 1048576 | tf_op jit(solution)/shard_map/all_to_all | solution.py:107
  34.5 0.0 collective-permute-done.2
  34.5 0.0 collective-permute-done.3
  34.5 0.0 collective-permute-done.4
  34.5 0.1 add_add_fusion
  34.6 1.6 %collective-permute-start.5 = (f32[32,109]{1,0:T(8,128)S(1)}, f32[32,109]{1,0:T(8,128)S(1)}, u32[]{:S(2)}, u32[]{:S(2)}) collective-permute-start(f32[32,109]{1,0:T(8,128)S(1)} %add_add_fusion), channel_id=1, source_target_pairs={{0,4},{4,0},{8,12},{12,8},{16,20},{20,16},{24,28},{28,24},{1,5},{5... | collective-permute-start | bytes 41864 | tf_op jit(solution)/shard_map/ppermute | solution.py:21
  36.2 2.2 %collective-permute-done.5 = f32[32,109]{1,0:T(8,128)S(1)} collective-permute-done((f32[32,109]{1,0:T(8,128)S(1)}, f32[32,109]{1,0:T(8,128)S(1)}, u32[]{:S(2)}, u32[]{:S(2)}) %collective-permute-start.5) | collective-permute-done | bytes 13984 | tf_op jit(solution)/shard_map/ppermute | solution.py:21
  38.4 0.0 collective-permute-start.6
  38.4 3.1 %collective-permute-start.7 = (f32[32,109]{1,0:T(8,128)S(1)}, f32[32,109]{1,0:T(8,128)S(1)}, u32[]{:S(2)}, u32[]{:S(2)}) collective-permute-start(f32[32,109]{1,0:T(8,128)S(1)} %add.122), channel_id=1, source_target_pairs={{0,2},{1,3},{2,0},{3,1},{4,6},{5,7},{6,4},{7,5},{8,10},{9,11},{10,... | collective-permute-start | bytes 41864 | tf_op jit(solution)/shard_map/ppermute | solution.py:21
  41.5 0.0 collective-permute-start.8
  41.5 0.0 collective-permute-done.6
  41.5 2.2 %collective-permute-done.7 = f32[32,109]{1,0:T(8,128)S(1)} collective-permute-done((f32[32,109]{1,0:T(8,128)S(1)}, f32[32,109]{1,0:T(8,128)S(1)}, u32[]{:S(2)}, u32[]{:S(2)}) %collective-permute-start.7) | collective-permute-done | bytes 13984 | tf_op jit(solution)/shard_map/ppermute | solution.py:21
  43.7 0.9 %collective-permute-done.8 = f32[32,109]{1,0:T(8,128)S(1)} collective-permute-done((f32[32,109]{1,0:T(8,128)S(1)}, f32[32,109]{1,0:T(8,128)S(1)}, u32[]{:S(2)}, u32[]{:S(2)}) %collective-permute-start.8) | collective-permute-done | bytes 13984 | tf_op jit(solution)/shard_map/ppermute | solution.py:21
  44.6 0.7 %slice_reduce_fusion = f32[8]{0:T(128)} fusion(f32[8,109]{1,0:T(8,128)S(1)} %fusion.33), kind=kLoop, calls=%fused_computation.53 | loop fusion | bytes 64 | tf_op jit(solution)/shard_map/slice | solution.py:118
  45.3 0.0 all-to-all-done
  45.3 0.9 %copy.88 = bf16[8,4,4,16,128]{4,3,2,1,0:T(8,128)(2,1)} copy(bf16[8,4,4,16,128]{4,3,1,0,2:T(8,128)(2,1)S(1)} %bitcast.97) | data formatting | bytes 1048576 | tf_op jit(solution)/shard_map/all_to_all | solution.py:107
  46.2 0.0 copy-done.1
  (26 shorter events, 0.5 us)
Async XLA Ops:
  0.6 12.3 %copy-start = (bf16[4,8,32,256]{3,2,1,0:T(8,128)(2,1)S(1)}, bf16[4,8,32,256]{3,2,1,0:T(8,128)(2,1)}, u32[]{:S(2)}) copy-start(bf16[4,8,32,256]{3,2,1,0:T(8,128)(2,1)} %param.6) | copy-start | bytes 1572868
  0.6 11.5 %copy-start.4 = (s32[8]{0:T(128)S(1)}, s32[8]{0:T(128)}, u32[]{:S(2)}) copy-start(s32[8]{0:T(128)} %param.7) | copy-start | bytes 100
  0.7 11.5 %copy-start.5 = (s32[4]{0:T(128)S(1)}, s32[4]{0:T(128)}, u32[]{:S(2)}) copy-start(s32[4]{0:T(128)} %param.8) | copy-start | bytes 52
  0.7 11.6 %copy-start.2 = (bf16[32,108]{1,0:T(8,128)(2,1)S(1)}, bf16[32,108]{1,0:T(8,128)(2,1)}, u32[]{:S(2)}) copy-start(bf16[32,108]{1,0:T(8,128)(2,1)} %param.9) | copy-start | bytes 20740
  1.6 11.3 %collective-permute-start = (bf16[4,32,256]{2,1,0:T(8,128)(2,1)S(1)}, bf16[4,32,256]{2,1,0:T(8,128)(2,1)S(1)}, u32[]{:S(2)}, u32[]{:S(2)}) collective-permute-start(bf16[4,32,256]{2,1,0:T(8,128)(2,1)S(1)} %slice_bitcast_fusion), channel_id=1, source_target_pairs={{0,4},{4,8},{8,12},{12,16},{16,20},{20,24},{24,28},{1,5},{5,9},{9,... | collective-permute-start | bytes 196616 | tf_op jit(solution)/shard_map/ppermute | solution.py:10
  8.6 12.3 %all-to-all-start.1 = ((bf16[8,4,64,128]{3,0,1,2:T(8,128)(2,1)}), bf16[8,4,64,128]{3,0,1,2:T(8,128)(2,1)S(1)}, u32[]{:S(2)}, u32[]{:S(2)}) async-start(bf16[8,4,64,128]{3,0,1,2:T(8,128)(2,1)} %copy.89), calls=%async_computation.1 | async-start | bytes 1048576 | tf_op jit(solution)/shard_map/all_to_all | solution.py:70
  13.1 3.2 %collective-permute-start.1 = (bf16[4,9,256]{2,0,1:T(4,128)(2,1)S(1)}, bf16[4,9,256]{2,0,1:T(4,128)(2,1)S(1)}, u32[]{:S(2)}, u32[]{:S(2)}) collective-permute-start(bf16[4,9,256]{2,0,1:T(4,128)(2,1)S(1)} %bitcast.99), channel_id=1, source_target_pairs={{0,1},{1,2},{2,3},{4,5},{5,6},{6,7},{8,9},{9,10},{10,11},{12,13},{... | collective-permute-start | bytes 55304 | tf_op jit(solution)/shard_map/ppermute | solution.py:10
  17.9 0.7 %copy-start.3 = (f32[32]{0:T(128)S(1)}, f32[32]{0:T(128)}, u32[]{:S(2)}) copy-start(f32[32]{0:T(128)} %param.10) | copy-start | bytes 388
  23.6 10.9 %collective-permute-start.2 = (f32[32,109]{1,0:T(8,128)S(1)}, f32[32,109]{1,0:T(8,128)S(1)}, u32[]{:S(2)}, u32[]{:S(2)}) collective-permute-start(f32[32,109]{1,0:T(8,128)S(1)} %pad_maximum_fusion.1), channel_id=1, source_target_pairs={{0,8},{4,12},{8,0},{12,4},{16,24},{20,28},{24,16},{28,20},{1,9},{5... | collective-permute-start | bytes 41864 | tf_op jit(solution)/shard_map/ppermute | solution.py:21
  25.2 9.3 %collective-permute-start.3 = (f32[32,109]{1,0:T(8,128)S(1)}, f32[32,109]{1,0:T(8,128)S(1)}, u32[]{:S(2)}, u32[]{:S(2)}) collective-permute-start(f32[32,109]{1,0:T(8,128)S(1)} %pad_maximum_fusion.1), channel_id=1, source_target_pairs={{0,16},{4,20},{8,24},{12,28},{16,0},{20,4},{24,8},{28,12},{1,17},{... | collective-permute-start | bytes 41864 | tf_op jit(solution)/shard_map/ppermute | solution.py:21
  27.8 6.8 %collective-permute-start.4 = (f32[32,109]{1,0:T(8,128)S(1)}, f32[32,109]{1,0:T(8,128)S(1)}, u32[]{:S(2)}, u32[]{:S(2)}) collective-permute-start(f32[32,109]{1,0:T(8,128)S(1)} %pad_maximum_fusion.1), channel_id=1, source_target_pairs={{0,24},{4,28},{8,16},{12,20},{16,8},{20,12},{24,0},{28,4},{1,25},{... | collective-permute-start | bytes 41864 | tf_op jit(solution)/shard_map/ppermute | solution.py:21
  29.0 16.3 %all-to-all-start = ((bf16[32,4,16,128]{3,2,1,0:T(8,128)(2,1)}), bf16[32,4,16,128]{3,2,1,0:T(8,128)(2,1)S(1)}, u32[]{:S(2)}, u32[]{:S(2)}) async-start(bf16[32,4,16,128]{3,2,1,0:T(8,128)(2,1)} %copy.87), calls=%async_computation | async-start | bytes 1048576 | tf_op jit(solution)/shard_map/all_to_all | solution.py:107
  34.6 3.7 %collective-permute-start.5 = (f32[32,109]{1,0:T(8,128)S(1)}, f32[32,109]{1,0:T(8,128)S(1)}, u32[]{:S(2)}, u32[]{:S(2)}) collective-permute-start(f32[32,109]{1,0:T(8,128)S(1)} %add_add_fusion), channel_id=1, source_target_pairs={{0,4},{4,0},{8,12},{12,8},{16,20},{20,16},{24,28},{28,24},{1,5},{5... | collective-permute-start | bytes 41864 | tf_op jit(solution)/shard_map/ppermute | solution.py:21
  38.4 3.1 %collective-permute-start.6 = (f32[32,109]{1,0:T(8,128)S(1)}, f32[32,109]{1,0:T(8,128)S(1)}, u32[]{:S(2)}, u32[]{:S(2)}) collective-permute-start(f32[32,109]{1,0:T(8,128)S(1)} %add.122), channel_id=1, source_target_pairs={{0,1},{1,0},{2,3},{3,2},{4,5},{5,4},{6,7},{7,6},{8,9},{9,8},{10,11... | collective-permute-start | bytes 41864 | tf_op jit(solution)/shard_map/ppermute | solution.py:21
  38.4 5.3 %collective-permute-start.7 = (f32[32,109]{1,0:T(8,128)S(1)}, f32[32,109]{1,0:T(8,128)S(1)}, u32[]{:S(2)}, u32[]{:S(2)}) collective-permute-start(f32[32,109]{1,0:T(8,128)S(1)} %add.122), channel_id=1, source_target_pairs={{0,2},{1,3},{2,0},{3,1},{4,6},{5,7},{6,4},{7,5},{8,10},{9,11},{10,... | collective-permute-start | bytes 41864 | tf_op jit(solution)/shard_map/ppermute | solution.py:21
  41.5 3.2 %collective-permute-start.8 = (f32[32,109]{1,0:T(8,128)S(1)}, f32[32,109]{1,0:T(8,128)S(1)}, u32[]{:S(2)}, u32[]{:S(2)}) collective-permute-start(f32[32,109]{1,0:T(8,128)S(1)} %add.122), channel_id=1, source_target_pairs={{0,3},{1,2},{2,1},{3,0},{4,7},{5,6},{6,5},{7,4},{8,11},{9,10},{10,... | collective-permute-start | bytes 41864 | tf_op jit(solution)/shard_map/ppermute | solution.py:21
  44.6 1.6 %copy-start.1 = (f32[8,109]{1,0:T(8,128)}, f32[8,109]{1,0:T(8,128)S(1)}, u32[]{:S(2)}) copy-start(f32[8,109]{1,0:T(8,128)S(1)} %fusion.33) | copy-start | bytes 10468

commit v19 on v14

--- a/solution.py
+++ b/solution.py
@@ -110,11 +110,13 @@
         grads.append(jnp.einsum("opqr,kpqr->ok", returned, part, preferred_element_type=jnp.float32))
     weight_full = jnp.stack(grads, axis=-1).reshape(out_chans, -1)
     bias_full = jnp.sum(grad_wide, axis=(1, 2, 3))
-    packed = jnp.concatenate([weight_full, bias_full[:, None]], axis=1)
-    total = butterfly_sum(butterfly_sum(packed, "gy"), "gx")
     share = out_chans // tiles_y
-    mine = lax.dynamic_slice_in_dim(total, lax.axis_index("gy") * share, share, 0)
-    weight_grad, bias_grad = mine[:, :-1], mine[:, -1]
+    width = weight_full.shape[1]
+    bias_rows = jnp.pad(bias_full.reshape(tiles_y, 1, share), ((0, 0), (0, 0), (0, width - share)))
+    packed = jnp.concatenate([weight_full.reshape(tiles_y, share, width), bias_rows], axis=1)
+    total = butterfly_sum(butterfly_sum(packed, "gx"), "gy")
+    mine = lax.dynamic_index_in_dim(total, lax.axis_index("gy"), 0, keepdims=False)
+    weight_grad, bias_grad = mine[:share], mine[share, :share]
     return (stem, weight_grad, bias_grad)
 
 

time: 50.2 us -> 69.1 us (1.38)
  the two profiles are of different devices: /device:TPU:0 before, /device:TPU:17 now
where the time goes in v19:
time: 69.1 us; the launch traced here: 68.7 us
  waiting for transfers between devices  30.7 us (44%)
  starting transfers between devices  22.4 us (32%)
  local copies, waits for them, and re-layouts  8.34 us (12%)
  matrix products  5.22 us (8%)
  other arithmetic  1.1 us (2%)
  between operations  0.96 us (1%)
    ppermute x7, waiting for transfers between devices, butterfly_sum(): lax.ppermute(value, axis, [(i, i ^ t) for i in range(size)])  29 us
    ppermute x2, starting transfers between devices, from_behind(): return lax.ppermute(block, axis, route)  6.65 us
    ppermute x7, starting transfers between devices, butterfly_sum(): lax.ppermute(value, axis, [(i, i ^ t) for i in range(size)])  6.35 us
    all_to_all x1, starting transfers between devices, local(): lax.all_to_all(stem_local, 'gy', split_axis=0, concat_axis=2, tiled=True)  4.98 us
    all_to_all x1, starting transfers between devices, local(): lax.all_to_all(grad_out, 'gy', split_axis=2, concat_axis=0, tiled=True)  4.39 us
    unnamed x25, local copies, waits for them, and re-layouts  2.98 us
    dot_general x3, matrix products, local(): jnp.einsum('ok,kpqr->opqr', kernel[:, :, off_z], part, preferred_element_...  2.78 us
    ppermute x2, waiting for transfers between devices, from_behind(): return lax.ppermute(block, axis, route)  1.69 us
  transfers between devices with their start and end apart: 11, of which 6 were waited for; matrix products, arithmetic and copies ran while one was open for 13% of the time, Pallas kernels for 0%

profile of v19, /device:TPU:17, one launch (start us, length us, event | category | flops | bytes accessed | tf_op | source)
XLA Modules:
  0.0 68.7 jit_solution(14615433859253637518)
XLA Ops:
  0.6 0.0 copy-start
  0.6 0.0 copy-start.4
  0.7 0.0 copy-start.5
  0.7 0.0 copy-start.2
  0.7 0.9 %slice_bitcast_fusion = bf16[4,32,256]{2,1,0:T(8,128)(2,1)S(1)} fusion(bf16[4,8,32,256]{3,2,1,0:T(8,128)(2,1)} %param.6), kind=kLoop, calls=%fused_computation.46 | loop fusion | bytes 131072 | tf_op jit(solution)/shard_map/squeeze | solution.py:73
  1.6 3.1 %collective-permute-start = (bf16[4,32,256]{2,1,0:T(8,128)(2,1)S(1)}, bf16[4,32,256]{2,1,0:T(8,128)(2,1)S(1)}, u32[]{:S(2)}, u32[]{:S(2)}) collective-permute-start(bf16[4,32,256]{2,1,0:T(8,128)(2,1)S(1)} %slice_bitcast_fusion), channel_id=1, source_target_pairs={{0,4},{4,8},{8,12},{12,16},{16,20},{20,24},{24,28},{1,5},{5,9},{9,... | collective-permute-start | bytes 196616 | tf_op jit(solution)/shard_map/ppermute | solution.py:10
  4.7 2.2 %copy.95 = bf16[8,4,64,128]{3,0,1,2:T(8,128)(2,1)} copy(bf16[8,4,64,128]{3,2,1,0:T(8,128)(2,1)} %param.11) | data formatting | bytes 1048576 | tf_op args[5]
  6.9 4.4 %all-to-all-start.1 = ((bf16[8,4,64,128]{3,0,1,2:T(8,128)(2,1)}), bf16[8,4,64,128]{3,0,1,2:T(8,128)(2,1)S(1)}, u32[]{:S(2)}, u32[]{:S(2)}) async-start(bf16[8,4,64,128]{3,0,1,2:T(8,128)(2,1)} %copy.95), calls=%async_computation.1 | async-start | bytes 1048576 | tf_op jit(solution)/shard_map/all_to_all | solution.py:70
  11.3 0.0 copy-done.4
  11.3 0.1 fusion.51
  11.5 0.1 fusion.41
  11.6 0.1 copy.87
  11.8 0.1 fusion.53
  11.9 0.1 broadcast_and_fusion
  11.9 0.1 fusion.55
  12.0 0.0 collective-permute-done
  12.0 0.1 select_select_fusion
  12.3 3.5 %collective-permute-start.1 = (bf16[4,9,256]{2,0,1:T(4,128)(2,1)S(1)}, bf16[4,9,256]{2,0,1:T(4,128)(2,1)S(1)}, u32[]{:S(2)}, u32[]{:S(2)}) collective-permute-start(bf16[4,9,256]{2,0,1:T(4,128)(2,1)S(1)} %bitcast.106), channel_id=1, source_target_pairs={{0,1},{1,2},{2,3},{4,5},{5,6},{6,7},{8,9},{9,10},{10,11},{12,13},{... | collective-permute-start | bytes 55304 | tf_op jit(solution)/shard_map/ppermute | solution.py:10
  15.8 0.1 copy.109
  15.9 0.1 copy.111
  16.0 0.1 copy.113
  16.1 1.7 %collective-permute-done.1 = bf16[4,9,256]{2,0,1:T(4,128)(2,1)S(1)} collective-permute-done((bf16[4,9,256]{2,0,1:T(4,128)(2,1)S(1)}, bf16[4,9,256]{2,0,1:T(4,128)(2,1)S(1)}, u32[]{:S(2)}, u32[]{:S(2)}) %collective-permute-start.1) | collective-permute-done | bytes 18464 | tf_op jit(solution)/shard_map/ppermute | solution.py:10
  17.8 1.1 %convolution_convert_fusion = bf16[4,9,48,384]{3,2,1,0:T(8,128)(2,1)S(1)} fusion(bf16[4,9,32,256]{3,2,1,0:T(8,128)(2,1)S(1)} %select_select_fusion, pred[33]{0:T(512)(128)(4,1)S(1)} %get-tuple-element.7, pred[33]{0:T(512)(128)(4,1)S(1)} %get-tuple-element.6, bf16[4,9,256]{2,1,0:T(8,128)(2,1)S(1)} %copy.84, s32[384]{0:T(512)S(1)} %fusion.45, ...), kind=kOutput, calls=%fused_computation | convolution fusion | flops 279191040 | bytes 1940130 | tf_op jit(solution)/shard_map/cxjy,cxyk->cxjk/dot_general | solution.py:86
  19.2 0.2 copy.85
  19.4 0.0 copy-start.3
  19.4 0.5 fusion.69
  20.0 0.1 copy-done.3
  20.1 0.4 convolution_add_fusion.2
  20.5 0.5 convolution_add_fusion.1
  21.0 0.0 all-to-all-done.1
  21.0 1.9 %fusion.67 = (f32[32]{0:T(128)S(1)}, bf16[32,4,16,128]{3,0,2,1:T(8,128)(2,1)S(1)}, bf16[32,4,16,128]{3,0,2,1:T(8,128)(2,1)}) fusion(pred[4,16]{1,0:T(4,128)(4,1)S(1)} %broadcast_and_fusion, f32[4,16,128,32]{2,3,1,0:T(8,128)S(1)} %convolution_add_fusion.1, bf16[32,36,1]{1,0,2:T(8,128)(2,1)S(1)} %copy.113, ...), kind=kOutput, calls=%fused_computation.116 | convolution fusion | flops 23592928 | bytes 3213760 | tf_op jit(solution)/shard_map/ok,kpqr->opqr/dot_general | solution.py:97
  22.9 0.5 convolution_bitcast_fusion
  23.3 0.0 copy-start.1
  23.4 0.5 convolution_bitcast_fusion.1
  23.8 0.5 convolution_bitcast_fusion.2
  24.3 0.1 reshape.122
  24.4 0.1 copy.98
  24.5 0.1 copy.97
  24.6 0.2 reshape_reshape.3
  24.8 0.1 select_maximum_fusion
  24.8 0.1 collective-permute-start.3
  25.0 2.4 %collective-permute-start.4 = (f32[4,9,108]{1,0,2:T(4,128)S(1)}, f32[4,9,108]{1,0,2:T(4,128)S(1)}, u32[]{:S(2)}, u32[]{:S(2)}) collective-permute-start(f32[4,9,108]{1,0,2:T(4,128)S(1)} %select_maximum_fusion), channel_id=1, source_target_pairs={{0,24},{4,28},{8,16},{12,20},{16,8},{20,12},{24,0},{28,4},{1,25},{... | collective-permute-start | bytes 46664 | tf_op jit(solution)/shard_map/ppermute | solution.py:21
  27.4 1.1 %collective-permute-start.2 = (f32[4,9,108]{1,0,2:T(4,128)S(1)}, f32[4,9,108]{1,0,2:T(4,128)S(1)}, u32[]{:S(2)}, u32[]{:S(2)}) collective-permute-start(f32[4,9,108]{1,0,2:T(4,128)S(1)} %select_maximum_fusion), channel_id=1, source_target_pairs={{0,8},{4,12},{8,0},{12,4},{16,24},{20,28},{24,16},{28,20},{1,9},{5... | collective-permute-start | bytes 46664 | tf_op jit(solution)/shard_map/ppermute | solution.py:21
  28.5 1.0 %copy.93 = bf16[32,4,16,128]{3,2,1,0:T(8,128)(2,1)} copy(bf16[32,4,16,128]{3,0,2,1:T(8,128)(2,1)S(1)} %copy-done.1) | data formatting | bytes 1048576 | tf_op jit(solution)/shard_map/convert_element_type | solution.py:101
  29.5 5.0 %all-to-all-start = ((bf16[32,4,16,128]{3,2,1,0:T(8,128)(2,1)}), bf16[32,4,16,128]{3,2,1,0:T(8,128)(2,1)S(1)}, u32[]{:S(2)}, u32[]{:S(2)}) async-start(bf16[32,4,16,128]{3,2,1,0:T(8,128)(2,1)} %copy.93), calls=%async_computation | async-start | bytes 1048576 | tf_op jit(solution)/shard_map/all_to_all | solution.py:106
  34.4 5.3 %collective-permute-done.3 = f32[4,9,108]{1,0,2:T(4,128)S(1)} collective-permute-done((f32[4,9,108]{1,0,2:T(4,128)S(1)}, f32[4,9,108]{1,0,2:T(4,128)S(1)}, u32[]{:S(2)}, u32[]{:S(2)}) %collective-permute-start.3) | collective-permute-done | bytes 15584 | tf_op jit(solution)/shard_map/ppermute | solution.py:21
  39.7 7.3 %collective-permute-done.4 = f32[4,9,108]{1,0,2:T(4,128)S(1)} collective-permute-done((f32[4,9,108]{1,0,2:T(4,128)S(1)}, f32[4,9,108]{1,0,2:T(4,128)S(1)}, u32[]{:S(2)}, u32[]{:S(2)}) %collective-permute-start.4) | collective-permute-done | bytes 15584 | tf_op jit(solution)/shard_map/ppermute | solution.py:21
  47.0 0.0 collective-permute-done.2
  47.0 0.1 add_add_fusion
  47.2 0.1 collective-permute-start.5
  47.2 6.6 %collective-permute-done.5 = f32[4,9,108]{1,0,2:T(4,128)S(1)} collective-permute-done((f32[4,9,108]{1,0,2:T(4,128)S(1)}, f32[4,9,108]{1,0,2:T(4,128)S(1)}, u32[]{:S(2)}, u32[]{:S(2)}) %collective-permute-start.5) | collective-permute-done | bytes 15584 | tf_op jit(solution)/shard_map/ppermute | solution.py:21
  53.8 0.1 add.118
  53.9 0.5 collective-permute-start.8
  54.4 2.2 %collective-permute-start.7 = (f32[4,9,108]{1,0,2:T(4,128)S(1)}, f32[4,9,108]{1,0,2:T(4,128)S(1)}, u32[]{:S(2)}, u32[]{:S(2)}) collective-permute-start(f32[4,9,108]{1,0,2:T(4,128)S(1)} %add.118), channel_id=1, source_target_pairs={{0,2},{1,3},{2,0},{3,1},{4,6},{5,7},{6,4},{7,5},{8,10},{9,11},{10,... | collective-permute-start | bytes 46664 | tf_op jit(solution)/shard_map/ppermute | solution.py:21
  56.6 0.0 collective-permute-start.6
  56.6 4.9 %collective-permute-done.8 = f32[4,9,108]{1,0,2:T(4,128)S(1)} collective-permute-done((f32[4,9,108]{1,0,2:T(4,128)S(1)}, f32[4,9,108]{1,0,2:T(4,128)S(1)}, u32[]{:S(2)}, u32[]{:S(2)}) %collective-permute-start.8) | collective-permute-done | bytes 15584 | tf_op jit(solution)/shard_map/ppermute | solution.py:21
  61.4 5.0 %collective-permute-done.7 = f32[4,9,108]{1,0,2:T(4,128)S(1)} collective-permute-done((f32[4,9,108]{1,0,2:T(4,128)S(1)}, f32[4,9,108]{1,0,2:T(4,128)S(1)}, u32[]{:S(2)}, u32[]{:S(2)}) %collective-permute-start.7) | collective-permute-done | bytes 15584 | tf_op jit(solution)/shard_map/ppermute | solution.py:21
  66.4 0.0 collective-permute-done.6
  66.4 0.2 fusion.31
  66.6 0.1 copy.100
  66.7 0.7 copy.99
  67.3 0.5 slice_bitcast_fusion.1
  67.9 0.0 all-to-all-done
  67.9 0.9 %copy.94 = bf16[8,4,4,16,128]{4,3,2,1,0:T(8,128)(2,1)} copy(bf16[8,4,4,16,128]{4,3,1,0,2:T(8,128)(2,1)S(1)} %bitcast.103) | data formatting | bytes 1048576 | tf_op jit(solution)/shard_map/all_to_all | solution.py:106
  (26 shorter events, 0.5 us)
Async XLA Ops:
  0.6 11.4 %copy-start = (bf16[4,8,32,256]{3,2,1,0:T(8,128)(2,1)S(1)}, bf16[4,8,32,256]{3,2,1,0:T(8,128)(2,1)}, u32[]{:S(2)}) copy-start(bf16[4,8,32,256]{3,2,1,0:T(8,128)(2,1)} %param.6) | copy-start | bytes 1572868
  0.6 10.6 %copy-start.4 = (s32[4]{0:T(128)S(1)}, s32[4]{0:T(128)}, u32[]{:S(2)}) copy-start(s32[4]{0:T(128)} %param.8) | copy-start | bytes 52
  0.7 10.6 %copy-start.5 = (s32[8]{0:T(128)S(1)}, s32[8]{0:T(128)}, u32[]{:S(2)}) copy-start(s32[8]{0:T(128)} %param.7) | copy-start | bytes 100
  0.7 10.9 %copy-start.2 = (bf16[32,108]{1,0:T(8,128)(2,1)S(1)}, bf16[32,108]{1,0:T(8,128)(2,1)}, u32[]{:S(2)}) copy-start(bf16[32,108]{1,0:T(8,128)(2,1)} %param.9) | copy-start | bytes 20740
  1.6 10.5 %collective-permute-start = (bf16[4,32,256]{2,1,0:T(8,128)(2,1)S(1)}, bf16[4,32,256]{2,1,0:T(8,128)(2,1)S(1)}, u32[]{:S(2)}, u32[]{:S(2)}) collective-permute-start(bf16[4,32,256]{2,1,0:T(8,128)(2,1)S(1)} %slice_bitcast_fusion), channel_id=1, source_target_pairs={{0,4},{4,8},{8,12},{12,16},{16,20},{20,24},{24,28},{1,5},{5,9},{9,... | collective-permute-start | bytes 196616 | tf_op jit(solution)/shard_map/ppermute | solution.py:10
  6.9 14.1 %all-to-all-start.1 = ((bf16[8,4,64,128]{3,0,1,2:T(8,128)(2,1)}), bf16[8,4,64,128]{3,0,1,2:T(8,128)(2,1)S(1)}, u32[]{:S(2)}, u32[]{:S(2)}) async-start(bf16[8,4,64,128]{3,0,1,2:T(8,128)(2,1)} %copy.95), calls=%async_computation.1 | async-start | bytes 1048576 | tf_op jit(solution)/shard_map/all_to_all | solution.py:70
  12.3 5.5 %collective-permute-start.1 = (bf16[4,9,256]{2,0,1:T(4,128)(2,1)S(1)}, bf16[4,9,256]{2,0,1:T(4,128)(2,1)S(1)}, u32[]{:S(2)}, u32[]{:S(2)}) collective-permute-start(bf16[4,9,256]{2,0,1:T(4,128)(2,1)S(1)} %bitcast.106), channel_id=1, source_target_pairs={{0,1},{1,2},{2,3},{4,5},{5,6},{6,7},{8,9},{9,10},{10,11},{12,13},{... | collective-permute-start | bytes 55304 | tf_op jit(solution)/shard_map/ppermute | solution.py:10
  19.4 0.7 copy-start.3
  23.3 5.1 %copy-start.1 = (bf16[32,4,16,128]{3,0,2,1:T(8,128)(2,1)S(1)}, bf16[32,4,16,128]{3,0,2,1:T(8,128)(2,1)}, u32[]{:S(2)}) copy-start(bf16[32,4,16,128]{3,0,2,1:T(8,128)(2,1)} %get-tuple-element.15) | copy-start | bytes 1572868
  24.8 14.9 %collective-permute-start.3 = (f32[4,9,108]{1,0,2:T(4,128)S(1)}, f32[4,9,108]{1,0,2:T(4,128)S(1)}, u32[]{:S(2)}, u32[]{:S(2)}) collective-permute-start(f32[4,9,108]{1,0,2:T(4,128)S(1)} %select_maximum_fusion), channel_id=1, source_target_pairs={{0,16},{4,20},{8,24},{12,28},{16,0},{20,4},{24,8},{28,12},{1,17},{... | collective-permute-start | bytes 46664 | tf_op jit(solution)/shard_map/ppermute | solution.py:21
  25.0 22.1 %collective-permute-start.4 = (f32[4,9,108]{1,0,2:T(4,128)S(1)}, f32[4,9,108]{1,0,2:T(4,128)S(1)}, u32[]{:S(2)}, u32[]{:S(2)}) collective-permute-start(f32[4,9,108]{1,0,2:T(4,128)S(1)} %select_maximum_fusion), channel_id=1, source_target_pairs={{0,24},{4,28},{8,16},{12,20},{16,8},{20,12},{24,0},{28,4},{1,25},{... | collective-permute-start | bytes 46664 | tf_op jit(solution)/shard_map/ppermute | solution.py:21
  27.4 19.6 %collective-permute-start.2 = (f32[4,9,108]{1,0,2:T(4,128)S(1)}, f32[4,9,108]{1,0,2:T(4,128)S(1)}, u32[]{:S(2)}, u32[]{:S(2)}) collective-permute-start(f32[4,9,108]{1,0,2:T(4,128)S(1)} %select_maximum_fusion), channel_id=1, source_target_pairs={{0,8},{4,12},{8,0},{12,4},{16,24},{20,28},{24,16},{28,20},{1,9},{5... | collective-permute-start | bytes 46664 | tf_op jit(solution)/shard_map/ppermute | solution.py:21
  29.5 38.4 %all-to-all-start = ((bf16[32,4,16,128]{3,2,1,0:T(8,128)(2,1)}), bf16[32,4,16,128]{3,2,1,0:T(8,128)(2,1)S(1)}, u32[]{:S(2)}, u32[]{:S(2)}) async-start(bf16[32,4,16,128]{3,2,1,0:T(8,128)(2,1)} %copy.93), calls=%async_computation | async-start | bytes 1048576 | tf_op jit(solution)/shard_map/all_to_all | solution.py:106
  47.2 6.7 %collective-permute-start.5 = (f32[4,9,108]{1,0,2:T(4,128)S(1)}, f32[4,9,108]{1,0,2:T(4,128)S(1)}, u32[]{:S(2)}, u32[]{:S(2)}) collective-permute-start(f32[4,9,108]{1,0,2:T(4,128)S(1)} %add_add_fusion), channel_id=1, source_target_pairs={{0,4},{4,0},{8,12},{12,8},{16,20},{20,16},{24,28},{28,24},{1,5},{5... | collective-permute-start | bytes 46664 | tf_op jit(solution)/shard_map/ppermute | solution.py:21
  53.9 7.5 %collective-permute-start.8 = (f32[4,9,108]{1,0,2:T(4,128)S(1)}, f32[4,9,108]{1,0,2:T(4,128)S(1)}, u32[]{:S(2)}, u32[]{:S(2)}) collective-permute-start(f32[4,9,108]{1,0,2:T(4,128)S(1)} %add.118), channel_id=1, source_target_pairs={{0,3},{1,2},{2,1},{3,0},{4,7},{5,6},{6,5},{7,4},{8,11},{9,10},{10,... | collective-permute-start | bytes 46664 | tf_op jit(solution)/shard_map/ppermute | solution.py:21
  54.4 12.0 %collective-permute-start.7 = (f32[4,9,108]{1,0,2:T(4,128)S(1)}, f32[4,9,108]{1,0,2:T(4,128)S(1)}, u32[]{:S(2)}, u32[]{:S(2)}) collective-permute-start(f32[4,9,108]{1,0,2:T(4,128)S(1)} %add.118), channel_id=1, source_target_pairs={{0,2},{1,3},{2,0},{3,1},{4,6},{5,7},{6,4},{7,5},{8,10},{9,11},{10,... | collective-permute-start | bytes 46664 | tf_op jit(solution)/shard_map/ppermute | solution.py:21
  56.6 9.9 %collective-permute-start.6 = (f32[4,9,108]{1,0,2:T(4,128)S(1)}, f32[4,9,108]{1,0,2:T(4,128)S(1)}, u32[]{:S(2)}, u32[]{:S(2)}) collective-permute-start(f32[4,9,108]{1,0,2:T(4,128)S(1)} %add.118), channel_id=1, source_target_pairs={{0,1},{1,0},{2,3},{3,2},{4,5},{5,4},{6,7},{7,6},{8,9},{9,8},{10,11... | collective-permute-start | bytes 46664 | tf_op jit(solution)/shard_map/ppermute | solution.py:21

commit v20 on v19

--- a/solution.py
+++ b/solution.py
@@ -112,11 +112,12 @@
     bias_full = jnp.sum(grad_wide, axis=(1, 2, 3))
     share = out_chans // tiles_y
     width = weight_full.shape[1]
-    bias_rows = jnp.pad(bias_full.reshape(tiles_y, 1, share), ((0, 0), (0, 0), (0, width - share)))
-    packed = jnp.concatenate([weight_full.reshape(tiles_y, share, width), bias_rows], axis=1)
+    bias_rows = jnp.pad(bias_full.reshape(tiles_y, share), ((0, 0), (0, width - share)))
+    packed = jnp.concatenate([weight_full, bias_rows], axis=0)
     total = butterfly_sum(butterfly_sum(packed, "gx"), "gy")
-    mine = lax.dynamic_index_in_dim(total, lax.axis_index("gy"), 0, keepdims=False)
-    weight_grad, bias_grad = mine[:share], mine[share, :share]
+    here = lax.axis_index("gy")
+    weight_grad = lax.dynamic_slice_in_dim(total, here * share, share, 0)
+    bias_grad = lax.dynamic_index_in_dim(total, out_chans + here, 0, keepdims=False)[:share]
     return (stem, weight_grad, bias_grad)
 
 

time: 69.1 us -> 55 us (0.80)
  the two profiles are of different devices: /device:TPU:17 before, /device:TPU:0 now
where the time goes in v20:
time: 55 us; the launch traced here: 54.7 us
  starting transfers between devices  23.9 us (43%)
  waiting for transfers between devices  15.8 us (29%)
  local copies, waits for them, and re-layouts  8.03 us (15%)
  matrix products  5.22 us (9%)
  between operations  1.02 us (2%)
  other arithmetic  0.7 us (1%)
    ppermute x7, starting transfers between devices, butterfly_sum(): lax.ppermute(value, axis, [(i, i ^ t) for i in range(size)])  9.78 us
    all_to_all x1, waiting for transfers between devices, local(): lax.all_to_all(stem_local, 'gy', split_axis=0, concat_axis=2, tiled=True)  7.59 us
    ppermute x2, starting transfers between devices, from_behind(): return lax.ppermute(block, axis, route)  7.21 us
    ppermute x7, waiting for transfers between devices, butterfly_sum(): lax.ppermute(value, axis, [(i, i ^ t) for i in range(size)])  6.29 us
    all_to_all x1, starting transfers between devices, local(): lax.all_to_all(grad_out, 'gy', split_axis=2, concat_axis=0, tiled=True)  3.47 us
    all_to_all x1, starting transfers between devices, local(): lax.all_to_all(stem_local, 'gy', split_axis=0, concat_axis=2, tiled=True)  3.47 us
    unnamed x25, local copies, waits for them, and re-layouts  2.98 us
    dot_general x3, matrix products, local(): jnp.einsum('ok,kpqr->opqr', kernel[:, :, off_z], part, preferred_element_...  2.78 us
  transfers between devices with their start and end apart: 11, of which 6 were waited for; matrix products, arithmetic and copies ran while one was open for 15% of the time, Pallas kernels for 0%

profile of v20, /device:TPU:0, one launch (start us, length us, event | category | flops | bytes accessed | tf_op | source)
XLA Modules:
  0.0 54.7 jit_solution(17241472336429297703)
XLA Ops:
  0.6 0.0 copy-start
  0.6 0.0 copy-start.4
  0.7 0.0 copy-start.5
  0.7 0.0 copy-start.2
  0.7 0.9 %slice_bitcast_fusion = bf16[4,32,256]{2,1,0:T(8,128)(2,1)S(1)} fusion(bf16[4,8,32,256]{3,2,1,0:T(8,128)(2,1)} %param.6), kind=kLoop, calls=%fused_computation.43 | loop fusion | bytes 131072 | tf_op jit(solution)/shard_map/squeeze | solution.py:73
  1.6 4.9 %collective-permute-start = (bf16[4,32,256]{2,1,0:T(8,128)(2,1)S(1)}, bf16[4,32,256]{2,1,0:T(8,128)(2,1)S(1)}, u32[]{:S(2)}, u32[]{:S(2)}) collective-permute-start(bf16[4,32,256]{2,1,0:T(8,128)(2,1)S(1)} %slice_bitcast_fusion), channel_id=1, source_target_pairs={{0,4},{4,8},{8,12},{12,16},{16,20},{20,24},{24,28},{1,5},{5,9},{9,... | collective-permute-start | bytes 196616 | tf_op jit(solution)/shard_map/ppermute | solution.py:10
  6.4 2.2 %copy.85 = bf16[8,4,64,128]{3,0,1,2:T(8,128)(2,1)} copy(bf16[8,4,64,128]{3,2,1,0:T(8,128)(2,1)} %param.11) | data formatting | bytes 1048576 | tf_op args[5]
  8.6 3.5 %all-to-all-start.1 = ((bf16[8,4,64,128]{3,0,1,2:T(8,128)(2,1)}), bf16[8,4,64,128]{3,0,1,2:T(8,128)(2,1)S(1)}, u32[]{:S(2)}, u32[]{:S(2)}) async-start(bf16[8,4,64,128]{3,0,1,2:T(8,128)(2,1)} %copy.85), calls=%async_computation.1 | async-start | bytes 1048576 | tf_op jit(solution)/shard_map/all_to_all | solution.py:70
  12.1 0.0 copy-done.4
  12.2 0.0 copy-done.5
  12.2 0.1 fusion.50
  12.3 0.1 fusion.40
  12.4 0.0 copy-done.2
  12.4 0.1 copy.77
  12.6 0.1 fusion.52
  12.7 0.1 broadcast_and_fusion
  12.8 0.1 fusion.54
  12.9 0.0 collective-permute-done
  12.9 0.0 copy-done
  12.9 0.1 select_select_fusion
  13.1 2.4 %collective-permute-start.1 = (bf16[4,9,256]{2,0,1:T(4,128)(2,1)S(1)}, bf16[4,9,256]{2,0,1:T(4,128)(2,1)S(1)}, u32[]{:S(2)}, u32[]{:S(2)}) collective-permute-start(bf16[4,9,256]{2,0,1:T(4,128)(2,1)S(1)} %bitcast.102), channel_id=1, source_target_pairs={{0,1},{1,2},{2,3},{4,5},{5,6},{6,7},{8,9},{9,10},{10,11},{12,13},{... | collective-permute-start | bytes 55304 | tf_op jit(solution)/shard_map/ppermute | solution.py:10
  15.5 0.1 copy.97
  15.6 0.1 copy.99
  15.7 0.1 copy.101
  15.8 0.5 collective-permute-done.1
  16.3 1.1 %convolution_convert_fusion = bf16[4,9,48,384]{3,2,1,0:T(8,128)(2,1)S(1)} fusion(bf16[4,9,32,256]{3,2,1,0:T(8,128)(2,1)S(1)} %select_select_fusion, pred[33]{0:T(512)(128)(4,1)S(1)} %get-tuple-element.10, pred[33]{0:T(512)(128)(4,1)S(1)} %get-tuple-element.9, bf16[4,9,256]{2,1,0:T(8,128)(2,1)S(1)} %copy.74, s32[384]{0:T(512)S(1)} %fusion.44, ...), kind=kOutput, calls=%fused_computation | convolution fusion | flops 279191040 | bytes 1940130 | tf_op jit(solution)/shard_map/cxjy,cxyk->cxjk/dot_general | solution.py:86
  17.7 0.2 copy.75
  17.9 0.0 copy-start.3
  18.0 0.5 fusion.68
  18.5 0.1 copy-done.3
  18.6 0.4 convolution_add_fusion.2
  19.1 0.5 convolution_add_fusion.1
  19.5 1.4 %all-to-all-done.1 = bf16[8,4,64,128]{3,0,1,2:T(8,128)(2,1)S(1)} async-done(((bf16[8,4,64,128]{3,0,1,2:T(8,128)(2,1)}), bf16[8,4,64,128]{3,0,1,2:T(8,128)(2,1)S(1)}, u32[]{:S(2)}, u32[]{:S(2)}) %all-to-all-start.1) | async-done | bytes 524320 | tf_op jit(solution)/shard_map/all_to_all | solution.py:70
  20.9 1.9 %fusion.66 = (f32[32]{0:T(128)S(1)}, bf16[32,4,16,128]{3,0,2,1:T(8,128)(2,1)S(1)}, bf16[32,4,16,128]{3,0,2,1:T(8,128)(2,1)}) fusion(pred[4,16]{1,0:T(4,128)(4,1)S(1)} %broadcast_and_fusion, f32[4,16,128,32]{2,3,1,0:T(8,128)S(1)} %convolution_add_fusion.1, bf16[32,36,1]{1,0,2:T(8,128)(2,1)S(1)} %copy.101, ...), kind=kOutput, calls=%fused_computation.116 | convolution fusion | flops 23592928 | bytes 3213760 | tf_op jit(solution)/shard_map/ok,kpqr->opqr/dot_general | solution.py:97
  22.8 0.5 convolution_bitcast_fusion
  23.2 0.0 copy-start.1
  23.2 0.5 convolution_bitcast_fusion.1
  23.7 0.5 convolution_bitcast_fusion.2
  24.2 0.1 reshape.126
  24.3 0.1 copy.87
  24.4 0.1 copy.88
  24.5 2.7 %collective-permute-start.3 = (f32[36,108]{1,0:T(8,128)S(1)}, f32[36,108]{1,0:T(8,128)S(1)}, u32[]{:S(2)}, u32[]{:S(2)}) collective-permute-start(f32[36,108]{1,0:T(8,128)S(1)} %select_maximum_fusion), channel_id=1, source_target_pairs={{0,16},{4,20},{8,24},{12,28},{16,0},{20,4},{24,8},{28,12},{1,17},{... | collective-permute-start | bytes 46664 | tf_op jit(solution)/shard_map/ppermute | solution.py:21
  27.1 1.3 %collective-permute-start.4 = (f32[36,108]{1,0:T(8,128)S(1)}, f32[36,108]{1,0:T(8,128)S(1)}, u32[]{:S(2)}, u32[]{:S(2)}) collective-permute-start(f32[36,108]{1,0:T(8,128)S(1)} %select_maximum_fusion), channel_id=1, source_target_pairs={{0,24},{4,28},{8,16},{12,20},{16,8},{20,12},{24,0},{28,4},{1,25},{... | collective-permute-start | bytes 46664 | tf_op jit(solution)/shard_map/ppermute | solution.py:21
  28.5 0.2 collective-permute-start.2
  28.7 0.5 collective-permute-done.3
  29.2 3.5 %collective-permute-done.4 = f32[36,108]{1,0:T(8,128)S(1)} collective-permute-done((f32[36,108]{1,0:T(8,128)S(1)}, f32[36,108]{1,0:T(8,128)S(1)}, u32[]{:S(2)}, u32[]{:S(2)}) %collective-permute-start.4) | collective-permute-done | bytes 15584 | tf_op jit(solution)/shard_map/ppermute | solution.py:21
  32.8 0.0 collective-permute-done.2
  32.8 1.6 %collective-permute-start.5 = (f32[36,108]{1,0:T(8,128)S(1)}, f32[36,108]{1,0:T(8,128)S(1)}, u32[]{:S(2)}, u32[]{:S(2)}) collective-permute-start(f32[36,108]{1,0:T(8,128)S(1)} %add_add_fusion.1), channel_id=1, source_target_pairs={{0,4},{4,0},{8,12},{12,8},{16,20},{20,16},{24,28},{28,24},{1,5},{5... | collective-permute-start | bytes 46664 | tf_op jit(solution)/shard_map/ppermute | solution.py:21
  34.4 2.2 %collective-permute-done.5 = f32[36,108]{1,0:T(8,128)S(1)} collective-permute-done((f32[36,108]{1,0:T(8,128)S(1)}, f32[36,108]{1,0:T(8,128)S(1)}, u32[]{:S(2)}, u32[]{:S(2)}) %collective-permute-start.5) | collective-permute-done | bytes 15584 | tf_op jit(solution)/shard_map/ppermute | solution.py:21
  36.6 3.8 %collective-permute-start.7 = (f32[36,108]{1,0:T(8,128)S(1)}, f32[36,108]{1,0:T(8,128)S(1)}, u32[]{:S(2)}, u32[]{:S(2)}) collective-permute-start(f32[36,108]{1,0:T(8,128)S(1)} %add.126), channel_id=1, source_target_pairs={{0,2},{1,3},{2,0},{3,1},{4,6},{5,7},{6,4},{7,5},{8,10},{9,11},{10,... | collective-permute-start | bytes 46664 | tf_op jit(solution)/shard_map/ppermute | solution.py:21
  40.4 0.0 collective-permute-start.8
  40.4 0.2 collective-permute-start.6
  40.6 0.0 copy-done.1
  40.6 1.0 %copy.83 = bf16[32,4,16,128]{3,2,1,0:T(8,128)(2,1)} copy(bf16[32,4,16,128]{3,0,2,1:T(8,128)(2,1)S(1)} %copy-done.1) | data formatting | bytes 1048576 | tf_op jit(solution)/shard_map/convert_element_type | solution.py:101
  41.6 3.5 %all-to-all-start = ((bf16[32,4,16,128]{3,2,1,0:T(8,128)(2,1)}), bf16[32,4,16,128]{3,2,1,0:T(8,128)(2,1)S(1)}, u32[]{:S(2)}, u32[]{:S(2)}) async-start(bf16[32,4,16,128]{3,2,1,0:T(8,128)(2,1)} %copy.83), calls=%async_computation | async-start | bytes 1048576 | tf_op jit(solution)/shard_map/all_to_all | solution.py:106
  45.1 0.0 collective-permute-done.7
  45.1 0.0 collective-permute-done.8
  45.1 0.0 collective-permute-done.6
  45.1 0.6 %constant_dynamic-slice_fusion.1 = f32[8,108]{1,0:T(8,128)} fusion(f32[36,108]{1,0:T(8,128)S(1)} %add_add_fusion, s32[]{:T(128)S(6)} %select_n.95), kind=kLoop, calls=%fused_computation.107 | loop fusion | bytes 6916 | tf_op jit(solution)/shard_map/dynamic_slice | solution.py:119
  45.7 0.5 slice_bitcast_fusion.1
  46.2 7.6 %all-to-all-done = bf16[32,4,16,128]{3,2,1,0:T(8,128)(2,1)S(1)} async-done(((bf16[32,4,16,128]{3,2,1,0:T(8,128)(2,1)}), bf16[32,4,16,128]{3,2,1,0:T(8,128)(2,1)S(1)}, u32[]{:S(2)}, u32[]{:S(2)}) %all-to-all-start) | async-done | bytes 524320 | tf_op jit(solution)/shard_map/all_to_all | solution.py:106
  53.8 0.9 %copy.84 = bf16[8,4,4,16,128]{4,3,2,1,0:T(8,128)(2,1)} copy(bf16[8,4,4,16,128]{4,3,1,0,2:T(8,128)(2,1)S(1)} %bitcast.100) | data formatting | bytes 1048576 | tf_op jit(solution)/shard_map/all_to_all | solution.py:106
  (28 shorter events, 0.6 us)
Async XLA Ops:
  0.6 12.3 %copy-start = (bf16[4,8,32,256]{3,2,1,0:T(8,128)(2,1)S(1)}, bf16[4,8,32,256]{3,2,1,0:T(8,128)(2,1)}, u32[]{:S(2)}) copy-start(bf16[4,8,32,256]{3,2,1,0:T(8,128)(2,1)} %param.6) | copy-start | bytes 1572868
  0.6 11.5 %copy-start.4 = (s32[4]{0:T(128)S(1)}, s32[4]{0:T(128)}, u32[]{:S(2)}) copy-start(s32[4]{0:T(128)} %param.8) | copy-start | bytes 52
  0.7 11.5 %copy-start.5 = (s32[8]{0:T(128)S(1)}, s32[8]{0:T(128)}, u32[]{:S(2)}) copy-start(s32[8]{0:T(128)} %param.7) | copy-start | bytes 100
  0.7 11.8 %copy-start.2 = (bf16[32,108]{1,0:T(8,128)(2,1)S(1)}, bf16[32,108]{1,0:T(8,128)(2,1)}, u32[]{:S(2)}) copy-start(bf16[32,108]{1,0:T(8,128)(2,1)} %param.9) | copy-start | bytes 20740
  1.6 11.3 %collective-permute-start = (bf16[4,32,256]{2,1,0:T(8,128)(2,1)S(1)}, bf16[4,32,256]{2,1,0:T(8,128)(2,1)S(1)}, u32[]{:S(2)}, u32[]{:S(2)}) collective-permute-start(bf16[4,32,256]{2,1,0:T(8,128)(2,1)S(1)} %slice_bitcast_fusion), channel_id=1, source_target_pairs={{0,4},{4,8},{8,12},{12,16},{16,20},{20,24},{24,28},{1,5},{5,9},{9,... | collective-permute-start | bytes 196616 | tf_op jit(solution)/shard_map/ppermute | solution.py:10
  8.6 12.3 %all-to-all-start.1 = ((bf16[8,4,64,128]{3,0,1,2:T(8,128)(2,1)}), bf16[8,4,64,128]{3,0,1,2:T(8,128)(2,1)S(1)}, u32[]{:S(2)}, u32[]{:S(2)}) async-start(bf16[8,4,64,128]{3,0,1,2:T(8,128)(2,1)} %copy.85), calls=%async_computation.1 | async-start | bytes 1048576 | tf_op jit(solution)/shard_map/all_to_all | solution.py:70
  13.1 3.2 %collective-permute-start.1 = (bf16[4,9,256]{2,0,1:T(4,128)(2,1)S(1)}, bf16[4,9,256]{2,0,1:T(4,128)(2,1)S(1)}, u32[]{:S(2)}, u32[]{:S(2)}) collective-permute-start(bf16[4,9,256]{2,0,1:T(4,128)(2,1)S(1)} %bitcast.102), channel_id=1, source_target_pairs={{0,1},{1,2},{2,3},{4,5},{5,6},{6,7},{8,9},{9,10},{10,11},{12,13},{... | collective-permute-start | bytes 55304 | tf_op jit(solution)/shard_map/ppermute | solution.py:10
  17.9 0.7 %copy-start.3 = (f32[32]{0:T(128)S(1)}, f32[32]{0:T(128)}, u32[]{:S(2)}) copy-start(f32[32]{0:T(128)} %param.10) | copy-start | bytes 388
  23.2 17.4 %copy-start.1 = (bf16[32,4,16,128]{3,0,2,1:T(8,128)(2,1)S(1)}, bf16[32,4,16,128]{3,0,2,1:T(8,128)(2,1)}, u32[]{:S(2)}) copy-start(bf16[32,4,16,128]{3,0,2,1:T(8,128)(2,1)} %get-tuple-element.18) | copy-start | bytes 1572868
  24.5 4.7 %collective-permute-start.3 = (f32[36,108]{1,0:T(8,128)S(1)}, f32[36,108]{1,0:T(8,128)S(1)}, u32[]{:S(2)}, u32[]{:S(2)}) collective-permute-start(f32[36,108]{1,0:T(8,128)S(1)} %select_maximum_fusion), channel_id=1, source_target_pairs={{0,16},{4,20},{8,24},{12,28},{16,0},{20,4},{24,8},{28,12},{1,17},{... | collective-permute-start | bytes 46664 | tf_op jit(solution)/shard_map/ppermute | solution.py:21
  27.1 5.6 %collective-permute-start.4 = (f32[36,108]{1,0:T(8,128)S(1)}, f32[36,108]{1,0:T(8,128)S(1)}, u32[]{:S(2)}, u32[]{:S(2)}) collective-permute-start(f32[36,108]{1,0:T(8,128)S(1)} %select_maximum_fusion), channel_id=1, source_target_pairs={{0,24},{4,28},{8,16},{12,20},{16,8},{20,12},{24,0},{28,4},{1,25},{... | collective-permute-start | bytes 46664 | tf_op jit(solution)/shard_map/ppermute | solution.py:21
  28.5 4.3 %collective-permute-start.2 = (f32[36,108]{1,0:T(8,128)S(1)}, f32[36,108]{1,0:T(8,128)S(1)}, u32[]{:S(2)}, u32[]{:S(2)}) collective-permute-start(f32[36,108]{1,0:T(8,128)S(1)} %select_maximum_fusion), channel_id=1, source_target_pairs={{0,8},{4,12},{8,0},{12,4},{16,24},{20,28},{24,16},{28,20},{1,9},{5... | collective-permute-start | bytes 46664 | tf_op jit(solution)/shard_map/ppermute | solution.py:21
  32.8 3.8 %collective-permute-start.5 = (f32[36,108]{1,0:T(8,128)S(1)}, f32[36,108]{1,0:T(8,128)S(1)}, u32[]{:S(2)}, u32[]{:S(2)}) collective-permute-start(f32[36,108]{1,0:T(8,128)S(1)} %add_add_fusion.1), channel_id=1, source_target_pairs={{0,4},{4,0},{8,12},{12,8},{16,20},{20,16},{24,28},{28,24},{1,5},{5... | collective-permute-start | bytes 46664 | tf_op jit(solution)/shard_map/ppermute | solution.py:21
  36.6 8.4 %collective-permute-start.7 = (f32[36,108]{1,0:T(8,128)S(1)}, f32[36,108]{1,0:T(8,128)S(1)}, u32[]{:S(2)}, u32[]{:S(2)}) collective-permute-start(f32[36,108]{1,0:T(8,128)S(1)} %add.126), channel_id=1, source_target_pairs={{0,2},{1,3},{2,0},{3,1},{4,6},{5,7},{6,4},{7,5},{8,10},{9,11},{10,... | collective-permute-start | bytes 46664 | tf_op jit(solution)/shard_map/ppermute | solution.py:21
  40.4 4.7 %collective-permute-start.8 = (f32[36,108]{1,0:T(8,128)S(1)}, f32[36,108]{1,0:T(8,128)S(1)}, u32[]{:S(2)}, u32[]{:S(2)}) collective-permute-start(f32[36,108]{1,0:T(8,128)S(1)} %add.126), channel_id=1, source_target_pairs={{0,3},{1,2},{2,1},{3,0},{4,7},{5,6},{6,5},{7,4},{8,11},{9,10},{10,... | collective-permute-start | bytes 46664 | tf_op jit(solution)/shard_map/ppermute | solution.py:21
  40.4 4.7 %collective-permute-start.6 = (f32[36,108]{1,0:T(8,128)S(1)}, f32[36,108]{1,0:T(8,128)S(1)}, u32[]{:S(2)}, u32[]{:S(2)}) collective-permute-start(f32[36,108]{1,0:T(8,128)S(1)} %add.126), channel_id=1, source_target_pairs={{0,1},{1,0},{2,3},{3,2},{4,5},{5,4},{6,7},{7,6},{8,9},{9,8},{10,11... | collective-permute-start | bytes 46664 | tf_op jit(solution)/shard_map/ppermute | solution.py:21
  41.6 12.3 %all-to-all-start = ((bf16[32,4,16,128]{3,2,1,0:T(8,128)(2,1)}), bf16[32,4,16,128]{3,2,1,0:T(8,128)(2,1)S(1)}, u32[]{:S(2)}, u32[]{:S(2)}) async-start(bf16[32,4,16,128]{3,2,1,0:T(8,128)(2,1)} %copy.83), calls=%async_computation | async-start | bytes 1048576 | tf_op jit(solution)/shard_map/all_to_all | solution.py:106

commit v21 on v8

--- a/solution.py
+++ b/solution.py
@@ -14,11 +14,15 @@
     size = lax.axis_size(axis)
     if size & (size - 1):
         return lax.psum(value, axis)
-    step = 1
-    while step < size:
-        swap = [(i, i ^ step) for i in range(size)]
-        value = value + lax.ppermute(value, axis, swap)
-        step *= 2
+    bits = size.bit_length() - 1
+    base = bits % 2
+    if base:
+        value = value + lax.ppermute(value, axis, [(i, i ^ 1) for i in range(size)])
+    while base < bits:
+        spans = [(1 << base) * t for t in range(1, 4)]
+        got = [lax.ppermute(value, axis, [(i, i ^ t) for i in range(size)]) for t in spans]
+        value = (value + got[0]) + (got[1] + got[2])
+        base += 2
     return value
 
 

time: 47.7 us -> 50.1 us (1.050)
  waiting for transfers between devices: 9.02 us -> 11.2 us
    ppermute x5 -> x7, waiting for transfers between devices: 7.12 us -> 9.28 us  [the longest x6 7.09 us: butterfly_sum(): lax.ppermute(value, axis, [(i, i ^ t) for i in range(size)])]
    ppermute x5 -> x7, starting transfers between devices: 7.93 us -> 8.12 us  [the longest x6 6.56 us: butterfly_sum(): lax.ppermute(value, axis, [(i, i ^ t) for i in range(size)])]
  transfers between devices with their start and end apart: 9 -> 11, of which waited for: 6 -> 5; matrix products, arithmetic and copies ran while one was open for 17% -> 16% of each run, Pallas kernels for 0% -> 0%
where the time goes in v21:
time: 50.1 us; the launch traced here: 49.7 us
  starting transfers between devices  23.9 us (48%)
  waiting for transfers between devices  11.2 us (22%)
  local copies, waits for them, and re-layouts  7.6 us (15%)
  matrix products  5.23 us (10%)
  between operations  0.99 us (2%)
  other arithmetic  0.84 us (2%)
    ppermute x2, starting transfers between devices, from_behind(): return lax.ppermute(block, axis, route)  7.21 us
    ppermute x6, waiting for transfers between devices, butterfly_sum(): lax.ppermute(value, axis, [(i, i ^ t) for i in range(size)])  7.09 us
    ppermute x6, starting transfers between devices, butterfly_sum(): lax.ppermute(value, axis, [(i, i ^ t) for i in range(size)])  6.56 us
    all_to_all x1, starting transfers between devices, local(): lax.all_to_all(stem_local, 'gy', split_axis=0, concat_axis=2, tiled=True)  5.07 us
    all_to_all x1, starting transfers between devices, local(): lax.all_to_all(grad_out, 'gy', split_axis=2, concat_axis=0, tiled=True)  3.47 us
    unnamed x27, local copies, waits for them, and re-layouts  2.99 us
    dot_general x3, matrix products, local(): jnp.einsum('ok,kpqr->opqr', kernel[:, :, off_z], part, preferred_element_...  2.78 us
    ppermute x1, waiting for transfers between devices, butterfly_sum(): value = value + lax.ppermute(value, axis, [(i, i ^ 1) for i in range(size)])  2.19 us
  transfers between devices with their start and end apart: 11, of which 5 were waited for; matrix products, arithmetic and copies ran while one was open for 16% of the time, Pallas kernels for 0%

profile of v21, /device:TPU:0, one launch (start us, length us, event | category | flops | bytes accessed | tf_op | source)
XLA Modules:
  0.0 49.7 jit_solution(4634199698186086517)
XLA Ops:
  0.6 0.0 copy-start
  0.6 0.0 copy-start.5
  0.7 0.0 copy-start.6
  0.7 0.0 copy-start.3
  0.7 0.9 %slice_bitcast_fusion = bf16[4,32,256]{2,1,0:T(8,128)(2,1)S(1)} fusion(bf16[4,8,32,256]{3,2,1,0:T(8,128)(2,1)} %param.6), kind=kLoop, calls=%fused_computation.43 | loop fusion | bytes 131072 | tf_op jit(solution)/shard_map/squeeze | solution.py:72
  1.6 4.9 %collective-permute-start = (bf16[4,32,256]{2,1,0:T(8,128)(2,1)S(1)}, bf16[4,32,256]{2,1,0:T(8,128)(2,1)S(1)}, u32[]{:S(2)}, u32[]{:S(2)}) collective-permute-start(bf16[4,32,256]{2,1,0:T(8,128)(2,1)S(1)} %slice_bitcast_fusion), channel_id=1, source_target_pairs={{0,4},{4,8},{8,12},{12,16},{16,20},{20,24},{24,28},{1,5},{5,9},{9,... | collective-permute-start | bytes 196616 | tf_op jit(solution)/shard_map/ppermute | solution.py:10
  6.4 2.2 %copy.89 = bf16[8,4,64,128]{3,0,1,2:T(8,128)(2,1)} copy(bf16[8,4,64,128]{3,2,1,0:T(8,128)(2,1)} %param.11) | data formatting | bytes 1048576 | tf_op args[5]
  8.6 3.5 %all-to-all-start.1 = ((bf16[8,4,64,128]{3,0,1,2:T(8,128)(2,1)}), bf16[8,4,64,128]{3,0,1,2:T(8,128)(2,1)S(1)}, u32[]{:S(2)}, u32[]{:S(2)}) async-start(bf16[8,4,64,128]{3,0,1,2:T(8,128)(2,1)} %copy.89), calls=%async_computation.1 | async-start | bytes 1048576 | tf_op jit(solution)/shard_map/all_to_all | solution.py:69
  12.1 0.0 copy-done.5
  12.2 0.0 copy-done.6
  12.2 0.1 fusion.51
  12.3 0.1 fusion.41
  12.4 0.0 copy-done.3
  12.4 0.1 copy.81
  12.6 0.1 fusion.53
  12.7 0.1 broadcast_and_fusion
  12.8 0.1 fusion.55
  12.9 0.0 collective-permute-done
  12.9 0.1 select_select_fusion
  13.1 2.4 %collective-permute-start.1 = (bf16[4,9,256]{2,0,1:T(4,128)(2,1)S(1)}, bf16[4,9,256]{2,0,1:T(4,128)(2,1)S(1)}, u32[]{:S(2)}, u32[]{:S(2)}) collective-permute-start(bf16[4,9,256]{2,0,1:T(4,128)(2,1)S(1)} %bitcast.102), channel_id=1, source_target_pairs={{0,1},{1,2},{2,3},{4,5},{5,6},{6,7},{8,9},{9,10},{10,11},{12,13},{... | collective-permute-start | bytes 55304 | tf_op jit(solution)/shard_map/ppermute | solution.py:10
  15.5 0.1 copy.102
  15.6 0.1 copy.104
  15.7 0.1 copy.106
  15.8 0.5 %collective-permute-done.1 = bf16[4,9,256]{2,0,1:T(4,128)(2,1)S(1)} collective-permute-done((bf16[4,9,256]{2,0,1:T(4,128)(2,1)S(1)}, bf16[4,9,256]{2,0,1:T(4,128)(2,1)S(1)}, u32[]{:S(2)}, u32[]{:S(2)}) %collective-permute-start.1) | collective-permute-done | bytes 18464 | tf_op jit(solution)/shard_map/ppermute | solution.py:10
  16.3 1.1 %convolution_convert_fusion = bf16[4,9,48,384]{3,2,1,0:T(8,128)(2,1)S(1)} fusion(bf16[4,9,32,256]{3,2,1,0:T(8,128)(2,1)S(1)} %select_select_fusion, pred[33]{0:T(512)(128)(4,1)S(1)} %get-tuple-element.7, pred[33]{0:T(512)(128)(4,1)S(1)} %get-tuple-element.6, bf16[4,9,256]{2,1,0:T(8,128)(2,1)S(1)} %copy.78, s32[384]{0:T(512)S(1)} %fusion.45, ...), kind=kOutput, calls=%fused_computation | convolution fusion | flops 279191040 | bytes 1940130 | tf_op jit(solution)/shard_map/cxjy,cxyk->cxjk/dot_general | solution.py:85
  17.7 0.2 copy.79
  17.9 0.0 copy-start.4
  18.0 0.5 %fusion.69 = (bf16[36,4,16,128]{3,2,1,0:T(8,128)(2,1)S(1)}, bf16[36,4,16,128]{3,2,1,0:T(8,128)(2,1)S(1)}, bf16[36,4,16,128]{3,2,1,0:T(8,128)(2,1)S(1)}) fusion(bf16[36,4,16,384]{3,2,1,0:T(8,128)(2,1)S(1)} %bitcast.99), kind=kLoop, calls=%fused_computation.116 | loop fusion | bytes 3538944 | tf_op jit(solution)/shard_map/slice | solution.py:95
  18.5 0.1 copy-done.4
  18.6 0.4 convolution_add_fusion.2
  19.1 0.5 convolution_add_fusion.1
  19.5 1.4 %all-to-all-done.1 = bf16[8,4,64,128]{3,0,1,2:T(8,128)(2,1)S(1)} async-done(((bf16[8,4,64,128]{3,0,1,2:T(8,128)(2,1)}), bf16[8,4,64,128]{3,0,1,2:T(8,128)(2,1)S(1)}, u32[]{:S(2)}, u32[]{:S(2)}) %all-to-all-start.1) | async-done | bytes 524320 | tf_op jit(solution)/shard_map/all_to_all | solution.py:69
  20.9 1.9 %fusion.67 = (f32[32]{0:T(128)S(1)}, bf16[32,4,16,128]{3,0,2,1:T(8,128)(2,1)S(1)}, bf16[32,4,16,128]{3,0,2,1:T(8,128)(2,1)}) fusion(pred[4,16]{1,0:T(4,128)(4,1)S(1)} %broadcast_and_fusion, f32[4,16,128,32]{2,3,1,0:T(8,128)S(1)} %convolution_add_fusion.1, bf16[32,36,1]{1,0,2:T(8,128)(2,1)S(1)} %copy.106, ...), kind=kOutput, calls=%fused_computation.115 | convolution fusion | flops 23592928 | bytes 3213760 | tf_op jit(solution)/shard_map/ok,kpqr->opqr/dot_general | solution.py:96
  22.8 0.5 convolution_bitcast_fusion
  23.2 0.0 copy-start.1
  23.2 0.5 convolution_bitcast_fusion.1
  23.7 0.5 convolution_bitcast_fusion.2
  24.2 0.1 copy.93
  24.3 0.1 copy.91
  24.4 0.1 copy.92
  24.5 0.1 pad_maximum_fusion.1
  24.6 1.6 %collective-permute-start.2 = (f32[32,109]{1,0:T(8,128)S(1)}, f32[32,109]{1,0:T(8,128)S(1)}, u32[]{:S(2)}, u32[]{:S(2)}) collective-permute-start(f32[32,109]{1,0:T(8,128)S(1)} %pad_maximum_fusion.1), channel_id=1, source_target_pairs={{0,4},{4,0},{8,12},{12,8},{16,20},{20,16},{24,28},{28,24},{1,5},{5... | collective-permute-start | bytes 41864 | tf_op jit(solution)/shard_map/ppermute | solution.py:20
  26.1 2.2 %collective-permute-done.2 = f32[32,109]{1,0:T(8,128)S(1)} collective-permute-done((f32[32,109]{1,0:T(8,128)S(1)}, f32[32,109]{1,0:T(8,128)S(1)}, u32[]{:S(2)}, u32[]{:S(2)}) %collective-permute-start.2) | collective-permute-done | bytes 13984 | tf_op jit(solution)/shard_map/ppermute | solution.py:20
  28.3 0.1 fusion.74
  28.4 2.6 %collective-permute-start.4 = (f32[32,109]{1,0:T(8,128)S(1)}, f32[32,109]{1,0:T(8,128)S(1)}, u32[]{:S(2)}, u32[]{:S(2)}) collective-permute-start(f32[32,109]{1,0:T(8,128)S(1)} %fusion.74), channel_id=1, source_target_pairs={{0,16},{4,20},{8,24},{12,28},{16,0},{20,4},{24,8},{28,12},{1,17},{... | collective-permute-start | bytes 41864 | tf_op jit(solution)/shard_map/ppermute | solution.py:23
  31.0 1.3 %collective-permute-start.5 = (f32[32,109]{1,0:T(8,128)S(1)}, f32[32,109]{1,0:T(8,128)S(1)}, u32[]{:S(2)}, u32[]{:S(2)}) collective-permute-start(f32[32,109]{1,0:T(8,128)S(1)} %fusion.74), channel_id=1, source_target_pairs={{0,24},{4,28},{8,16},{12,20},{16,8},{20,12},{24,0},{28,4},{1,25},{... | collective-permute-start | bytes 41864 | tf_op jit(solution)/shard_map/ppermute | solution.py:23
  32.3 0.2 collective-permute-start.3
  32.6 0.0 copy-done.1
  32.6 1.0 %copy.87 = bf16[32,4,16,128]{3,2,1,0:T(8,128)(2,1)} copy(bf16[32,4,16,128]{3,0,2,1:T(8,128)(2,1)S(1)} %copy-done.1) | data formatting | bytes 1048576 | tf_op jit(solution)/shard_map/convert_element_type | solution.py:100
  33.6 5.1 %all-to-all-start = ((bf16[32,4,16,128]{3,2,1,0:T(8,128)(2,1)}), bf16[32,4,16,128]{3,2,1,0:T(8,128)(2,1)S(1)}, u32[]{:S(2)}, u32[]{:S(2)}) async-start(bf16[32,4,16,128]{3,2,1,0:T(8,128)(2,1)} %copy.87), calls=%async_computation | async-start | bytes 1048576 | tf_op jit(solution)/shard_map/all_to_all | solution.py:105
  38.6 0.0 collective-permute-done.4
  38.6 0.0 collective-permute-done.5
  38.6 0.0 collective-permute-done.3
  38.7 1.8 %collective-permute-start.8 = (f32[32,109]{1,0:T(8,128)S(1)}, f32[32,109]{1,0:T(8,128)S(1)}, u32[]{:S(2)}, u32[]{:S(2)}) collective-permute-start(f32[32,109]{1,0:T(8,128)S(1)} %add_add_fusion), channel_id=1, source_target_pairs={{0,3},{1,2},{2,1},{3,0},{4,7},{5,6},{6,5},{7,4},{8,11},{9,10},{10,... | collective-permute-start | bytes 41864 | tf_op jit(solution)/shard_map/ppermute | solution.py:23
  40.5 0.6 %collective-permute-start.7 = (f32[32,109]{1,0:T(8,128)S(1)}, f32[32,109]{1,0:T(8,128)S(1)}, u32[]{:S(2)}, u32[]{:S(2)}) collective-permute-start(f32[32,109]{1,0:T(8,128)S(1)} %add_add_fusion), channel_id=1, source_target_pairs={{0,2},{1,3},{2,0},{3,1},{4,6},{5,7},{6,4},{7,5},{8,10},{9,11},{10,... | collective-permute-start | bytes 41864 | tf_op jit(solution)/shard_map/ppermute | solution.py:23
  41.0 0.0 collective-permute-start.6
  41.1 6.0 %collective-permute-done.8 = f32[32,109]{1,0:T(8,128)S(1)} collective-permute-done((f32[32,109]{1,0:T(8,128)S(1)}, f32[32,109]{1,0:T(8,128)S(1)}, u32[]{:S(2)}, u32[]{:S(2)}) %collective-permute-start.8) | collective-permute-done | bytes 13984 | tf_op jit(solution)/shard_map/ppermute | solution.py:23
  47.0 1.1 %collective-permute-done.7 = f32[32,109]{1,0:T(8,128)S(1)} collective-permute-done((f32[32,109]{1,0:T(8,128)S(1)}, f32[32,109]{1,0:T(8,128)S(1)}, u32[]{:S(2)}, u32[]{:S(2)}) %collective-permute-start.7) | collective-permute-done | bytes 13984 | tf_op jit(solution)/shard_map/ppermute | solution.py:23
  48.1 0.0 collective-permute-done.6
  48.1 0.0 copy-start.2
  48.2 0.7 %slice_reduce_fusion = f32[8]{0:T(128)} fusion(f32[8,109]{1,0:T(8,128)S(1)} %fusion.35), kind=kLoop, calls=%fused_computation.56 | loop fusion | bytes 64 | tf_op jit(solution)/shard_map/slice | solution.py:116
  48.9 0.0 all-to-all-done
  48.9 0.9 %copy.88 = bf16[8,4,4,16,128]{4,3,2,1,0:T(8,128)(2,1)} copy(bf16[8,4,4,16,128]{4,3,1,0,2:T(8,128)(2,1)S(1)} %bitcast.100) | data formatting | bytes 1048576 | tf_op jit(solution)/shard_map/all_to_all | solution.py:105
  49.7 0.0 copy-done.2
  (26 shorter events, 0.5 us)
Async XLA Ops:
  0.6 12.3 %copy-start = (bf16[4,8,32,256]{3,2,1,0:T(8,128)(2,1)S(1)}, bf16[4,8,32,256]{3,2,1,0:T(8,128)(2,1)}, u32[]{:S(2)}) copy-start(bf16[4,8,32,256]{3,2,1,0:T(8,128)(2,1)} %param.6) | copy-start | bytes 1572868
  0.6 11.5 %copy-start.5 = (s32[4]{0:T(128)S(1)}, s32[4]{0:T(128)}, u32[]{:S(2)}) copy-start(s32[4]{0:T(128)} %param.8) | copy-start | bytes 52
  0.7 11.5 %copy-start.6 = (s32[8]{0:T(128)S(1)}, s32[8]{0:T(128)}, u32[]{:S(2)}) copy-start(s32[8]{0:T(128)} %param.7) | copy-start | bytes 100
  0.7 11.8 %copy-start.3 = (bf16[32,108]{1,0:T(8,128)(2,1)S(1)}, bf16[32,108]{1,0:T(8,128)(2,1)}, u32[]{:S(2)}) copy-start(bf16[32,108]{1,0:T(8,128)(2,1)} %param.9) | copy-start | bytes 20740
  1.6 11.3 %collective-permute-start = (bf16[4,32,256]{2,1,0:T(8,128)(2,1)S(1)}, bf16[4,32,256]{2,1,0:T(8,128)(2,1)S(1)}, u32[]{:S(2)}, u32[]{:S(2)}) collective-permute-start(bf16[4,32,256]{2,1,0:T(8,128)(2,1)S(1)} %slice_bitcast_fusion), channel_id=1, source_target_pairs={{0,4},{4,8},{8,12},{12,16},{16,20},{20,24},{24,28},{1,5},{5,9},{9,... | collective-permute-start | bytes 196616 | tf_op jit(solution)/shard_map/ppermute | solution.py:10
  8.6 12.3 %all-to-all-start.1 = ((bf16[8,4,64,128]{3,0,1,2:T(8,128)(2,1)}), bf16[8,4,64,128]{3,0,1,2:T(8,128)(2,1)S(1)}, u32[]{:S(2)}, u32[]{:S(2)}) async-start(bf16[8,4,64,128]{3,0,1,2:T(8,128)(2,1)} %copy.89), calls=%async_computation.1 | async-start | bytes 1048576 | tf_op jit(solution)/shard_map/all_to_all | solution.py:69
  13.1 3.2 %collective-permute-start.1 = (bf16[4,9,256]{2,0,1:T(4,128)(2,1)S(1)}, bf16[4,9,256]{2,0,1:T(4,128)(2,1)S(1)}, u32[]{:S(2)}, u32[]{:S(2)}) collective-permute-start(bf16[4,9,256]{2,0,1:T(4,128)(2,1)S(1)} %bitcast.102), channel_id=1, source_target_pairs={{0,1},{1,2},{2,3},{4,5},{5,6},{6,7},{8,9},{9,10},{10,11},{12,13},{... | collective-permute-start | bytes 55304 | tf_op jit(solution)/shard_map/ppermute | solution.py:10
  17.9 0.7 %copy-start.4 = (f32[32]{0:T(128)S(1)}, f32[32]{0:T(128)}, u32[]{:S(2)}) copy-start(f32[32]{0:T(128)} %param.10) | copy-start | bytes 388
  23.2 9.3 %copy-start.1 = (bf16[32,4,16,128]{3,0,2,1:T(8,128)(2,1)S(1)}, bf16[32,4,16,128]{3,0,2,1:T(8,128)(2,1)}, u32[]{:S(2)}) copy-start(bf16[32,4,16,128]{3,0,2,1:T(8,128)(2,1)} %get-tuple-element.15) | copy-start | bytes 1572868
  24.6 3.7 %collective-permute-start.2 = (f32[32,109]{1,0:T(8,128)S(1)}, f32[32,109]{1,0:T(8,128)S(1)}, u32[]{:S(2)}, u32[]{:S(2)}) collective-permute-start(f32[32,109]{1,0:T(8,128)S(1)} %pad_maximum_fusion.1), channel_id=1, source_target_pairs={{0,4},{4,0},{8,12},{12,8},{16,20},{20,16},{24,28},{28,24},{1,5},{5... | collective-permute-start | bytes 41864 | tf_op jit(solution)/shard_map/ppermute | solution.py:20
  28.4 10.2 %collective-permute-start.4 = (f32[32,109]{1,0:T(8,128)S(1)}, f32[32,109]{1,0:T(8,128)S(1)}, u32[]{:S(2)}, u32[]{:S(2)}) collective-permute-start(f32[32,109]{1,0:T(8,128)S(1)} %fusion.74), channel_id=1, source_target_pairs={{0,16},{4,20},{8,24},{12,28},{16,0},{20,4},{24,8},{28,12},{1,17},{... | collective-permute-start | bytes 41864 | tf_op jit(solution)/shard_map/ppermute | solution.py:23
  31.0 7.7 %collective-permute-start.5 = (f32[32,109]{1,0:T(8,128)S(1)}, f32[32,109]{1,0:T(8,128)S(1)}, u32[]{:S(2)}, u32[]{:S(2)}) collective-permute-start(f32[32,109]{1,0:T(8,128)S(1)} %fusion.74), channel_id=1, source_target_pairs={{0,24},{4,28},{8,16},{12,20},{16,8},{20,12},{24,0},{28,4},{1,25},{... | collective-permute-start | bytes 41864 | tf_op jit(solution)/shard_map/ppermute | solution.py:23
  32.3 6.3 %collective-permute-start.3 = (f32[32,109]{1,0:T(8,128)S(1)}, f32[32,109]{1,0:T(8,128)S(1)}, u32[]{:S(2)}, u32[]{:S(2)}) collective-permute-start(f32[32,109]{1,0:T(8,128)S(1)} %fusion.74), channel_id=1, source_target_pairs={{0,8},{4,12},{8,0},{12,4},{16,24},{20,28},{24,16},{28,20},{1,9},{5... | collective-permute-start | bytes 41864 | tf_op jit(solution)/shard_map/ppermute | solution.py:23
  33.6 15.3 %all-to-all-start = ((bf16[32,4,16,128]{3,2,1,0:T(8,128)(2,1)}), bf16[32,4,16,128]{3,2,1,0:T(8,128)(2,1)S(1)}, u32[]{:S(2)}, u32[]{:S(2)}) async-start(bf16[32,4,16,128]{3,2,1,0:T(8,128)(2,1)} %copy.87), calls=%async_computation | async-start | bytes 1048576 | tf_op jit(solution)/shard_map/all_to_all | solution.py:105
  38.7 8.4 %collective-permute-start.8 = (f32[32,109]{1,0:T(8,128)S(1)}, f32[32,109]{1,0:T(8,128)S(1)}, u32[]{:S(2)}, u32[]{:S(2)}) collective-permute-start(f32[32,109]{1,0:T(8,128)S(1)} %add_add_fusion), channel_id=1, source_target_pairs={{0,3},{1,2},{2,1},{3,0},{4,7},{5,6},{6,5},{7,4},{8,11},{9,10},{10,... | collective-permute-start | bytes 41864 | tf_op jit(solution)/shard_map/ppermute | solution.py:23
  40.5 7.7 %collective-permute-start.7 = (f32[32,109]{1,0:T(8,128)S(1)}, f32[32,109]{1,0:T(8,128)S(1)}, u32[]{:S(2)}, u32[]{:S(2)}) collective-permute-start(f32[32,109]{1,0:T(8,128)S(1)} %add_add_fusion), channel_id=1, source_target_pairs={{0,2},{1,3},{2,0},{3,1},{4,6},{5,7},{6,4},{7,5},{8,10},{9,11},{10,... | collective-permute-start | bytes 41864 | tf_op jit(solution)/shard_map/ppermute | solution.py:23
  41.0 7.1 %collective-permute-start.6 = (f32[32,109]{1,0:T(8,128)S(1)}, f32[32,109]{1,0:T(8,128)S(1)}, u32[]{:S(2)}, u32[]{:S(2)}) collective-permute-start(f32[32,109]{1,0:T(8,128)S(1)} %add_add_fusion), channel_id=1, source_target_pairs={{0,1},{1,0},{2,3},{3,2},{4,5},{5,4},{6,7},{7,6},{8,9},{9,8},{10,11... | collective-permute-start | bytes 41864 | tf_op jit(solution)/shard_map/ppermute | solution.py:23
  48.1 1.6 %copy-start.2 = (f32[8,109]{1,0:T(8,128)}, f32[8,109]{1,0:T(8,128)S(1)}, u32[]{:S(2)}) copy-start(f32[8,109]{1,0:T(8,128)S(1)} %fusion.35) | copy-start | bytes 10468
